TPU v7x, 512 devices: a whole 4x8x8 slice. The times are simulated.
512 devices in a mesh: dp: 8 (over z), expert: 16 (over y, core), etp: 4 (over x).
Axes of the slice: x: 4, y: 8, z: 8, core: 2. Of those that a mesh axis runs over, the one named last changes fastest.
Arguments:
- tokens: bfloat16 [3072, 4096], P(('dp', 'expert')), may hold values from -6 to 6
- cotangent: bfloat16 [3072, 4096], P(('dp', 'expert')), may hold values from -3 to 3
- route_weights: float32 [3072, 8], P(('dp', 'expert')), may hold values from 0.05 to 0.3
- expert_ids: int32 [3072, 8], P(('dp', 'expert')), may hold values from 0 to 15, as said below
- w_gate: bfloat16 [16, 1536, 4096], P('expert', 'etp', 'dp'), may hold values from -0.09375 to 0.09375
- w_up: bfloat16 [16, 1536, 4096], P('expert', 'etp', 'dp'), may hold values from -0.09375 to 0.09375
- w_down: bfloat16 [16, 1536, 4096], P('expert', 'etp', 'dp'), may hold values from -0.15625 to 0.15625
Outputs:
- mixed: bfloat16 [3072, 4096], P(('dp', 'expert'), 'etp')
- grad_tokens: bfloat16 [3072, 4096], P(('dp', 'expert'), 'etp')
- grad_gate: float32 [16, 1536, 4096], P('expert', 'etp', 'dp')
Inputs may be any that keep to these rules, and one draw needn't show every extreme that they name: `expert_ids`: each row names 8 different experts. Within each aligned block of 24 rows no expert is named by more than 16 rows; in every run of 16 consecutive blocks starting at a multiple of 16, one expert is named by exactly 16 rows of every block.
All inputs are finite; a program needn't handle non-finite values.
Results may differ from a plain program's by a relative error of at most 0.012.
Values may be sent and summed in bfloat16 or wider, within the bound.
No kernel may reach another device: no remote copies, remote signals or barrier semaphores. Data moves between devices by JAX's collectives and lax.ppermute only.
A program may use at most 64 MiB of HBM per device.

v0:
```python
import jax
import jax.numpy as jnp
from jax import lax
from jax.sharding import PartitionSpec as P


def on_device(tokens, cotangent, route_weights, expert_ids, w_gate, w_up, w_down):
    tok_count, model_width = tokens.shape
    top_count = expert_ids.shape[1]
    experts = lax.axis_size("expert")
    capacity = tok_count // experts * top_count + min(top_count, tok_count % experts)
    slot_rows = experts * capacity
    named_count = jnp.sum(
        (expert_ids[:, :, None] == jnp.arange(experts, dtype=jnp.int32)).astype(jnp.int32), axis=1
    )
    before = jnp.cumsum(named_count, axis=0) - named_count
    position = jnp.take_along_axis(before, expert_ids, axis=1)
    slot_index = (expert_ids * capacity + position).reshape(-1)
    copies = jnp.broadcast_to(tokens[:, None, :], (tok_count, top_count, model_width)).reshape(
        -1, model_width
    )
    scaled = (
        (route_weights[:, :, None] * cotangent[:, None, :].astype(jnp.float32))
        .astype(jnp.bfloat16)
        .reshape(-1, model_width)
    )
    empty_slots = jnp.zeros((slot_rows, model_width), jnp.bfloat16)
    send_rows = empty_slots.at[slot_index].set(copies).reshape(experts, capacity, model_width)
    send_grads = empty_slots.at[slot_index].set(scaled).reshape(experts, capacity, model_width)
    recv_rows, recv_grads = (
        lax.all_to_all(send_rows, "expert", split_axis=0, concat_axis=0, tiled=True),
        lax.all_to_all(send_grads, "expert", split_axis=0, concat_axis=0, tiled=True),
    )
    flat_rows = recv_rows.reshape(slot_rows, model_width)
    flat_grads = recv_grads.reshape(slot_rows, model_width)
    gate_full, up_full, down_full = (
        lax.all_gather(w_gate[0], "dp", axis=1, tiled=True),
        lax.all_gather(w_up[0], "dp", axis=1, tiled=True),
        lax.all_gather(w_down[0], "dp", axis=1, tiled=True),
    )
    contract_last = (((1,), (1,)), ((), ()))
    gate_value = lax.dot_general(
        flat_rows, gate_full, contract_last, preferred_element_type=jnp.float32
    )
    up_value = lax.dot_general(
        flat_rows, up_full, contract_last, preferred_element_type=jnp.float32
    )
    sigmoid_gate = jax.nn.sigmoid(gate_value)
    active = gate_value * sigmoid_gate
    hidden = (active * up_value).astype(jnp.bfloat16)
    mixed_slots = jnp.dot(hidden, down_full, preferred_element_type=jnp.float32).astype(
        jnp.bfloat16
    )
    d_hidden = lax.dot_general(
        flat_grads, down_full, contract_last, preferred_element_type=jnp.float32
    )
    d_gate = (
        d_hidden * up_value * sigmoid_gate * (1.0 + gate_value * (1.0 - sigmoid_gate))
    ).astype(jnp.bfloat16)
    d_up = (d_hidden * active).astype(jnp.bfloat16)
    input_slots = (
        jnp.dot(d_gate, gate_full, preferred_element_type=jnp.float32)
        + jnp.dot(d_up, up_full, preferred_element_type=jnp.float32)
    ).astype(jnp.bfloat16)
    weight_grads = lax.psum_scatter(
        lax.dot_general(
            flat_rows, d_gate, (((0,), (0,)), ((), ())), preferred_element_type=jnp.float32
        ).astype(jnp.bfloat16),
        "dp",
        scatter_dimension=0,
        tiled=True,
    ).astype(jnp.float32)
    grad_gate = jnp.transpose(weight_grads)[None]
    back_mixed, back_input = (
        lax.all_to_all(
            mixed_slots.reshape(experts, capacity, model_width),
            "expert",
            split_axis=0,
            concat_axis=0,
            tiled=True,
        ),
        lax.all_to_all(
            input_slots.reshape(experts, capacity, model_width),
            "expert",
            split_axis=0,
            concat_axis=0,
            tiled=True,
        ),
    )
    token_mixed = back_mixed.reshape(slot_rows, model_width)[slot_index].reshape(
        tok_count, top_count, model_width
    )
    token_input = back_input.reshape(slot_rows, model_width)[slot_index].reshape(
        tok_count, top_count, model_width
    )
    mixed_part = jnp.sum(route_weights[:, :, None] * token_mixed.astype(jnp.float32), axis=1)
    input_part = jnp.sum(token_input.astype(jnp.float32), axis=1)
    mixed, grad_tokens = (
        lax.psum_scatter(
            mixed_part.astype(jnp.bfloat16), "etp", scatter_dimension=1, tiled=True
        ).astype(jnp.float32),
        lax.psum_scatter(
            input_part.astype(jnp.bfloat16), "etp", scatter_dimension=1, tiled=True
        ).astype(jnp.float32),
    )
    return (mixed.astype(jnp.bfloat16), grad_tokens.astype(jnp.bfloat16), grad_gate)


def solution(mesh):
    in_specs = (
        P(("dp", "expert"), None),
        P(("dp", "expert"), None),
        P(("dp", "expert"), None),
        P(("dp", "expert"), None),
        P("expert", "etp", "dp"),
        P("expert", "etp", "dp"),
        P("expert", "etp", "dp"),
    )
    out_specs = (P(("dp", "expert"), "etp"), P(("dp", "expert"), "etp"), P("expert", "etp", "dp"))
    return jax.shard_map(
        on_device, mesh=mesh, in_specs=in_specs, out_specs=out_specs, check_vma=False
    )
```

profile of v0, /device:TPU:1, one launch (start us, length us, event | category | flops | bytes accessed | tf_op | source)
XLA Modules:
  0.0 310.7 jit_solution(12427213311101825373)
XLA Ops:
  7.2 0.7 all-gather.9.cloned.1.call-update
  8.0 0.7 all-gather.11.cloned.1.call-update
  8.7 0.8 copy.22
  9.4 0.7 convert_reduce_fusion
  10.4 1.6 gather_fusion.2
  12.1 0.1 reshape.88
  12.2 4.4 %scatter_custom_fusion = bf16[256,4096]{1,0:T(8,128)(2,1)} fusion(s32[192]{0:T(256)S(1)} %bitcast.61, bf16[]{:T(256)} %constant.10.clone.1, bf16[24,4096]{1,0:T(8,128)(2,1)S(1)} %copy-done), kind=kCustom, calls=%fused_computation.25 | custom fusion | bytes 2293762 | tf_op jit(solution)/shard_map/scatter | solution.py:28
  16.6 10.5 %all-to-all-start = ((bf16[16,16,4096]{2,1,0:T(8,128)(2,1)}), bf16[16,16,4096]{2,1,0:T(8,128)(2,1)S(1)}, u32[]{:S(2)}, u32[]{:S(2)}) async-start(bf16[16,16,4096]{2,1,0:T(8,128)(2,1)} %bitcast.59), calls=%async_computation | async-start | bytes 4194304 | tf_op jit(solution)/shard_map/all_to_all | solution.py:31
  27.1 0.7 all-gather.7.cloned.1.call-update
  28.0 4.3 %scatter_custom_fusion.1 = bf16[256,4096]{1,0:T(8,128)(2,1)} fusion(s32[192]{0:T(256)S(1)} %bitcast.62, f32[24,4096]{1,0:T(8,128)S(1)} %convert_element_type.51, f32[192]{0:T(256)S(1)} %mul.59, bf16[]{:T(256)} %constant.10.clone.1), kind=kCustom, calls=%fused_computation.23 | custom fusion | flops 1572864 | bytes 2491394 | tf_op jit(solution)/shard_map/scatter | solution.py:29
  32.4 43.7 %all-to-all-done = bf16[16,16,4096]{2,1,0:T(8,128)(2,1)S(1)} async-done(((bf16[16,16,4096]{2,1,0:T(8,128)(2,1)}), bf16[16,16,4096]{2,1,0:T(8,128)(2,1)S(1)}, u32[]{:S(2)}, u32[]{:S(2)}) %all-to-all-start) | async-done | bytes 2097184 | tf_op jit(solution)/shard_map/all_to_all | solution.py:31
  76.1 5.0 %all-to-all-start.2 = ((bf16[16,16,4096]{2,1,0:T(8,128)(2,1)}), bf16[16,16,4096]{2,1,0:T(8,128)(2,1)}, u32[]{:S(2)}, u32[]{:S(2)}) async-start(bf16[16,16,4096]{2,1,0:T(8,128)(2,1)} %bitcast.60), calls=%async_computation.3 | async-start | bytes 4194304 | tf_op jit(solution)/shard_map/all_to_all | solution.py:32
  81.1 3.9 %fusion.7 = f32[256,384]{1,0:T(8,128)} fusion(bf16[256,4096]{1,0:T(8,128)(2,1)S(1)} %bitcast.54, bf16[1,384,4096]{2,1,0:T(8,128)(2,1)} %all-gather.9.cloned.1.call-done), kind=kOutput, calls=%fused_computation.17 | convolution fusion | flops 805306368 | bytes 5636096 | tf_op jit(solution)/shard_map/dot_general | solution.py:45
  85.0 45.1 %all-to-all-done.2 = bf16[16,16,4096]{2,1,0:T(8,128)(2,1)} async-done(((bf16[16,16,4096]{2,1,0:T(8,128)(2,1)}), bf16[16,16,4096]{2,1,0:T(8,128)(2,1)}, u32[]{:S(2)}, u32[]{:S(2)}) %all-to-all-start.2) | async-done | bytes 2097184 | tf_op jit(solution)/shard_map/all_to_all | solution.py:32
  130.1 3.8 %fusion.3 = f32[256,384]{1,0:T(8,128)S(1)} fusion(bf16[256,4096]{1,0:T(8,128)(2,1)} %bitcast.13, bf16[1,384,4096]{2,1,0:T(8,128)(2,1)} %all-gather.11.cloned.1.call-done), kind=kOutput, calls=%fused_computation.13 | convolution fusion | flops 805306368 | bytes 5636096 | tf_op jit(solution)/shard_map/dot_general | solution.py:54
  133.9 27.4 %all-gather.7.cloned.1.call-done = bf16[1,384,4096]{2,1,0:T(8,128)(2,1)} async-done(((bf16[1,384,512]{2,1,0:T(8,128)(2,1)}), bf16[1,384,4096]{2,1,0:T(8,128)(2,1)}) %all-gather.7.cloned.1.call-update) | async-done | bytes 3145744 | tf_op jit(solution)/shard_map/all_gather | solution.py:37
  161.3 3.4 %multiply_convert_fusion.1 = (bf16[256,384]{1,0:T(8,128)(2,1)S(1)}, f32[256,384]{1,0:T(8,128)S(1)}) fusion(f32[256,384]{1,0:T(8,128)S(1)} %fusion.3, f32[256,384]{1,0:T(8,128)} %fusion.7, bf16[256,4096]{1,0:T(8,128)(2,1)S(1)} %bitcast.55, bf16[1,384,4096]{2,1,0:T(8,128)(2,1)} %all-gather.7.cloned.1.call-done), kind=kOutput, calls=%fused_computation.34 | convolution fusion | flops 806289408 | bytes 6619136 | tf_op jit(solution)/shard_map/dot_general | solution.py:42
  164.8 2.6 convolution_convert_fusion.1
  167.4 7.4 %all-to-all-start.1 = ((bf16[16,16,4096]{2,1,0:T(8,128)(2,1)}), bf16[16,16,4096]{2,1,0:T(8,128)(2,1)S(1)}, u32[]{:S(2)}, u32[]{:S(2)}) async-start(bf16[16,16,4096]{2,1,0:T(8,128)(2,1)} %bitcast.58), calls=%async_computation.1 | async-start | bytes 4194304 | tf_op jit(solution)/shard_map/all_to_all | solution.py:75
  174.8 4.6 %convolution_convert_fusion = bf16[4096,384]{1,0:T(8,128)(2,1)} fusion(bf16[256,4096]{1,0:T(8,128)(2,1)} %bitcast.56, bf16[256,384]{1,0:T(8,128)(2,1)S(1)} %get-tuple-element.12), kind=kOutput, calls=%fused_computation.5 | convolution fusion | flops 806879232 | bytes 5439488 | tf_op jit(solution)/shard_map/dot_general | solution.py:66
  179.4 3.3 %fusion.9 = f32[256,4096]{1,0:T(8,128)S(1)} fusion(bf16[256,384]{1,0:T(8,128)(2,1)S(1)} %get-tuple-element.12, bf16[1,384,4096]{2,1,0:T(8,128)(2,1)} %all-gather.7.cloned.1.call-done), kind=kOutput, calls=%fused_computation.19 | convolution fusion | flops 805306368 | bytes 7536640 | tf_op jit(solution)/shard_map/dot_general | solution.py:62
  182.7 2.7 fusion
  185.4 38.3 %all-to-all-done.1 = bf16[16,16,4096]{2,1,0:T(8,128)(2,1)S(1)} async-done(((bf16[16,16,4096]{2,1,0:T(8,128)(2,1)}), bf16[16,16,4096]{2,1,0:T(8,128)(2,1)S(1)}, u32[]{:S(2)}, u32[]{:S(2)}) %all-to-all-start.1) | async-done | bytes 2097184 | tf_op jit(solution)/shard_map/all_to_all | solution.py:75
  223.7 5.0 %all-to-all-start.3 = ((bf16[16,16,4096]{2,1,0:T(8,128)(2,1)}), bf16[16,16,4096]{2,1,0:T(8,128)(2,1)}, u32[]{:S(2)}, u32[]{:S(2)}) async-start(bf16[16,16,4096]{2,1,0:T(8,128)(2,1)} %bitcast.57), calls=%async_computation.4 | async-start | bytes 4194304 | tf_op jit(solution)/shard_map/all_to_all | solution.py:82
  228.8 2.7 gather_fusion
  231.5 3.3 %fusion.1 = bf16[24,4096]{1,0:T(8,128)(2,1)} fusion(bf16[192,4096]{1,0:T(8,128)(2,1)} %gather_fusion, f32[24,8]{1,0:T(8,128)S(1)} %copy.21), kind=kLoop, calls=%fused_computation.10 | loop fusion | flops 2260992 | bytes 1770240 | tf_op jit(solution)/shard_map/reduce_sum | solution.py:96
  234.9 42.9 %all-to-all-done.3 = bf16[16,16,4096]{2,1,0:T(8,128)(2,1)} async-done(((bf16[16,16,4096]{2,1,0:T(8,128)(2,1)}), bf16[16,16,4096]{2,1,0:T(8,128)(2,1)}, u32[]{:S(2)}, u32[]{:S(2)}) %all-to-all-start.3) | async-done | bytes 2097184 | tf_op jit(solution)/shard_map/all_to_all | solution.py:82
  277.8 4.9 %gather_fusion.1 = bf16[192,4096]{1,0:T(8,128)(2,1)S(1)} fusion(bf16[256,4096]{1,0:T(8,128)(2,1)} %bitcast.15, s32[1024]{0:T(1024)S(1)} %pad_clamp_fusion), kind=kCustom, calls=%fused_computation.1 | custom fusion | bytes 3146496 | tf_op jit(solution)/shard_map/gather | solution.py:93
  282.7 1.7 bitcast_reduce_fusion
  284.5 1.0 convert_bitcast_fusion
  285.5 1.1 copy.29
  286.7 17.1 %reduce-scatter.6.cloned.1.call-done = bf16[24,1024]{1,0:T(8,128)(2,1)} async-done(((bf16[24,4096]{1,0:T(8,128)(2,1)}), bf16[24,1024]{1,0:T(8,128)(2,1)}) %reduce-scatter.6.cloned.1.call-update) | async-done | bytes 49168 | tf_op jit(solution)/shard_map/reduce_scatter | solution.py:102
  (39 shorter events, 0.9 us)
Async XLA Ops:
  7.2 5.0 %copy-start = (bf16[24,4096]{1,0:T(8,128)(2,1)S(1)}, bf16[24,4096]{1,0:T(8,128)(2,1)}, u32[]{:S(2)}) copy-start(bf16[24,4096]{1,0:T(8,128)(2,1)} %param.7) | copy-start | bytes 589828
  7.2 73.9 %all-gather.9.cloned.1.call-start = ((), (), s32[]{:S(2)}) async-start(), calls=%async_computation.11 | async-start | bytes 3538944 | tf_op jit(solution)/shard_map/all_gather | solution.py:38
  7.9 122.2 %all-gather.11.cloned.1.call-start = ((), (), s32[]{:S(2)}) async-start(), calls=%async_computation.12 | async-start | bytes 3538944 | tf_op jit(solution)/shard_map/all_gather | solution.py:39
  16.6 11.3 %copy-start.5 = (bf16[24,4096]{1,0:T(8,128)(2,1)S(1)}, bf16[24,4096]{1,0:T(8,128)(2,1)}, u32[]{:S(2)}) copy-start(bf16[24,4096]{1,0:T(8,128)(2,1)} %param.8) | copy-start | bytes 589828
  16.6 11.3 %copy-start.6 = (f32[24,8]{0,1:T(8,128)S(1)}, f32[24,8]{0,1:T(8,128)}, u32[]{:S(2)}) copy-start(f32[24,8]{0,1:T(8,128)} %param.9) | copy-start | bytes 2308
  16.6 59.5 %all-to-all-start = ((bf16[16,16,4096]{2,1,0:T(8,128)(2,1)}), bf16[16,16,4096]{2,1,0:T(8,128)(2,1)S(1)}, u32[]{:S(2)}, u32[]{:S(2)}) async-start(bf16[16,16,4096]{2,1,0:T(8,128)(2,1)} %bitcast.59), calls=%async_computation | async-start | bytes 4194304 | tf_op jit(solution)/shard_map/all_to_all | solution.py:31
  27.1 134.2 %all-gather.7.cloned.1.call-start = ((), (), s32[]{:S(2)}) async-start(), calls=%async_computation.10 | async-start | bytes 3538944 | tf_op jit(solution)/shard_map/all_gather | solution.py:37
  76.1 85.3 %copy-start.1 = (bf16[16,16,4096]{2,1,0:T(8,128)(2,1)}, bf16[16,16,4096]{2,1,0:T(8,128)(2,1)S(1)}, u32[]{:S(2)}) copy-start(bf16[16,16,4096]{2,1,0:T(8,128)(2,1)S(1)} %all-to-all-done) | copy-start | bytes 6291460
  76.1 54.0 %all-to-all-start.2 = ((bf16[16,16,4096]{2,1,0:T(8,128)(2,1)}), bf16[16,16,4096]{2,1,0:T(8,128)(2,1)}, u32[]{:S(2)}, u32[]{:S(2)}) async-start(bf16[16,16,4096]{2,1,0:T(8,128)(2,1)} %bitcast.60), calls=%async_computation.3 | async-start | bytes 4194304 | tf_op jit(solution)/shard_map/all_to_all | solution.py:32
  161.3 3.4 %copy-start.2 = (bf16[1,384,4096]{2,1,0:T(8,128)(2,1)S(1)}, bf16[1,384,4096]{2,1,0:T(8,128)(2,1)}, u32[]{:S(2)}) copy-start(bf16[1,384,4096]{2,1,0:T(8,128)(2,1)} %all-gather.11.cloned.1.call-done) | copy-start | bytes 9437188
  161.3 3.4 %copy-start.4 = (f32[256,384]{1,0:T(8,128)S(1)}, f32[256,384]{1,0:T(8,128)}, u32[]{:S(2)}) copy-start(f32[256,384]{1,0:T(8,128)} %fusion.7) | copy-start | bytes 1179652
  167.4 56.3 %all-to-all-start.1 = ((bf16[16,16,4096]{2,1,0:T(8,128)(2,1)}), bf16[16,16,4096]{2,1,0:T(8,128)(2,1)S(1)}, u32[]{:S(2)}, u32[]{:S(2)}) async-start(bf16[16,16,4096]{2,1,0:T(8,128)(2,1)} %bitcast.58), calls=%async_computation.1 | async-start | bytes 4194304 | tf_op jit(solution)/shard_map/all_to_all | solution.py:75
  174.8 109.7 %reduce-scatter.8.cloned.1.call-start = ((), (), s32[]{:S(2)}) async-start(), calls=%async_computation.9 | async-start | bytes 3538944 | tf_op jit(solution)/shard_map/reduce_scatter | solution.py:65
  179.4 3.3 %copy-start.3 = (bf16[1,384,4096]{2,1,0:T(8,128)(2,1)S(1)}, bf16[1,384,4096]{2,1,0:T(8,128)(2,1)}, u32[]{:S(2)}) copy-start(bf16[1,384,4096]{2,1,0:T(8,128)(2,1)} %all-gather.9.cloned.1.call-done) | copy-start | bytes 9437188
  223.7 54.0 %all-to-all-start.3 = ((bf16[16,16,4096]{2,1,0:T(8,128)(2,1)}), bf16[16,16,4096]{2,1,0:T(8,128)(2,1)}, u32[]{:S(2)}, u32[]{:S(2)}) async-start(bf16[16,16,4096]{2,1,0:T(8,128)(2,1)} %bitcast.57), calls=%async_computation.4 | async-start | bytes 4194304 | tf_op jit(solution)/shard_map/all_to_all | solution.py:82
  228.7 58.0 %reduce-scatter.4.cloned.1.call-start = ((), (), s32[]{:S(2)}) async-start(), calls=%async_computation.7 | async-start | bytes 245760 | tf_op jit(solution)/shard_map/reduce_scatter | solution.py:99
  234.8 69.0 %reduce-scatter.6.cloned.1.call-start = ((), (), s32[]{:S(2)}) async-start(), calls=%async_computation.8 | async-start | bytes 245760 | tf_op jit(solution)/shard_map/reduce_scatter | solution.py:102
Sparse Core Ops, SparseCore 0:
  10.1 53.9 all-gather.8
  66.2 46.4 all-gather.10
  114.8 46.4 all-gather.6
  179.5 45.2 reduce-scatter.7
  234.9 22.3 reduce-scatter.3
  284.6 19.2 reduce-scatter.5
where the time goes:
time: 313 us; the launch traced here: 311 us
  waiting for transfers between devices  217 us (69%)
  starting transfers between devices  28.1 us (9%)
  matrix products  24.2 us (8%)
  local copies, waits for them, and re-layouts  16.1 us (5%)
  between operations  14.3 us (5%)
  other arithmetic  11.2 us (4%)
    all_to_all x1, waiting for transfers between devices, on_device(): lax.all_to_all(send_grads, 'expert', split_axis=0, concat_axis=0, tiled=T...  45.1 us
    all_to_all x1, waiting for transfers between devices, on_device(): lax.all_to_all(send_rows, 'expert', split_axis=0, concat_axis=0, tiled=True)  43.7 us
    all_to_all x1, waiting for transfers between devices, on_device(): lax.all_to_all(input_slots.reshape(experts, capacity, model_width), 'expe...  42.9 us
    all_to_all x1, waiting for transfers between devices, on_device(): lax.all_to_all(mixed_slots.reshape(experts, capacity, model_width), 'expe...  38.3 us
    all_gather x1, waiting for transfers between devices, on_device(): lax.all_gather(w_gate[0], 'dp', axis=1, tiled=True)  27.4 us
    reduce_scatter x1, waiting for transfers between devices, on_device(): lax.psum_scatter(input_part.astype(jnp.bfloat16), 'etp', scatter_dimensio...  17.1 us
    all_to_all x1, starting transfers between devices, on_device(): lax.all_to_all(send_rows, 'expert', split_axis=0, concat_axis=0, tiled=True)  10.5 us
    all_to_all x1, starting transfers between devices, on_device(): lax.all_to_all(mixed_slots.reshape(experts, capacity, model_width), 'expe...  7.39 us
  transfers between devices with their start and end apart: 10, of which 6 were waited for; matrix products, arithmetic and copies ran while one was open for 15% of the time, Pallas kernels for 0%

commit v1 on v0

v1 whole, which is shorter than its diff:
```python
import jax
import jax.numpy as jnp
from jax import lax
from jax.sharding import PartitionSpec as P


def on_device(tokens, cotangent, route_weights, expert_ids, w_gate, w_up, w_down):
    tok_count, model_width = tokens.shape
    top_count = expert_ids.shape[1]
    experts = lax.axis_size("expert")
    shares = lax.axis_size("etp")
    part = model_width // shares
    share_idx = lax.axis_index("etp")
    capacity = tok_count // experts * top_count + min(top_count, tok_count % experts)
    slot_rows = experts * capacity
    named_count = jnp.sum(
        (expert_ids[:, :, None] == jnp.arange(experts, dtype=jnp.int32)).astype(jnp.int32), axis=1
    )
    before = jnp.cumsum(named_count, axis=0) - named_count
    position = jnp.take_along_axis(before, expert_ids, axis=1)
    slot_index = (expert_ids * capacity + position).reshape(-1)

    tok_part = lax.dynamic_slice_in_dim(tokens, share_idx * part, part, axis=1)
    cot_part = lax.dynamic_slice_in_dim(cotangent, share_idx * part, part, axis=1)
    copies = jnp.broadcast_to(tok_part[:, None, :], (tok_count, top_count, part))
    scaled = (route_weights[:, :, None] * cot_part[:, None, :].astype(jnp.float32)).astype(jnp.bfloat16)
    both = jnp.concatenate([copies, scaled], axis=2).reshape(-1, 2 * part)
    empty_slots = jnp.zeros((slot_rows, 2 * part), jnp.bfloat16)
    send = empty_slots.at[slot_index].set(both).reshape(experts, capacity, 2 * part)
    recv = lax.all_to_all(send, "expert", split_axis=0, concat_axis=0, tiled=True)
    recv = recv.reshape(1, slot_rows, 2 * part)
    spread = jnp.broadcast_to(recv, (shares, slot_rows, 2 * part))
    gathered = lax.all_to_all(spread, "etp", split_axis=0, concat_axis=0, tiled=True)
    rows4 = gathered[:, :, :part]
    grads4 = gathered[:, :, part:]

    gate_full, up_full, down_full = (
        lax.all_gather(w_gate[0], "dp", axis=1, tiled=True),
        lax.all_gather(w_up[0], "dp", axis=1, tiled=True),
        lax.all_gather(w_down[0], "dp", axis=1, tiled=True),
    )
    hidden_units = gate_full.shape[0]
    gate4 = gate_full.reshape(hidden_units, shares, part)
    up4 = up_full.reshape(hidden_units, shares, part)
    down4 = down_full.reshape(hidden_units, shares, part)

    gate_value = jnp.einsum("jsc,fjc->sf", rows4, gate4, preferred_element_type=jnp.float32)
    up_value = jnp.einsum("jsc,fjc->sf", rows4, up4, preferred_element_type=jnp.float32)
    sigmoid_gate = jax.nn.sigmoid(gate_value)
    active = gate_value * sigmoid_gate
    hidden = (active * up_value).astype(jnp.bfloat16)
    mixed4 = jnp.einsum("sf,fjc->jsc", hidden, down4, preferred_element_type=jnp.float32).astype(
        jnp.bfloat16
    )
    d_hidden = jnp.einsum("jsc,fjc->sf", grads4, down4, preferred_element_type=jnp.float32)
    d_gate = (
        d_hidden * up_value * sigmoid_gate * (1.0 + gate_value * (1.0 - sigmoid_gate))
    ).astype(jnp.bfloat16)
    d_up = (d_hidden * active).astype(jnp.bfloat16)
    input4 = (
        jnp.einsum("sf,fjc->jsc", d_gate, gate4, preferred_element_type=jnp.float32)
        + jnp.einsum("sf,fjc->jsc", d_up, up4, preferred_element_type=jnp.float32)
    ).astype(jnp.bfloat16)
    gate_term = jnp.einsum(
        "sf,jsc->fjc", d_gate, rows4, preferred_element_type=jnp.float32
    ).astype(jnp.bfloat16).reshape(hidden_units, model_width)
    weight_grads = lax.psum_scatter(gate_term, "dp", scatter_dimension=1, tiled=True)
    grad_gate = weight_grads.astype(jnp.float32)[None]

    outs4 = jnp.concatenate([mixed4, input4], axis=2)
    summed = lax.all_to_all(outs4, "etp", split_axis=0, concat_axis=0, tiled=True)
    slot_out = jnp.sum(summed.astype(jnp.float32), axis=0).astype(jnp.bfloat16)
    back = lax.all_to_all(
        slot_out.reshape(experts, capacity, 2 * part), "expert", split_axis=0, concat_axis=0, tiled=True
    )
    token_out = back.reshape(slot_rows, 2 * part)[slot_index].reshape(tok_count, top_count, 2 * part)
    token_out = token_out.astype(jnp.float32)
    mixed = jnp.sum(route_weights[:, :, None] * token_out[:, :, :part], axis=1)
    grad_tokens = jnp.sum(token_out[:, :, part:], axis=1)
    return (mixed.astype(jnp.bfloat16), grad_tokens.astype(jnp.bfloat16), grad_gate)


def solution(mesh):
    in_specs = (
        P(("dp", "expert"), None),
        P(("dp", "expert"), None),
        P(("dp", "expert"), None),
        P(("dp", "expert"), None),
        P("expert", "etp", "dp"),
        P("expert", "etp", "dp"),
        P("expert", "etp", "dp"),
    )
    out_specs = (P(("dp", "expert"), "etp"), P(("dp", "expert"), "etp"), P("expert", "etp", "dp"))
    return jax.shard_map(
        on_device, mesh=mesh, in_specs=in_specs, out_specs=out_specs, check_vma=False
    )
```

time: 313 us -> 285 us (0.911)
  waiting for transfers between devices: 217 us -> 99.1 us
  blocking collectives: 0 us -> 104 us
  starting transfers between devices: 28.1 us -> 19.1 us
  matrix products: 24.2 us -> 21 us
    all_to_all x4 -> x2, waiting for transfers between devices: 170 us -> 54.9 us  [the longest x1 27.9 us: on_device(): lax.all_to_all(slot_out.reshape(experts, capacity, 2 * part), 'expert', s...]
    all_to_all x0 -> x2, blocking collectives: none -> 104 us  [the longest x1 51.8 us: on_device(): lax.all_to_all(outs4, 'etp', split_axis=0, concat_axis=0, tiled=True)]
    reduce_scatter x3 -> x1, waiting for transfers between devices: 17.2 us -> 0.01 us  [on_device(): lax.psum_scatter(gate_term, 'dp', scatter_dimension=1, tiled=True)]
    all_gather x1, waiting for transfers between devices: 27.4 us -> 44.1 us  [on_device(): lax.all_gather(w_gate[0], 'dp', axis=1, tiled=True)]
    all_to_all x4 -> x2, starting transfers between devices: 27.9 us -> 18.9 us  [the longest x1 10.3 us: on_device(): lax.all_to_all(send, 'expert', split_axis=0, concat_axis=0, tiled=True)]
    unnamed x17 -> x22, local copies, waits for them, and re-layouts: 2.02 us -> 9.35 us
    gather x2 -> x1, local copies, waits for them, and re-layouts: 7.63 us -> 1.14 us  [on_device(): back.reshape(slot_rows, 2 * part)[slot_index]]
    scatter x1 -> x0, local copies, waits for them, and re-layouts: 4.38 us -> none  [on_device(): empty_slots.at[slot_index].set(copies)]
  transfers between devices with their start and end apart: 10 -> 6, of which waited for: 6 -> 3; matrix products, arithmetic and copies ran while one was open for 15% -> 11% of each run, Pallas kernels for 0% -> 0%
where the time goes in v1:
time: 285 us; the launch traced here: 284 us
  blocking collectives  104 us (36%)
  waiting for transfers between devices  99.1 us (35%)
  matrix products  21 us (7%)
  starting transfers between devices  19.1 us (7%)
  local copies, waits for them, and re-layouts  15.9 us (6%)
  between operations  14 us (5%)
  other arithmetic  11.5 us (4%)
    all_to_all x1, blocking collectives, on_device(): lax.all_to_all(outs4, 'etp', split_axis=0, concat_axis=0, tiled=True)  51.8 us
    all_to_all x1, blocking collectives, on_device(): lax.all_to_all(spread, 'etp', split_axis=0, concat_axis=0, tiled=True)  51.8 us
    all_gather x1, waiting for transfers between devices, on_device(): lax.all_gather(w_gate[0], 'dp', axis=1, tiled=True)  44.1 us
    all_to_all x1, waiting for transfers between devices, on_device(): lax.all_to_all(slot_out.reshape(experts, capacity, 2 * part), 'expert', s...  27.9 us
    all_to_all x1, waiting for transfers between devices, on_device(): lax.all_to_all(send, 'expert', split_axis=0, concat_axis=0, tiled=True)  26.9 us
    all_to_all x1, starting transfers between devices, on_device(): lax.all_to_all(send, 'expert', split_axis=0, concat_axis=0, tiled=True)  10.3 us
    unnamed x22, local copies, waits for them, and re-layouts  9.35 us
    all_to_all x1, starting transfers between devices, on_device(): lax.all_to_all(slot_out.reshape(experts, capacity, 2 * part), 'expert', s...  8.59 us
  transfers between devices with their start and end apart: 6, of which 3 were waited for; matrix products, arithmetic and copies ran while one was open for 11% of the time, Pallas kernels for 0%

profile of v1, /device:TPU:1, one launch (start us, length us, event | category | flops | bytes accessed | tf_op | source)
XLA Modules:
  0.0 284.1 jit_solution(17996853384464367442)
XLA Ops:
  7.2 1.9 copy.42
  9.2 1.9 copy.44
  11.2 0.8 copy.32
  12.0 0.8 copy.33
  12.8 0.7 convert_reduce_fusion
  13.7 1.6 gather_fusion.1
  15.5 0.8 dynamic-slice_convert_fusion
  16.6 2.8 scatter_custom_fusion
  19.4 10.3 %all-to-all-start = ((bf16[16,16,2048]{2,1,0:T(8,128)(2,1)}), bf16[16,16,2048]{2,1,0:T(8,128)(2,1)S(1)}, u32[]{:S(2)}, u32[]{:S(2)}) async-start(bf16[16,16,2048]{2,1,0:T(8,128)(2,1)} %bitcast.4), calls=%async_computation | async-start | bytes 2097152 | tf_op jit(solution)/shard_map/all_to_all | solution.py:30
  29.8 0.9 copy.40
  30.8 26.9 %all-to-all-done = bf16[16,16,2048]{2,1,0:T(8,128)(2,1)S(1)} async-done(((bf16[16,16,2048]{2,1,0:T(8,128)(2,1)}), bf16[16,16,2048]{2,1,0:T(8,128)(2,1)S(1)}, u32[]{:S(2)}, u32[]{:S(2)}) %all-to-all-start) | async-done | bytes 1048608 | tf_op jit(solution)/shard_map/all_to_all | solution.py:30
  57.7 0.5 broadcast_in_dim.37
  58.2 51.8 %all_to_all.20 = bf16[4,256,2048]{2,1,0:T(8,128)(2,1)} all-to-all(bf16[4,256,2048]{2,1,0:T(8,128)(2,1)S(1)} %broadcast_in_dim.37), channel_id=1, replica_groups=mesh['dp'=8,'expert'=16,'etp'=4] {'etp'}, dimensions={0} | all-to-all | bytes 8388608 | tf_op jit(solution)/shard_map/all_to_all | solution.py:33
  110.0 3.8 %fusion.11 = f32[256,384]{1,0:T(8,128)S(1)} fusion(bf16[384,4,1024]{0,2,1:T(8,128)(2,1)} %bitcast.60, bf16[4,256,2048]{2,1,0:T(8,128)(2,1)} %all_to_all.20), kind=kOutput, calls=%fused_computation.16 | convolution fusion | flops 805306368 | bytes 5636096 | tf_op jit(solution)/shard_map/jsc,fjc->sf/dot_general | solution.py:48
  113.8 3.9 %fusion.14 = f32[256,384]{1,0:T(8,128)S(1)} fusion(bf16[384,4,1024]{0,2,1:T(8,128)(2,1)} %bitcast.58, bf16[4,256,2048]{2,1,0:T(8,128)(2,1)} %all_to_all.20), kind=kOutput, calls=%fused_computation.17 | convolution fusion | flops 805306368 | bytes 5636096 | tf_op jit(solution)/shard_map/jsc,fjc->sf/dot_general | solution.py:55
  117.7 44.1 %all-gather.7.cloned.1.call-done = bf16[1,384,4096]{1,2,0:T(8,128)(2,1)} async-done(((bf16[1,384,512]{1,2,0:T(8,128)(2,1)}), bf16[1,384,4096]{1,2,0:T(8,128)(2,1)}) %all-gather.7.cloned.1.call-update) | async-done | bytes 3145744 | tf_op jit(solution)/shard_map/all_gather | solution.py:38
  161.9 4.0 %multiply_convert_fusion.1 = (bf16[256,384]{1,0:T(8,128)(2,1)S(1)}, f32[256,384]{1,0:T(8,128)S(1)}) fusion(f32[256,384]{1,0:T(8,128)S(1)} %fusion.14, f32[256,384]{1,0:T(8,128)S(1)} %fusion.11, bf16[384,4,1024]{0,2,1:T(8,128)(2,1)} %bitcast.56, bf16[4,256,2048]{2,1,0:T(8,128)(2,1)} %all_to_all.20), kind=kOutput, calls=%fused_computation.31 | convolution fusion | flops 806289408 | bytes 6619136 | tf_op jit(solution)/shard_map/jsc,fjc->sf/dot_general | solution.py:47
  165.9 3.3 %fusion.30 = f32[256,4,1024]{2,0,1:T(8,128)} fusion(bf16[384,4,1024]{0,2,1:T(8,128)(2,1)S(1)} %bitcast.57, bf16[256,384]{1,0:T(8,128)(2,1)S(1)} %get-tuple-element.11), kind=kOutput, calls=%fused_computation.38 | convolution fusion | flops 805306368 | bytes 7536640 | tf_op jit(solution)/shard_map/sf,fjc->jsc/dot_general | solution.py:61
  169.2 1.0 convolution_convert_fusion
  170.2 2.8 copy.50
  173.0 1.9 copy-done.3
  174.9 3.8 %fusion.2 = bf16[4,256,1024]{2,1,0:T(8,128)(2,1)S(1)} fusion(f32[256,4,1024]{2,0,1:T(8,128)} %fusion.30, bf16[384,4,1024]{0,2,1:T(8,128)(2,1)S(1)} %bitcast.61, f32[256,384]{1,0:T(8,128)} %copy-done.4, f32[256,384]{1,0:T(8,128)S(1)} %get-tuple-element.12), kind=kOutput, calls=%fused_computation.9 | convolution fusion | flops 807993344 | bytes 10223616 | tf_op jit(solution)/shard_map/sf,fjc->jsc/dot_general | solution.py:62
  178.7 1.3 convert_bitcast_fusion
  180.0 0.4 pad_maximum_fusion
  180.4 51.8 %all_to_all.21 = bf16[4,256,2048]{2,1,0:T(8,128)(2,1)} all-to-all(bf16[4,256,2048]{2,1,0:T(8,128)(2,1)S(1)} %pad_maximum_fusion), channel_id=1, replica_groups=mesh['dp'=8,'expert'=16,'etp'=4] {'etp'}, dimensions={0} | all-to-all | bytes 8388608 | tf_op jit(solution)/shard_map/all_to_all | solution.py:71
  232.2 4.2 %reduce_sum.40 = bf16[256,2048]{1,0:T(8,128)(2,1)} reduce(bf16[4,256,2048]{2,1,0:T(8,128)(2,1)} %all_to_all.21, bf16[]{:T(256)} %constant.11.clone.1), dimensions={0}, to_apply=%region_3.4 | reduce | flops 1572864 | bytes 5242882 | tf_op jit(solution)/shard_map/reduce_sum | solution.py:72
  236.5 8.6 %all-to-all-start.3 = ((bf16[16,16,2048]{2,1,0:T(8,128)(2,1)}), bf16[16,16,2048]{2,1,0:T(8,128)(2,1)S(1)}, u32[]{:S(2)}, u32[]{:S(2)}) async-start(bf16[16,16,2048]{2,1,0:T(8,128)(2,1)} %bitcast.17), calls=%async_computation.3 | async-start | bytes 2097152 | tf_op jit(solution)/shard_map/all_to_all | solution.py:73
  245.1 27.9 %all-to-all-done.3 = bf16[16,16,2048]{2,1,0:T(8,128)(2,1)S(1)} async-done(((bf16[16,16,2048]{2,1,0:T(8,128)(2,1)}), bf16[16,16,2048]{2,1,0:T(8,128)(2,1)S(1)}, u32[]{:S(2)}, u32[]{:S(2)}) %all-to-all-start.3) | async-done | bytes 1048608 | tf_op jit(solution)/shard_map/all_to_all | solution.py:73
  273.0 1.1 gather_fusion
  274.3 1.1 slice_reduce_fusion
  275.4 1.0 bitcast_convert_fusion.1
  276.4 1.1 copy.51
  (40 shorter events, 1.1 us)
Async XLA Ops:
  7.2 102.8 %all-gather.9.cloned.1.call-start = ((), (), s32[]{:S(2)}) async-start(), calls=%async_computation.7 | async-start | bytes 3538944 | tf_op jit(solution)/shard_map/all_gather | solution.py:39
  9.2 104.7 %all-gather.11.cloned.1.call-start = ((), (), s32[]{:S(2)}) async-start(), calls=%async_computation.8 | async-start | bytes 3538944 | tf_op jit(solution)/shard_map/all_gather | solution.py:40
  15.3 14.4 %copy-start.7 = (bf16[1,384,512]{2,1,0:T(8,128)(2,1)S(1)}, bf16[1,384,512]{2,1,0:T(8,128)(2,1)}, u32[]{:S(2)}) copy-start(bf16[1,384,512]{2,1,0:T(8,128)(2,1)} %param.11) | copy-start | bytes 1179652
  19.4 38.3 %all-to-all-start = ((bf16[16,16,2048]{2,1,0:T(8,128)(2,1)}), bf16[16,16,2048]{2,1,0:T(8,128)(2,1)S(1)}, u32[]{:S(2)}, u32[]{:S(2)}) async-start(bf16[16,16,2048]{2,1,0:T(8,128)(2,1)} %bitcast.4), calls=%async_computation | async-start | bytes 2097152 | tf_op jit(solution)/shard_map/all_to_all | solution.py:30
  29.7 132.1 %all-gather.7.cloned.1.call-start = ((), (), s32[]{:S(2)}) async-start(), calls=%async_computation.6 | async-start | bytes 3538944 | tf_op jit(solution)/shard_map/all_gather | solution.py:38
  30.7 244.7 %reduce-scatter.2.cloned.1.call-start = ((), (), s32[]{:S(2)}) async-start(), calls=%async_computation.5 | async-start | bytes 3538944 | tf_op jit(solution)/shard_map/reduce_scatter | solution.py:67
  113.8 48.1 %copy-start.5 = (f32[256,384]{1,0:T(8,128)}, f32[256,384]{1,0:T(8,128)S(1)}, u32[]{:S(2)}) copy-start(f32[256,384]{1,0:T(8,128)S(1)} %fusion.11) | copy-start | bytes 1179652
  117.7 48.2 %copy-start.4 = (f32[256,384]{1,0:T(8,128)}, f32[256,384]{1,0:T(8,128)S(1)}, u32[]{:S(2)}) copy-start(f32[256,384]{1,0:T(8,128)S(1)} %fusion.14) | copy-start | bytes 1179652
  161.9 4.0 %copy-start.1 = (bf16[1,384,4096]{1,2,0:T(8,128)(2,1)S(1)}, bf16[1,384,4096]{1,2,0:T(8,128)(2,1)}, u32[]{:S(2)}) copy-start(bf16[1,384,4096]{1,2,0:T(8,128)(2,1)} %all-gather.7.cloned.1.call-done) | copy-start | bytes 9437188
  165.9 3.3 %copy-start = (bf16[4,256,2048]{2,1,0:T(8,128)(2,1)S(1)}, bf16[4,256,2048]{2,1,0:T(8,128)(2,1)}, u32[]{:S(2)}) copy-start(bf16[4,256,2048]{2,1,0:T(8,128)(2,1)} %all_to_all.20) | copy-start | bytes 12582916
  173.0 1.9 copy-start.3
  174.9 3.8 %copy-start.2 = (bf16[1,384,4096]{1,2,0:T(8,128)(2,1)S(1)}, bf16[1,384,4096]{1,2,0:T(8,128)(2,1)}, u32[]{:S(2)}) copy-start(bf16[1,384,4096]{1,2,0:T(8,128)(2,1)} %all-gather.11.cloned.1.call-done) | copy-start | bytes 9437188
  174.9 3.8 %copy-start.6 = (f32[256,384]{1,0:T(8,128)S(1)}, f32[256,384]{1,0:T(8,128)}, u32[]{:S(2)}) copy-start(f32[256,384]{1,0:T(8,128)} %copy-done.5) | copy-start | bytes 1179652
  236.5 36.5 %all-to-all-start.3 = ((bf16[16,16,2048]{2,1,0:T(8,128)(2,1)}), bf16[16,16,2048]{2,1,0:T(8,128)(2,1)S(1)}, u32[]{:S(2)}, u32[]{:S(2)}) async-start(bf16[16,16,2048]{2,1,0:T(8,128)(2,1)} %bitcast.17), calls=%async_computation.3 | async-start | bytes 2097152 | tf_op jit(solution)/shard_map/all_to_all | solution.py:73
Sparse Core Ops, SparseCore 0:
  10.1 53.9 all-gather.8
  66.1 46.5 all-gather.10
  115.3 46.4 all-gather.6
  173.1 45.5 reduce-scatter.1

commit v2 on v1

--- a/solution.py
+++ b/solution.py
@@ -2,6 +2,53 @@
 import jax.numpy as jnp
 from jax import lax
 from jax.sharding import PartitionSpec as P
+
+
+def ring_gather(piece, axis, n, along=0):
+    idx = lax.axis_index(axis)
+    fwd = [(i, (i + 1) % n) for i in range(n)]
+    bwd = [(i, (i - 1) % n) for i in range(n)]
+    shape = list(piece.shape)
+    shape.insert(along, n)
+    out = jnp.zeros(shape, piece.dtype)
+    put = lambda buf, val, at: lax.dynamic_update_index_in_dim(buf, val, at % n, along)
+    out = put(out, piece, idx)
+    left = right = piece
+    half = n // 2
+    for k in range(1, half):
+        left = lax.ppermute(left, axis, fwd)
+        right = lax.ppermute(right, axis, bwd)
+        out = put(out, left, idx - k)
+        out = put(out, right, idx + k)
+    m = piece.shape[0] // 2
+    first = lax.ppermute(left[:m], axis, fwd)
+    second = lax.ppermute(right[m:], axis, bwd)
+    return put(out, jnp.concatenate([first, second], axis=0), idx + half)
+
+
+def ring_reduce_scatter(chunks, axis, n):
+    idx = lax.axis_index(axis)
+    fwd = [(i, (i + 1) % n) for i in range(n)]
+    bwd = [(i, (i - 1) % n) for i in range(n)]
+    pick = lambda at: lax.dynamic_index_in_dim(chunks, at % n, 0, keepdims=False).astype(jnp.float32)
+    half = n // 2
+    m = chunks.shape[1] // 2
+    to_right = pick(idx + half)[:m]
+    to_left = pick(idx - half)[m:]
+    for k in range(2, half + 1):
+        got_left = lax.ppermute(to_right.astype(chunks.dtype), axis, fwd).astype(jnp.float32)
+        got_right = lax.ppermute(to_left.astype(chunks.dtype), axis, bwd).astype(jnp.float32)
+        own_r = pick(idx + half - k + 1)
+        own_l = pick(idx - half + k - 1)
+        if k == 2:
+            to_right = own_r.at[:m].add(got_left)
+            to_left = own_l.at[m:].add(got_right)
+        else:
+            to_right = own_r + got_left
+            to_left = own_l + got_right
+    got_left = lax.ppermute(to_right.astype(chunks.dtype), axis, fwd).astype(jnp.float32)
+    got_right = lax.ppermute(to_left.astype(chunks.dtype), axis, bwd).astype(jnp.float32)
+    return pick(idx) + got_left + got_right
 
 
 def on_device(tokens, cotangent, route_weights, expert_ids, w_gate, w_up, w_down):
@@ -29,15 +76,14 @@
     send = empty_slots.at[slot_index].set(both).reshape(experts, capacity, 2 * part)
     recv = lax.all_to_all(send, "expert", split_axis=0, concat_axis=0, tiled=True)
     recv = recv.reshape(1, slot_rows, 2 * part)
-    spread = jnp.broadcast_to(recv, (shares, slot_rows, 2 * part))
-    gathered = lax.all_to_all(spread, "etp", split_axis=0, concat_axis=0, tiled=True)
+    gathered = ring_gather(recv[0], "etp", shares)
     rows4 = gathered[:, :, :part]
     grads4 = gathered[:, :, part:]
 
     gate_full, up_full, down_full = (
         lax.all_gather(w_gate[0], "dp", axis=1, tiled=True),
         lax.all_gather(w_up[0], "dp", axis=1, tiled=True),
-        lax.all_gather(w_down[0], "dp", axis=1, tiled=True),
+        ring_gather(w_down[0], "dp", lax.axis_size("dp"), along=1).reshape(w_down.shape[1], -1),
     )
     hidden_units = gate_full.shape[0]
     gate4 = gate_full.reshape(hidden_units, shares, part)
@@ -68,8 +114,7 @@
     grad_gate = weight_grads.astype(jnp.float32)[None]
 
     outs4 = jnp.concatenate([mixed4, input4], axis=2)
-    summed = lax.all_to_all(outs4, "etp", split_axis=0, concat_axis=0, tiled=True)
-    slot_out = jnp.sum(summed.astype(jnp.float32), axis=0).astype(jnp.bfloat16)
+    slot_out = ring_reduce_scatter(outs4, "etp", shares).astype(jnp.bfloat16)
     back = lax.all_to_all(
         slot_out.reshape(experts, capacity, 2 * part), "expert", split_axis=0, concat_axis=0, tiled=True
     )

time: 285 us -> 254 us (0.89)
  blocking collectives: 104 us -> 0 us
  starting transfers between devices: 19.1 us -> 76.8 us
  local copies, waits for them, and re-layouts: 15.9 us -> 26.4 us
  waiting for transfers between devices: 99.1 us -> 103 us
    all_to_all x2 -> x0, blocking collectives: 104 us -> none  [the longest x1 51.8 us: on_device(): lax.all_to_all(outs4, 'etp', split_axis=0, concat_axis=0, tiled=True)]
    ppermute x0 -> x16, waiting for transfers between devices: none -> 74.8 us  [the longest x4 27.1 us: ring_gather(): left = lax.ppermute(left, axis, fwd)]
    ppermute x0 -> x16, starting transfers between devices: none -> 53.2 us  [the longest x4 21.1 us: ring_gather(): right = lax.ppermute(right, axis, bwd)]
    all_gather x1, waiting for transfers between devices: 44.1 us -> 0.02 us  [on_device(): lax.all_gather(w_gate[0], 'dp', axis=1, tiled=True)]
    all_to_all x1, waiting for transfers between devices: 26.9 us -> 0.01 us  [on_device(): lax.all_to_all(send, 'expert', split_axis=0, concat_axis=0, tiled=True)]
    dynamic_update_slice x0 -> x10, local copies, waits for them, and re-layouts: none -> 5.98 us  [ring_gather(): lax.dynamic_update_index_in_dim(buf, val, at % n, along)]
    all_to_all x1, starting transfers between devices: 8.59 us -> 13.1 us  [on_device(): lax.all_to_all(slot_out.reshape(experts, capacity, 2 * part), 'expert', s...]
    reduce_sum x1 -> x0, other arithmetic: 4.25 us -> none  [on_device(): slot_out = jnp.sum(summed.astype(jnp.float32), axis=0).astype(jnp.bfloat16)]
  transfers between devices with their start and end apart: 6 -> 21, of which waited for: 3 -> 10; matrix products, arithmetic and copies ran while one was open for 11% -> 15% of each run, Pallas kernels for 0% -> 0%
where the time goes in v2:
time: 254 us; the launch traced here: 253 us
  waiting for transfers between devices  103 us (41%)
  starting transfers between devices  76.8 us (30%)
  local copies, waits for them, and re-layouts  26.4 us (10%)
  matrix products  22.9 us (9%)
  between operations  14.5 us (6%)
  other arithmetic  9.21 us (4%)
    all_to_all x1, waiting for transfers between devices, on_device(): lax.all_to_all(slot_out.reshape(experts, capacity, 2 * part), 'expert', s...  27.9 us
    ppermute x4, waiting for transfers between devices, ring_gather(): left = lax.ppermute(left, axis, fwd)  27.1 us
    ppermute x4, starting transfers between devices, ring_gather(): right = lax.ppermute(right, axis, bwd)  21.1 us
    ppermute x2, waiting for transfers between devices, ring_reduce_scatter(): lax.ppermute(to_left.astype(chunks.dtype), axis, bwd).astype(jnp.float32)  20.6 us
    all_to_all x1, starting transfers between devices, on_device(): lax.all_to_all(slot_out.reshape(experts, capacity, 2 * part), 'expert', s...  13.1 us
    ppermute x2, waiting for transfers between devices, ring_gather(): second = lax.ppermute(right[m:], axis, bwd)  12.5 us
    all_to_all x1, starting transfers between devices, on_device(): lax.all_to_all(send, 'expert', split_axis=0, concat_axis=0, tiled=True)  10.3 us
    ppermute x2, waiting for transfers between devices, ring_gather(): first = lax.ppermute(left[:m], axis, fwd)  10.2 us
  transfers between devices with their start and end apart: 21, of which 10 were waited for; matrix products, arithmetic and copies ran while one was open for 15% of the time, Pallas kernels for 0%

profile of v2, /device:TPU:1, one launch (start us, length us, event | category | flops | bytes accessed | tf_op | source)
XLA Modules:
  0.0 252.6 jit_solution(2300230864996546127)
XLA Ops:
  15.9 2.9 %scatter_custom_fusion = bf16[256,2048]{1,0:T(8,128)(2,1)} fusion(s32[192]{0:T(256)S(1)} %bitcast.119, bf16[192,1024]{1,0:T(8,128)(2,1)S(1)} %fusion.35, bf16[]{:T(256)} %constant.256, bf16[192,1024]{1,0:T(8,128)(2,1)S(1)} %broadcast_bitcast_fusion, bf16[]{:T(256)} %constant.213.clone.1), kind=kCustom, calls=%fused_computation.50 | custom fusion | flops 1572864 | bytes 1835012 | tf_op jit(solution)/shard_map/scatter | solution.py:76
  18.8 10.3 %all-to-all-start = ((bf16[16,16,2048]{2,1,0:T(8,128)(2,1)}), bf16[16,16,2048]{2,1,0:T(8,128)(2,1)S(1)}, u32[]{:S(2)}, u32[]{:S(2)}) async-start(bf16[16,16,2048]{2,1,0:T(8,128)(2,1)} %bitcast.14), calls=%async_computation | async-start | bytes 2097152 | tf_op jit(solution)/shard_map/all_to_all | solution.py:77
  29.4 2.3 collective-permute-start
  31.7 8.6 %collective-permute-start.1 = (bf16[384,512]{0,1:T(8,128)(2,1)S(1)}, bf16[384,512]{0,1:T(8,128)(2,1)S(1)}, u32[]{:S(2)}, u32[]{:S(2)}) collective-permute-start(bf16[384,512]{0,1:T(8,128)(2,1)S(1)} %bitcast.118), channel_id=1, source_target_pairs={{0,448},{64,0},{128,64},{192,128},{256,192},{320,256},{384,320},{4... | collective-permute-start | bytes 1179656 | tf_op jit(solution)/shard_map/ppermute | solution.py:20
  40.5 2.0 broadcast_in_dim.70
  43.3 13.1 %collective-permute-done = bf16[384,512]{0,1:T(8,128)(2,1)S(1)} collective-permute-done((bf16[384,512]{0,1:T(8,128)(2,1)S(1)}, bf16[384,512]{0,1:T(8,128)(2,1)S(1)}, u32[]{:S(2)}, u32[]{:S(2)}) %collective-permute-start) | collective-permute-done | bytes 393248 | tf_op jit(solution)/shard_map/ppermute | solution.py:19
  58.4 4.6 %collective-permute-start.3 = (bf16[384,512]{0,1:T(8,128)(2,1)S(1)}, bf16[384,512]{0,1:T(8,128)(2,1)S(1)}, u32[]{:S(2)}, u32[]{:S(2)}) collective-permute-start(bf16[384,512]{0,1:T(8,128)(2,1)S(1)} %collective-permute-done.1), channel_id=1, source_target_pairs={{0,448},{64,0},{128,64},{192,128},{256,192},{320,256},{384,320},{4... | collective-permute-start | bytes 1179656 | tf_op jit(solution)/shard_map/ppermute | solution.py:20
  64.6 14.0 %collective-permute-done.2 = bf16[384,512]{0,1:T(8,128)(2,1)S(1)} collective-permute-done((bf16[384,512]{0,1:T(8,128)(2,1)S(1)}, bf16[384,512]{0,1:T(8,128)(2,1)S(1)}, u32[]{:S(2)}, u32[]{:S(2)}) %collective-permute-start.2) | collective-permute-done | bytes 393248 | tf_op jit(solution)/shard_map/ppermute | solution.py:19
  80.5 4.6 %collective-permute-start.5 = (bf16[384,512]{0,1:T(8,128)(2,1)S(1)}, bf16[384,512]{0,1:T(8,128)(2,1)S(1)}, u32[]{:S(2)}, u32[]{:S(2)}) collective-permute-start(bf16[384,512]{0,1:T(8,128)(2,1)S(1)} %collective-permute-done.3), channel_id=1, source_target_pairs={{0,448},{64,0},{128,64},{192,128},{256,192},{320,256},{384,320},{4... | collective-permute-start | bytes 1179656 | tf_op jit(solution)/shard_map/ppermute | solution.py:20
  85.9 3.1 %collective-permute-start.8 = (bf16[256,2048]{1,0:T(8,128)(2,1)S(1)}, bf16[256,2048]{1,0:T(8,128)(2,1)S(1)}, u32[]{:S(2)}, u32[]{:S(2)}) collective-permute-start(bf16[256,2048]{1,0:T(8,128)(2,1)S(1)} %bitcast.110), channel_id=1, source_target_pairs={{0,1},{1,2},{2,3},{3,0},{4,5},{5,6},{6,7},{7,4},{8,9},{9,10},{10,1... | collective-permute-start | bytes 3145736 | tf_op jit(solution)/shard_map/ppermute | solution.py:19
  89.0 3.4 %collective-permute-start.9 = (bf16[256,2048]{1,0:T(8,128)(2,1)S(1)}, bf16[256,2048]{1,0:T(8,128)(2,1)S(1)}, u32[]{:S(2)}, u32[]{:S(2)}) collective-permute-start(bf16[256,2048]{1,0:T(8,128)(2,1)S(1)} %bitcast.111), channel_id=1, source_target_pairs={{0,3},{1,0},{2,1},{3,2},{4,7},{5,4},{6,5},{7,6},{8,11},{9,8},{10,9... | collective-permute-start | bytes 3145736 | tf_op jit(solution)/shard_map/ppermute | solution.py:20
  93.3 3.8 %collective-permute-start.7 = (bf16[192,512]{0,1:T(8,128)(2,1)S(1)}, bf16[192,512]{0,1:T(8,128)(2,1)S(1)}, u32[]{:S(2)}, u32[]{:S(2)}) collective-permute-start(bf16[192,512]{0,1:T(8,128)(2,1)S(1)} %slice.91), channel_id=1, source_target_pairs={{0,448},{64,0},{128,64},{192,128},{256,192},{320,256},{384,320},{4... | collective-permute-start | bytes 589832 | tf_op jit(solution)/shard_map/ppermute | solution.py:25
  100.8 7.4 %collective-permute-done.7 = bf16[192,512]{0,1:T(8,128)(2,1)S(1)} collective-permute-done((bf16[192,512]{0,1:T(8,128)(2,1)S(1)}, bf16[192,512]{0,1:T(8,128)(2,1)S(1)}, u32[]{:S(2)}, u32[]{:S(2)}) %collective-permute-start.7) | collective-permute-done | bytes 196640 | tf_op jit(solution)/shard_map/ppermute | solution.py:25
  108.2 5.0 %collective-permute-done.6 = bf16[192,512]{0,1:T(8,128)(2,1)S(1)} collective-permute-done((bf16[192,512]{0,1:T(8,128)(2,1)S(1)}, bf16[192,512]{0,1:T(8,128)(2,1)S(1)}, u32[]{:S(2)}, u32[]{:S(2)}) %collective-permute-start.6) | collective-permute-done | bytes 196640 | tf_op jit(solution)/shard_map/ppermute | solution.py:24
  114.8 4.4 %collective-permute-start.11 = (bf16[128,2048]{1,0:T(8,128)(2,1)S(1)}, bf16[128,2048]{1,0:T(8,128)(2,1)S(1)}, u32[]{:S(2)}, u32[]{:S(2)}) collective-permute-start(bf16[128,2048]{1,0:T(8,128)(2,1)S(1)} %slice.93), channel_id=1, source_target_pairs={{0,3},{1,0},{2,1},{3,2},{4,7},{5,4},{6,5},{7,6},{8,11},{9,8},{10,9... | collective-permute-start | bytes 1572872 | tf_op jit(solution)/shard_map/ppermute | solution.py:25
  119.3 2.1 collective-permute-start.10
  121.6 5.1 %collective-permute-done.11 = bf16[128,2048]{1,0:T(8,128)(2,1)S(1)} collective-permute-done((bf16[128,2048]{1,0:T(8,128)(2,1)S(1)}, bf16[128,2048]{1,0:T(8,128)(2,1)S(1)}, u32[]{:S(2)}, u32[]{:S(2)}) %collective-permute-start.11) | collective-permute-done | bytes 524320 | tf_op jit(solution)/shard_map/ppermute | solution.py:25
  126.7 5.2 %collective-permute-done.10 = bf16[128,2048]{1,0:T(8,128)(2,1)S(1)} collective-permute-done((bf16[128,2048]{1,0:T(8,128)(2,1)S(1)}, bf16[128,2048]{1,0:T(8,128)(2,1)S(1)}, u32[]{:S(2)}, u32[]{:S(2)}) %collective-permute-start.10) | collective-permute-done | bytes 524320 | tf_op jit(solution)/shard_map/ppermute | solution.py:24
  134.0 3.1 %fusion.16 = f32[256,384]{1,0:T(8,128)S(1)} fusion(bf16[384,4,1024]{0,2,1:T(8,128)(2,1)} %bitcast.9, bf16[4,256,2048]{2,1,0:T(8,128)(2,1)S(1)} %fusion.29), kind=kOutput, calls=%fused_computation.29 | convolution fusion | flops 805306368 | bytes 5636096 | tf_op jit(solution)/shard_map/jsc,fjc->sf/dot_general | solution.py:101
  137.1 3.8 %fusion.13 = f32[256,384]{1,0:T(8,128)S(1)} fusion(bf16[384,4,1024]{0,2,1:T(8,128)(2,1)} %bitcast.115, bf16[4,256,2048]{2,1,0:T(8,128)(2,1)} %copy-done), kind=kOutput, calls=%fused_computation.28 | convolution fusion | flops 805306368 | bytes 5636096 | tf_op jit(solution)/shard_map/jsc,fjc->sf/dot_general | solution.py:94
  141.0 4.7 %multiply_convert_fusion.1 = (bf16[256,384]{1,0:T(8,128)(2,1)S(1)}, f32[256,384]{1,0:T(8,128)}) fusion(f32[256,384]{1,0:T(8,128)S(1)} %fusion.16, f32[256,384]{1,0:T(8,128)S(1)} %fusion.13, bf16[384,4,1024]{0,2,1:T(8,128)(2,1)} %bitcast.113, bf16[4,256,2048]{2,1,0:T(8,128)(2,1)} %copy-done), kind=kOutput, calls=%fused_computation.73 | convolution fusion | flops 806289408 | bytes 6619136 | tf_op jit(solution)/shard_map/jsc,fjc->sf/dot_general | solution.py:93
  145.7 3.3 %fusion.48 = f32[256,4,1024]{0,2,1:T(8,128)} fusion(bf16[384,4,1024]{0,2,1:T(8,128)(2,1)S(1)} %bitcast.114, bf16[256,384]{1,0:T(8,128)(2,1)S(1)} %get-tuple-element.39), kind=kOutput, calls=%fused_computation.80 | convolution fusion | flops 805306368 | bytes 7536640 | tf_op jit(solution)/shard_map/sf,fjc->jsc/dot_general | solution.py:107
  150.0 2.9 %copy.60 = bf16[384,4,1024]{0,2,1:T(8,128)(2,1)} copy(bf16[384,4,1024]{2,0,1:T(8,128)(2,1)S(1)} %convolution_convert_fusion) | data formatting | bytes 6291456 | tf_op jit(solution)/shard_map/convert_element_type | solution.py:112
  154.7 3.7 %fusion.4 = bf16[4,256,1024]{1,2,0:T(8,128)(2,1)S(1)} fusion(f32[256,4,1024]{0,2,1:T(8,128)} %fusion.48, bf16[384,4,1024]{0,2,1:T(8,128)(2,1)S(1)} %bitcast.116, f32[256,384]{1,0:T(8,128)S(1)} %fusion.16, f32[256,384]{1,0:T(8,128)} %get-tuple-element.40), kind=kOutput, calls=%fused_computation.21 | convolution fusion | flops 807993344 | bytes 10223616 | tf_op jit(solution)/shard_map/sf,fjc->jsc/dot_general | solution.py:108
  158.5 3.2 %convert_bitcast_fusion = bf16[4,256,1024]{1,2,0:T(8,128)(2,1)S(1)} fusion(bf16[384,4,1024]{0,2,1:T(8,128)(2,1)} %bitcast.9, f32[256,384]{1,0:T(8,128)S(1)} %copy-done.8, f32[256,384]{1,0:T(8,128)S(1)} %copy-done.4), kind=kOutput, calls=%fused_computation.20 | convolution fusion | flops 806944768 | bytes 6029312 | tf_op jit(solution)/shard_map/sf,fjc->jsc/dot_general | solution.py:98
  163.7 3.4 %collective-permute-start.12 = (bf16[128,2048]{0,1:T(8,128)(2,1)S(1)}, bf16[128,2048]{0,1:T(8,128)(2,1)S(1)}, u32[]{:S(2)}, u32[]{:S(2)}) collective-permute-start(bf16[128,2048]{0,1:T(8,128)(2,1)S(1)} %get-tuple-element.35), channel_id=1, source_target_pairs={{0,1},{1,2},{2,3},{3,0},{4,5},{5,6},{6,7},{7,4},{8,9},{9,10},{10,1... | collective-permute-start | bytes 1572872 | tf_op jit(solution)/shard_map/ppermute | solution.py:39
  167.8 4.7 %collective-permute-done.14 = bf16[128,2048]{0,1:T(8,128)(2,1)S(1)} collective-permute-done((bf16[128,2048]{0,1:T(8,128)(2,1)S(1)}, bf16[128,2048]{0,1:T(8,128)(2,1)S(1)}, u32[]{:S(2)}, u32[]{:S(2)}) %collective-permute-start.14) | collective-permute-done | bytes 524320 | tf_op jit(solution)/shard_map/ppermute | solution.py:40
  172.6 3.4 %collective-permute-start.15 = (bf16[256,2048]{0,1:T(8,128)(2,1)S(1)}, bf16[256,2048]{0,1:T(8,128)(2,1)S(1)}, u32[]{:S(2)}, u32[]{:S(2)}) collective-permute-start(bf16[256,2048]{0,1:T(8,128)(2,1)S(1)} %convert_element_type.121), channel_id=1, source_target_pairs={{0,3},{1,0},{2,1},{3,2},{4,7},{5,4},{6,5},{7,6},{8,11},{9,8},{10,9... | collective-permute-start | bytes 3145736 | tf_op jit(solution)/shard_map/ppermute | solution.py:50
  178.2 15.9 %collective-permute-done.15 = bf16[256,2048]{0,1:T(8,128)(2,1)S(1)} collective-permute-done((bf16[256,2048]{0,1:T(8,128)(2,1)S(1)}, bf16[256,2048]{0,1:T(8,128)(2,1)S(1)}, u32[]{:S(2)}, u32[]{:S(2)}) %collective-permute-start.15) | collective-permute-done | bytes 1048608 | tf_op jit(solution)/shard_map/ppermute | solution.py:50
  194.2 4.4 %collective-permute-done.13 = bf16[256,2048]{0,1:T(8,128)(2,1)S(1)} collective-permute-done((bf16[256,2048]{0,1:T(8,128)(2,1)S(1)}, bf16[256,2048]{0,1:T(8,128)(2,1)S(1)}, u32[]{:S(2)}, u32[]{:S(2)}) %collective-permute-start.13) | collective-permute-done | bytes 1048608 | tf_op jit(solution)/shard_map/ppermute | solution.py:49
  200.4 13.1 %all-to-all-start.1 = ((bf16[16,16,2048]{2,1,0:T(8,128)(2,1)}), bf16[16,16,2048]{2,1,0:T(8,128)(2,1)S(1)}, u32[]{:S(2)}, u32[]{:S(2)}) async-start(bf16[16,16,2048]{2,1,0:T(8,128)(2,1)} %bitcast.37), calls=%async_computation.1 | async-start | bytes 2097152 | tf_op jit(solution)/shard_map/all_to_all | solution.py:118
  213.5 27.9 %all-to-all-done.1 = bf16[16,16,2048]{2,1,0:T(8,128)(2,1)S(1)} async-done(((bf16[16,16,2048]{2,1,0:T(8,128)(2,1)}), bf16[16,16,2048]{2,1,0:T(8,128)(2,1)S(1)}, u32[]{:S(2)}, u32[]{:S(2)}) %all-to-all-start.1) | async-done | bytes 1048608 | tf_op jit(solution)/shard_map/all_to_all | solution.py:118
  (94 shorter events, 38.6 us)
Async XLA Ops:
  7.2 130.0 %all-gather.7.cloned.1.call-start = ((), (), s32[]{:S(2)}) async-start(), calls=%async_computation.5 | async-start | bytes 3538944 | tf_op jit(solution)/shard_map/all_gather | solution.py:85
  9.1 131.8 %all-gather.5.cloned.1.call-start = ((), (), s32[]{:S(2)}) async-start(), calls=%async_computation.4 | async-start | bytes 3538944 | tf_op jit(solution)/shard_map/all_gather | solution.py:84
  12.9 2.8 %copy-start.6 = (f32[24,8]{0,1:T(8,128)S(1)}, f32[24,8]{0,1:T(8,128)}, u32[]{:S(2)}) copy-start(f32[24,8]{0,1:T(8,128)} %param.13) | copy-start | bytes 2308
  14.5 14.7 %copy-start.5 = (bf16[1,384,512]{2,1,0:T(8,128)(2,1)S(1)}, bf16[1,384,512]{2,1,0:T(8,128)(2,1)}, u32[]{:S(2)}) copy-start(bf16[1,384,512]{2,1,0:T(8,128)(2,1)} %param.17) | copy-start | bytes 1179652
  18.8 67.1 %all-to-all-start = ((bf16[16,16,2048]{2,1,0:T(8,128)(2,1)}), bf16[16,16,2048]{2,1,0:T(8,128)(2,1)S(1)}, u32[]{:S(2)}, u32[]{:S(2)}) async-start(bf16[16,16,2048]{2,1,0:T(8,128)(2,1)} %bitcast.14), calls=%async_computation | async-start | bytes 2097152 | tf_op jit(solution)/shard_map/all_to_all | solution.py:77
  29.1 214.7 %reduce-scatter.2.cloned.1.call-start = ((), (), s32[]{:S(2)}) async-start(), calls=%async_computation.3 | async-start | bytes 3538944 | tf_op jit(solution)/shard_map/reduce_scatter | solution.py:113
  29.4 27.0 %collective-permute-start = (bf16[384,512]{0,1:T(8,128)(2,1)S(1)}, bf16[384,512]{0,1:T(8,128)(2,1)S(1)}, u32[]{:S(2)}, u32[]{:S(2)}) collective-permute-start(bf16[384,512]{0,1:T(8,128)(2,1)S(1)} %bitcast.117), channel_id=1, source_target_pairs={{0,64},{64,128},{128,192},{192,256},{256,320},{320,384},{384,448},... | collective-permute-start | bytes 1179656 | tf_op jit(solution)/shard_map/ppermute | solution.py:19
  31.7 26.6 %collective-permute-start.1 = (bf16[384,512]{0,1:T(8,128)(2,1)S(1)}, bf16[384,512]{0,1:T(8,128)(2,1)S(1)}, u32[]{:S(2)}, u32[]{:S(2)}) collective-permute-start(bf16[384,512]{0,1:T(8,128)(2,1)S(1)} %bitcast.118), channel_id=1, source_target_pairs={{0,448},{64,0},{128,64},{192,128},{256,192},{320,256},{384,320},{4... | collective-permute-start | bytes 1179656 | tf_op jit(solution)/shard_map/ppermute | solution.py:20
  56.4 22.1 %collective-permute-start.2 = (bf16[384,512]{0,1:T(8,128)(2,1)S(1)}, bf16[384,512]{0,1:T(8,128)(2,1)S(1)}, u32[]{:S(2)}, u32[]{:S(2)}) collective-permute-start(bf16[384,512]{0,1:T(8,128)(2,1)S(1)} %collective-permute-done), channel_id=1, source_target_pairs={{0,64},{64,128},{128,192},{192,256},{256,320},{320,384},{384,448},... | collective-permute-start | bytes 1179656 | tf_op jit(solution)/shard_map/ppermute | solution.py:19
  58.4 22.1 %collective-permute-start.3 = (bf16[384,512]{0,1:T(8,128)(2,1)S(1)}, bf16[384,512]{0,1:T(8,128)(2,1)S(1)}, u32[]{:S(2)}, u32[]{:S(2)}) collective-permute-start(bf16[384,512]{0,1:T(8,128)(2,1)S(1)} %collective-permute-done.1), channel_id=1, source_target_pairs={{0,448},{64,0},{128,64},{192,128},{256,192},{320,256},{384,320},{4... | collective-permute-start | bytes 1179656 | tf_op jit(solution)/shard_map/ppermute | solution.py:20
  78.6 18.6 %collective-permute-start.4 = (bf16[384,512]{0,1:T(8,128)(2,1)S(1)}, bf16[384,512]{0,1:T(8,128)(2,1)S(1)}, u32[]{:S(2)}, u32[]{:S(2)}) collective-permute-start(bf16[384,512]{0,1:T(8,128)(2,1)S(1)} %collective-permute-done.2), channel_id=1, source_target_pairs={{0,64},{64,128},{128,192},{192,256},{256,320},{320,384},{384,448},... | collective-permute-start | bytes 1179656 | tf_op jit(solution)/shard_map/ppermute | solution.py:19
  80.5 12.7 %collective-permute-start.5 = (bf16[384,512]{0,1:T(8,128)(2,1)S(1)}, bf16[384,512]{0,1:T(8,128)(2,1)S(1)}, u32[]{:S(2)}, u32[]{:S(2)}) collective-permute-start(bf16[384,512]{0,1:T(8,128)(2,1)S(1)} %collective-permute-done.3), channel_id=1, source_target_pairs={{0,448},{64,0},{128,64},{192,128},{256,192},{320,256},{384,320},{4... | collective-permute-start | bytes 1179656 | tf_op jit(solution)/shard_map/ppermute | solution.py:20
  85.9 33.4 %collective-permute-start.8 = (bf16[256,2048]{1,0:T(8,128)(2,1)S(1)}, bf16[256,2048]{1,0:T(8,128)(2,1)S(1)}, u32[]{:S(2)}, u32[]{:S(2)}) collective-permute-start(bf16[256,2048]{1,0:T(8,128)(2,1)S(1)} %bitcast.110), channel_id=1, source_target_pairs={{0,1},{1,2},{2,3},{3,0},{4,5},{5,6},{6,7},{7,4},{8,9},{9,10},{10,1... | collective-permute-start | bytes 3145736 | tf_op jit(solution)/shard_map/ppermute | solution.py:19
  89.0 25.7 %collective-permute-start.9 = (bf16[256,2048]{1,0:T(8,128)(2,1)S(1)}, bf16[256,2048]{1,0:T(8,128)(2,1)S(1)}, u32[]{:S(2)}, u32[]{:S(2)}) collective-permute-start(bf16[256,2048]{1,0:T(8,128)(2,1)S(1)} %bitcast.111), channel_id=1, source_target_pairs={{0,3},{1,0},{2,1},{3,2},{4,7},{5,4},{6,5},{7,6},{8,11},{9,8},{10,9... | collective-permute-start | bytes 3145736 | tf_op jit(solution)/shard_map/ppermute | solution.py:20
  93.3 14.9 %collective-permute-start.7 = (bf16[192,512]{0,1:T(8,128)(2,1)S(1)}, bf16[192,512]{0,1:T(8,128)(2,1)S(1)}, u32[]{:S(2)}, u32[]{:S(2)}) collective-permute-start(bf16[192,512]{0,1:T(8,128)(2,1)S(1)} %slice.91), channel_id=1, source_target_pairs={{0,448},{64,0},{128,64},{192,128},{256,192},{320,256},{384,320},{4... | collective-permute-start | bytes 589832 | tf_op jit(solution)/shard_map/ppermute | solution.py:25
  97.2 16.0 %collective-permute-start.6 = (bf16[192,512]{0,1:T(8,128)(2,1)S(1)}, bf16[192,512]{0,1:T(8,128)(2,1)S(1)}, u32[]{:S(2)}, u32[]{:S(2)}) collective-permute-start(bf16[192,512]{0,1:T(8,128)(2,1)S(1)} %slice.90), channel_id=1, source_target_pairs={{0,64},{64,128},{128,192},{192,256},{256,320},{320,384},{384,448},... | collective-permute-start | bytes 589832 | tf_op jit(solution)/shard_map/ppermute | solution.py:24
  114.8 11.9 %collective-permute-start.11 = (bf16[128,2048]{1,0:T(8,128)(2,1)S(1)}, bf16[128,2048]{1,0:T(8,128)(2,1)S(1)}, u32[]{:S(2)}, u32[]{:S(2)}) collective-permute-start(bf16[128,2048]{1,0:T(8,128)(2,1)S(1)} %slice.93), channel_id=1, source_target_pairs={{0,3},{1,0},{2,1},{3,2},{4,7},{5,4},{6,5},{7,6},{8,11},{9,8},{10,9... | collective-permute-start | bytes 1572872 | tf_op jit(solution)/shard_map/ppermute | solution.py:25
  119.3 12.6 %collective-permute-start.10 = (bf16[128,2048]{1,0:T(8,128)(2,1)S(1)}, bf16[128,2048]{1,0:T(8,128)(2,1)S(1)}, u32[]{:S(2)}, u32[]{:S(2)}) collective-permute-start(bf16[128,2048]{1,0:T(8,128)(2,1)S(1)} %slice.92), channel_id=1, source_target_pairs={{0,1},{1,2},{2,3},{3,0},{4,5},{5,6},{6,7},{7,4},{8,9},{9,10},{10,1... | collective-permute-start | bytes 1572872 | tf_op jit(solution)/shard_map/ppermute | solution.py:24
  132.0 1.9 copy-start
  140.9 4.8 %copy-start.7 = (f32[256,384]{1,0:T(8,128)}, f32[256,384]{1,0:T(8,128)S(1)}, u32[]{:S(2)}) copy-start(f32[256,384]{1,0:T(8,128)S(1)} %fusion.13) | copy-start | bytes 1179652
  140.9 4.7 %copy-start.2 = (bf16[1,384,4096]{1,2,0:T(8,128)(2,1)S(1)}, bf16[1,384,4096]{1,2,0:T(8,128)(2,1)}, u32[]{:S(2)}) copy-start(bf16[1,384,4096]{1,2,0:T(8,128)(2,1)} %all-gather.5.cloned.1.call-done) | copy-start | bytes 9437188
  145.7 3.3 %copy-start.1 = (bf16[4,256,2048]{2,1,0:T(8,128)(2,1)S(1)}, bf16[4,256,2048]{2,1,0:T(8,128)(2,1)}, u32[]{:S(2)}) copy-start(bf16[4,256,2048]{2,1,0:T(8,128)(2,1)} %copy-done) | copy-start | bytes 12582916
  152.9 1.9 copy-start.3
  154.7 3.7 %copy-start.4 = (f32[256,384]{1,0:T(8,128)S(1)}, f32[256,384]{1,0:T(8,128)}, u32[]{:S(2)}) copy-start(f32[256,384]{1,0:T(8,128)} %get-tuple-element.40) | copy-start | bytes 1179652
  154.7 3.7 %copy-start.8 = (f32[256,384]{1,0:T(8,128)S(1)}, f32[256,384]{1,0:T(8,128)}, u32[]{:S(2)}) copy-start(f32[256,384]{1,0:T(8,128)} %copy-done.7) | copy-start | bytes 1179652
  161.8 10.6 %collective-permute-start.14 = (bf16[128,2048]{0,1:T(8,128)(2,1)S(1)}, bf16[128,2048]{0,1:T(8,128)(2,1)S(1)}, u32[]{:S(2)}, u32[]{:S(2)}) collective-permute-start(bf16[128,2048]{0,1:T(8,128)(2,1)S(1)} %get-tuple-element.36), channel_id=1, source_target_pairs={{0,3},{1,0},{2,1},{3,2},{4,7},{5,4},{6,5},{7,6},{8,11},{9,8},{10,9... | collective-permute-start | bytes 1572872 | tf_op jit(solution)/shard_map/ppermute | solution.py:40
  163.7 12.3 %collective-permute-start.12 = (bf16[128,2048]{0,1:T(8,128)(2,1)S(1)}, bf16[128,2048]{0,1:T(8,128)(2,1)S(1)}, u32[]{:S(2)}, u32[]{:S(2)}) collective-permute-start(bf16[128,2048]{0,1:T(8,128)(2,1)S(1)} %get-tuple-element.35), channel_id=1, source_target_pairs={{0,1},{1,2},{2,3},{3,0},{4,5},{5,6},{6,7},{7,4},{8,9},{9,10},{10,1... | collective-permute-start | bytes 1572872 | tf_op jit(solution)/shard_map/ppermute | solution.py:39
  172.6 21.5 %collective-permute-start.15 = (bf16[256,2048]{0,1:T(8,128)(2,1)S(1)}, bf16[256,2048]{0,1:T(8,128)(2,1)S(1)}, u32[]{:S(2)}, u32[]{:S(2)}) collective-permute-start(bf16[256,2048]{0,1:T(8,128)(2,1)S(1)} %convert_element_type.121), channel_id=1, source_target_pairs={{0,3},{1,0},{2,1},{3,2},{4,7},{5,4},{6,5},{7,6},{8,11},{9,8},{10,9... | collective-permute-start | bytes 3145736 | tf_op jit(solution)/shard_map/ppermute | solution.py:50
  176.3 22.2 %collective-permute-start.13 = (bf16[256,2048]{0,1:T(8,128)(2,1)S(1)}, bf16[256,2048]{0,1:T(8,128)(2,1)S(1)}, u32[]{:S(2)}, u32[]{:S(2)}) collective-permute-start(bf16[256,2048]{0,1:T(8,128)(2,1)S(1)} %convert_element_type.115), channel_id=1, source_target_pairs={{0,1},{1,2},{2,3},{3,0},{4,5},{5,6},{6,7},{7,4},{8,9},{9,10},{10,1... | collective-permute-start | bytes 3145736 | tf_op jit(solution)/shard_map/ppermute | solution.py:49
  200.4 41.0 %all-to-all-start.1 = ((bf16[16,16,2048]{2,1,0:T(8,128)(2,1)}), bf16[16,16,2048]{2,1,0:T(8,128)(2,1)S(1)}, u32[]{:S(2)}, u32[]{:S(2)}) async-start(bf16[16,16,2048]{2,1,0:T(8,128)(2,1)} %bitcast.37), calls=%async_computation.1 | async-start | bytes 2097152 | tf_op jit(solution)/shard_map/all_to_all | solution.py:118
Sparse Core Ops, SparseCore 0:
  10.7 70.7 all-gather.6
  83.5 52.1 all-gather.4
  153.0 46.5 reduce-scatter.1

commit v3 on v2

--- a/solution.py
+++ b/solution.py
@@ -69,16 +69,21 @@
 
     tok_part = lax.dynamic_slice_in_dim(tokens, share_idx * part, part, axis=1)
     cot_part = lax.dynamic_slice_in_dim(cotangent, share_idx * part, part, axis=1)
-    copies = jnp.broadcast_to(tok_part[:, None, :], (tok_count, top_count, part))
-    scaled = (route_weights[:, :, None] * cot_part[:, None, :].astype(jnp.float32)).astype(jnp.bfloat16)
-    both = jnp.concatenate([copies, scaled], axis=2).reshape(-1, 2 * part)
-    empty_slots = jnp.zeros((slot_rows, 2 * part), jnp.bfloat16)
-    send = empty_slots.at[slot_index].set(both).reshape(experts, capacity, 2 * part)
-    recv = lax.all_to_all(send, "expert", split_axis=0, concat_axis=0, tiled=True)
-    recv = recv.reshape(1, slot_rows, 2 * part)
-    gathered = ring_gather(recv[0], "etp", shares)
-    rows4 = gathered[:, :, :part]
-    grads4 = gathered[:, :, part:]
+    copies = jnp.broadcast_to(tok_part[:, None, :], (tok_count, top_count, part)).reshape(-1, part)
+    scaled = (
+        (route_weights[:, :, None] * cot_part[:, None, :].astype(jnp.float32))
+        .astype(jnp.bfloat16)
+        .reshape(-1, part)
+    )
+    empty_slots = jnp.zeros((slot_rows, part), jnp.bfloat16)
+
+    def dispatch(values):
+        send = empty_slots.at[slot_index].set(values).reshape(experts, capacity, part)
+        recv = lax.all_to_all(send, "expert", split_axis=0, concat_axis=0, tiled=True)
+        return ring_gather(recv.reshape(slot_rows, part), "etp", shares)
+
+    rows4 = dispatch(copies)
+    grads4 = dispatch(scaled)
 
     gate_full, up_full, down_full = (
         lax.all_gather(w_gate[0], "dp", axis=1, tiled=True),
@@ -113,15 +118,16 @@
     weight_grads = lax.psum_scatter(gate_term, "dp", scatter_dimension=1, tiled=True)
     grad_gate = weight_grads.astype(jnp.float32)[None]
 
-    outs4 = jnp.concatenate([mixed4, input4], axis=2)
-    slot_out = ring_reduce_scatter(outs4, "etp", shares).astype(jnp.bfloat16)
-    back = lax.all_to_all(
-        slot_out.reshape(experts, capacity, 2 * part), "expert", split_axis=0, concat_axis=0, tiled=True
-    )
-    token_out = back.reshape(slot_rows, 2 * part)[slot_index].reshape(tok_count, top_count, 2 * part)
-    token_out = token_out.astype(jnp.float32)
-    mixed = jnp.sum(route_weights[:, :, None] * token_out[:, :, :part], axis=1)
-    grad_tokens = jnp.sum(token_out[:, :, part:], axis=1)
+    def collect(outs4):
+        slot_out = ring_reduce_scatter(outs4, "etp", shares).astype(jnp.bfloat16)
+        back = lax.all_to_all(
+            slot_out.reshape(experts, capacity, part), "expert", split_axis=0, concat_axis=0, tiled=True
+        )
+        token_out = back.reshape(slot_rows, part)[slot_index].reshape(tok_count, top_count, part)
+        return token_out.astype(jnp.float32)
+
+    mixed = jnp.sum(route_weights[:, :, None] * collect(mixed4), axis=1)
+    grad_tokens = jnp.sum(collect(input4), axis=1)
     return (mixed.astype(jnp.bfloat16), grad_tokens.astype(jnp.bfloat16), grad_gate)
 
 

time: 254 us -> 282 us (1.11)
  blocking collectives: 0 us -> 28.8 us
  waiting for transfers between devices: 103 us -> 76.1 us
  starting transfers between devices: 76.8 us -> 99.6 us
  local copies, waits for them, and re-layouts: 26.4 us -> 35 us
  matrix products: 22.9 us -> 16.2 us
    all_to_all x0 -> x1, blocking collectives: none -> 28.8 us  [collect(): lax.all_to_all(slot_out.reshape(experts, capacity, part), 'expert', split...]
    ppermute x2 -> x4, waiting for transfers between devices: 20.6 us -> 2.67 us  [ring_reduce_scatter(): lax.ppermute(to_left.astype(chunks.dtype), axis, bwd).astype(jnp.float32)]
    ppermute x2 -> x4, starting transfers between devices: 5.33 us -> 19 us  [ring_reduce_scatter(): lax.ppermute(to_left.astype(chunks.dtype), axis, bwd).astype(jnp.float32)]
    all_to_all x2 -> x3, waiting for transfers between devices: 27.9 us -> 18.2 us  [the longest x1 15.7 us: collect(): lax.all_to_all(slot_out.reshape(experts, capacity, part), 'expert', split...]
    ppermute x4 -> x5, waiting for transfers between devices: 27.1 us -> 18.8 us  [ring_gather(): left = lax.ppermute(left, axis, fwd)]
    ppermute x2 -> x4, waiting for transfers between devices: 4.39 us -> 11.3 us  [ring_reduce_scatter(): lax.ppermute(to_right.astype(chunks.dtype), axis, fwd).astype(jnp.float32)]
    dynamic_update_slice x10 -> x13, local copies, waits for them, and re-layouts: 5.98 us -> 12 us  [ring_gather(): lax.dynamic_update_index_in_dim(buf, val, at % n, along)]
    ppermute x4 -> x5, starting transfers between devices: 21.1 us -> 25.6 us  [ring_gather(): right = lax.ppermute(right, axis, bwd)]
  transfers between devices with their start and end apart: 21 -> 30, of which waited for: 10 -> 11; matrix products, arithmetic and copies ran while one was open for 15% -> 16% of each run, Pallas kernels for 0% -> 0%
where the time goes in v3:
time: 282 us; the launch traced here: 280 us
  starting transfers between devices  99.6 us (35%)
  waiting for transfers between devices  76.1 us (27%)
  local copies, waits for them, and re-layouts  35 us (12%)
  blocking collectives  28.8 us (10%)
  matrix products  16.2 us (6%)
  between operations  14.8 us (5%)
  other arithmetic  9.55 us (3%)
    all_to_all x1, blocking collectives, collect(): lax.all_to_all(slot_out.reshape(experts, capacity, part), 'expert', split...  28.8 us
    ppermute x5, starting transfers between devices, ring_gather(): right = lax.ppermute(right, axis, bwd)  25.6 us
    ppermute x4, starting transfers between devices, ring_reduce_scatter(): lax.ppermute(to_left.astype(chunks.dtype), axis, bwd).astype(jnp.float32)  19 us
    ppermute x5, waiting for transfers between devices, ring_gather(): left = lax.ppermute(left, axis, fwd)  18.8 us
    all_to_all x2, starting transfers between devices, dispatch(): lax.all_to_all(send, 'expert', split_axis=0, concat_axis=0, tiled=True)  15.9 us
    all_to_all x1, waiting for transfers between devices, collect(): lax.all_to_all(slot_out.reshape(experts, capacity, part), 'expert', split...  15.7 us
    ppermute x3, waiting for transfers between devices, ring_gather(): second = lax.ppermute(right[m:], axis, bwd)  13.2 us
    dynamic_update_slice x13, local copies, waits for them, and re-layouts, ring_gather(): lax.dynamic_update_index_in_dim(buf, val, at % n, along)  12 us
  transfers between devices with their start and end apart: 30, of which 11 were waited for; matrix products, arithmetic and copies ran while one was open for 16% of the time, Pallas kernels for 0%

profile of v3, /device:TPU:1, one launch (start us, length us, event | category | flops | bytes accessed | tf_op | source)
XLA Modules:
  0.0 280.0 jit_solution(15046849314413057600)
XLA Ops:
  7.2 2.0 copy.44
  15.8 2.3 scatter_custom_fusion.1
  18.1 10.9 %all-to-all-start.2 = ((bf16[16,16,1024]{2,1,0:T(8,128)(2,1)}), bf16[16,16,1024]{2,1,0:T(8,128)(2,1)}, u32[]{:S(2)}, u32[]{:S(2)}) async-start(bf16[16,16,1024]{2,1,0:T(8,128)(2,1)} %bitcast.40), calls=%async_computation.2 | async-start | bytes 1048576 | tf_op jit(solution)/shard_map/all_to_all | solution.py:82
  31.8 8.4 %collective-permute-start.1 = (bf16[384,512]{0,1:T(8,128)(2,1)}, bf16[384,512]{0,1:T(8,128)(2,1)}, u32[]{:S(2)}, u32[]{:S(2)}) collective-permute-start(bf16[384,512]{0,1:T(8,128)(2,1)} %bitcast.1), channel_id=1, source_target_pairs={{0,448},{64,0},{128,64},{192,128},{256,192},{320,256},{384,320},{4... | collective-permute-start | bytes 1179656 | tf_op jit(solution)/shard_map/ppermute | solution.py:20
  40.3 2.2 scatter_custom_fusion
  43.9 2.5 all-to-all-done.2
  46.4 5.0 %all-to-all-start = ((bf16[16,16,1024]{2,1,0:T(8,128)(2,1)}), bf16[16,16,1024]{2,1,0:T(8,128)(2,1)}, u32[]{:S(2)}, u32[]{:S(2)}) async-start(bf16[16,16,1024]{2,1,0:T(8,128)(2,1)} %bitcast.181), calls=%async_computation | async-start | bytes 1048576 | tf_op jit(solution)/shard_map/all_to_all | solution.py:82
  51.6 5.0 %collective-permute-done = bf16[384,512]{0,1:T(8,128)(2,1)} collective-permute-done((bf16[384,512]{0,1:T(8,128)(2,1)}, bf16[384,512]{0,1:T(8,128)(2,1)}, u32[]{:S(2)}, u32[]{:S(2)}) %collective-permute-start) | collective-permute-done | bytes 393248 | tf_op jit(solution)/shard_map/ppermute | solution.py:19
  58.5 4.6 %collective-permute-start.3 = (bf16[384,512]{0,1:T(8,128)(2,1)}, bf16[384,512]{0,1:T(8,128)(2,1)}, u32[]{:S(2)}, u32[]{:S(2)}) collective-permute-start(bf16[384,512]{0,1:T(8,128)(2,1)} %collective-permute-done.1), channel_id=1, source_target_pairs={{0,448},{64,0},{128,64},{192,128},{256,192},{320,256},{384,320},{4... | collective-permute-start | bytes 1179656 | tf_op jit(solution)/shard_map/ppermute | solution.py:20
  65.3 13.7 %collective-permute-done.2 = bf16[384,512]{0,1:T(8,128)(2,1)} collective-permute-done((bf16[384,512]{0,1:T(8,128)(2,1)}, bf16[384,512]{0,1:T(8,128)(2,1)}, u32[]{:S(2)}, u32[]{:S(2)}) %collective-permute-start.2) | collective-permute-done | bytes 393248 | tf_op jit(solution)/shard_map/ppermute | solution.py:19
  80.9 4.6 %collective-permute-start.5 = (bf16[384,512]{0,1:T(8,128)(2,1)}, bf16[384,512]{0,1:T(8,128)(2,1)}, u32[]{:S(2)}, u32[]{:S(2)}) collective-permute-start(bf16[384,512]{0,1:T(8,128)(2,1)} %collective-permute-done.3), channel_id=1, source_target_pairs={{0,448},{64,0},{128,64},{192,128},{256,192},{320,256},{384,320},{4... | collective-permute-start | bytes 1179656 | tf_op jit(solution)/shard_map/ppermute | solution.py:20
  87.7 3.1 %collective-permute-start.16 = (bf16[256,1024]{1,0:T(8,128)(2,1)}, bf16[256,1024]{1,0:T(8,128)(2,1)}, u32[]{:S(2)}, u32[]{:S(2)}) collective-permute-start(bf16[256,1024]{1,0:T(8,128)(2,1)} %bitcast.42), channel_id=1, source_target_pairs={{0,1},{1,2},{2,3},{3,0},{4,5},{5,6},{6,7},{7,4},{8,9},{9,10},{10,1... | collective-permute-start | bytes 1572872 | tf_op jit(solution)/shard_map/ppermute | solution.py:19
  90.8 3.4 %collective-permute-start.17 = (bf16[256,1024]{1,0:T(8,128)(2,1)}, bf16[256,1024]{1,0:T(8,128)(2,1)}, u32[]{:S(2)}, u32[]{:S(2)}) collective-permute-start(bf16[256,1024]{1,0:T(8,128)(2,1)} %bitcast.42), channel_id=1, source_target_pairs={{0,3},{1,0},{2,1},{3,2},{4,7},{5,4},{6,5},{7,6},{8,11},{9,8},{10,9... | collective-permute-start | bytes 1572872 | tf_op jit(solution)/shard_map/ppermute | solution.py:20
  99.0 4.6 %collective-permute-start.9 = (bf16[256,1024]{1,0:T(8,128)(2,1)}, bf16[256,1024]{1,0:T(8,128)(2,1)S(1)}, u32[]{:S(2)}, u32[]{:S(2)}) collective-permute-start(bf16[256,1024]{1,0:T(8,128)(2,1)} %bitcast.15), channel_id=1, source_target_pairs={{0,3},{1,0},{2,1},{3,2},{4,7},{5,4},{6,5},{7,6},{8,11},{9,8},{10,9... | collective-permute-start | bytes 1572872 | tf_op jit(solution)/shard_map/ppermute | solution.py:20
  108.7 11.8 %collective-permute-done.6 = bf16[192,512]{0,1:T(8,128)(2,1)S(1)} collective-permute-done((bf16[192,512]{0,1:T(8,128)(2,1)S(1)}, bf16[192,512]{0,1:T(8,128)(2,1)S(1)}, u32[]{:S(2)}, u32[]{:S(2)}) %collective-permute-start.6) | collective-permute-done | bytes 196640 | tf_op jit(solution)/shard_map/ppermute | solution.py:24
  123.4 11.2 %collective-permute-done.7 = bf16[192,512]{0,1:T(8,128)(2,1)S(1)} collective-permute-done((bf16[192,512]{0,1:T(8,128)(2,1)S(1)}, bf16[192,512]{0,1:T(8,128)(2,1)S(1)}, u32[]{:S(2)}, u32[]{:S(2)}) %collective-permute-start.7) | collective-permute-done | bytes 196640 | tf_op jit(solution)/shard_map/ppermute | solution.py:25
  139.0 4.6 %collective-permute-start.19 = (bf16[128,1024]{1,0:T(8,128)(2,1)S(1)}, bf16[128,1024]{1,0:T(8,128)(2,1)S(1)}, u32[]{:S(2)}, u32[]{:S(2)}) collective-permute-start(bf16[128,1024]{1,0:T(8,128)(2,1)S(1)} %slice.147), channel_id=1, source_target_pairs={{0,3},{1,0},{2,1},{3,2},{4,7},{5,4},{6,5},{7,6},{8,11},{9,8},{10,9... | collective-permute-start | bytes 786440 | tf_op jit(solution)/shard_map/ppermute | solution.py:25
  145.5 4.8 %collective-permute-start.11 = (bf16[128,1024]{1,0:T(8,128)(2,1)S(1)}, bf16[128,1024]{1,0:T(8,128)(2,1)S(1)}, u32[]{:S(2)}, u32[]{:S(2)}) collective-permute-start(bf16[128,1024]{1,0:T(8,128)(2,1)S(1)} %slice.141), channel_id=1, source_target_pairs={{0,3},{1,0},{2,1},{3,2},{4,7},{5,4},{6,5},{7,6},{8,11},{9,8},{10,9... | collective-permute-start | bytes 786440 | tf_op jit(solution)/shard_map/ppermute | solution.py:25
  156.1 3.3 %convolution_bitcast_fusion.1 = f32[256,384]{1,0:T(8,128)S(1)} fusion(bf16[4,256,1024]{2,1,0:T(8,128)(2,1)S(1)} %fusion.14, bf16[384,4,1024]{0,2,1:T(8,128)(2,1)} %bitcast.178), kind=kOutput, calls=%fused_computation.17 | convolution fusion | flops 805306368 | bytes 5636096 | tf_op jit(solution)/shard_map/jsc,fjc->sf/dot_general | solution.py:99
  159.4 4.0 %multiply_convert_fusion.1 = (bf16[256,384]{1,0:T(8,128)(2,1)S(1)}, f32[256,384]{1,0:T(8,128)}) fusion(f32[256,384]{1,0:T(8,128)S(1)} %convolution_bitcast_fusion, f32[256,384]{1,0:T(8,128)S(1)} %convolution_bitcast_fusion.1, bf16[4,256,1024]{2,1,0:T(8,128)(2,1)S(1)} %fusion.14, bf16[384,4,1024]{0,2,1:T(8,128)(2,1)} %bitcast.174), kind=kOutput, calls=%fused_computation.70 | convolution fusion | flops 806289408 | bytes 6619136 | tf_op jit(solution)/shard_map/jsc,fjc->sf/dot_general | solution.py:98
  163.4 2.6 convolution_convert_fusion
  166.0 2.8 %copy.52 = bf16[384,4,1024]{0,2,1:T(8,128)(2,1)} copy(bf16[384,4,1024]{2,0,1:T(8,128)(2,1)S(1)} %convolution_convert_fusion) | data formatting | bytes 6291456 | tf_op jit(solution)/shard_map/convert_element_type | solution.py:117
  170.7 2.4 convolution_convert_fusion.1
  173.6 2.1 collective-permute-start.12
  175.7 5.3 %collective-permute-start.14 = (bf16[128,1024]{1,0:T(8,128)(2,1)S(1)}, bf16[128,1024]{1,0:T(8,128)(2,1)S(1)}, u32[]{:S(2)}, u32[]{:S(2)}) collective-permute-start(bf16[128,1024]{1,0:T(8,128)(2,1)S(1)} %slice_bitcast_fusion.6), channel_id=1, source_target_pairs={{0,3},{1,0},{2,1},{3,2},{4,7},{5,4},{6,5},{7,6},{8,11},{9,8},{10,9... | collective-permute-start | bytes 786440 | tf_op jit(solution)/shard_map/ppermute | solution.py:40
  186.2 4.6 %collective-permute-start.22 = (bf16[128,1024]{1,0:T(8,128)(2,1)S(1)}, bf16[128,1024]{1,0:T(8,128)(2,1)S(1)}, u32[]{:S(2)}, u32[]{:S(2)}) collective-permute-start(bf16[128,1024]{1,0:T(8,128)(2,1)S(1)} %slice_bitcast_fusion.4), channel_id=1, source_target_pairs={{0,3},{1,0},{2,1},{3,2},{4,7},{5,4},{6,5},{7,6},{8,11},{9,8},{10,9... | collective-permute-start | bytes 786440 | tf_op jit(solution)/shard_map/ppermute | solution.py:40
  192.8 4.6 %collective-permute-start.15 = (bf16[256,1024]{1,0:T(8,128)(2,1)S(1)}, bf16[256,1024]{1,0:T(8,128)(2,1)S(1)}, u32[]{:S(2)}, u32[]{:S(2)}) collective-permute-start(bf16[256,1024]{1,0:T(8,128)(2,1)S(1)} %fusion.11), channel_id=1, source_target_pairs={{0,3},{1,0},{2,1},{3,2},{4,7},{5,4},{6,5},{7,6},{8,11},{9,8},{10,9... | collective-permute-start | bytes 1572872 | tf_op jit(solution)/shard_map/ppermute | solution.py:50
  199.5 4.6 %collective-permute-start.23 = (bf16[256,1024]{1,0:T(8,128)(2,1)S(1)}, bf16[256,1024]{1,0:T(8,128)(2,1)S(1)}, u32[]{:S(2)}, u32[]{:S(2)}) collective-permute-start(bf16[256,1024]{1,0:T(8,128)(2,1)S(1)} %fusion.7), channel_id=1, source_target_pairs={{0,3},{1,0},{2,1},{3,2},{4,7},{5,4},{6,5},{7,6},{8,11},{9,8},{10,9... | collective-permute-start | bytes 1572872 | tf_op jit(solution)/shard_map/ppermute | solution.py:50
  206.8 9.9 %collective-permute-done.21 = bf16[256,1024]{1,0:T(8,128)(2,1)S(1)} collective-permute-done((bf16[256,1024]{1,0:T(8,128)(2,1)S(1)}, bf16[256,1024]{1,0:T(8,128)(2,1)S(1)}, u32[]{:S(2)}, u32[]{:S(2)}) %collective-permute-start.21) | collective-permute-done | bytes 524320 | tf_op jit(solution)/shard_map/ppermute | solution.py:49
  219.5 28.8 %all_to_all.20 = bf16[16,16,1024]{2,1,0:T(8,128)(2,1)S(1)} all-to-all(bf16[16,16,1024]{2,1,0:T(8,128)(2,1)S(1)} %bitcast.180), channel_id=1, replica_groups=mesh['dp'=8,'expert'=16,'etp'=4] {'expert'}, dimensions={0} | all-to-all | bytes 1048576 | tf_op jit(solution)/shard_map/all_to_all | solution.py:123
  248.3 3.5 %all-to-all-start.1 = ((bf16[16,16,1024]{2,1,0:T(8,128)(2,1)}), bf16[16,16,1024]{2,1,0:T(8,128)(2,1)S(1)}, u32[]{:S(2)}, u32[]{:S(2)}) async-start(bf16[16,16,1024]{2,1,0:T(8,128)(2,1)} %bitcast.36), calls=%async_computation.1 | async-start | bytes 1048576 | tf_op jit(solution)/shard_map/all_to_all | solution.py:123
  252.8 15.7 %all-to-all-done.1 = bf16[16,16,1024]{2,1,0:T(8,128)(2,1)S(1)} async-done(((bf16[16,16,1024]{2,1,0:T(8,128)(2,1)}), bf16[16,16,1024]{2,1,0:T(8,128)(2,1)S(1)}, u32[]{:S(2)}, u32[]{:S(2)}) %all-to-all-start.1) | async-done | bytes 524320 | tf_op jit(solution)/shard_map/all_to_all | solution.py:123
  (132 shorter events, 66.6 us)
Async XLA Ops:
  7.2 33.1 %copy-start = (bf16[24,4096]{1,0:T(8,128)(2,1)S(1)}, bf16[24,4096]{1,0:T(8,128)(2,1)}, u32[]{:S(2)}) copy-start(bf16[24,4096]{1,0:T(8,128)(2,1)} %param.15) | copy-start | bytes 589828
  7.2 148.9 %all-gather.7.cloned.1.call-start = ((), (), s32[]{:S(2)}) async-start(), calls=%async_computation.7 | async-start | bytes 3538944 | tf_op jit(solution)/shard_map/all_gather | solution.py:90
  9.3 150.1 %all-gather.5.cloned.1.call-start = ((), (), s32[]{:S(2)}) async-start(), calls=%async_computation.6 | async-start | bytes 3538944 | tf_op jit(solution)/shard_map/all_gather | solution.py:89
  18.1 28.3 %all-to-all-start.2 = ((bf16[16,16,1024]{2,1,0:T(8,128)(2,1)}), bf16[16,16,1024]{2,1,0:T(8,128)(2,1)}, u32[]{:S(2)}, u32[]{:S(2)}) async-start(bf16[16,16,1024]{2,1,0:T(8,128)(2,1)} %bitcast.40), calls=%async_computation.2 | async-start | bytes 1048576 | tf_op jit(solution)/shard_map/all_to_all | solution.py:82
  29.9 26.8 %collective-permute-start = (bf16[384,512]{0,1:T(8,128)(2,1)}, bf16[384,512]{0,1:T(8,128)(2,1)}, u32[]{:S(2)}, u32[]{:S(2)}) collective-permute-start(bf16[384,512]{0,1:T(8,128)(2,1)} %bitcast.1), channel_id=1, source_target_pairs={{0,64},{64,128},{128,192},{192,256},{256,320},{320,384},{384,448},... | collective-permute-start | bytes 1179656 | tf_op jit(solution)/shard_map/ppermute | solution.py:19
  31.8 26.8 %collective-permute-start.1 = (bf16[384,512]{0,1:T(8,128)(2,1)}, bf16[384,512]{0,1:T(8,128)(2,1)}, u32[]{:S(2)}, u32[]{:S(2)}) collective-permute-start(bf16[384,512]{0,1:T(8,128)(2,1)} %bitcast.1), channel_id=1, source_target_pairs={{0,448},{64,0},{128,64},{192,128},{256,192},{320,256},{384,320},{4... | collective-permute-start | bytes 1179656 | tf_op jit(solution)/shard_map/ppermute | solution.py:20
  46.4 47.8 %all-to-all-start = ((bf16[16,16,1024]{2,1,0:T(8,128)(2,1)}), bf16[16,16,1024]{2,1,0:T(8,128)(2,1)}, u32[]{:S(2)}, u32[]{:S(2)}) async-start(bf16[16,16,1024]{2,1,0:T(8,128)(2,1)} %bitcast.181), calls=%async_computation | async-start | bytes 1048576 | tf_op jit(solution)/shard_map/all_to_all | solution.py:82
  51.4 219.9 %reduce-scatter.2.cloned.1.call-start = ((), (), s32[]{:S(2)}) async-start(), calls=%async_computation.5 | async-start | bytes 3538944 | tf_op jit(solution)/shard_map/reduce_scatter | solution.py:118
  56.6 22.4 %collective-permute-start.2 = (bf16[384,512]{0,1:T(8,128)(2,1)}, bf16[384,512]{0,1:T(8,128)(2,1)}, u32[]{:S(2)}, u32[]{:S(2)}) collective-permute-start(bf16[384,512]{0,1:T(8,128)(2,1)} %collective-permute-done), channel_id=1, source_target_pairs={{0,64},{64,128},{128,192},{192,256},{256,320},{320,384},{384,448},... | collective-permute-start | bytes 1179656 | tf_op jit(solution)/shard_map/ppermute | solution.py:19
  58.5 22.4 %collective-permute-start.3 = (bf16[384,512]{0,1:T(8,128)(2,1)}, bf16[384,512]{0,1:T(8,128)(2,1)}, u32[]{:S(2)}, u32[]{:S(2)}) collective-permute-start(bf16[384,512]{0,1:T(8,128)(2,1)} %collective-permute-done.1), channel_id=1, source_target_pairs={{0,448},{64,0},{128,64},{192,128},{256,192},{320,256},{384,320},{4... | collective-permute-start | bytes 1179656 | tf_op jit(solution)/shard_map/ppermute | solution.py:20
  79.0 20.0 %collective-permute-start.4 = (bf16[384,512]{0,1:T(8,128)(2,1)}, bf16[384,512]{0,1:T(8,128)(2,1)}, u32[]{:S(2)}, u32[]{:S(2)}) collective-permute-start(bf16[384,512]{0,1:T(8,128)(2,1)} %collective-permute-done.2), channel_id=1, source_target_pairs={{0,64},{64,128},{128,192},{192,256},{256,320},{320,384},{384,448},... | collective-permute-start | bytes 1179656 | tf_op jit(solution)/shard_map/ppermute | solution.py:19
  80.9 23.6 %collective-permute-start.5 = (bf16[384,512]{0,1:T(8,128)(2,1)}, bf16[384,512]{0,1:T(8,128)(2,1)}, u32[]{:S(2)}, u32[]{:S(2)}) collective-permute-start(bf16[384,512]{0,1:T(8,128)(2,1)} %collective-permute-done.3), channel_id=1, source_target_pairs={{0,448},{64,0},{128,64},{192,128},{256,192},{320,256},{384,320},{4... | collective-permute-start | bytes 1179656 | tf_op jit(solution)/shard_map/ppermute | solution.py:20
  87.7 47.2 %collective-permute-start.16 = (bf16[256,1024]{1,0:T(8,128)(2,1)}, bf16[256,1024]{1,0:T(8,128)(2,1)}, u32[]{:S(2)}, u32[]{:S(2)}) collective-permute-start(bf16[256,1024]{1,0:T(8,128)(2,1)} %bitcast.42), channel_id=1, source_target_pairs={{0,1},{1,2},{2,3},{3,0},{4,5},{5,6},{6,7},{7,4},{8,9},{9,10},{10,1... | collective-permute-start | bytes 1572872 | tf_op jit(solution)/shard_map/ppermute | solution.py:19
  90.8 47.2 %collective-permute-start.17 = (bf16[256,1024]{1,0:T(8,128)(2,1)}, bf16[256,1024]{1,0:T(8,128)(2,1)}, u32[]{:S(2)}, u32[]{:S(2)}) collective-permute-start(bf16[256,1024]{1,0:T(8,128)(2,1)} %bitcast.42), channel_id=1, source_target_pairs={{0,3},{1,0},{2,1},{3,2},{4,7},{5,4},{6,5},{7,6},{8,11},{9,8},{10,9... | collective-permute-start | bytes 1572872 | tf_op jit(solution)/shard_map/ppermute | solution.py:20
  94.2 49.4 %collective-permute-start.8 = (bf16[256,1024]{1,0:T(8,128)(2,1)}, bf16[256,1024]{1,0:T(8,128)(2,1)S(1)}, u32[]{:S(2)}, u32[]{:S(2)}) collective-permute-start(bf16[256,1024]{1,0:T(8,128)(2,1)} %bitcast.15), channel_id=1, source_target_pairs={{0,1},{1,2},{2,3},{3,0},{4,5},{5,6},{6,7},{7,4},{8,9},{9,10},{10,1... | collective-permute-start | bytes 1572872 | tf_op jit(solution)/shard_map/ppermute | solution.py:19
  99.0 46.5 %collective-permute-start.9 = (bf16[256,1024]{1,0:T(8,128)(2,1)}, bf16[256,1024]{1,0:T(8,128)(2,1)S(1)}, u32[]{:S(2)}, u32[]{:S(2)}) collective-permute-start(bf16[256,1024]{1,0:T(8,128)(2,1)} %bitcast.15), channel_id=1, source_target_pairs={{0,3},{1,0},{2,1},{3,2},{4,7},{5,4},{6,5},{7,6},{8,11},{9,8},{10,9... | collective-permute-start | bytes 1572872 | tf_op jit(solution)/shard_map/ppermute | solution.py:20
  104.5 15.9 %collective-permute-start.6 = (bf16[192,512]{0,1:T(8,128)(2,1)S(1)}, bf16[192,512]{0,1:T(8,128)(2,1)S(1)}, u32[]{:S(2)}, u32[]{:S(2)}) collective-permute-start(bf16[192,512]{0,1:T(8,128)(2,1)S(1)} %slice.138), channel_id=1, source_target_pairs={{0,64},{64,128},{128,192},{192,256},{256,320},{320,384},{384,448},... | collective-permute-start | bytes 589832 | tf_op jit(solution)/shard_map/ppermute | solution.py:24
  120.5 14.2 %collective-permute-start.7 = (bf16[192,512]{0,1:T(8,128)(2,1)S(1)}, bf16[192,512]{0,1:T(8,128)(2,1)S(1)}, u32[]{:S(2)}, u32[]{:S(2)}) collective-permute-start(bf16[192,512]{0,1:T(8,128)(2,1)S(1)} %slice.139), channel_id=1, source_target_pairs={{0,448},{64,0},{128,64},{192,128},{256,192},{320,256},{384,320},{4... | collective-permute-start | bytes 589832 | tf_op jit(solution)/shard_map/ppermute | solution.py:25
  134.8 19.9 %copy-start.5 = (bf16[384,8,512]{0,2,1:T(8,128)(2,1)}, bf16[384,8,512]{0,2,1:T(8,128)(2,1)S(1)}, u32[]{:S(2)}) copy-start(bf16[384,8,512]{0,2,1:T(8,128)(2,1)S(1)} %fusion.18) | copy-start | bytes 9437188
  136.0 16.5 %collective-permute-start.18 = (bf16[128,1024]{1,0:T(8,128)(2,1)S(1)}, bf16[128,1024]{1,0:T(8,128)(2,1)S(1)}, u32[]{:S(2)}, u32[]{:S(2)}) collective-permute-start(bf16[128,1024]{1,0:T(8,128)(2,1)S(1)} %slice.146), channel_id=1, source_target_pairs={{0,1},{1,2},{2,3},{3,0},{4,5},{5,6},{6,7},{7,4},{8,9},{9,10},{10,1... | collective-permute-start | bytes 786440 | tf_op jit(solution)/shard_map/ppermute | solution.py:24
  139.0 13.6 %collective-permute-start.19 = (bf16[128,1024]{1,0:T(8,128)(2,1)S(1)}, bf16[128,1024]{1,0:T(8,128)(2,1)S(1)}, u32[]{:S(2)}, u32[]{:S(2)}) collective-permute-start(bf16[128,1024]{1,0:T(8,128)(2,1)S(1)} %slice.147), channel_id=1, source_target_pairs={{0,3},{1,0},{2,1},{3,2},{4,7},{5,4},{6,5},{7,6},{8,11},{9,8},{10,9... | collective-permute-start | bytes 786440 | tf_op jit(solution)/shard_map/ppermute | solution.py:25
  143.6 9.1 %collective-permute-start.10 = (bf16[128,1024]{1,0:T(8,128)(2,1)S(1)}, bf16[128,1024]{1,0:T(8,128)(2,1)S(1)}, u32[]{:S(2)}, u32[]{:S(2)}) collective-permute-start(bf16[128,1024]{1,0:T(8,128)(2,1)S(1)} %slice.140), channel_id=1, source_target_pairs={{0,1},{1,2},{2,3},{3,0},{4,5},{5,6},{6,7},{7,4},{8,9},{9,10},{10,1... | collective-permute-start | bytes 786440 | tf_op jit(solution)/shard_map/ppermute | solution.py:24
  145.5 9.1 %collective-permute-start.11 = (bf16[128,1024]{1,0:T(8,128)(2,1)S(1)}, bf16[128,1024]{1,0:T(8,128)(2,1)S(1)}, u32[]{:S(2)}, u32[]{:S(2)}) collective-permute-start(bf16[128,1024]{1,0:T(8,128)(2,1)S(1)} %slice.141), channel_id=1, source_target_pairs={{0,3},{1,0},{2,1},{3,2},{4,7},{5,4},{6,5},{7,6},{8,11},{9,8},{10,9... | collective-permute-start | bytes 786440 | tf_op jit(solution)/shard_map/ppermute | solution.py:25
  173.6 17.1 %collective-permute-start.12 = (bf16[128,1024]{1,0:T(8,128)(2,1)S(1)}, bf16[128,1024]{1,0:T(8,128)(2,1)S(1)}, u32[]{:S(2)}, u32[]{:S(2)}) collective-permute-start(bf16[128,1024]{1,0:T(8,128)(2,1)S(1)} %slice_bitcast_fusion.7), channel_id=1, source_target_pairs={{0,1},{1,2},{2,3},{3,0},{4,5},{5,6},{6,7},{7,4},{8,9},{9,10},{10,1... | collective-permute-start | bytes 786440 | tf_op jit(solution)/shard_map/ppermute | solution.py:39
  175.7 17.0 %collective-permute-start.14 = (bf16[128,1024]{1,0:T(8,128)(2,1)S(1)}, bf16[128,1024]{1,0:T(8,128)(2,1)S(1)}, u32[]{:S(2)}, u32[]{:S(2)}) collective-permute-start(bf16[128,1024]{1,0:T(8,128)(2,1)S(1)} %slice_bitcast_fusion.6), channel_id=1, source_target_pairs={{0,3},{1,0},{2,1},{3,2},{4,7},{5,4},{6,5},{7,6},{8,11},{9,8},{10,9... | collective-permute-start | bytes 786440 | tf_op jit(solution)/shard_map/ppermute | solution.py:40
  184.2 13.2 %collective-permute-start.20 = (bf16[128,1024]{1,0:T(8,128)(2,1)S(1)}, bf16[128,1024]{1,0:T(8,128)(2,1)S(1)}, u32[]{:S(2)}, u32[]{:S(2)}) collective-permute-start(bf16[128,1024]{1,0:T(8,128)(2,1)S(1)} %slice_bitcast_fusion.5), channel_id=1, source_target_pairs={{0,1},{1,2},{2,3},{3,0},{4,5},{5,6},{6,7},{7,4},{8,9},{9,10},{10,1... | collective-permute-start | bytes 786440 | tf_op jit(solution)/shard_map/ppermute | solution.py:39
  186.2 13.3 %collective-permute-start.22 = (bf16[128,1024]{1,0:T(8,128)(2,1)S(1)}, bf16[128,1024]{1,0:T(8,128)(2,1)S(1)}, u32[]{:S(2)}, u32[]{:S(2)}) collective-permute-start(bf16[128,1024]{1,0:T(8,128)(2,1)S(1)} %slice_bitcast_fusion.4), channel_id=1, source_target_pairs={{0,3},{1,0},{2,1},{3,2},{4,7},{5,4},{6,5},{7,6},{8,11},{9,8},{10,9... | collective-permute-start | bytes 786440 | tf_op jit(solution)/shard_map/ppermute | solution.py:40
  190.8 14.7 %collective-permute-start.13 = (bf16[256,1024]{1,0:T(8,128)(2,1)S(1)}, bf16[256,1024]{1,0:T(8,128)(2,1)S(1)}, u32[]{:S(2)}, u32[]{:S(2)}) collective-permute-start(bf16[256,1024]{1,0:T(8,128)(2,1)S(1)} %fusion.13), channel_id=1, source_target_pairs={{0,1},{1,2},{2,3},{3,0},{4,5},{5,6},{6,7},{7,4},{8,9},{9,10},{10,1... | collective-permute-start | bytes 1572872 | tf_op jit(solution)/shard_map/ppermute | solution.py:49
  192.8 14.0 %collective-permute-start.15 = (bf16[256,1024]{1,0:T(8,128)(2,1)S(1)}, bf16[256,1024]{1,0:T(8,128)(2,1)S(1)}, u32[]{:S(2)}, u32[]{:S(2)}) collective-permute-start(bf16[256,1024]{1,0:T(8,128)(2,1)S(1)} %fusion.11), channel_id=1, source_target_pairs={{0,3},{1,0},{2,1},{3,2},{4,7},{5,4},{6,5},{7,6},{8,11},{9,8},{10,9... | collective-permute-start | bytes 1572872 | tf_op jit(solution)/shard_map/ppermute | solution.py:50
  197.5 19.3 %collective-permute-start.21 = (bf16[256,1024]{1,0:T(8,128)(2,1)S(1)}, bf16[256,1024]{1,0:T(8,128)(2,1)S(1)}, u32[]{:S(2)}, u32[]{:S(2)}) collective-permute-start(bf16[256,1024]{1,0:T(8,128)(2,1)S(1)} %fusion.9), channel_id=1, source_target_pairs={{0,1},{1,2},{2,3},{3,0},{4,5},{5,6},{6,7},{7,4},{8,9},{9,10},{10,1... | collective-permute-start | bytes 1572872 | tf_op jit(solution)/shard_map/ppermute | solution.py:49
  199.5 18.6 %collective-permute-start.23 = (bf16[256,1024]{1,0:T(8,128)(2,1)S(1)}, bf16[256,1024]{1,0:T(8,128)(2,1)S(1)}, u32[]{:S(2)}, u32[]{:S(2)}) collective-permute-start(bf16[256,1024]{1,0:T(8,128)(2,1)S(1)} %fusion.7), channel_id=1, source_target_pairs={{0,3},{1,0},{2,1},{3,2},{4,7},{5,4},{6,5},{7,6},{8,11},{9,8},{10,9... | collective-permute-start | bytes 1572872 | tf_op jit(solution)/shard_map/ppermute | solution.py:50
  248.3 20.2 %all-to-all-start.1 = ((bf16[16,16,1024]{2,1,0:T(8,128)(2,1)}), bf16[16,16,1024]{2,1,0:T(8,128)(2,1)S(1)}, u32[]{:S(2)}, u32[]{:S(2)}) async-start(bf16[16,16,1024]{2,1,0:T(8,128)(2,1)} %bitcast.36), calls=%async_computation.1 | async-start | bytes 1048576 | tf_op jit(solution)/shard_map/all_to_all | solution.py:123
  (12 other events, 79.5 us)
Sparse Core Ops, SparseCore 0:
  10.1 70.7 all-gather.6
  83.0 55.0 all-gather.4
  169.0 51.2 reduce-scatter.1

commit v4 on v2

--- a/solution.py
+++ b/solution.py
@@ -4,7 +4,7 @@
 from jax.sharding import PartitionSpec as P
 
 
-def ring_gather(piece, axis, n, along=0):
+def ring_gather(piece, axis, n, along=0, tie=None):
     idx = lax.axis_index(axis)
     fwd = [(i, (i + 1) % n) for i in range(n)]
     bwd = [(i, (i - 1) % n) for i in range(n)]
@@ -18,12 +18,15 @@
     for k in range(1, half):
         left = lax.ppermute(left, axis, fwd)
         right = lax.ppermute(right, axis, bwd)
+        if k == 1 and tie is not None:
+            left, right, tie = lax.optimization_barrier((left, right, tie))
         out = put(out, left, idx - k)
         out = put(out, right, idx + k)
     m = piece.shape[0] // 2
     first = lax.ppermute(left[:m], axis, fwd)
     second = lax.ppermute(right[m:], axis, bwd)
-    return put(out, jnp.concatenate([first, second], axis=0), idx + half)
+    out = put(out, jnp.concatenate([first, second], axis=0), idx + half)
+    return out if tie is None else (out, tie)
 
 
 def ring_reduce_scatter(chunks, axis, n):
@@ -74,17 +77,17 @@
     both = jnp.concatenate([copies, scaled], axis=2).reshape(-1, 2 * part)
     empty_slots = jnp.zeros((slot_rows, 2 * part), jnp.bfloat16)
     send = empty_slots.at[slot_index].set(both).reshape(experts, capacity, 2 * part)
+    stacked = jnp.stack([w_gate[0], w_up[0], w_down[0]], axis=1)
+    full, send = ring_gather(stacked, "dp", lax.axis_size("dp"), along=2, tie=send)
+    gate_full, up_full, down_full = (
+        full[:, i].reshape(w_gate.shape[1], model_width) for i in range(3)
+    )
     recv = lax.all_to_all(send, "expert", split_axis=0, concat_axis=0, tiled=True)
     recv = recv.reshape(1, slot_rows, 2 * part)
-    gathered = ring_gather(recv[0], "etp", shares)
+    gathered = lax.all_gather(recv[0], "etp", axis=0, tiled=False)
     rows4 = gathered[:, :, :part]
     grads4 = gathered[:, :, part:]
 
-    gate_full, up_full, down_full = (
-        lax.all_gather(w_gate[0], "dp", axis=1, tiled=True),
-        lax.all_gather(w_up[0], "dp", axis=1, tiled=True),
-        ring_gather(w_down[0], "dp", lax.axis_size("dp"), along=1).reshape(w_down.shape[1], -1),
-    )
     hidden_units = gate_full.shape[0]
     gate4 = gate_full.reshape(hidden_units, shares, part)
     up4 = up_full.reshape(hidden_units, shares, part)

time: 254 us -> 300 us (1.18)
  blocking collectives: 0 us -> 37.1 us
  starting transfers between devices: 76.8 us -> 54.4 us
  local copies, waits for them, and re-layouts: 26.4 us -> 42.9 us
  waiting for transfers between devices: 103 us -> 115 us
  other arithmetic: 9.21 us -> 15.4 us
  matrix products: 22.9 us -> 19.3 us
    all_to_all x0 -> x1, blocking collectives: none -> 37.1 us  [on_device(): lax.all_to_all(send, 'expert', split_axis=0, concat_axis=0, tiled=True)]
    ppermute x4 -> x3, waiting for transfers between devices: 27.1 us -> 53.1 us  [ring_gather(): left = lax.ppermute(left, axis, fwd)]
    ppermute x2, waiting for transfers between devices: 4.39 us -> 24.5 us  [ring_reduce_scatter(): lax.ppermute(to_right.astype(chunks.dtype), axis, fwd).astype(jnp.float32)]
    ppermute x2, waiting for transfers between devices: 20.6 us -> 2.35 us  [ring_reduce_scatter(): lax.ppermute(to_left.astype(chunks.dtype), axis, bwd).astype(jnp.float32)]
    all_to_all x1 -> x0, starting transfers between devices: 10.3 us -> none  [on_device(): lax.all_to_all(send, 'expert', split_axis=0, concat_axis=0, tiled=True)]
    ppermute x2 -> x1, waiting for transfers between devices: 12.5 us -> 3.81 us  [ring_gather(): second = lax.ppermute(right[m:], axis, bwd)]
    ppermute x2 -> x1, waiting for transfers between devices: 10.2 us -> 2.08 us  [ring_gather(): first = lax.ppermute(left[:m], axis, fwd)]
    dynamic_update_slice x10 -> x6, local copies, waits for them, and re-layouts: 5.98 us -> 13.4 us  [ring_gather(): lax.dynamic_update_index_in_dim(buf, val, at % n, along)]
  transfers between devices with their start and end apart: 21 -> 15, of which waited for: 10 -> 10; matrix products, arithmetic and copies ran while one was open for 15% -> 18% of each run, Pallas kernels for 0% -> 0%
where the time goes in v4:
time: 300 us; the launch traced here: 298 us
  waiting for transfers between devices  115 us (38%)
  starting transfers between devices  54.4 us (18%)
  local copies, waits for them, and re-layouts  42.9 us (14%)
  blocking collectives  37.1 us (12%)
  matrix products  19.3 us (6%)
  other arithmetic  15.4 us (5%)
  between operations  14.7 us (5%)
    ppermute x3, waiting for transfers between devices, ring_gather(): left = lax.ppermute(left, axis, fwd)  53.1 us
    all_to_all x1, blocking collectives, on_device(): lax.all_to_all(send, 'expert', split_axis=0, concat_axis=0, tiled=True)  37.1 us
    all_to_all x1, waiting for transfers between devices, on_device(): lax.all_to_all(slot_out.reshape(experts, capacity, 2 * part), 'expert', s...  28 us
    ppermute x2, waiting for transfers between devices, ring_reduce_scatter(): lax.ppermute(to_right.astype(chunks.dtype), axis, fwd).astype(jnp.float32)  24.5 us
    ppermute x3, starting transfers between devices, ring_gather(): right = lax.ppermute(right, axis, bwd)  18.8 us
    dynamic_update_slice x6, local copies, waits for them, and re-layouts, ring_gather(): lax.dynamic_update_index_in_dim(buf, val, at % n, along)  13.4 us
    ppermute x2, starting transfers between devices, ring_reduce_scatter(): lax.ppermute(to_left.astype(chunks.dtype), axis, bwd).astype(jnp.float32)  8.77 us
    ppermute x3, starting transfers between devices, ring_gather(): left = lax.ppermute(left, axis, fwd)  8.65 us
  transfers between devices with their start and end apart: 15, of which 10 were waited for; matrix products, arithmetic and copies ran while one was open for 18% of the time, Pallas kernels for 0%

profile of v4, /device:TPU:1, one launch (start us, length us, event | category | flops | bytes accessed | tf_op | source)
XLA Modules:
  0.0 298.5 jit_solution(8838200278263055865)
XLA Ops:
  12.1 4.8 %collective-permute-start = (bf16[384,3,512]{0,2,1:T(8,128)(2,1)}, bf16[384,3,512]{0,2,1:T(8,128)(2,1)}, u32[]{:S(2)}, u32[]{:S(2)}) collective-permute-start(bf16[384,3,512]{0,2,1:T(8,128)(2,1)} %pad_maximum_fusion), channel_id=1, source_target_pairs={{0,64},{64,128},{128,192},{192,256},{256,320},{320,384},{384,448},... | collective-permute-start | bytes 3538952 | tf_op jit(solution)/shard_map/ppermute | solution.py:19
  16.9 8.6 %collective-permute-start.1 = (bf16[384,3,512]{0,2,1:T(8,128)(2,1)}, bf16[384,3,512]{0,2,1:T(8,128)(2,1)}, u32[]{:S(2)}, u32[]{:S(2)}) collective-permute-start(bf16[384,3,512]{0,2,1:T(8,128)(2,1)} %pad_maximum_fusion), channel_id=1, source_target_pairs={{0,448},{64,0},{128,64},{192,128},{256,192},{320,256},{384,320},{4... | collective-permute-start | bytes 3538952 | tf_op jit(solution)/shard_map/ppermute | solution.py:20
  30.9 18.6 %collective-permute-done = bf16[384,3,512]{0,2,1:T(8,128)(2,1)} collective-permute-done((bf16[384,3,512]{0,2,1:T(8,128)(2,1)}, bf16[384,3,512]{0,2,1:T(8,128)(2,1)}, u32[]{:S(2)}, u32[]{:S(2)}) %collective-permute-start) | collective-permute-done | bytes 1179680 | tf_op jit(solution)/shard_map/ppermute | solution.py:19
  50.4 37.1 %all_to_all.10 = bf16[16,16,2048]{2,1,0:T(8,128)(2,1)} all-to-all(bf16[16,16,2048]{2,1,0:T(8,128)(2,1)S(1)} %bitcast.118), channel_id=1, replica_groups=mesh['dp'=8,'expert'=16,'etp'=4] {'expert'}, dimensions={0} | all-to-all | bytes 2097152 | tf_op jit(solution)/shard_map/all_to_all | solution.py:85
  89.5 5.3 %collective-permute-start.3 = (bf16[384,3,512]{0,2,1:T(8,128)(2,1)}, bf16[384,3,512]{0,2,1:T(8,128)(2,1)}, u32[]{:S(2)}, u32[]{:S(2)}) collective-permute-start(bf16[384,3,512]{0,2,1:T(8,128)(2,1)} %collective-permute-done.1), channel_id=1, source_target_pairs={{0,448},{64,0},{128,64},{192,128},{256,192},{320,256},{384,320},{4... | collective-permute-start | bytes 3538952 | tf_op jit(solution)/shard_map/ppermute | solution.py:20
  94.9 23.9 %collective-permute-done.2 = bf16[384,3,512]{0,2,1:T(8,128)(2,1)} collective-permute-done((bf16[384,3,512]{0,2,1:T(8,128)(2,1)}, bf16[384,3,512]{0,2,1:T(8,128)(2,1)}, u32[]{:S(2)}, u32[]{:S(2)}) %collective-permute-start.2) | collective-permute-done | bytes 1179680 | tf_op jit(solution)/shard_map/ppermute | solution.py:19
  120.7 4.8 %collective-permute-start.5 = (bf16[384,3,512]{0,2,1:T(8,128)(2,1)}, bf16[384,3,512]{0,2,1:T(8,128)(2,1)}, u32[]{:S(2)}, u32[]{:S(2)}) collective-permute-start(bf16[384,3,512]{0,2,1:T(8,128)(2,1)} %collective-permute-done.3), channel_id=1, source_target_pairs={{0,448},{64,0},{128,64},{192,128},{256,192},{320,256},{384,320},{4... | collective-permute-start | bytes 3538952 | tf_op jit(solution)/shard_map/ppermute | solution.py:20
  125.7 5.0 %broadcast_in_dim.54 = bf16[384,3,8,512]{0,3,2,1:T(8,128)(2,1)} broadcast(bf16[]{:T(256)} %constant.189.clone.1), dimensions={} | broadcast | bytes 9437186 | tf_op jit(solution)/shard_map/broadcast_in_dim | solution.py:13
  131.8 2.4 bitcast_dynamic-update-slice_fusion.4
  134.3 2.4 bitcast_dynamic-update-slice_fusion.3
  136.7 2.4 bitcast_dynamic-update-slice_fusion.2
  139.1 10.6 %collective-permute-done.4 = bf16[384,3,512]{0,2,1:T(8,128)(2,1)S(1)} collective-permute-done((bf16[384,3,512]{0,2,1:T(8,128)(2,1)}, bf16[384,3,512]{0,2,1:T(8,128)(2,1)S(1)}, u32[]{:S(2)}, u32[]{:S(2)}) %collective-permute-start.4) | collective-permute-done | bytes 1179680 | tf_op jit(solution)/shard_map/ppermute | solution.py:19
  154.5 5.0 %collective-permute-start.7 = (bf16[192,3,512]{2,0,1:T(8,128)(2,1)}, bf16[192,3,512]{2,0,1:T(8,128)(2,1)}, u32[]{:S(2)}, u32[]{:S(2)}) collective-permute-start(bf16[192,3,512]{2,0,1:T(8,128)(2,1)} %copy.94), channel_id=1, source_target_pairs={{0,448},{64,0},{128,64},{192,128},{256,192},{320,256},{384,320},{4... | collective-permute-start | bytes 1769480 | tf_op jit(solution)/shard_map/ppermute | solution.py:27
  159.5 2.4 bitcast_dynamic-update-slice_fusion.1
  163.1 2.5 bitcast_dynamic-update-slice_fusion.6
  165.6 2.1 collective-permute-done.6
  167.9 3.8 %collective-permute-done.7 = bf16[192,3,512]{2,0,1:T(8,128)(2,1)} collective-permute-done((bf16[192,3,512]{2,0,1:T(8,128)(2,1)}, bf16[192,3,512]{2,0,1:T(8,128)(2,1)}, u32[]{:S(2)}, u32[]{:S(2)}) %collective-permute-start.7) | collective-permute-done | bytes 589856 | tf_op jit(solution)/shard_map/ppermute | solution.py:27
  174.6 5.9 %fusion.53 = (bf16[384,1,8,512]{0,3,2,1:T(8,128)(2,1)S(1)}, bf16[384,1,8,512]{0,3,2,1:T(8,128)(2,1)}, bf16[384,1,8,512]{0,3,2,1:T(8,128)(2,1)}) fusion(bf16[384,3,8,512]{0,3,2,1:T(8,128)(2,1)} %fusion.19), kind=kLoop, calls=%fused_computation.90 | loop fusion | bytes 18874368 | tf_op jit(solution)/shard_map/slice | solution.py:83
  180.6 3.9 %fusion.16 = f32[256,384]{1,0:T(8,128)S(1)} fusion(bf16[384,4,1024]{0,2,1:T(8,128)(2,1)} %bitcast.125, bf16[4,256,2048]{2,1,0:T(8,128)(2,1)} %all-gather.2.cloned.1.call-done), kind=kOutput, calls=%fused_computation.29 | convolution fusion | flops 805306368 | bytes 5636096 | tf_op jit(solution)/shard_map/jsc,fjc->sf/dot_general | solution.py:104
  184.5 3.0 %fusion.13 = f32[256,384]{1,0:T(8,128)S(1)} fusion(bf16[384,4,1024]{0,2,1:T(8,128)(2,1)S(1)} %bitcast.116, bf16[4,256,2048]{2,1,0:T(8,128)(2,1)} %all-gather.2.cloned.1.call-done), kind=kOutput, calls=%fused_computation.28 | convolution fusion | flops 805306368 | bytes 5636096 | tf_op jit(solution)/shard_map/jsc,fjc->sf/dot_general | solution.py:97
  187.6 2.1 multiply_convert_fusion.1
  189.7 3.2 %fusion.47 = f32[4,1024,256]{2,1,0:T(8,128)} fusion(bf16[384,4,1024]{0,2,1:T(8,128)(2,1)S(1)} %bitcast.111, bf16[256,384]{1,0:T(8,128)(2,1)S(1)} %get-tuple-element.51), kind=kOutput, calls=%fused_computation.76 | convolution fusion | flops 805306368 | bytes 7536640 | tf_op jit(solution)/shard_map/sf,fjc->jsc/dot_general | solution.py:110
  193.9 2.8 copy.102
  197.7 4.6 %fusion.4 = bf16[4,256,1024]{1,2,0:T(8,128)(2,1)S(1)} fusion(f32[4,1024,256]{2,1,0:T(8,128)} %fusion.47, bf16[384,4,1024]{0,2,1:T(8,128)(2,1)} %bitcast.115, f32[256,384]{1,0:T(8,128)S(1)} %fusion.16, f32[256,384]{1,0:T(8,128)S(1)} %copy-done.4), kind=kOutput, calls=%fused_computation.21 | convolution fusion | flops 807993344 | bytes 10223616 | tf_op jit(solution)/shard_map/sf,fjc->jsc/dot_general | solution.py:111
  205.3 2.5 collective-permute-start.8
  207.8 4.2 %collective-permute-start.10 = (bf16[128,2048]{0,1:T(8,128)(2,1)}, bf16[128,2048]{0,1:T(8,128)(2,1)S(1)}, u32[]{:S(2)}, u32[]{:S(2)}) collective-permute-start(bf16[128,2048]{0,1:T(8,128)(2,1)} %get-tuple-element.48), channel_id=1, source_target_pairs={{0,3},{1,0},{2,1},{3,2},{4,7},{5,4},{6,5},{7,6},{8,11},{9,8},{10,9... | collective-permute-start | bytes 1572872 | tf_op jit(solution)/shard_map/ppermute | solution.py:43
  213.8 6.6 %collective-permute-done.8 = bf16[128,2048]{0,1:T(8,128)(2,1)S(1)} collective-permute-done((bf16[128,2048]{0,1:T(8,128)(2,1)S(1)}, bf16[128,2048]{0,1:T(8,128)(2,1)S(1)}, u32[]{:S(2)}, u32[]{:S(2)}) %collective-permute-start.8) | collective-permute-done | bytes 524320 | tf_op jit(solution)/shard_map/ppermute | solution.py:42
  223.9 4.6 %collective-permute-start.11 = (bf16[256,2048]{0,1:T(8,128)(2,1)}, bf16[256,2048]{0,1:T(8,128)(2,1)}, u32[]{:S(2)}, u32[]{:S(2)}) collective-permute-start(bf16[256,2048]{0,1:T(8,128)(2,1)} %convert_element_type.121), channel_id=1, source_target_pairs={{0,3},{1,0},{2,1},{3,2},{4,7},{5,4},{6,5},{7,6},{8,11},{9,8},{10,9... | collective-permute-start | bytes 3145736 | tf_op jit(solution)/shard_map/ppermute | solution.py:53
  228.4 17.9 %collective-permute-done.9 = bf16[256,2048]{0,1:T(8,128)(2,1)} collective-permute-done((bf16[256,2048]{0,1:T(8,128)(2,1)S(1)}, bf16[256,2048]{0,1:T(8,128)(2,1)}, u32[]{:S(2)}, u32[]{:S(2)}) %collective-permute-start.9) | collective-permute-done | bytes 1048608 | tf_op jit(solution)/shard_map/ppermute | solution.py:52
  246.3 2.3 collective-permute-done.11
  252.1 6.9 %all-to-all-start.1 = ((bf16[16,16,2048]{2,1,0:T(8,128)(2,1)}), bf16[16,16,2048]{2,1,0:T(8,128)(2,1)S(1)}, u32[]{:S(2)}, u32[]{:S(2)}) async-start(bf16[16,16,2048]{2,1,0:T(8,128)(2,1)} %bitcast.41), calls=%async_computation.1 | async-start | bytes 2097152 | tf_op jit(solution)/shard_map/all_to_all | solution.py:121
  259.0 28.0 %all-to-all-done.1 = bf16[16,16,2048]{2,1,0:T(8,128)(2,1)S(1)} async-done(((bf16[16,16,2048]{2,1,0:T(8,128)(2,1)}), bf16[16,16,2048]{2,1,0:T(8,128)(2,1)S(1)}, u32[]{:S(2)}, u32[]{:S(2)}) %all-to-all-start.1) | async-done | bytes 1048608 | tf_op jit(solution)/shard_map/all_to_all | solution.py:121
  (81 shorter events, 43.3 us)
Async XLA Ops:
  7.2 18.3 %copy-start.5 = (s32[24,8]{0,1:T(8,128)S(1)}, s32[24,8]{0,1:T(8,128)}, u32[]{:S(2)}) copy-start(s32[24,8]{0,1:T(8,128)} %param.14) | copy-start | bytes 2308
  7.2 18.4 %copy-start.6 = (f32[24,8]{0,1:T(8,128)S(1)}, f32[24,8]{0,1:T(8,128)}, u32[]{:S(2)}) copy-start(f32[24,8]{0,1:T(8,128)} %param.13) | copy-start | bytes 2308
  7.2 173.4 %all-gather.2.cloned.1.call-start = ((), (), s32[]{:S(2)}) async-start(), calls=%async_computation.3 | async-start | bytes 5242880 | tf_op jit(solution)/shard_map/all_gather | solution.py:87
  12.1 37.5 %collective-permute-start = (bf16[384,3,512]{0,2,1:T(8,128)(2,1)}, bf16[384,3,512]{0,2,1:T(8,128)(2,1)}, u32[]{:S(2)}, u32[]{:S(2)}) collective-permute-start(bf16[384,3,512]{0,2,1:T(8,128)(2,1)} %pad_maximum_fusion), channel_id=1, source_target_pairs={{0,64},{64,128},{128,192},{192,256},{256,320},{320,384},{384,448},... | collective-permute-start | bytes 3538952 | tf_op jit(solution)/shard_map/ppermute | solution.py:19
  16.9 33.5 %collective-permute-start.1 = (bf16[384,3,512]{0,2,1:T(8,128)(2,1)}, bf16[384,3,512]{0,2,1:T(8,128)(2,1)}, u32[]{:S(2)}, u32[]{:S(2)}) collective-permute-start(bf16[384,3,512]{0,2,1:T(8,128)(2,1)} %pad_maximum_fusion), channel_id=1, source_target_pairs={{0,448},{64,0},{128,64},{192,128},{256,192},{320,256},{384,320},{4... | collective-permute-start | bytes 3538952 | tf_op jit(solution)/shard_map/ppermute | solution.py:20
  87.5 201.9 %reduce-scatter.2.cloned.1.call-start = ((), (), s32[]{:S(2)}) async-start(), calls=%async_computation.4 | async-start | bytes 3538944 | tf_op jit(solution)/shard_map/reduce_scatter | solution.py:116
  87.6 31.1 %collective-permute-start.2 = (bf16[384,3,512]{0,2,1:T(8,128)(2,1)}, bf16[384,3,512]{0,2,1:T(8,128)(2,1)}, u32[]{:S(2)}, u32[]{:S(2)}) collective-permute-start(bf16[384,3,512]{0,2,1:T(8,128)(2,1)} %collective-permute-done), channel_id=1, source_target_pairs={{0,64},{64,128},{128,192},{192,256},{256,320},{320,384},{384,448},... | collective-permute-start | bytes 3538952 | tf_op jit(solution)/shard_map/ppermute | solution.py:19
  89.5 31.1 %collective-permute-start.3 = (bf16[384,3,512]{0,2,1:T(8,128)(2,1)}, bf16[384,3,512]{0,2,1:T(8,128)(2,1)}, u32[]{:S(2)}, u32[]{:S(2)}) collective-permute-start(bf16[384,3,512]{0,2,1:T(8,128)(2,1)} %collective-permute-done.1), channel_id=1, source_target_pairs={{0,448},{64,0},{128,64},{192,128},{256,192},{320,256},{384,320},{4... | collective-permute-start | bytes 3538952 | tf_op jit(solution)/shard_map/ppermute | solution.py:20
  118.7 31.0 %collective-permute-start.4 = (bf16[384,3,512]{0,2,1:T(8,128)(2,1)}, bf16[384,3,512]{0,2,1:T(8,128)(2,1)S(1)}, u32[]{:S(2)}, u32[]{:S(2)}) collective-permute-start(bf16[384,3,512]{0,2,1:T(8,128)(2,1)} %collective-permute-done.2), channel_id=1, source_target_pairs={{0,64},{64,128},{128,192},{192,256},{256,320},{320,384},{384,448},... | collective-permute-start | bytes 3538952 | tf_op jit(solution)/shard_map/ppermute | solution.py:19
  120.7 31.3 %collective-permute-start.5 = (bf16[384,3,512]{0,2,1:T(8,128)(2,1)}, bf16[384,3,512]{0,2,1:T(8,128)(2,1)}, u32[]{:S(2)}, u32[]{:S(2)}) collective-permute-start(bf16[384,3,512]{0,2,1:T(8,128)(2,1)} %collective-permute-done.3), channel_id=1, source_target_pairs={{0,448},{64,0},{128,64},{192,128},{256,192},{320,256},{384,320},{4... | collective-permute-start | bytes 3538952 | tf_op jit(solution)/shard_map/ppermute | solution.py:20
  150.0 17.6 %collective-permute-start.6 = (bf16[192,3,512]{2,0,1:T(8,128)(2,1)S(1)}, bf16[192,3,512]{2,0,1:T(8,128)(2,1)S(1)}, u32[]{:S(2)}, u32[]{:S(2)}) collective-permute-start(bf16[192,3,512]{2,0,1:T(8,128)(2,1)S(1)} %copy.93), channel_id=1, source_target_pairs={{0,64},{64,128},{128,192},{192,256},{256,320},{320,384},{384,448},... | collective-permute-start | bytes 1769480 | tf_op jit(solution)/shard_map/ppermute | solution.py:26
  154.5 17.2 %collective-permute-start.7 = (bf16[192,3,512]{2,0,1:T(8,128)(2,1)}, bf16[192,3,512]{2,0,1:T(8,128)(2,1)}, u32[]{:S(2)}, u32[]{:S(2)}) collective-permute-start(bf16[192,3,512]{2,0,1:T(8,128)(2,1)} %copy.94), channel_id=1, source_target_pairs={{0,448},{64,0},{128,64},{192,128},{256,192},{320,256},{384,320},{4... | collective-permute-start | bytes 1769480 | tf_op jit(solution)/shard_map/ppermute | solution.py:27
  180.6 3.9 %copy-start.1 = (bf16[384,1,8,512]{0,3,2,1:T(8,128)(2,1)S(1)}, bf16[384,1,8,512]{0,3,2,1:T(8,128)(2,1)}, u32[]{:S(2)}) copy-start(bf16[384,1,8,512]{0,3,2,1:T(8,128)(2,1)} %get-tuple-element.45) | copy-start | bytes 9437188
  184.5 3.1 %copy-start.3 = (bf16[4,256,2048]{2,1,0:T(8,128)(2,1)S(1)}, bf16[4,256,2048]{2,1,0:T(8,128)(2,1)}, u32[]{:S(2)}) copy-start(bf16[4,256,2048]{2,1,0:T(8,128)(2,1)} %all-gather.2.cloned.1.call-done) | copy-start | bytes 12582916
  187.6 2.1 copy-start.7
  196.7 1.0 copy-start.4
  197.7 4.6 %copy-start.2 = (bf16[384,1,8,512]{0,3,2,1:T(8,128)(2,1)S(1)}, bf16[384,1,8,512]{0,3,2,1:T(8,128)(2,1)}, u32[]{:S(2)}) copy-start(bf16[384,1,8,512]{0,3,2,1:T(8,128)(2,1)} %get-tuple-element.46) | copy-start | bytes 9437188
  197.7 4.6 %copy-start.8 = (f32[256,384]{1,0:T(8,128)S(1)}, f32[256,384]{1,0:T(8,128)}, u32[]{:S(2)}) copy-start(f32[256,384]{1,0:T(8,128)} %copy-done.7) | copy-start | bytes 1179652
  203.7 1.5 copy-start
  205.3 15.2 %collective-permute-start.8 = (bf16[128,2048]{0,1:T(8,128)(2,1)S(1)}, bf16[128,2048]{0,1:T(8,128)(2,1)S(1)}, u32[]{:S(2)}, u32[]{:S(2)}) collective-permute-start(bf16[128,2048]{0,1:T(8,128)(2,1)S(1)} %get-tuple-element.47), channel_id=1, source_target_pairs={{0,1},{1,2},{2,3},{3,0},{4,5},{5,6},{6,7},{7,4},{8,9},{9,10},{10,1... | collective-permute-start | bytes 1572872 | tf_op jit(solution)/shard_map/ppermute | solution.py:42
  207.8 14.8 %collective-permute-start.10 = (bf16[128,2048]{0,1:T(8,128)(2,1)}, bf16[128,2048]{0,1:T(8,128)(2,1)S(1)}, u32[]{:S(2)}, u32[]{:S(2)}) collective-permute-start(bf16[128,2048]{0,1:T(8,128)(2,1)} %get-tuple-element.48), channel_id=1, source_target_pairs={{0,3},{1,0},{2,1},{3,2},{4,7},{5,4},{6,5},{7,6},{8,11},{9,8},{10,9... | collective-permute-start | bytes 1572872 | tf_op jit(solution)/shard_map/ppermute | solution.py:43
  220.7 25.6 %collective-permute-start.9 = (bf16[256,2048]{0,1:T(8,128)(2,1)S(1)}, bf16[256,2048]{0,1:T(8,128)(2,1)}, u32[]{:S(2)}, u32[]{:S(2)}) collective-permute-start(bf16[256,2048]{0,1:T(8,128)(2,1)S(1)} %convert_element_type.115), channel_id=1, source_target_pairs={{0,1},{1,2},{2,3},{3,0},{4,5},{5,6},{6,7},{7,4},{8,9},{9,10},{10,1... | collective-permute-start | bytes 3145736 | tf_op jit(solution)/shard_map/ppermute | solution.py:52
  223.9 24.8 %collective-permute-start.11 = (bf16[256,2048]{0,1:T(8,128)(2,1)}, bf16[256,2048]{0,1:T(8,128)(2,1)}, u32[]{:S(2)}, u32[]{:S(2)}) collective-permute-start(bf16[256,2048]{0,1:T(8,128)(2,1)} %convert_element_type.121), channel_id=1, source_target_pairs={{0,3},{1,0},{2,1},{3,2},{4,7},{5,4},{6,5},{7,6},{8,11},{9,8},{10,9... | collective-permute-start | bytes 3145736 | tf_op jit(solution)/shard_map/ppermute | solution.py:53
  252.1 34.9 %all-to-all-start.1 = ((bf16[16,16,2048]{2,1,0:T(8,128)(2,1)}), bf16[16,16,2048]{2,1,0:T(8,128)(2,1)S(1)}, u32[]{:S(2)}, u32[]{:S(2)}) async-start(bf16[16,16,2048]{2,1,0:T(8,128)(2,1)} %bitcast.41), calls=%async_computation.1 | async-start | bytes 2097152 | tf_op jit(solution)/shard_map/all_to_all | solution.py:121
Sparse Core Ops, SparseCore 0:
  87.7 48.2 all-gather.1
  196.9 42.6 reduce-scatter.1

commit v5 on v2

--- a/solution.py
+++ b/solution.py
@@ -81,8 +81,7 @@
     grads4 = gathered[:, :, part:]
 
     gate_full, up_full, down_full = (
-        lax.all_gather(w_gate[0], "dp", axis=1, tiled=True),
-        lax.all_gather(w_up[0], "dp", axis=1, tiled=True),
+        *lax.all_gather(jnp.stack([w_gate[0], w_up[0]]), "dp", axis=2, tiled=True),
         ring_gather(w_down[0], "dp", lax.axis_size("dp"), along=1).reshape(w_down.shape[1], -1),
     )
     hidden_units = gate_full.shape[0]

time: 254 us -> 261 us (1.028)
  waiting for transfers between devices: 103 us -> 113 us
  matrix products: 22.9 us -> 17.7 us
    ppermute x4, waiting for transfers between devices: 0.01 us -> 8.49 us  [ring_gather(): right = lax.ppermute(right, axis, bwd)]
    another operation x0 -> x1, local copies, waits for them, and re-layouts: none -> 3.62 us  [on_device(): gate_full, up_full, down_full = (*lax.all_gather(jnp.stack([w_gate[0], w_...]
    dot_general x1, matrix products: 4.71 us -> 2.01 us  [on_device(): jnp.einsum('jsc,fjc->sf', rows4, gate4, preferred_element_type=jnp.float32)]
    unnamed x26 -> x28, local copies, waits for them, and re-layouts: 10.1 us -> 8.61 us
  transfers between devices with their start and end apart: 21 -> 20, of which waited for: 10 -> 11; matrix products, arithmetic and copies ran while one was open for 15% -> 12% of each run, Pallas kernels for 0% -> 0%
where the time goes in v5:
time: 261 us; the launch traced here: 260 us
  waiting for transfers between devices  113 us (43%)
  starting transfers between devices  77.6 us (30%)
  local copies, waits for them, and re-layouts  28.2 us (11%)
  matrix products  17.7 us (7%)
  between operations  14.8 us (6%)
  other arithmetic  9.39 us (4%)
    all_to_all x1, waiting for transfers between devices, on_device(): lax.all_to_all(slot_out.reshape(experts, capacity, 2 * part), 'expert', s...  27.9 us
    ppermute x4, waiting for transfers between devices, ring_gather(): left = lax.ppermute(left, axis, fwd)  27.5 us
    ppermute x4, starting transfers between devices, ring_gather(): right = lax.ppermute(right, axis, bwd)  21.1 us
    ppermute x2, waiting for transfers between devices, ring_reduce_scatter(): lax.ppermute(to_left.astype(chunks.dtype), axis, bwd).astype(jnp.float32)  20.8 us
    ppermute x2, waiting for transfers between devices, ring_gather(): second = lax.ppermute(right[m:], axis, bwd)  12.8 us
    all_to_all x1, starting transfers between devices, on_device(): lax.all_to_all(slot_out.reshape(experts, capacity, 2 * part), 'expert', s...  12.2 us
    ppermute x2, waiting for transfers between devices, ring_gather(): first = lax.ppermute(left[:m], axis, fwd)  10.5 us
    all_to_all x1, starting transfers between devices, on_device(): lax.all_to_all(send, 'expert', split_axis=0, concat_axis=0, tiled=True)  10.3 us
  transfers between devices with their start and end apart: 20, of which 11 were waited for; matrix products, arithmetic and copies ran while one was open for 12% of the time, Pallas kernels for 0%

profile of v5, /device:TPU:1, one launch (start us, length us, event | category | flops | bytes accessed | tf_op | source)
XLA Modules:
  0.0 260.4 jit_solution(6338227212646230169)
XLA Ops:
  14.0 2.8 %scatter_custom_fusion = bf16[256,2048]{1,0:T(8,128)(2,1)} fusion(s32[192]{0:T(256)S(1)} %bitcast.119, bf16[192,1024]{1,0:T(8,128)(2,1)S(1)} %fusion.35, bf16[]{:T(256)} %constant.256, bf16[192,1024]{1,0:T(8,128)(2,1)S(1)} %broadcast_bitcast_fusion, bf16[]{:T(256)} %constant.213.clone.1), kind=kCustom, calls=%fused_computation.50 | custom fusion | flops 1572864 | bytes 1835012 | tf_op jit(solution)/shard_map/scatter | solution.py:76
  16.8 10.3 %all-to-all-start = ((bf16[16,16,2048]{2,1,0:T(8,128)(2,1)}), bf16[16,16,2048]{2,1,0:T(8,128)(2,1)S(1)}, u32[]{:S(2)}, u32[]{:S(2)}) async-start(bf16[16,16,2048]{2,1,0:T(8,128)(2,1)} %bitcast.14), calls=%async_computation | async-start | bytes 2097152 | tf_op jit(solution)/shard_map/all_to_all | solution.py:77
  27.4 2.3 collective-permute-start
  29.7 8.6 %collective-permute-start.1 = (bf16[384,512]{0,1:T(8,128)(2,1)S(1)}, bf16[384,512]{0,1:T(8,128)(2,1)S(1)}, u32[]{:S(2)}, u32[]{:S(2)}) collective-permute-start(bf16[384,512]{0,1:T(8,128)(2,1)S(1)} %bitcast.118), channel_id=1, source_target_pairs={{0,448},{64,0},{128,64},{192,128},{256,192},{320,256},{384,320},{4... | collective-permute-start | bytes 1179656 | tf_op jit(solution)/shard_map/ppermute | solution.py:20
  41.2 13.2 %collective-permute-done = bf16[384,512]{0,1:T(8,128)(2,1)S(1)} collective-permute-done((bf16[384,512]{0,1:T(8,128)(2,1)S(1)}, bf16[384,512]{0,1:T(8,128)(2,1)S(1)}, u32[]{:S(2)}, u32[]{:S(2)}) %collective-permute-start) | collective-permute-done | bytes 393248 | tf_op jit(solution)/shard_map/ppermute | solution.py:19
  56.4 4.6 %collective-permute-start.3 = (bf16[384,512]{0,1:T(8,128)(2,1)S(1)}, bf16[384,512]{0,1:T(8,128)(2,1)S(1)}, u32[]{:S(2)}, u32[]{:S(2)}) collective-permute-start(bf16[384,512]{0,1:T(8,128)(2,1)S(1)} %collective-permute-done.1), channel_id=1, source_target_pairs={{0,448},{64,0},{128,64},{192,128},{256,192},{320,256},{384,320},{4... | collective-permute-start | bytes 1179656 | tf_op jit(solution)/shard_map/ppermute | solution.py:20
  62.5 14.3 %collective-permute-done.2 = bf16[384,512]{0,1:T(8,128)(2,1)S(1)} collective-permute-done((bf16[384,512]{0,1:T(8,128)(2,1)S(1)}, bf16[384,512]{0,1:T(8,128)(2,1)S(1)}, u32[]{:S(2)}, u32[]{:S(2)}) %collective-permute-start.2) | collective-permute-done | bytes 393248 | tf_op jit(solution)/shard_map/ppermute | solution.py:19
  78.8 4.6 %collective-permute-start.5 = (bf16[384,512]{0,1:T(8,128)(2,1)S(1)}, bf16[384,512]{0,1:T(8,128)(2,1)S(1)}, u32[]{:S(2)}, u32[]{:S(2)}) collective-permute-start(bf16[384,512]{0,1:T(8,128)(2,1)S(1)} %collective-permute-done.3), channel_id=1, source_target_pairs={{0,448},{64,0},{128,64},{192,128},{256,192},{320,256},{384,320},{4... | collective-permute-start | bytes 1179656 | tf_op jit(solution)/shard_map/ppermute | solution.py:20
  84.2 3.1 %collective-permute-start.8 = (bf16[256,2048]{1,0:T(8,128)(2,1)S(1)}, bf16[256,2048]{1,0:T(8,128)(2,1)S(1)}, u32[]{:S(2)}, u32[]{:S(2)}) collective-permute-start(bf16[256,2048]{1,0:T(8,128)(2,1)S(1)} %bitcast.114), channel_id=1, source_target_pairs={{0,1},{1,2},{2,3},{3,0},{4,5},{5,6},{6,7},{7,4},{8,9},{9,10},{10,1... | collective-permute-start | bytes 3145736 | tf_op jit(solution)/shard_map/ppermute | solution.py:19
  87.3 3.4 %collective-permute-start.9 = (bf16[256,2048]{1,0:T(8,128)(2,1)S(1)}, bf16[256,2048]{1,0:T(8,128)(2,1)S(1)}, u32[]{:S(2)}, u32[]{:S(2)}) collective-permute-start(bf16[256,2048]{1,0:T(8,128)(2,1)S(1)} %bitcast.115), channel_id=1, source_target_pairs={{0,3},{1,0},{2,1},{3,2},{4,7},{5,4},{6,5},{7,6},{8,11},{9,8},{10,9... | collective-permute-start | bytes 3145736 | tf_op jit(solution)/shard_map/ppermute | solution.py:20
  91.5 8.5 %collective-permute-done.5 = bf16[384,512]{0,1:T(8,128)(2,1)S(1)} collective-permute-done((bf16[384,512]{0,1:T(8,128)(2,1)S(1)}, bf16[384,512]{0,1:T(8,128)(2,1)S(1)}, u32[]{:S(2)}, u32[]{:S(2)}) %collective-permute-start.5) | collective-permute-done | bytes 393248 | tf_op jit(solution)/shard_map/ppermute | solution.py:20
  100.1 5.4 %collective-permute-start.7 = (bf16[192,512]{0,1:T(8,128)(2,1)S(1)}, bf16[192,512]{0,1:T(8,128)(2,1)S(1)}, u32[]{:S(2)}, u32[]{:S(2)}) collective-permute-start(bf16[192,512]{0,1:T(8,128)(2,1)S(1)} %slice.91), channel_id=1, source_target_pairs={{0,448},{64,0},{128,64},{192,128},{256,192},{320,256},{384,320},{4... | collective-permute-start | bytes 589832 | tf_op jit(solution)/shard_map/ppermute | solution.py:25
  109.1 7.2 %collective-permute-done.7 = bf16[192,512]{0,1:T(8,128)(2,1)S(1)} collective-permute-done((bf16[192,512]{0,1:T(8,128)(2,1)S(1)}, bf16[192,512]{0,1:T(8,128)(2,1)S(1)}, u32[]{:S(2)}, u32[]{:S(2)}) %collective-permute-start.7) | collective-permute-done | bytes 196640 | tf_op jit(solution)/shard_map/ppermute | solution.py:25
  116.3 5.4 %collective-permute-done.6 = bf16[192,512]{0,1:T(8,128)(2,1)S(1)} collective-permute-done((bf16[192,512]{0,1:T(8,128)(2,1)S(1)}, bf16[192,512]{0,1:T(8,128)(2,1)S(1)}, u32[]{:S(2)}, u32[]{:S(2)}) %collective-permute-start.6) | collective-permute-done | bytes 196640 | tf_op jit(solution)/shard_map/ppermute | solution.py:24
  123.3 4.4 %collective-permute-start.11 = (bf16[128,2048]{1,0:T(8,128)(2,1)S(1)}, bf16[128,2048]{1,0:T(8,128)(2,1)S(1)}, u32[]{:S(2)}, u32[]{:S(2)}) collective-permute-start(bf16[128,2048]{1,0:T(8,128)(2,1)S(1)} %slice.93), channel_id=1, source_target_pairs={{0,3},{1,0},{2,1},{3,2},{4,7},{5,4},{6,5},{7,6},{8,11},{9,8},{10,9... | collective-permute-start | bytes 1572872 | tf_op jit(solution)/shard_map/ppermute | solution.py:25
  127.8 2.1 collective-permute-start.10
  130.2 5.5 %collective-permute-done.11 = bf16[128,2048]{1,0:T(8,128)(2,1)S(1)} collective-permute-done((bf16[128,2048]{1,0:T(8,128)(2,1)S(1)}, bf16[128,2048]{1,0:T(8,128)(2,1)S(1)}, u32[]{:S(2)}, u32[]{:S(2)}) %collective-permute-start.11) | collective-permute-done | bytes 524320 | tf_op jit(solution)/shard_map/ppermute | solution.py:25
  135.7 5.1 %collective-permute-done.10 = bf16[128,2048]{1,0:T(8,128)(2,1)S(1)} collective-permute-done((bf16[128,2048]{1,0:T(8,128)(2,1)S(1)}, bf16[128,2048]{1,0:T(8,128)(2,1)S(1)}, u32[]{:S(2)}, u32[]{:S(2)}) %collective-permute-start.10) | collective-permute-done | bytes 524320 | tf_op jit(solution)/shard_map/ppermute | solution.py:24
  143.0 3.1 %fusion.16 = f32[256,384]{1,0:T(8,128)S(1)} fusion(bf16[384,4,1024]{0,2,1:T(8,128)(2,1)} %bitcast.9, bf16[4,256,2048]{2,1,0:T(8,128)(2,1)S(1)} %fusion.29), kind=kOutput, calls=%fused_computation.29 | convolution fusion | flops 805306368 | bytes 5636096 | tf_op jit(solution)/shard_map/jsc,fjc->sf/dot_general | solution.py:100
  146.2 3.6 %fusion.54 = (bf16[1,384,4096]{1,2,0:T(8,128)(2,1)S(1)}, bf16[1,384,4096]{1,2,0:T(8,128)(2,1)S(1)}) fusion(bf16[2,384,4096]{1,2,0:T(8,128)(2,1)} %all-gather.2.cloned.1.call-done), kind=kLoop, calls=%fused_computation.95 | loop fusion | bytes 12582912 | tf_op jit(solution)/shard_map/unstack | solution.py:83
  153.5 3.3 %fusion.48 = f32[4,1024,256]{2,1,0:T(8,128)} fusion(bf16[384,4,1024]{0,2,1:T(8,128)(2,1)S(1)} %bitcast.108, bf16[256,384]{1,0:T(8,128)(2,1)S(1)} %get-tuple-element.41), kind=kOutput, calls=%fused_computation.81 | convolution fusion | flops 805306368 | bytes 7536640 | tf_op jit(solution)/shard_map/sf,fjc->jsc/dot_general | solution.py:106
  157.9 2.8 %copy.52 = bf16[384,4,1024]{0,2,1:T(8,128)(2,1)} copy(bf16[384,4,1024]{2,0,1:T(8,128)(2,1)S(1)} %convolution_convert_fusion) | data formatting | bytes 6291456 | tf_op jit(solution)/shard_map/convert_element_type | solution.py:111
  162.6 3.7 %fusion.4 = bf16[4,256,1024]{1,2,0:T(8,128)(2,1)S(1)} fusion(f32[4,1024,256]{2,1,0:T(8,128)} %fusion.48, bf16[384,4,1024]{0,2,1:T(8,128)(2,1)S(1)} %bitcast.113, f32[256,384]{1,0:T(8,128)S(1)} %fusion.16, f32[256,384]{1,0:T(8,128)} %get-tuple-element.42), kind=kOutput, calls=%fused_computation.21 | convolution fusion | flops 807993344 | bytes 10223616 | tf_op jit(solution)/shard_map/sf,fjc->jsc/dot_general | solution.py:107
  166.3 3.2 %convert_bitcast_fusion = bf16[4,256,1024]{1,2,0:T(8,128)(2,1)S(1)} fusion(bf16[384,4,1024]{0,2,1:T(8,128)(2,1)} %bitcast.9, f32[256,384]{1,0:T(8,128)S(1)} %copy-done.9, f32[256,384]{1,0:T(8,128)S(1)} %copy-done.4), kind=kOutput, calls=%fused_computation.20 | convolution fusion | flops 806944768 | bytes 6029312 | tf_op jit(solution)/shard_map/sf,fjc->jsc/dot_general | solution.py:97
  171.6 3.4 %collective-permute-start.12 = (bf16[128,2048]{0,1:T(8,128)(2,1)S(1)}, bf16[128,2048]{0,1:T(8,128)(2,1)S(1)}, u32[]{:S(2)}, u32[]{:S(2)}) collective-permute-start(bf16[128,2048]{0,1:T(8,128)(2,1)S(1)} %get-tuple-element.37), channel_id=1, source_target_pairs={{0,1},{1,2},{2,3},{3,0},{4,5},{5,6},{6,7},{7,4},{8,9},{9,10},{10,1... | collective-permute-start | bytes 1572872 | tf_op jit(solution)/shard_map/ppermute | solution.py:39
  175.6 5.0 %collective-permute-done.14 = bf16[128,2048]{0,1:T(8,128)(2,1)S(1)} collective-permute-done((bf16[128,2048]{0,1:T(8,128)(2,1)S(1)}, bf16[128,2048]{0,1:T(8,128)(2,1)S(1)}, u32[]{:S(2)}, u32[]{:S(2)}) %collective-permute-start.14) | collective-permute-done | bytes 524320 | tf_op jit(solution)/shard_map/ppermute | solution.py:40
  180.8 3.4 %collective-permute-start.15 = (bf16[256,2048]{0,1:T(8,128)(2,1)S(1)}, bf16[256,2048]{0,1:T(8,128)(2,1)S(1)}, u32[]{:S(2)}, u32[]{:S(2)}) collective-permute-start(bf16[256,2048]{0,1:T(8,128)(2,1)S(1)} %convert_element_type.121), channel_id=1, source_target_pairs={{0,3},{1,0},{2,1},{3,2},{4,7},{5,4},{6,5},{7,6},{8,11},{9,8},{10,9... | collective-permute-start | bytes 3145736 | tf_op jit(solution)/shard_map/ppermute | solution.py:50
  184.5 2.1 collective-permute-start.13
  186.6 15.7 %collective-permute-done.15 = bf16[256,2048]{0,1:T(8,128)(2,1)S(1)} collective-permute-done((bf16[256,2048]{0,1:T(8,128)(2,1)S(1)}, bf16[256,2048]{0,1:T(8,128)(2,1)S(1)}, u32[]{:S(2)}, u32[]{:S(2)}) %collective-permute-start.15) | collective-permute-done | bytes 1048608 | tf_op jit(solution)/shard_map/ppermute | solution.py:50
  202.3 4.6 %collective-permute-done.13 = bf16[256,2048]{0,1:T(8,128)(2,1)S(1)} collective-permute-done((bf16[256,2048]{0,1:T(8,128)(2,1)S(1)}, bf16[256,2048]{0,1:T(8,128)(2,1)S(1)}, u32[]{:S(2)}, u32[]{:S(2)}) %collective-permute-start.13) | collective-permute-done | bytes 1048608 | tf_op jit(solution)/shard_map/ppermute | solution.py:49
  208.8 12.2 %all-to-all-start.1 = ((bf16[16,16,2048]{2,1,0:T(8,128)(2,1)}), bf16[16,16,2048]{2,1,0:T(8,128)(2,1)S(1)}, u32[]{:S(2)}, u32[]{:S(2)}) async-start(bf16[16,16,2048]{2,1,0:T(8,128)(2,1)} %bitcast.37), calls=%async_computation.1 | async-start | bytes 2097152 | tf_op jit(solution)/shard_map/all_to_all | solution.py:117
  221.0 27.9 %all-to-all-done.1 = bf16[16,16,2048]{2,1,0:T(8,128)(2,1)S(1)} async-done(((bf16[16,16,2048]{2,1,0:T(8,128)(2,1)}), bf16[16,16,2048]{2,1,0:T(8,128)(2,1)S(1)}, u32[]{:S(2)}, u32[]{:S(2)}) %all-to-all-start.1) | async-done | bytes 1048608 | tf_op jit(solution)/shard_map/all_to_all | solution.py:117
  (95 shorter events, 40.5 us)
Async XLA Ops:
  7.2 3.5 %copy-start.6 = (s32[24,8]{0,1:T(8,128)S(1)}, s32[24,8]{0,1:T(8,128)}, u32[]{:S(2)}) copy-start(s32[24,8]{0,1:T(8,128)} %param.14) | copy-start | bytes 2308
  7.2 139.0 %all-gather.2.cloned.1.call-start = ((), (), s32[]{:S(2)}) async-start(), calls=%async_computation.3 | async-start | bytes 7077888 | tf_op jit(solution)/shard_map/all_gather | solution.py:84
  11.0 1.8 copy-start.7
  12.6 14.6 %copy-start.5 = (bf16[1,384,512]{2,1,0:T(8,128)(2,1)S(1)}, bf16[1,384,512]{2,1,0:T(8,128)(2,1)}, u32[]{:S(2)}) copy-start(bf16[1,384,512]{2,1,0:T(8,128)(2,1)} %param.17) | copy-start | bytes 1179652
  16.8 67.3 %all-to-all-start = ((bf16[16,16,2048]{2,1,0:T(8,128)(2,1)}), bf16[16,16,2048]{2,1,0:T(8,128)(2,1)S(1)}, u32[]{:S(2)}, u32[]{:S(2)}) async-start(bf16[16,16,2048]{2,1,0:T(8,128)(2,1)} %bitcast.14), calls=%async_computation | async-start | bytes 2097152 | tf_op jit(solution)/shard_map/all_to_all | solution.py:77
  27.1 224.2 %reduce-scatter.2.cloned.1.call-start = ((), (), s32[]{:S(2)}) async-start(), calls=%async_computation.4 | async-start | bytes 3538944 | tf_op jit(solution)/shard_map/reduce_scatter | solution.py:112
  27.4 27.0 %collective-permute-start = (bf16[384,512]{0,1:T(8,128)(2,1)S(1)}, bf16[384,512]{0,1:T(8,128)(2,1)S(1)}, u32[]{:S(2)}, u32[]{:S(2)}) collective-permute-start(bf16[384,512]{0,1:T(8,128)(2,1)S(1)} %bitcast.117), channel_id=1, source_target_pairs={{0,64},{64,128},{128,192},{192,256},{256,320},{320,384},{384,448},... | collective-permute-start | bytes 1179656 | tf_op jit(solution)/shard_map/ppermute | solution.py:19
  29.7 26.6 %collective-permute-start.1 = (bf16[384,512]{0,1:T(8,128)(2,1)S(1)}, bf16[384,512]{0,1:T(8,128)(2,1)S(1)}, u32[]{:S(2)}, u32[]{:S(2)}) collective-permute-start(bf16[384,512]{0,1:T(8,128)(2,1)S(1)} %bitcast.118), channel_id=1, source_target_pairs={{0,448},{64,0},{128,64},{192,128},{256,192},{320,256},{384,320},{4... | collective-permute-start | bytes 1179656 | tf_op jit(solution)/shard_map/ppermute | solution.py:20
  54.5 22.4 %collective-permute-start.2 = (bf16[384,512]{0,1:T(8,128)(2,1)S(1)}, bf16[384,512]{0,1:T(8,128)(2,1)S(1)}, u32[]{:S(2)}, u32[]{:S(2)}) collective-permute-start(bf16[384,512]{0,1:T(8,128)(2,1)S(1)} %collective-permute-done), channel_id=1, source_target_pairs={{0,64},{64,128},{128,192},{192,256},{256,320},{320,384},{384,448},... | collective-permute-start | bytes 1179656 | tf_op jit(solution)/shard_map/ppermute | solution.py:19
  56.4 22.4 %collective-permute-start.3 = (bf16[384,512]{0,1:T(8,128)(2,1)S(1)}, bf16[384,512]{0,1:T(8,128)(2,1)S(1)}, u32[]{:S(2)}, u32[]{:S(2)}) collective-permute-start(bf16[384,512]{0,1:T(8,128)(2,1)S(1)} %collective-permute-done.1), channel_id=1, source_target_pairs={{0,448},{64,0},{128,64},{192,128},{256,192},{320,256},{384,320},{4... | collective-permute-start | bytes 1179656 | tf_op jit(solution)/shard_map/ppermute | solution.py:20
  76.8 28.7 %collective-permute-start.4 = (bf16[384,512]{0,1:T(8,128)(2,1)S(1)}, bf16[384,512]{0,1:T(8,128)(2,1)S(1)}, u32[]{:S(2)}, u32[]{:S(2)}) collective-permute-start(bf16[384,512]{0,1:T(8,128)(2,1)S(1)} %collective-permute-done.2), channel_id=1, source_target_pairs={{0,64},{64,128},{128,192},{192,256},{256,320},{320,384},{384,448},... | collective-permute-start | bytes 1179656 | tf_op jit(solution)/shard_map/ppermute | solution.py:19
  78.8 21.2 %collective-permute-start.5 = (bf16[384,512]{0,1:T(8,128)(2,1)S(1)}, bf16[384,512]{0,1:T(8,128)(2,1)S(1)}, u32[]{:S(2)}, u32[]{:S(2)}) collective-permute-start(bf16[384,512]{0,1:T(8,128)(2,1)S(1)} %collective-permute-done.3), channel_id=1, source_target_pairs={{0,448},{64,0},{128,64},{192,128},{256,192},{320,256},{384,320},{4... | collective-permute-start | bytes 1179656 | tf_op jit(solution)/shard_map/ppermute | solution.py:20
  84.2 43.6 %collective-permute-start.8 = (bf16[256,2048]{1,0:T(8,128)(2,1)S(1)}, bf16[256,2048]{1,0:T(8,128)(2,1)S(1)}, u32[]{:S(2)}, u32[]{:S(2)}) collective-permute-start(bf16[256,2048]{1,0:T(8,128)(2,1)S(1)} %bitcast.114), channel_id=1, source_target_pairs={{0,1},{1,2},{2,3},{3,0},{4,5},{5,6},{6,7},{7,4},{8,9},{9,10},{10,1... | collective-permute-start | bytes 3145736 | tf_op jit(solution)/shard_map/ppermute | solution.py:19
  87.3 36.0 %collective-permute-start.9 = (bf16[256,2048]{1,0:T(8,128)(2,1)S(1)}, bf16[256,2048]{1,0:T(8,128)(2,1)S(1)}, u32[]{:S(2)}, u32[]{:S(2)}) collective-permute-start(bf16[256,2048]{1,0:T(8,128)(2,1)S(1)} %bitcast.115), channel_id=1, source_target_pairs={{0,3},{1,0},{2,1},{3,2},{4,7},{5,4},{6,5},{7,6},{8,11},{9,8},{10,9... | collective-permute-start | bytes 3145736 | tf_op jit(solution)/shard_map/ppermute | solution.py:20
  100.1 16.2 %collective-permute-start.7 = (bf16[192,512]{0,1:T(8,128)(2,1)S(1)}, bf16[192,512]{0,1:T(8,128)(2,1)S(1)}, u32[]{:S(2)}, u32[]{:S(2)}) collective-permute-start(bf16[192,512]{0,1:T(8,128)(2,1)S(1)} %slice.91), channel_id=1, source_target_pairs={{0,448},{64,0},{128,64},{192,128},{256,192},{320,256},{384,320},{4... | collective-permute-start | bytes 589832 | tf_op jit(solution)/shard_map/ppermute | solution.py:25
  105.6 16.1 %collective-permute-start.6 = (bf16[192,512]{0,1:T(8,128)(2,1)S(1)}, bf16[192,512]{0,1:T(8,128)(2,1)S(1)}, u32[]{:S(2)}, u32[]{:S(2)}) collective-permute-start(bf16[192,512]{0,1:T(8,128)(2,1)S(1)} %slice.90), channel_id=1, source_target_pairs={{0,64},{64,128},{128,192},{192,256},{256,320},{320,384},{384,448},... | collective-permute-start | bytes 589832 | tf_op jit(solution)/shard_map/ppermute | solution.py:24
  123.3 12.4 %collective-permute-start.11 = (bf16[128,2048]{1,0:T(8,128)(2,1)S(1)}, bf16[128,2048]{1,0:T(8,128)(2,1)S(1)}, u32[]{:S(2)}, u32[]{:S(2)}) collective-permute-start(bf16[128,2048]{1,0:T(8,128)(2,1)S(1)} %slice.93), channel_id=1, source_target_pairs={{0,3},{1,0},{2,1},{3,2},{4,7},{5,4},{6,5},{7,6},{8,11},{9,8},{10,9... | collective-permute-start | bytes 1572872 | tf_op jit(solution)/shard_map/ppermute | solution.py:25
  127.8 13.0 %collective-permute-start.10 = (bf16[128,2048]{1,0:T(8,128)(2,1)S(1)}, bf16[128,2048]{1,0:T(8,128)(2,1)S(1)}, u32[]{:S(2)}, u32[]{:S(2)}) collective-permute-start(bf16[128,2048]{1,0:T(8,128)(2,1)S(1)} %slice.92), channel_id=1, source_target_pairs={{0,1},{1,2},{2,3},{3,0},{4,5},{5,6},{6,7},{7,4},{8,9},{9,10},{10,1... | collective-permute-start | bytes 1572872 | tf_op jit(solution)/shard_map/ppermute | solution.py:24
  140.9 2.1 copy-start.2
  146.1 4.0 %copy-start.3 = (bf16[4,256,2048]{2,1,0:T(8,128)(2,1)S(1)}, bf16[4,256,2048]{2,1,0:T(8,128)(2,1)}, u32[]{:S(2)}) copy-start(bf16[4,256,2048]{2,1,0:T(8,128)(2,1)} %copy-done.2) | copy-start | bytes 12582916
  149.8 1.7 copy-start
  151.5 2.0 copy-start.8
  160.7 1.9 copy-start.1
  162.6 3.7 %copy-start.4 = (f32[256,384]{1,0:T(8,128)S(1)}, f32[256,384]{1,0:T(8,128)}, u32[]{:S(2)}) copy-start(f32[256,384]{1,0:T(8,128)} %get-tuple-element.42) | copy-start | bytes 1179652
  162.6 3.7 %copy-start.9 = (f32[256,384]{1,0:T(8,128)S(1)}, f32[256,384]{1,0:T(8,128)}, u32[]{:S(2)}) copy-start(f32[256,384]{1,0:T(8,128)} %copy-done.8) | copy-start | bytes 1179652
  169.6 11.0 %collective-permute-start.14 = (bf16[128,2048]{0,1:T(8,128)(2,1)S(1)}, bf16[128,2048]{0,1:T(8,128)(2,1)S(1)}, u32[]{:S(2)}, u32[]{:S(2)}) collective-permute-start(bf16[128,2048]{0,1:T(8,128)(2,1)S(1)} %get-tuple-element.38), channel_id=1, source_target_pairs={{0,3},{1,0},{2,1},{3,2},{4,7},{5,4},{6,5},{7,6},{8,11},{9,8},{10,9... | collective-permute-start | bytes 1572872 | tf_op jit(solution)/shard_map/ppermute | solution.py:40
  171.6 12.7 %collective-permute-start.12 = (bf16[128,2048]{0,1:T(8,128)(2,1)S(1)}, bf16[128,2048]{0,1:T(8,128)(2,1)S(1)}, u32[]{:S(2)}, u32[]{:S(2)}) collective-permute-start(bf16[128,2048]{0,1:T(8,128)(2,1)S(1)} %get-tuple-element.37), channel_id=1, source_target_pairs={{0,1},{1,2},{2,3},{3,0},{4,5},{5,6},{6,7},{7,4},{8,9},{9,10},{10,1... | collective-permute-start | bytes 1572872 | tf_op jit(solution)/shard_map/ppermute | solution.py:39
  180.8 21.5 %collective-permute-start.15 = (bf16[256,2048]{0,1:T(8,128)(2,1)S(1)}, bf16[256,2048]{0,1:T(8,128)(2,1)S(1)}, u32[]{:S(2)}, u32[]{:S(2)}) collective-permute-start(bf16[256,2048]{0,1:T(8,128)(2,1)S(1)} %convert_element_type.121), channel_id=1, source_target_pairs={{0,3},{1,0},{2,1},{3,2},{4,7},{5,4},{6,5},{7,6},{8,11},{9,8},{10,9... | collective-permute-start | bytes 3145736 | tf_op jit(solution)/shard_map/ppermute | solution.py:50
  184.5 22.5 %collective-permute-start.13 = (bf16[256,2048]{0,1:T(8,128)(2,1)S(1)}, bf16[256,2048]{0,1:T(8,128)(2,1)S(1)}, u32[]{:S(2)}, u32[]{:S(2)}) collective-permute-start(bf16[256,2048]{0,1:T(8,128)(2,1)S(1)} %convert_element_type.115), channel_id=1, source_target_pairs={{0,1},{1,2},{2,3},{3,0},{4,5},{5,6},{6,7},{7,4},{8,9},{9,10},{10,1... | collective-permute-start | bytes 3145736 | tf_op jit(solution)/shard_map/ppermute | solution.py:49
  208.8 40.1 %all-to-all-start.1 = ((bf16[16,16,2048]{2,1,0:T(8,128)(2,1)}), bf16[16,16,2048]{2,1,0:T(8,128)(2,1)S(1)}, u32[]{:S(2)}, u32[]{:S(2)}) async-start(bf16[16,16,2048]{2,1,0:T(8,128)(2,1)} %bitcast.37), calls=%async_computation.1 | async-start | bytes 2097152 | tf_op jit(solution)/shard_map/all_to_all | solution.py:117
Sparse Core Ops, SparseCore 0:
  10.8 114.1 all-gather.1
  160.8 46.5 reduce-scatter.1

commit v6 on v5

--- a/solution.py
+++ b/solution.py
@@ -80,10 +80,9 @@
     rows4 = gathered[:, :, :part]
     grads4 = gathered[:, :, part:]
 
-    gate_full, up_full, down_full = (
-        *lax.all_gather(jnp.stack([w_gate[0], w_up[0]]), "dp", axis=2, tiled=True),
-        ring_gather(w_down[0], "dp", lax.axis_size("dp"), along=1).reshape(w_down.shape[1], -1),
-    )
+    gate_full = lax.all_gather(w_gate[0], "dp", axis=1, tiled=True)
+    pair = ring_gather(jnp.stack([w_up[0], w_down[0]], axis=1), "dp", lax.axis_size("dp"), along=2)
+    up_full, down_full = (pair[:, i].reshape(w_up.shape[1], model_width) for i in range(2))
     hidden_units = gate_full.shape[0]
     gate4 = gate_full.reshape(hidden_units, shares, part)
     up4 = up_full.reshape(hidden_units, shares, part)

time: 261 us -> 256 us (0.981)
  waiting for transfers between devices: 113 us -> 100 us
  local copies, waits for them, and re-layouts: 28.2 us -> 31.4 us
    another operation x1 -> x0, local copies, waits for them, and re-layouts: 3.62 us -> none  [on_device(): gate_full, up_full, down_full = (*lax.all_gather(jnp.stack([w_gate[0], w_...]
    slice x0 -> x1, local copies, waits for them, and re-layouts: none -> 3.59 us  [on_device(): pair[:, i].reshape(w_up.shape[1], model_width)]
    ppermute x4, waiting for transfers between devices: 8.49 us -> 5.22 us  [ring_gather(): right = lax.ppermute(right, axis, bwd)]
    ppermute x2, waiting for transfers between devices: 12.8 us -> 9.52 us  [ring_gather(): second = lax.ppermute(right[m:], axis, bwd)]
    dot_general x1, matrix products: 2.01 us -> 4.7 us  [on_device(): jnp.einsum('jsc,fjc->sf', rows4, gate4, preferred_element_type=jnp.float32)]
    dynamic_update_slice x10 -> x9, local copies, waits for them, and re-layouts: 5.9 us -> 8.52 us  [ring_gather(): lax.dynamic_update_index_in_dim(buf, val, at % n, along)]
    unnamed x28 -> x34, local copies, waits for them, and re-layouts: 8.61 us -> 7.53 us
  transfers between devices with their start and end apart: 20 -> 20, of which waited for: 11 -> 12; matrix products, arithmetic and copies ran while one was open for 12% -> 15% of each run, Pallas kernels for 0% -> 0%
where the time goes in v6:
time: 256 us; the launch traced here: 253 us
  waiting for transfers between devices  100 us (39%)
  starting transfers between devices  79.7 us (31%)
  local copies, waits for them, and re-layouts  31.4 us (12%)
  matrix products  16.7 us (7%)
  between operations  14.9 us (6%)
  other arithmetic  10.7 us (4%)
    all_to_all x1, waiting for transfers between devices, on_device(): lax.all_to_all(slot_out.reshape(experts, capacity, 2 * part), 'expert', s...  27.9 us
    ppermute x4, waiting for transfers between devices, ring_gather(): left = lax.ppermute(left, axis, fwd)  25.8 us
    ppermute x4, starting transfers between devices, ring_gather(): right = lax.ppermute(right, axis, bwd)  21.8 us
    ppermute x2, waiting for transfers between devices, ring_reduce_scatter(): lax.ppermute(to_left.astype(chunks.dtype), axis, bwd).astype(jnp.float32)  19.9 us
    all_to_all x1, starting transfers between devices, on_device(): lax.all_to_all(slot_out.reshape(experts, capacity, 2 * part), 'expert', s...  14.1 us
    ppermute x4, starting transfers between devices, ring_gather(): left = lax.ppermute(left, axis, fwd)  11.7 us
    ppermute x2, waiting for transfers between devices, ring_gather(): second = lax.ppermute(right[m:], axis, bwd)  9.52 us
    ppermute x2, starting transfers between devices, ring_gather(): second = lax.ppermute(right[m:], axis, bwd)  9.21 us
  transfers between devices with their start and end apart: 20, of which 12 were waited for; matrix products, arithmetic and copies ran while one was open for 15% of the time, Pallas kernels for 0%

profile of v6, /device:TPU:1, one launch (start us, length us, event | category | flops | bytes accessed | tf_op | source)
XLA Modules:
  0.0 253.3 jit_solution(8294049840820316151)
XLA Ops:
  10.7 4.8 %collective-permute-start = (bf16[384,2,512]{0,2,1:T(8,128)(2,1)}, bf16[384,2,512]{0,2,1:T(8,128)(2,1)S(1)}, u32[]{:S(2)}, u32[]{:S(2)}) collective-permute-start(bf16[384,2,512]{0,2,1:T(8,128)(2,1)} %pad_maximum_fusion), channel_id=1, source_target_pairs={{0,64},{64,128},{128,192},{192,256},{256,320},{320,384},{384,448},... | collective-permute-start | bytes 2359304 | tf_op jit(solution)/shard_map/ppermute | solution.py:19
  15.5 8.6 %collective-permute-start.1 = (bf16[384,2,512]{0,2,1:T(8,128)(2,1)}, bf16[384,2,512]{0,2,1:T(8,128)(2,1)S(1)}, u32[]{:S(2)}, u32[]{:S(2)}) collective-permute-start(bf16[384,2,512]{0,2,1:T(8,128)(2,1)} %pad_maximum_fusion), channel_id=1, source_target_pairs={{0,448},{64,0},{128,64},{192,128},{256,192},{320,256},{384,320},{4... | collective-permute-start | bytes 2359304 | tf_op jit(solution)/shard_map/ppermute | solution.py:20
  28.4 2.8 %scatter_custom_fusion = bf16[256,2048]{1,0:T(8,128)(2,1)} fusion(s32[192]{0:T(256)S(1)} %bitcast.142, bf16[192,1024]{1,0:T(8,128)(2,1)S(1)} %fusion.36, bf16[]{:T(256)} %constant.256, bf16[192,1024]{1,0:T(8,128)(2,1)S(1)} %broadcast_bitcast_fusion, bf16[]{:T(256)} %constant.213.clone.1), kind=kCustom, calls=%fused_computation.53 | custom fusion | flops 1572864 | bytes 1835012 | tf_op jit(solution)/shard_map/scatter | solution.py:76
  31.2 8.1 %all-to-all-start = ((bf16[16,16,2048]{2,1,0:T(8,128)(2,1)}), bf16[16,16,2048]{2,1,0:T(8,128)(2,1)S(1)}, u32[]{:S(2)}, u32[]{:S(2)}) async-start(bf16[16,16,2048]{2,1,0:T(8,128)(2,1)} %bitcast.22), calls=%async_computation | async-start | bytes 2097152 | tf_op jit(solution)/shard_map/all_to_all | solution.py:77
  42.2 5.3 %collective-permute-start.3 = (bf16[384,2,512]{0,2,1:T(8,128)(2,1)S(1)}, bf16[384,2,512]{0,2,1:T(8,128)(2,1)}, u32[]{:S(2)}, u32[]{:S(2)}) collective-permute-start(bf16[384,2,512]{0,2,1:T(8,128)(2,1)S(1)} %collective-permute-done.1), channel_id=1, source_target_pairs={{0,448},{64,0},{128,64},{192,128},{256,192},{320,256},{384,320},{4... | collective-permute-start | bytes 2359304 | tf_op jit(solution)/shard_map/ppermute | solution.py:20
  47.7 3.5 %broadcast_in_dim.70 = bf16[384,2,8,512]{0,3,2,1:T(8,128)(2,1)} broadcast(bf16[]{:T(256)} %constant.213.clone.1), dimensions={} | broadcast | bytes 6291458 | tf_op jit(solution)/shard_map/broadcast_in_dim | solution.py:13
  53.1 25.5 %collective-permute-done.2 = bf16[384,2,512]{0,2,1:T(8,128)(2,1)} collective-permute-done((bf16[384,2,512]{0,2,1:T(8,128)(2,1)S(1)}, bf16[384,2,512]{0,2,1:T(8,128)(2,1)}, u32[]{:S(2)}, u32[]{:S(2)}) %collective-permute-start.2) | collective-permute-done | bytes 786464 | tf_op jit(solution)/shard_map/ppermute | solution.py:19
  80.6 4.6 %collective-permute-start.5 = (bf16[384,2,512]{0,2,1:T(8,128)(2,1)}, bf16[384,2,512]{0,2,1:T(8,128)(2,1)S(1)}, u32[]{:S(2)}, u32[]{:S(2)}) collective-permute-start(bf16[384,2,512]{0,2,1:T(8,128)(2,1)} %collective-permute-done.3), channel_id=1, source_target_pairs={{0,448},{64,0},{128,64},{192,128},{256,192},{320,256},{384,320},{4... | collective-permute-start | bytes 2359304 | tf_op jit(solution)/shard_map/ppermute | solution.py:20
  86.1 2.1 bitcast_dynamic-update-slice_fusion.6
  88.2 2.1 bitcast_dynamic-update-slice_fusion.5
  90.4 3.1 %collective-permute-start.8 = (bf16[256,2048]{1,0:T(8,128)(2,1)S(1)}, bf16[256,2048]{1,0:T(8,128)(2,1)S(1)}, u32[]{:S(2)}, u32[]{:S(2)}) collective-permute-start(bf16[256,2048]{1,0:T(8,128)(2,1)S(1)} %bitcast.131), channel_id=1, source_target_pairs={{0,1},{1,2},{2,3},{3,0},{4,5},{5,6},{6,7},{7,4},{8,9},{9,10},{10,1... | collective-permute-start | bytes 3145736 | tf_op jit(solution)/shard_map/ppermute | solution.py:19
  93.5 3.4 %collective-permute-start.9 = (bf16[256,2048]{1,0:T(8,128)(2,1)S(1)}, bf16[256,2048]{1,0:T(8,128)(2,1)S(1)}, u32[]{:S(2)}, u32[]{:S(2)}) collective-permute-start(bf16[256,2048]{1,0:T(8,128)(2,1)S(1)} %bitcast.132), channel_id=1, source_target_pairs={{0,3},{1,0},{2,1},{3,2},{4,7},{5,4},{6,5},{7,6},{8,11},{9,8},{10,9... | collective-permute-start | bytes 3145736 | tf_op jit(solution)/shard_map/ppermute | solution.py:20
  97.5 4.5 %collective-permute-done.5 = bf16[384,2,512]{0,2,1:T(8,128)(2,1)S(1)} collective-permute-done((bf16[384,2,512]{0,2,1:T(8,128)(2,1)}, bf16[384,2,512]{0,2,1:T(8,128)(2,1)S(1)}, u32[]{:S(2)}, u32[]{:S(2)}) %collective-permute-start.5) | collective-permute-done | bytes 786464 | tf_op jit(solution)/shard_map/ppermute | solution.py:20
  102.3 5.2 %collective-permute-start.7 = (bf16[192,2,512]{0,2,1:T(8,128)(2,1)S(1)}, bf16[192,2,512]{0,2,1:T(8,128)(2,1)S(1)}, u32[]{:S(2)}, u32[]{:S(2)}) collective-permute-start(bf16[192,2,512]{0,2,1:T(8,128)(2,1)S(1)} %slice.99), channel_id=1, source_target_pairs={{0,448},{64,0},{128,64},{192,128},{256,192},{320,256},{384,320},{4... | collective-permute-start | bytes 1179656 | tf_op jit(solution)/shard_map/ppermute | solution.py:25
  111.5 5.1 %collective-permute-done.7 = bf16[192,2,512]{0,2,1:T(8,128)(2,1)S(1)} collective-permute-done((bf16[192,2,512]{0,2,1:T(8,128)(2,1)S(1)}, bf16[192,2,512]{0,2,1:T(8,128)(2,1)S(1)}, u32[]{:S(2)}, u32[]{:S(2)}) %collective-permute-start.7) | collective-permute-done | bytes 393248 | tf_op jit(solution)/shard_map/ppermute | solution.py:25
  116.6 3.9 %collective-permute-done.6 = bf16[192,2,512]{0,2,1:T(8,128)(2,1)S(1)} collective-permute-done((bf16[192,2,512]{0,2,1:T(8,128)(2,1)S(1)}, bf16[192,2,512]{0,2,1:T(8,128)(2,1)S(1)}, u32[]{:S(2)}, u32[]{:S(2)}) %collective-permute-start.6) | collective-permute-done | bytes 393248 | tf_op jit(solution)/shard_map/ppermute | solution.py:24
  121.8 3.6 %fusion.54 = (bf16[384,1,8,512]{0,3,2,1:T(8,128)(2,1)S(1)}, bf16[384,1,8,512]{0,3,2,1:T(8,128)(2,1)S(1)}) fusion(bf16[384,2,8,512]{0,3,2,1:T(8,128)(2,1)} %fusion.31), kind=kLoop, calls=%fused_computation.95 | loop fusion | bytes 12582912 | tf_op jit(solution)/shard_map/slice | solution.py:85
  125.4 4.0 %collective-permute-start.11 = (bf16[128,2048]{1,0:T(8,128)(2,1)S(1)}, bf16[128,2048]{1,0:T(8,128)(2,1)S(1)}, u32[]{:S(2)}, u32[]{:S(2)}) collective-permute-start(bf16[128,2048]{1,0:T(8,128)(2,1)S(1)} %slice.102), channel_id=1, source_target_pairs={{0,3},{1,0},{2,1},{3,2},{4,7},{5,4},{6,5},{7,6},{8,11},{9,8},{10,9... | collective-permute-start | bytes 1572872 | tf_op jit(solution)/shard_map/ppermute | solution.py:25
  131.9 4.4 %collective-permute-done.11 = bf16[128,2048]{1,0:T(8,128)(2,1)S(1)} collective-permute-done((bf16[128,2048]{1,0:T(8,128)(2,1)S(1)}, bf16[128,2048]{1,0:T(8,128)(2,1)S(1)}, u32[]{:S(2)}, u32[]{:S(2)}) %collective-permute-start.11) | collective-permute-done | bytes 524320 | tf_op jit(solution)/shard_map/ppermute | solution.py:25
  136.3 4.8 %collective-permute-done.10 = bf16[128,2048]{1,0:T(8,128)(2,1)S(1)} collective-permute-done((bf16[128,2048]{1,0:T(8,128)(2,1)S(1)}, bf16[128,2048]{1,0:T(8,128)(2,1)S(1)}, u32[]{:S(2)}, u32[]{:S(2)}) %collective-permute-start.10) | collective-permute-done | bytes 524320 | tf_op jit(solution)/shard_map/ppermute | solution.py:24
  144.4 4.7 %multiply_convert_fusion.1 = (bf16[256,384]{1,0:T(8,128)(2,1)S(1)}, f32[256,384]{1,0:T(8,128)}) fusion(f32[256,384]{1,0:T(8,128)S(1)} %fusion.16, f32[256,384]{1,0:T(8,128)S(1)} %fusion.13, bf16[384,4,1024]{0,2,1:T(8,128)(2,1)} %bitcast.138, bf16[4,256,2048]{2,1,0:T(8,128)(2,1)} %copy-done.2), kind=kOutput, calls=%fused_computation.74 | convolution fusion | flops 806289408 | bytes 6619136 | tf_op jit(solution)/shard_map/jsc,fjc->sf/dot_general | solution.py:91
  149.1 3.3 %fusion.48 = f32[256,4,1024]{0,2,1:T(8,128)} fusion(bf16[384,4,1024]{0,2,1:T(8,128)(2,1)S(1)} %bitcast.139, bf16[256,384]{1,0:T(8,128)(2,1)S(1)} %get-tuple-element.41), kind=kOutput, calls=%fused_computation.81 | convolution fusion | flops 805306368 | bytes 7536640 | tf_op jit(solution)/shard_map/sf,fjc->jsc/dot_general | solution.py:105
  153.4 2.8 %copy.76 = bf16[384,4,1024]{0,2,1:T(8,128)(2,1)} copy(bf16[384,4,1024]{2,0,1:T(8,128)(2,1)S(1)} %convolution_convert_fusion) | data formatting | bytes 6291456 | tf_op jit(solution)/shard_map/convert_element_type | solution.py:110
  158.2 3.8 %fusion = bf16[4,256,1024]{1,2,0:T(8,128)(2,1)S(1)} fusion(f32[256,4,1024]{0,2,1:T(8,128)} %fusion.48, bf16[384,4,1024]{0,2,1:T(8,128)(2,1)S(1)} %bitcast.130, f32[256,384]{1,0:T(8,128)S(1)} %fusion.16, f32[256,384]{1,0:T(8,128)} %get-tuple-element.42), kind=kOutput, calls=%fused_computation.14 | convolution fusion | flops 807993344 | bytes 10223616 | tf_op jit(solution)/shard_map/sf,fjc->jsc/dot_general | solution.py:106
  165.4 3.4 %collective-permute-start.12 = (bf16[128,2048]{0,1:T(8,128)(2,1)S(1)}, bf16[128,2048]{0,1:T(8,128)(2,1)S(1)}, u32[]{:S(2)}, u32[]{:S(2)}) collective-permute-start(bf16[128,2048]{0,1:T(8,128)(2,1)S(1)} %get-tuple-element.37), channel_id=1, source_target_pairs={{0,1},{1,2},{2,3},{3,0},{4,5},{5,6},{6,7},{7,4},{8,9},{9,10},{10,1... | collective-permute-start | bytes 1572872 | tf_op jit(solution)/shard_map/ppermute | solution.py:39
  169.4 4.0 %collective-permute-done.14 = bf16[128,2048]{0,1:T(8,128)(2,1)S(1)} collective-permute-done((bf16[128,2048]{0,1:T(8,128)(2,1)S(1)}, bf16[128,2048]{0,1:T(8,128)(2,1)S(1)}, u32[]{:S(2)}, u32[]{:S(2)}) %collective-permute-start.14) | collective-permute-done | bytes 524320 | tf_op jit(solution)/shard_map/ppermute | solution.py:40
  173.6 3.1 %collective-permute-start.15 = (bf16[256,2048]{0,1:T(8,128)(2,1)S(1)}, bf16[256,2048]{0,1:T(8,128)(2,1)S(1)}, u32[]{:S(2)}, u32[]{:S(2)}) collective-permute-start(bf16[256,2048]{0,1:T(8,128)(2,1)S(1)} %convert_element_type.117), channel_id=1, source_target_pairs={{0,3},{1,0},{2,1},{3,2},{4,7},{5,4},{6,5},{7,6},{8,11},{9,8},{10,9... | collective-permute-start | bytes 3145736 | tf_op jit(solution)/shard_map/ppermute | solution.py:50
  176.9 2.2 collective-permute-start.13
  179.2 15.9 %collective-permute-done.15 = bf16[256,2048]{0,1:T(8,128)(2,1)S(1)} collective-permute-done((bf16[256,2048]{0,1:T(8,128)(2,1)S(1)}, bf16[256,2048]{0,1:T(8,128)(2,1)S(1)}, u32[]{:S(2)}, u32[]{:S(2)}) %collective-permute-start.15) | collective-permute-done | bytes 1048608 | tf_op jit(solution)/shard_map/ppermute | solution.py:50
  195.1 2.9 %collective-permute-done.13 = bf16[256,2048]{0,1:T(8,128)(2,1)S(1)} collective-permute-done((bf16[256,2048]{0,1:T(8,128)(2,1)S(1)}, bf16[256,2048]{0,1:T(8,128)(2,1)S(1)}, u32[]{:S(2)}, u32[]{:S(2)}) %collective-permute-start.13) | collective-permute-done | bytes 1048608 | tf_op jit(solution)/shard_map/ppermute | solution.py:49
  199.9 14.1 %all-to-all-start.1 = ((bf16[16,16,2048]{2,1,0:T(8,128)(2,1)}), bf16[16,16,2048]{2,1,0:T(8,128)(2,1)S(1)}, u32[]{:S(2)}, u32[]{:S(2)}) async-start(bf16[16,16,2048]{2,1,0:T(8,128)(2,1)} %bitcast.46), calls=%async_computation.1 | async-start | bytes 2097152 | tf_op jit(solution)/shard_map/all_to_all | solution.py:116
  213.9 27.9 %all-to-all-done.1 = bf16[16,16,2048]{2,1,0:T(8,128)(2,1)S(1)} async-done(((bf16[16,16,2048]{2,1,0:T(8,128)(2,1)}), bf16[16,16,2048]{2,1,0:T(8,128)(2,1)S(1)}, u32[]{:S(2)}, u32[]{:S(2)}) %all-to-all-start.1) | async-done | bytes 1048608 | tf_op jit(solution)/shard_map/all_to_all | solution.py:116
  (101 shorter events, 40.8 us)
Async XLA Ops:
  7.2 16.9 %copy-start.8 = (bf16[1,384,512]{2,1,0:T(8,128)(2,1)S(1)}, bf16[1,384,512]{2,1,0:T(8,128)(2,1)}, u32[]{:S(2)}) copy-start(bf16[1,384,512]{2,1,0:T(8,128)(2,1)} %param.15) | copy-start | bytes 1179652
  7.2 17.9 %copy-start.9 = (s32[24,8]{0,1:T(8,128)S(1)}, s32[24,8]{0,1:T(8,128)}, u32[]{:S(2)}) copy-start(s32[24,8]{0,1:T(8,128)} %param.14) | copy-start | bytes 2308
  7.2 137.2 %all-gather.3.cloned.1.call-start = ((), (), s32[]{:S(2)}) async-start(), calls=%async_computation.4 | async-start | bytes 3538944 | tf_op jit(solution)/shard_map/all_gather | solution.py:83
  10.7 29.0 %collective-permute-start = (bf16[384,2,512]{0,2,1:T(8,128)(2,1)}, bf16[384,2,512]{0,2,1:T(8,128)(2,1)S(1)}, u32[]{:S(2)}, u32[]{:S(2)}) collective-permute-start(bf16[384,2,512]{0,2,1:T(8,128)(2,1)} %pad_maximum_fusion), channel_id=1, source_target_pairs={{0,64},{64,128},{128,192},{192,256},{256,320},{320,384},{384,448},... | collective-permute-start | bytes 2359304 | tf_op jit(solution)/shard_map/ppermute | solution.py:19
  15.5 26.7 %collective-permute-start.1 = (bf16[384,2,512]{0,2,1:T(8,128)(2,1)}, bf16[384,2,512]{0,2,1:T(8,128)(2,1)S(1)}, u32[]{:S(2)}, u32[]{:S(2)}) collective-permute-start(bf16[384,2,512]{0,2,1:T(8,128)(2,1)} %pad_maximum_fusion), channel_id=1, source_target_pairs={{0,448},{64,0},{128,64},{192,128},{256,192},{320,256},{384,320},{4... | collective-permute-start | bytes 2359304 | tf_op jit(solution)/shard_map/ppermute | solution.py:20
  31.2 59.1 %all-to-all-start = ((bf16[16,16,2048]{2,1,0:T(8,128)(2,1)}), bf16[16,16,2048]{2,1,0:T(8,128)(2,1)S(1)}, u32[]{:S(2)}, u32[]{:S(2)}) async-start(bf16[16,16,2048]{2,1,0:T(8,128)(2,1)} %bitcast.22), calls=%async_computation | async-start | bytes 2097152 | tf_op jit(solution)/shard_map/all_to_all | solution.py:77
  39.3 205.0 %reduce-scatter.2.cloned.1.call-start = ((), (), s32[]{:S(2)}) async-start(), calls=%async_computation.3 | async-start | bytes 3538944 | tf_op jit(solution)/shard_map/reduce_scatter | solution.py:111
  39.6 39.0 %collective-permute-start.2 = (bf16[384,2,512]{0,2,1:T(8,128)(2,1)S(1)}, bf16[384,2,512]{0,2,1:T(8,128)(2,1)}, u32[]{:S(2)}, u32[]{:S(2)}) collective-permute-start(bf16[384,2,512]{0,2,1:T(8,128)(2,1)S(1)} %collective-permute-done), channel_id=1, source_target_pairs={{0,64},{64,128},{128,192},{192,256},{256,320},{320,384},{384,448},... | collective-permute-start | bytes 2359304 | tf_op jit(solution)/shard_map/ppermute | solution.py:19
  42.2 38.3 %collective-permute-start.3 = (bf16[384,2,512]{0,2,1:T(8,128)(2,1)S(1)}, bf16[384,2,512]{0,2,1:T(8,128)(2,1)}, u32[]{:S(2)}, u32[]{:S(2)}) collective-permute-start(bf16[384,2,512]{0,2,1:T(8,128)(2,1)S(1)} %collective-permute-done.1), channel_id=1, source_target_pairs={{0,448},{64,0},{128,64},{192,128},{256,192},{320,256},{384,320},{4... | collective-permute-start | bytes 2359304 | tf_op jit(solution)/shard_map/ppermute | solution.py:20
  78.6 28.9 %collective-permute-start.4 = (bf16[384,2,512]{0,2,1:T(8,128)(2,1)}, bf16[384,2,512]{0,2,1:T(8,128)(2,1)S(1)}, u32[]{:S(2)}, u32[]{:S(2)}) collective-permute-start(bf16[384,2,512]{0,2,1:T(8,128)(2,1)} %collective-permute-done.2), channel_id=1, source_target_pairs={{0,64},{64,128},{128,192},{192,256},{256,320},{320,384},{384,448},... | collective-permute-start | bytes 2359304 | tf_op jit(solution)/shard_map/ppermute | solution.py:19
  80.6 21.5 %collective-permute-start.5 = (bf16[384,2,512]{0,2,1:T(8,128)(2,1)}, bf16[384,2,512]{0,2,1:T(8,128)(2,1)S(1)}, u32[]{:S(2)}, u32[]{:S(2)}) collective-permute-start(bf16[384,2,512]{0,2,1:T(8,128)(2,1)} %collective-permute-done.3), channel_id=1, source_target_pairs={{0,448},{64,0},{128,64},{192,128},{256,192},{320,256},{384,320},{4... | collective-permute-start | bytes 2359304 | tf_op jit(solution)/shard_map/ppermute | solution.py:20
  90.4 39.1 %collective-permute-start.8 = (bf16[256,2048]{1,0:T(8,128)(2,1)S(1)}, bf16[256,2048]{1,0:T(8,128)(2,1)S(1)}, u32[]{:S(2)}, u32[]{:S(2)}) collective-permute-start(bf16[256,2048]{1,0:T(8,128)(2,1)S(1)} %bitcast.131), channel_id=1, source_target_pairs={{0,1},{1,2},{2,3},{3,0},{4,5},{5,6},{6,7},{7,4},{8,9},{9,10},{10,1... | collective-permute-start | bytes 3145736 | tf_op jit(solution)/shard_map/ppermute | solution.py:19
  93.5 31.9 %collective-permute-start.9 = (bf16[256,2048]{1,0:T(8,128)(2,1)S(1)}, bf16[256,2048]{1,0:T(8,128)(2,1)S(1)}, u32[]{:S(2)}, u32[]{:S(2)}) collective-permute-start(bf16[256,2048]{1,0:T(8,128)(2,1)S(1)} %bitcast.132), channel_id=1, source_target_pairs={{0,3},{1,0},{2,1},{3,2},{4,7},{5,4},{6,5},{7,6},{8,11},{9,8},{10,9... | collective-permute-start | bytes 3145736 | tf_op jit(solution)/shard_map/ppermute | solution.py:20
  102.3 14.3 %collective-permute-start.7 = (bf16[192,2,512]{0,2,1:T(8,128)(2,1)S(1)}, bf16[192,2,512]{0,2,1:T(8,128)(2,1)S(1)}, u32[]{:S(2)}, u32[]{:S(2)}) collective-permute-start(bf16[192,2,512]{0,2,1:T(8,128)(2,1)S(1)} %slice.99), channel_id=1, source_target_pairs={{0,448},{64,0},{128,64},{192,128},{256,192},{320,256},{384,320},{4... | collective-permute-start | bytes 1179656 | tf_op jit(solution)/shard_map/ppermute | solution.py:25
  107.6 13.0 %collective-permute-start.6 = (bf16[192,2,512]{0,2,1:T(8,128)(2,1)S(1)}, bf16[192,2,512]{0,2,1:T(8,128)(2,1)S(1)}, u32[]{:S(2)}, u32[]{:S(2)}) collective-permute-start(bf16[192,2,512]{0,2,1:T(8,128)(2,1)S(1)} %slice.98), channel_id=1, source_target_pairs={{0,64},{64,128},{128,192},{192,256},{256,320},{320,384},{384,448},... | collective-permute-start | bytes 1179656 | tf_op jit(solution)/shard_map/ppermute | solution.py:24
  125.3 15.8 %copy-start = (bf16[384,1,8,512]{0,3,2,1:T(8,128)(2,1)}, bf16[384,1,8,512]{0,3,2,1:T(8,128)(2,1)S(1)}, u32[]{:S(2)}) copy-start(bf16[384,1,8,512]{0,3,2,1:T(8,128)(2,1)S(1)} %get-tuple-element.35) | copy-start | bytes 9437188
  125.4 17.1 %copy-start.5 = (bf16[384,1,8,512]{0,3,2,1:T(8,128)(2,1)}, bf16[384,1,8,512]{0,3,2,1:T(8,128)(2,1)S(1)}, u32[]{:S(2)}) copy-start(bf16[384,1,8,512]{0,3,2,1:T(8,128)(2,1)S(1)} %get-tuple-element.36) | copy-start | bytes 9437188
  125.4 10.8 %collective-permute-start.11 = (bf16[128,2048]{1,0:T(8,128)(2,1)S(1)}, bf16[128,2048]{1,0:T(8,128)(2,1)S(1)}, u32[]{:S(2)}, u32[]{:S(2)}) collective-permute-start(bf16[128,2048]{1,0:T(8,128)(2,1)S(1)} %slice.102), channel_id=1, source_target_pairs={{0,3},{1,0},{2,1},{3,2},{4,7},{5,4},{6,5},{7,6},{8,11},{9,8},{10,9... | collective-permute-start | bytes 1572872 | tf_op jit(solution)/shard_map/ppermute | solution.py:25
  129.5 11.6 %collective-permute-start.10 = (bf16[128,2048]{1,0:T(8,128)(2,1)S(1)}, bf16[128,2048]{1,0:T(8,128)(2,1)S(1)}, u32[]{:S(2)}, u32[]{:S(2)}) collective-permute-start(bf16[128,2048]{1,0:T(8,128)(2,1)S(1)} %slice.101), channel_id=1, source_target_pairs={{0,1},{1,2},{2,3},{3,0},{4,5},{5,6},{6,7},{7,4},{8,9},{9,10},{10,1... | collective-permute-start | bytes 1572872 | tf_op jit(solution)/shard_map/ppermute | solution.py:24
  141.2 2.0 copy-start.2
  142.4 2.0 copy-start.11
  144.4 4.7 %copy-start.4 = (bf16[1,384,4096]{1,2,0:T(8,128)(2,1)S(1)}, bf16[1,384,4096]{1,2,0:T(8,128)(2,1)}, u32[]{:S(2)}) copy-start(bf16[1,384,4096]{1,2,0:T(8,128)(2,1)} %all-gather.3.cloned.1.call-done) | copy-start | bytes 9437188
  149.1 3.3 %copy-start.3 = (bf16[4,256,2048]{2,1,0:T(8,128)(2,1)S(1)}, bf16[4,256,2048]{2,1,0:T(8,128)(2,1)}, u32[]{:S(2)}) copy-start(bf16[4,256,2048]{2,1,0:T(8,128)(2,1)} %copy-done.2) | copy-start | bytes 12582916
  156.3 1.9 copy-start.1
  158.2 3.8 %copy-start.6 = (bf16[384,1,8,512]{0,3,2,1:T(8,128)(2,1)S(1)}, bf16[384,1,8,512]{0,3,2,1:T(8,128)(2,1)}, u32[]{:S(2)}) copy-start(bf16[384,1,8,512]{0,3,2,1:T(8,128)(2,1)} %copy-done.5) | copy-start | bytes 9437188
  158.2 3.8 %copy-start.7 = (f32[256,384]{1,0:T(8,128)S(1)}, f32[256,384]{1,0:T(8,128)}, u32[]{:S(2)}) copy-start(f32[256,384]{1,0:T(8,128)} %get-tuple-element.42) | copy-start | bytes 1179652
  158.2 3.8 %copy-start.12 = (f32[256,384]{1,0:T(8,128)S(1)}, f32[256,384]{1,0:T(8,128)}, u32[]{:S(2)}) copy-start(f32[256,384]{1,0:T(8,128)} %copy-done.11) | copy-start | bytes 1179652
  163.4 9.9 %collective-permute-start.14 = (bf16[128,2048]{0,1:T(8,128)(2,1)S(1)}, bf16[128,2048]{0,1:T(8,128)(2,1)S(1)}, u32[]{:S(2)}, u32[]{:S(2)}) collective-permute-start(bf16[128,2048]{0,1:T(8,128)(2,1)S(1)} %get-tuple-element.38), channel_id=1, source_target_pairs={{0,3},{1,0},{2,1},{3,2},{4,7},{5,4},{6,5},{7,6},{8,11},{9,8},{10,9... | collective-permute-start | bytes 1572872 | tf_op jit(solution)/shard_map/ppermute | solution.py:40
  165.4 11.3 %collective-permute-start.12 = (bf16[128,2048]{0,1:T(8,128)(2,1)S(1)}, bf16[128,2048]{0,1:T(8,128)(2,1)S(1)}, u32[]{:S(2)}, u32[]{:S(2)}) collective-permute-start(bf16[128,2048]{0,1:T(8,128)(2,1)S(1)} %get-tuple-element.37), channel_id=1, source_target_pairs={{0,1},{1,2},{2,3},{3,0},{4,5},{5,6},{6,7},{7,4},{8,9},{9,10},{10,1... | collective-permute-start | bytes 1572872 | tf_op jit(solution)/shard_map/ppermute | solution.py:39
  173.6 21.5 %collective-permute-start.15 = (bf16[256,2048]{0,1:T(8,128)(2,1)S(1)}, bf16[256,2048]{0,1:T(8,128)(2,1)S(1)}, u32[]{:S(2)}, u32[]{:S(2)}) collective-permute-start(bf16[256,2048]{0,1:T(8,128)(2,1)S(1)} %convert_element_type.117), channel_id=1, source_target_pairs={{0,3},{1,0},{2,1},{3,2},{4,7},{5,4},{6,5},{7,6},{8,11},{9,8},{10,9... | collective-permute-start | bytes 3145736 | tf_op jit(solution)/shard_map/ppermute | solution.py:50
  176.9 21.1 %collective-permute-start.13 = (bf16[256,2048]{0,1:T(8,128)(2,1)S(1)}, bf16[256,2048]{0,1:T(8,128)(2,1)S(1)}, u32[]{:S(2)}, u32[]{:S(2)}) collective-permute-start(bf16[256,2048]{0,1:T(8,128)(2,1)S(1)} %convert_element_type.111), channel_id=1, source_target_pairs={{0,1},{1,2},{2,3},{3,0},{4,5},{5,6},{6,7},{7,4},{8,9},{9,10},{10,1... | collective-permute-start | bytes 3145736 | tf_op jit(solution)/shard_map/ppermute | solution.py:49
  199.9 42.0 %all-to-all-start.1 = ((bf16[16,16,2048]{2,1,0:T(8,128)(2,1)}), bf16[16,16,2048]{2,1,0:T(8,128)(2,1)S(1)}, u32[]{:S(2)}, u32[]{:S(2)}) async-start(bf16[16,16,2048]{2,1,0:T(8,128)(2,1)} %bitcast.46), calls=%async_computation.1 | async-start | bytes 2097152 | tf_op jit(solution)/shard_map/all_to_all | solution.py:116
  (1 other events, 1.8 us)
Sparse Core Ops, SparseCore 0:
  25.2 68.1 all-gather.2
  156.4 53.0 reduce-scatter.1

commit v7 on v6

--- a/solution.py
+++ b/solution.py
@@ -2,28 +2,6 @@
 import jax.numpy as jnp
 from jax import lax
 from jax.sharding import PartitionSpec as P
-
-
-def ring_gather(piece, axis, n, along=0):
-    idx = lax.axis_index(axis)
-    fwd = [(i, (i + 1) % n) for i in range(n)]
-    bwd = [(i, (i - 1) % n) for i in range(n)]
-    shape = list(piece.shape)
-    shape.insert(along, n)
-    out = jnp.zeros(shape, piece.dtype)
-    put = lambda buf, val, at: lax.dynamic_update_index_in_dim(buf, val, at % n, along)
-    out = put(out, piece, idx)
-    left = right = piece
-    half = n // 2
-    for k in range(1, half):
-        left = lax.ppermute(left, axis, fwd)
-        right = lax.ppermute(right, axis, bwd)
-        out = put(out, left, idx - k)
-        out = put(out, right, idx + k)
-    m = piece.shape[0] // 2
-    first = lax.ppermute(left[:m], axis, fwd)
-    second = lax.ppermute(right[m:], axis, bwd)
-    return put(out, jnp.concatenate([first, second], axis=0), idx + half)
 
 
 def ring_reduce_scatter(chunks, axis, n):
@@ -51,6 +29,55 @@
     return pick(idx) + got_left + got_right
 
 
+class Ring:
+    def __init__(self, piece, axis, n, along=0):
+        self.piece, self.axis, self.n, self.along = piece, axis, n, along
+        self.left = self.right = piece
+        self.hop = 0
+        self.got = []
+
+    def active(self):
+        return self.hop < self.n // 2
+
+    def step(self):
+        n, half = self.n, self.n // 2
+        fwd = [(i, (i + 1) % n) for i in range(n)]
+        bwd = [(i, (i - 1) % n) for i in range(n)]
+        self.hop += 1
+        if self.hop < half:
+            self.left = lax.ppermute(self.left, self.axis, fwd)
+            self.right = lax.ppermute(self.right, self.axis, bwd)
+        else:
+            m = self.piece.shape[0] // 2
+            self.left = lax.ppermute(self.left[:m], self.axis, fwd)
+            self.right = lax.ppermute(self.right[m:], self.axis, bwd)
+
+    def record(self):
+        if self.hop < self.n // 2:
+            self.got += [(-self.hop, self.left), (self.hop, self.right)]
+        else:
+            self.got.append((self.hop, jnp.concatenate([self.left, self.right], axis=0)))
+
+    def result(self):
+        idx = lax.axis_index(self.axis)
+        shape = list(self.piece.shape)
+        shape.insert(self.along, self.n)
+        out = jnp.zeros(shape, self.piece.dtype)
+        for offset, val in [(0, self.piece)] + self.got:
+            out = lax.dynamic_update_index_in_dim(out, val, (idx + offset) % self.n, self.along)
+        return out
+
+
+def lockstep(rings):
+    live = [r for r in rings if r.active()]
+    for r in live:
+        r.step()
+    held = lax.optimization_barrier(tuple((r.left, r.right) for r in live))
+    for r, (left, right) in zip(live, held):
+        r.left, r.right = left, right
+        r.record()
+
+
 def on_device(tokens, cotangent, route_weights, expert_ids, w_gate, w_up, w_down):
     tok_count, model_width = tokens.shape
     top_count = expert_ids.shape[1]
@@ -75,14 +102,20 @@
     empty_slots = jnp.zeros((slot_rows, 2 * part), jnp.bfloat16)
     send = empty_slots.at[slot_index].set(both).reshape(experts, capacity, 2 * part)
     recv = lax.all_to_all(send, "expert", split_axis=0, concat_axis=0, tiled=True)
-    recv = recv.reshape(1, slot_rows, 2 * part)
-    gathered = ring_gather(recv[0], "etp", shares)
+
+    gate_full = lax.all_gather(w_gate[0], "dp", axis=1, tiled=True)
+    weights = Ring(jnp.stack([w_up[0], w_down[0]], axis=1), "dp", lax.axis_size("dp"), along=2)
+    lockstep([weights])
+    weights.left, weights.right, recv = lax.optimization_barrier((weights.left, weights.right, recv))
+    rows = Ring(recv.reshape(slot_rows, 2 * part), "etp", shares)
+    while weights.active() or rows.active():
+        lockstep([weights, rows])
+    pair = weights.result()
+    up_full, down_full = (pair[:, i].reshape(w_up.shape[1], model_width) for i in range(2))
+    gathered = rows.result()
     rows4 = gathered[:, :, :part]
     grads4 = gathered[:, :, part:]
 
-    gate_full = lax.all_gather(w_gate[0], "dp", axis=1, tiled=True)
-    pair = ring_gather(jnp.stack([w_up[0], w_down[0]], axis=1), "dp", lax.axis_size("dp"), along=2)
-    up_full, down_full = (pair[:, i].reshape(w_up.shape[1], model_width) for i in range(2))
     hidden_units = gate_full.shape[0]
     gate4 = gate_full.reshape(hidden_units, shares, part)
     up4 = up_full.reshape(hidden_units, shares, part)

time: 256 us -> 262 us (1.023)
  waiting for transfers between devices: 100 us -> 108 us
  starting transfers between devices: 79.7 us -> 76.8 us
  local copies, waits for them, and re-layouts: 31.4 us -> 34.3 us
    all_to_all x1, starting transfers between devices: 14.1 us -> 8.49 us  [on_device(): lax.all_to_all(slot_out.reshape(experts, capacity, 2 * part), 'expert', s...]
    ppermute x2, starting transfers between devices: 5.05 us -> 9.09 us  [ring_reduce_scatter(): lax.ppermute(to_left.astype(chunks.dtype), axis, bwd).astype(jnp.float32)]
    ppermute x12, waiting for transfers between devices: 49.2 us -> 52.1 us  [the longest x4 35.5 us: step(): self.left = lax.ppermute(self.left, self.axis, fwd)]
    unnamed x34 -> x36, local copies, waits for them, and re-layouts: 7.53 us -> 7.01 us
  transfers between devices with their start and end apart: 20 -> 20, of which waited for: 12 -> 11; matrix products, arithmetic and copies ran while one was open for 15% -> 14% of each run, Pallas kernels for 0% -> 0%
where the time goes in v7:
time: 262 us; the launch traced here: 261 us
  waiting for transfers between devices  108 us (41%)
  starting transfers between devices  76.8 us (29%)
  local copies, waits for them, and re-layouts  34.3 us (13%)
  matrix products  16.6 us (6%)
  between operations  14.8 us (6%)
  other arithmetic  10.5 us (4%)
    ppermute x4, waiting for transfers between devices, step(): self.left = lax.ppermute(self.left, self.axis, fwd)  35.5 us
    all_to_all x1, waiting for transfers between devices, on_device(): lax.all_to_all(slot_out.reshape(experts, capacity, 2 * part), 'expert', s...  28 us
    ppermute x2, waiting for transfers between devices, ring_reduce_scatter(): lax.ppermute(to_left.astype(chunks.dtype), axis, bwd).astype(jnp.float32)  22.2 us
    ppermute x4, starting transfers between devices, step(): self.right = lax.ppermute(self.right, self.axis, bwd)  22 us
    dynamic_update_slice x9, local copies, waits for them, and re-layouts, result(): lax.dynamic_update_index_in_dim(out, val, (idx + offset) % self.n, self.a...  10.9 us
    all_to_all x1, starting transfers between devices, on_device(): lax.all_to_all(send, 'expert', split_axis=0, concat_axis=0, tiled=True)  10.3 us
    ppermute x4, starting transfers between devices, step(): self.left = lax.ppermute(self.left, self.axis, fwd)  9.64 us
    ppermute x2, starting transfers between devices, ring_reduce_scatter(): lax.ppermute(to_left.astype(chunks.dtype), axis, bwd).astype(jnp.float32)  9.09 us
  transfers between devices with their start and end apart: 20, of which 11 were waited for; matrix products, arithmetic and copies ran while one was open for 14% of the time, Pallas kernels for 0%

profile of v7, /device:TPU:1, one launch (start us, length us, event | category | flops | bytes accessed | tf_op | source)
XLA Modules:
  0.0 260.6 jit_solution(9109225481225816806)
XLA Ops:
  11.9 2.8 %scatter_custom_fusion = bf16[256,2048]{1,0:T(8,128)(2,1)} fusion(s32[192]{0:T(256)S(1)} %bitcast.142, bf16[192,1024]{1,0:T(8,128)(2,1)S(1)} %fusion.36, bf16[]{:T(256)} %constant.255, bf16[192,1024]{1,0:T(8,128)(2,1)S(1)} %broadcast_bitcast_fusion, bf16[]{:T(256)} %constant.212.clone.1), kind=kCustom, calls=%fused_computation.51 | custom fusion | flops 1572864 | bytes 1835012 | tf_op jit(solution)/shard_map/scatter | solution.py:103
  14.7 10.3 %all-to-all-start = ((bf16[16,16,2048]{2,1,0:T(8,128)(2,1)}), bf16[16,16,2048]{2,1,0:T(8,128)(2,1)S(1)}, u32[]{:S(2)}, u32[]{:S(2)}) async-start(bf16[16,16,2048]{2,1,0:T(8,128)(2,1)} %bitcast.12), calls=%async_computation | async-start | bytes 2097152 | tf_op jit(solution)/shard_map/all_to_all | solution.py:104
  25.6 2.3 collective-permute-start
  28.0 8.6 %collective-permute-start.1 = (bf16[384,2,512]{0,2,1:T(8,128)(2,1)S(1)}, bf16[384,2,512]{0,2,1:T(8,128)(2,1)}, u32[]{:S(2)}, u32[]{:S(2)}) collective-permute-start(bf16[384,2,512]{0,2,1:T(8,128)(2,1)S(1)} %pad_maximum_fusion), channel_id=1, source_target_pairs={{0,448},{64,0},{128,64},{192,128},{256,192},{320,256},{384,320},{4... | collective-permute-start | bytes 2359304 | tf_op jit(solution)/shard_map/ppermute | solution.py:49
  37.6 15.0 %collective-permute-done = bf16[384,2,512]{0,2,1:T(8,128)(2,1)} collective-permute-done((bf16[384,2,512]{0,2,1:T(8,128)(2,1)S(1)}, bf16[384,2,512]{0,2,1:T(8,128)(2,1)}, u32[]{:S(2)}, u32[]{:S(2)}) %collective-permute-start) | collective-permute-done | bytes 786464 | tf_op jit(solution)/shard_map/ppermute | solution.py:48
  52.5 3.6 %collective-permute-done.1 = bf16[384,2,512]{0,2,1:T(8,128)(2,1)} collective-permute-done((bf16[384,2,512]{0,2,1:T(8,128)(2,1)S(1)}, bf16[384,2,512]{0,2,1:T(8,128)(2,1)}, u32[]{:S(2)}, u32[]{:S(2)}) %collective-permute-start.1) | collective-permute-done | bytes 786464 | tf_op jit(solution)/shard_map/ppermute | solution.py:49
  56.1 3.4 %collective-permute-start.4 = (bf16[256,2048]{1,0:T(8,128)(2,1)S(1)}, bf16[256,2048]{1,0:T(8,128)(2,1)}, u32[]{:S(2)}, u32[]{:S(2)}) collective-permute-start(bf16[256,2048]{1,0:T(8,128)(2,1)S(1)} %bitcast.131), channel_id=1, source_target_pairs={{0,1},{1,2},{2,3},{3,0},{4,5},{5,6},{6,7},{7,4},{8,9},{9,10},{10,1... | collective-permute-start | bytes 3145736 | tf_op jit(solution)/shard_map/ppermute | solution.py:48
  59.5 3.2 %collective-permute-start.5 = (bf16[256,2048]{1,0:T(8,128)(2,1)S(1)}, bf16[256,2048]{1,0:T(8,128)(2,1)S(1)}, u32[]{:S(2)}, u32[]{:S(2)}) collective-permute-start(bf16[256,2048]{1,0:T(8,128)(2,1)S(1)} %bitcast.132), channel_id=1, source_target_pairs={{0,3},{1,0},{2,1},{3,2},{4,7},{5,4},{6,5},{7,6},{8,11},{9,8},{10,9... | collective-permute-start | bytes 3145736 | tf_op jit(solution)/shard_map/ppermute | solution.py:49
  62.8 3.5 %broadcast_in_dim.70 = bf16[384,2,8,512]{0,3,2,1:T(8,128)(2,1)} broadcast(bf16[]{:T(256)} %constant.212.clone.1), dimensions={} | broadcast | bytes 6291458 | tf_op jit(solution)/shard_map/broadcast_in_dim | solution.py:65
  69.2 5.7 %collective-permute-start.3 = (bf16[384,2,512]{0,2,1:T(8,128)(2,1)}, bf16[384,2,512]{0,2,1:T(8,128)(2,1)}, u32[]{:S(2)}, u32[]{:S(2)}) collective-permute-start(bf16[384,2,512]{0,2,1:T(8,128)(2,1)} %collective-permute-done.1), channel_id=1, source_target_pairs={{0,448},{64,0},{128,64},{192,128},{256,192},{320,256},{384,320},{4... | collective-permute-start | bytes 2359304 | tf_op jit(solution)/shard_map/ppermute | solution.py:49
  79.9 20.5 %collective-permute-done.2 = bf16[384,2,512]{0,2,1:T(8,128)(2,1)S(1)} collective-permute-done((bf16[384,2,512]{0,2,1:T(8,128)(2,1)}, bf16[384,2,512]{0,2,1:T(8,128)(2,1)S(1)}, u32[]{:S(2)}, u32[]{:S(2)}) %collective-permute-start.2) | collective-permute-done | bytes 786464 | tf_op jit(solution)/shard_map/ppermute | solution.py:48
  102.4 4.5 %collective-permute-start.7 = (bf16[384,2,512]{0,2,1:T(8,128)(2,1)}, bf16[384,2,512]{0,2,1:T(8,128)(2,1)S(1)}, u32[]{:S(2)}, u32[]{:S(2)}) collective-permute-start(bf16[384,2,512]{0,2,1:T(8,128)(2,1)} %collective-permute-done.3), channel_id=1, source_target_pairs={{0,448},{64,0},{128,64},{192,128},{256,192},{320,256},{384,320},{4... | collective-permute-start | bytes 2359304 | tf_op jit(solution)/shard_map/ppermute | solution.py:49
  108.0 3.0 %collective-permute-start.8 = (bf16[128,2048]{1,0:T(8,128)(2,1)S(1)}, bf16[128,2048]{1,0:T(8,128)(2,1)S(1)}, u32[]{:S(2)}, u32[]{:S(2)}) collective-permute-start(bf16[128,2048]{1,0:T(8,128)(2,1)S(1)} %slice.80), channel_id=1, source_target_pairs={{0,1},{1,2},{2,3},{3,0},{4,5},{5,6},{6,7},{7,4},{8,9},{9,10},{10,1... | collective-permute-start | bytes 1572872 | tf_op jit(solution)/shard_map/ppermute | solution.py:52
  111.1 3.5 %collective-permute-start.9 = (bf16[128,2048]{1,0:T(8,128)(2,1)S(1)}, bf16[128,2048]{1,0:T(8,128)(2,1)S(1)}, u32[]{:S(2)}, u32[]{:S(2)}) collective-permute-start(bf16[128,2048]{1,0:T(8,128)(2,1)S(1)} %slice.81), channel_id=1, source_target_pairs={{0,3},{1,0},{2,1},{3,2},{4,7},{5,4},{6,5},{7,6},{8,11},{9,8},{10,9... | collective-permute-start | bytes 1572872 | tf_op jit(solution)/shard_map/ppermute | solution.py:53
  119.1 3.7 %collective-permute-done.8 = bf16[128,2048]{1,0:T(8,128)(2,1)S(1)} collective-permute-done((bf16[128,2048]{1,0:T(8,128)(2,1)S(1)}, bf16[128,2048]{1,0:T(8,128)(2,1)S(1)}, u32[]{:S(2)}, u32[]{:S(2)}) %collective-permute-start.8) | collective-permute-done | bytes 524320 | tf_op jit(solution)/shard_map/ppermute | solution.py:52
  124.4 3.1 %collective-permute-start.10 = (bf16[192,2,512]{0,2,1:T(8,128)(2,1)S(1)}, bf16[192,2,512]{0,2,1:T(8,128)(2,1)S(1)}, u32[]{:S(2)}, u32[]{:S(2)}) collective-permute-start(bf16[192,2,512]{0,2,1:T(8,128)(2,1)S(1)} %slice.82), channel_id=1, source_target_pairs={{0,64},{64,128},{128,192},{192,256},{256,320},{320,384},{384,448},... | collective-permute-start | bytes 1179656 | tf_op jit(solution)/shard_map/ppermute | solution.py:52
  127.8 3.5 %collective-permute-start.11 = (bf16[192,2,512]{0,2,1:T(8,128)(2,1)S(1)}, bf16[192,2,512]{0,2,1:T(8,128)(2,1)S(1)}, u32[]{:S(2)}, u32[]{:S(2)}) collective-permute-start(bf16[192,2,512]{0,2,1:T(8,128)(2,1)S(1)} %slice.83), channel_id=1, source_target_pairs={{0,448},{64,0},{128,64},{192,128},{256,192},{320,256},{384,320},{4... | collective-permute-start | bytes 1179656 | tf_op jit(solution)/shard_map/ppermute | solution.py:53
  133.5 4.4 %collective-permute-done.10 = bf16[192,2,512]{0,2,1:T(8,128)(2,1)S(1)} collective-permute-done((bf16[192,2,512]{0,2,1:T(8,128)(2,1)S(1)}, bf16[192,2,512]{0,2,1:T(8,128)(2,1)S(1)}, u32[]{:S(2)}, u32[]{:S(2)}) %collective-permute-start.10) | collective-permute-done | bytes 393248 | tf_op jit(solution)/shard_map/ppermute | solution.py:52
  138.0 3.3 %collective-permute-done.11 = bf16[192,2,512]{0,2,1:T(8,128)(2,1)S(1)} collective-permute-done((bf16[192,2,512]{0,2,1:T(8,128)(2,1)S(1)}, bf16[192,2,512]{0,2,1:T(8,128)(2,1)S(1)}, u32[]{:S(2)}, u32[]{:S(2)}) %collective-permute-start.11) | collective-permute-done | bytes 393248 | tf_op jit(solution)/shard_map/ppermute | solution.py:53
  142.5 3.6 %fusion.54 = (bf16[384,1,8,512]{0,3,2,1:T(8,128)(2,1)S(1)}, bf16[384,1,8,512]{0,3,2,1:T(8,128)(2,1)S(1)}) fusion(bf16[384,2,8,512]{0,3,2,1:T(8,128)(2,1)} %fusion.35), kind=kLoop, calls=%fused_computation.95 | loop fusion | bytes 12582912 | tf_op jit(solution)/shard_map/slice | solution.py:114
  150.2 4.7 %multiply_convert_fusion.1 = (bf16[256,384]{1,0:T(8,128)(2,1)S(1)}, f32[256,384]{1,0:T(8,128)}) fusion(f32[256,384]{1,0:T(8,128)S(1)} %fusion.16, f32[256,384]{1,0:T(8,128)S(1)} %fusion.13, bf16[384,4,1024]{0,2,1:T(8,128)(2,1)} %bitcast.138, bf16[4,256,2048]{2,1,0:T(8,128)(2,1)} %copy-done.2), kind=kOutput, calls=%fused_computation.74 | convolution fusion | flops 806289408 | bytes 6619136 | tf_op jit(solution)/shard_map/jsc,fjc->sf/dot_general | solution.py:124
  154.8 3.2 %fusion.48 = f32[256,4,1024]{0,2,1:T(8,128)} fusion(bf16[384,4,1024]{0,2,1:T(8,128)(2,1)S(1)} %bitcast.139, bf16[256,384]{1,0:T(8,128)(2,1)S(1)} %get-tuple-element.71), kind=kOutput, calls=%fused_computation.81 | convolution fusion | flops 805306368 | bytes 7536640 | tf_op jit(solution)/shard_map/sf,fjc->jsc/dot_general | solution.py:138
  159.1 2.8 %copy.76 = bf16[384,4,1024]{0,2,1:T(8,128)(2,1)} copy(bf16[384,4,1024]{2,0,1:T(8,128)(2,1)S(1)} %convolution_convert_fusion) | data formatting | bytes 6291456 | tf_op jit(solution)/shard_map/convert_element_type | solution.py:143
  163.8 3.8 %fusion = bf16[4,256,1024]{1,2,0:T(8,128)(2,1)S(1)} fusion(f32[256,4,1024]{0,2,1:T(8,128)} %fusion.48, bf16[384,4,1024]{0,2,1:T(8,128)(2,1)S(1)} %bitcast.130, f32[256,384]{1,0:T(8,128)S(1)} %fusion.16, f32[256,384]{1,0:T(8,128)} %get-tuple-element.72), kind=kOutput, calls=%fused_computation.14 | convolution fusion | flops 807993344 | bytes 10223616 | tf_op jit(solution)/shard_map/sf,fjc->jsc/dot_general | solution.py:139
  169.1 4.1 %collective-permute-start.14 = (bf16[128,2048]{0,1:T(8,128)(2,1)S(1)}, bf16[128,2048]{0,1:T(8,128)(2,1)S(1)}, u32[]{:S(2)}, u32[]{:S(2)}) collective-permute-start(bf16[128,2048]{0,1:T(8,128)(2,1)S(1)} %get-tuple-element.68), channel_id=1, source_target_pairs={{0,3},{1,0},{2,1},{3,2},{4,7},{5,4},{6,5},{7,6},{8,11},{9,8},{10,9... | collective-permute-start | bytes 1572872 | tf_op jit(solution)/shard_map/ppermute | solution.py:18
  175.7 6.0 %collective-permute-done.14 = bf16[128,2048]{0,1:T(8,128)(2,1)S(1)} collective-permute-done((bf16[128,2048]{0,1:T(8,128)(2,1)S(1)}, bf16[128,2048]{0,1:T(8,128)(2,1)S(1)}, u32[]{:S(2)}, u32[]{:S(2)}) %collective-permute-start.14) | collective-permute-done | bytes 524320 | tf_op jit(solution)/shard_map/ppermute | solution.py:18
  182.0 5.0 %collective-permute-start.15 = (bf16[256,2048]{0,1:T(8,128)(2,1)S(1)}, bf16[256,2048]{0,1:T(8,128)(2,1)S(1)}, u32[]{:S(2)}, u32[]{:S(2)}) collective-permute-start(bf16[256,2048]{0,1:T(8,128)(2,1)S(1)} %convert_element_type.117), channel_id=1, source_target_pairs={{0,3},{1,0},{2,1},{3,2},{4,7},{5,4},{6,5},{7,6},{8,11},{9,8},{10,9... | collective-permute-start | bytes 3145736 | tf_op jit(solution)/shard_map/ppermute | solution.py:28
  187.2 2.1 collective-permute-start.13
  189.3 16.2 %collective-permute-done.15 = bf16[256,2048]{0,1:T(8,128)(2,1)S(1)} collective-permute-done((bf16[256,2048]{0,1:T(8,128)(2,1)S(1)}, bf16[256,2048]{0,1:T(8,128)(2,1)S(1)}, u32[]{:S(2)}, u32[]{:S(2)}) %collective-permute-start.15) | collective-permute-done | bytes 1048608 | tf_op jit(solution)/shard_map/ppermute | solution.py:28
  205.6 5.3 %collective-permute-done.13 = bf16[256,2048]{0,1:T(8,128)(2,1)S(1)} collective-permute-done((bf16[256,2048]{0,1:T(8,128)(2,1)S(1)}, bf16[256,2048]{0,1:T(8,128)(2,1)S(1)}, u32[]{:S(2)}, u32[]{:S(2)}) %collective-permute-start.13) | collective-permute-done | bytes 1048608 | tf_op jit(solution)/shard_map/ppermute | solution.py:27
  212.7 8.5 %all-to-all-start.1 = ((bf16[16,16,2048]{2,1,0:T(8,128)(2,1)}), bf16[16,16,2048]{2,1,0:T(8,128)(2,1)S(1)}, u32[]{:S(2)}, u32[]{:S(2)}) async-start(bf16[16,16,2048]{2,1,0:T(8,128)(2,1)} %bitcast.46), calls=%async_computation.1 | async-start | bytes 2097152 | tf_op jit(solution)/shard_map/all_to_all | solution.py:149
  221.2 28.0 %all-to-all-done.1 = bf16[16,16,2048]{2,1,0:T(8,128)(2,1)S(1)} async-done(((bf16[16,16,2048]{2,1,0:T(8,128)(2,1)}), bf16[16,16,2048]{2,1,0:T(8,128)(2,1)S(1)}, u32[]{:S(2)}, u32[]{:S(2)}) %all-to-all-start.1) | async-done | bytes 1048608 | tf_op jit(solution)/shard_map/all_to_all | solution.py:149
  (103 shorter events, 44.5 us)
Async XLA Ops:
  10.5 14.6 %copy-start.8 = (bf16[1,384,512]{2,1,0:T(8,128)(2,1)S(1)}, bf16[1,384,512]{2,1,0:T(8,128)(2,1)}, u32[]{:S(2)}) copy-start(bf16[1,384,512]{2,1,0:T(8,128)(2,1)} %param.17) | copy-start | bytes 1179652
  10.5 14.8 %copy-start.9 = (bf16[1,384,512]{2,1,0:T(8,128)(2,1)S(1)}, bf16[1,384,512]{2,1,0:T(8,128)(2,1)}, u32[]{:S(2)}) copy-start(bf16[1,384,512]{2,1,0:T(8,128)(2,1)} %param.16) | copy-start | bytes 1179652
  11.9 24.7 %copy-start.10 = (bf16[1,384,512]{2,1,0:T(8,128)(2,1)S(1)}, bf16[1,384,512]{2,1,0:T(8,128)(2,1)}, u32[]{:S(2)}) copy-start(bf16[1,384,512]{2,1,0:T(8,128)(2,1)} %param.15) | copy-start | bytes 1179652
  14.7 41.4 %all-to-all-start = ((bf16[16,16,2048]{2,1,0:T(8,128)(2,1)}), bf16[16,16,2048]{2,1,0:T(8,128)(2,1)S(1)}, u32[]{:S(2)}, u32[]{:S(2)}) async-start(bf16[16,16,2048]{2,1,0:T(8,128)(2,1)} %bitcast.12), calls=%async_computation | async-start | bytes 2097152 | tf_op jit(solution)/shard_map/all_to_all | solution.py:104
  25.1 125.1 %all-gather.3.cloned.1.call-start = ((), (), s32[]{:S(2)}) async-start(), calls=%async_computation.4 | async-start | bytes 3538944 | tf_op jit(solution)/shard_map/all_gather | solution.py:106
  25.6 26.9 %collective-permute-start = (bf16[384,2,512]{0,2,1:T(8,128)(2,1)S(1)}, bf16[384,2,512]{0,2,1:T(8,128)(2,1)}, u32[]{:S(2)}, u32[]{:S(2)}) collective-permute-start(bf16[384,2,512]{0,2,1:T(8,128)(2,1)S(1)} %pad_maximum_fusion), channel_id=1, source_target_pairs={{0,64},{64,128},{128,192},{192,256},{256,320},{320,384},{384,448},... | collective-permute-start | bytes 2359304 | tf_op jit(solution)/shard_map/ppermute | solution.py:48
  28.0 28.2 %collective-permute-start.1 = (bf16[384,2,512]{0,2,1:T(8,128)(2,1)S(1)}, bf16[384,2,512]{0,2,1:T(8,128)(2,1)}, u32[]{:S(2)}, u32[]{:S(2)}) collective-permute-start(bf16[384,2,512]{0,2,1:T(8,128)(2,1)S(1)} %pad_maximum_fusion), channel_id=1, source_target_pairs={{0,448},{64,0},{128,64},{192,128},{256,192},{320,256},{384,320},{4... | collective-permute-start | bytes 2359304 | tf_op jit(solution)/shard_map/ppermute | solution.py:49
  37.5 214.0 %reduce-scatter.2.cloned.1.call-start = ((), (), s32[]{:S(2)}) async-start(), calls=%async_computation.3 | async-start | bytes 3538944 | tf_op jit(solution)/shard_map/reduce_scatter | solution.py:144
  56.1 44.3 %collective-permute-start.4 = (bf16[256,2048]{1,0:T(8,128)(2,1)S(1)}, bf16[256,2048]{1,0:T(8,128)(2,1)}, u32[]{:S(2)}, u32[]{:S(2)}) collective-permute-start(bf16[256,2048]{1,0:T(8,128)(2,1)S(1)} %bitcast.131), channel_id=1, source_target_pairs={{0,1},{1,2},{2,3},{3,0},{4,5},{5,6},{6,7},{7,4},{8,9},{9,10},{10,1... | collective-permute-start | bytes 3145736 | tf_op jit(solution)/shard_map/ppermute | solution.py:48
  59.5 40.9 %collective-permute-start.5 = (bf16[256,2048]{1,0:T(8,128)(2,1)S(1)}, bf16[256,2048]{1,0:T(8,128)(2,1)S(1)}, u32[]{:S(2)}, u32[]{:S(2)}) collective-permute-start(bf16[256,2048]{1,0:T(8,128)(2,1)S(1)} %bitcast.132), channel_id=1, source_target_pairs={{0,3},{1,0},{2,1},{3,2},{4,7},{5,4},{6,5},{7,6},{8,11},{9,8},{10,9... | collective-permute-start | bytes 3145736 | tf_op jit(solution)/shard_map/ppermute | solution.py:49
  67.2 33.2 %collective-permute-start.2 = (bf16[384,2,512]{0,2,1:T(8,128)(2,1)}, bf16[384,2,512]{0,2,1:T(8,128)(2,1)S(1)}, u32[]{:S(2)}, u32[]{:S(2)}) collective-permute-start(bf16[384,2,512]{0,2,1:T(8,128)(2,1)} %collective-permute-done), channel_id=1, source_target_pairs={{0,64},{64,128},{128,192},{192,256},{256,320},{320,384},{384,448},... | collective-permute-start | bytes 2359304 | tf_op jit(solution)/shard_map/ppermute | solution.py:48
  69.2 31.2 %collective-permute-start.3 = (bf16[384,2,512]{0,2,1:T(8,128)(2,1)}, bf16[384,2,512]{0,2,1:T(8,128)(2,1)}, u32[]{:S(2)}, u32[]{:S(2)}) collective-permute-start(bf16[384,2,512]{0,2,1:T(8,128)(2,1)} %collective-permute-done.1), channel_id=1, source_target_pairs={{0,448},{64,0},{128,64},{192,128},{256,192},{320,256},{384,320},{4... | collective-permute-start | bytes 2359304 | tf_op jit(solution)/shard_map/ppermute | solution.py:49
  100.4 23.9 %collective-permute-start.6 = (bf16[384,2,512]{0,2,1:T(8,128)(2,1)S(1)}, bf16[384,2,512]{0,2,1:T(8,128)(2,1)S(1)}, u32[]{:S(2)}, u32[]{:S(2)}) collective-permute-start(bf16[384,2,512]{0,2,1:T(8,128)(2,1)S(1)} %collective-permute-done.2), channel_id=1, source_target_pairs={{0,64},{64,128},{128,192},{192,256},{256,320},{320,384},{384,448},... | collective-permute-start | bytes 2359304 | tf_op jit(solution)/shard_map/ppermute | solution.py:48
  102.4 21.9 %collective-permute-start.7 = (bf16[384,2,512]{0,2,1:T(8,128)(2,1)}, bf16[384,2,512]{0,2,1:T(8,128)(2,1)S(1)}, u32[]{:S(2)}, u32[]{:S(2)}) collective-permute-start(bf16[384,2,512]{0,2,1:T(8,128)(2,1)} %collective-permute-done.3), channel_id=1, source_target_pairs={{0,448},{64,0},{128,64},{192,128},{256,192},{320,256},{384,320},{4... | collective-permute-start | bytes 2359304 | tf_op jit(solution)/shard_map/ppermute | solution.py:49
  108.0 14.8 %collective-permute-start.8 = (bf16[128,2048]{1,0:T(8,128)(2,1)S(1)}, bf16[128,2048]{1,0:T(8,128)(2,1)S(1)}, u32[]{:S(2)}, u32[]{:S(2)}) collective-permute-start(bf16[128,2048]{1,0:T(8,128)(2,1)S(1)} %slice.80), channel_id=1, source_target_pairs={{0,1},{1,2},{2,3},{3,0},{4,5},{5,6},{6,7},{7,4},{8,9},{9,10},{10,1... | collective-permute-start | bytes 1572872 | tf_op jit(solution)/shard_map/ppermute | solution.py:52
  111.1 13.3 %collective-permute-start.9 = (bf16[128,2048]{1,0:T(8,128)(2,1)S(1)}, bf16[128,2048]{1,0:T(8,128)(2,1)S(1)}, u32[]{:S(2)}, u32[]{:S(2)}) collective-permute-start(bf16[128,2048]{1,0:T(8,128)(2,1)S(1)} %slice.81), channel_id=1, source_target_pairs={{0,3},{1,0},{2,1},{3,2},{4,7},{5,4},{6,5},{7,6},{8,11},{9,8},{10,9... | collective-permute-start | bytes 1572872 | tf_op jit(solution)/shard_map/ppermute | solution.py:53
  124.4 13.5 %collective-permute-start.10 = (bf16[192,2,512]{0,2,1:T(8,128)(2,1)S(1)}, bf16[192,2,512]{0,2,1:T(8,128)(2,1)S(1)}, u32[]{:S(2)}, u32[]{:S(2)}) collective-permute-start(bf16[192,2,512]{0,2,1:T(8,128)(2,1)S(1)} %slice.82), channel_id=1, source_target_pairs={{0,64},{64,128},{128,192},{192,256},{256,320},{320,384},{384,448},... | collective-permute-start | bytes 1179656 | tf_op jit(solution)/shard_map/ppermute | solution.py:52
  127.8 13.5 %collective-permute-start.11 = (bf16[192,2,512]{0,2,1:T(8,128)(2,1)S(1)}, bf16[192,2,512]{0,2,1:T(8,128)(2,1)S(1)}, u32[]{:S(2)}, u32[]{:S(2)}) collective-permute-start(bf16[192,2,512]{0,2,1:T(8,128)(2,1)S(1)} %slice.83), channel_id=1, source_target_pairs={{0,448},{64,0},{128,64},{192,128},{256,192},{320,256},{384,320},{4... | collective-permute-start | bytes 1179656 | tf_op jit(solution)/shard_map/ppermute | solution.py:53
  132.4 15.3 %copy-start.2 = (bf16[4,256,2048]{2,1,0:T(8,128)(2,1)}, bf16[4,256,2048]{2,1,0:T(8,128)(2,1)S(1)}, u32[]{:S(2)}) copy-start(bf16[4,256,2048]{2,1,0:T(8,128)(2,1)S(1)} %fusion.29) | copy-start | bytes 12582916
  146.1 2.8 %copy-start.5 = (bf16[384,1,8,512]{0,3,2,1:T(8,128)(2,1)}, bf16[384,1,8,512]{0,3,2,1:T(8,128)(2,1)S(1)}, u32[]{:S(2)}) copy-start(bf16[384,1,8,512]{0,3,2,1:T(8,128)(2,1)S(1)} %get-tuple-element.66) | copy-start | bytes 9437188
  147.8 2.4 copy-start.12
  150.1 4.7 %copy-start.4 = (bf16[1,384,4096]{1,2,0:T(8,128)(2,1)S(1)}, bf16[1,384,4096]{1,2,0:T(8,128)(2,1)}, u32[]{:S(2)}) copy-start(bf16[1,384,4096]{1,2,0:T(8,128)(2,1)} %all-gather.3.cloned.1.call-done) | copy-start | bytes 9437188
  154.8 3.2 %copy-start.3 = (bf16[4,256,2048]{2,1,0:T(8,128)(2,1)S(1)}, bf16[4,256,2048]{2,1,0:T(8,128)(2,1)}, u32[]{:S(2)}) copy-start(bf16[4,256,2048]{2,1,0:T(8,128)(2,1)} %copy-done.2) | copy-start | bytes 12582916
  161.9 1.9 copy-start.1
  163.8 3.8 %copy-start.6 = (bf16[384,1,8,512]{0,3,2,1:T(8,128)(2,1)S(1)}, bf16[384,1,8,512]{0,3,2,1:T(8,128)(2,1)}, u32[]{:S(2)}) copy-start(bf16[384,1,8,512]{0,3,2,1:T(8,128)(2,1)} %copy-done.5) | copy-start | bytes 9437188
  163.8 3.8 %copy-start.7 = (f32[256,384]{1,0:T(8,128)S(1)}, f32[256,384]{1,0:T(8,128)}, u32[]{:S(2)}) copy-start(f32[256,384]{1,0:T(8,128)} %get-tuple-element.72) | copy-start | bytes 1179652
  163.8 3.8 %copy-start.13 = (f32[256,384]{1,0:T(8,128)S(1)}, f32[256,384]{1,0:T(8,128)}, u32[]{:S(2)}) copy-start(f32[256,384]{1,0:T(8,128)} %copy-done.12) | copy-start | bytes 1179652
  169.1 12.7 %collective-permute-start.14 = (bf16[128,2048]{0,1:T(8,128)(2,1)S(1)}, bf16[128,2048]{0,1:T(8,128)(2,1)S(1)}, u32[]{:S(2)}, u32[]{:S(2)}) collective-permute-start(bf16[128,2048]{0,1:T(8,128)(2,1)S(1)} %get-tuple-element.68), channel_id=1, source_target_pairs={{0,3},{1,0},{2,1},{3,2},{4,7},{5,4},{6,5},{7,6},{8,11},{9,8},{10,9... | collective-permute-start | bytes 1572872 | tf_op jit(solution)/shard_map/ppermute | solution.py:18
  173.2 13.8 %collective-permute-start.12 = (bf16[128,2048]{0,1:T(8,128)(2,1)S(1)}, bf16[128,2048]{0,1:T(8,128)(2,1)S(1)}, u32[]{:S(2)}, u32[]{:S(2)}) collective-permute-start(bf16[128,2048]{0,1:T(8,128)(2,1)S(1)} %get-tuple-element.67), channel_id=1, source_target_pairs={{0,1},{1,2},{2,3},{3,0},{4,5},{5,6},{6,7},{7,4},{8,9},{9,10},{10,1... | collective-permute-start | bytes 1572872 | tf_op jit(solution)/shard_map/ppermute | solution.py:17
  182.0 23.6 %collective-permute-start.15 = (bf16[256,2048]{0,1:T(8,128)(2,1)S(1)}, bf16[256,2048]{0,1:T(8,128)(2,1)S(1)}, u32[]{:S(2)}, u32[]{:S(2)}) collective-permute-start(bf16[256,2048]{0,1:T(8,128)(2,1)S(1)} %convert_element_type.117), channel_id=1, source_target_pairs={{0,3},{1,0},{2,1},{3,2},{4,7},{5,4},{6,5},{7,6},{8,11},{9,8},{10,9... | collective-permute-start | bytes 3145736 | tf_op jit(solution)/shard_map/ppermute | solution.py:28
  187.2 23.6 %collective-permute-start.13 = (bf16[256,2048]{0,1:T(8,128)(2,1)S(1)}, bf16[256,2048]{0,1:T(8,128)(2,1)S(1)}, u32[]{:S(2)}, u32[]{:S(2)}) collective-permute-start(bf16[256,2048]{0,1:T(8,128)(2,1)S(1)} %convert_element_type.111), channel_id=1, source_target_pairs={{0,1},{1,2},{2,3},{3,0},{4,5},{5,6},{6,7},{7,4},{8,9},{9,10},{10,1... | collective-permute-start | bytes 3145736 | tf_op jit(solution)/shard_map/ppermute | solution.py:27
  212.7 36.5 %all-to-all-start.1 = ((bf16[16,16,2048]{2,1,0:T(8,128)(2,1)}), bf16[16,16,2048]{2,1,0:T(8,128)(2,1)S(1)}, u32[]{:S(2)}, u32[]{:S(2)}) async-start(bf16[16,16,2048]{2,1,0:T(8,128)(2,1)} %bitcast.46), calls=%async_computation.1 | async-start | bytes 2097152 | tf_op jit(solution)/shard_map/all_to_all | solution.py:149
  (2 other events, 3.6 us)
Sparse Core Ops, SparseCore 0:
  37.6 55.3 all-gather.2
  162.1 47.7 reduce-scatter.1

commit v8 on v7

--- a/solution.py
+++ b/solution.py
@@ -103,15 +103,14 @@
     send = empty_slots.at[slot_index].set(both).reshape(experts, capacity, 2 * part)
     recv = lax.all_to_all(send, "expert", split_axis=0, concat_axis=0, tiled=True)
 
-    gate_full = lax.all_gather(w_gate[0], "dp", axis=1, tiled=True)
-    weights = Ring(jnp.stack([w_up[0], w_down[0]], axis=1), "dp", lax.axis_size("dp"), along=2)
+    weights = Ring(jnp.stack([w_gate[0], w_up[0], w_down[0]], axis=1), "dp", lax.axis_size("dp"), along=2)
     lockstep([weights])
     weights.left, weights.right, recv = lax.optimization_barrier((weights.left, weights.right, recv))
     rows = Ring(recv.reshape(slot_rows, 2 * part), "etp", shares)
     while weights.active() or rows.active():
         lockstep([weights, rows])
-    pair = weights.result()
-    up_full, down_full = (pair[:, i].reshape(w_up.shape[1], model_width) for i in range(2))
+    full = weights.result()
+    gate_full, up_full, down_full = (full[:, i].reshape(w_up.shape[1], model_width) for i in range(3))
     gathered = rows.result()
     rows4 = gathered[:, :, :part]
     grads4 = gathered[:, :, part:]
@@ -141,8 +140,9 @@
     gate_term = jnp.einsum(
         "sf,jsc->fjc", d_gate, rows4, preferred_element_type=jnp.float32
     ).astype(jnp.bfloat16).reshape(hidden_units, model_width)
-    weight_grads = lax.psum_scatter(gate_term, "dp", scatter_dimension=1, tiled=True)
-    grad_gate = weight_grads.astype(jnp.float32)[None]
+    groups = lax.axis_size("dp")
+    term_chunks = gate_term.reshape(hidden_units, groups, model_width // groups).transpose(1, 0, 2)
+    grad_gate = ring_reduce_scatter(term_chunks, "dp", groups)[None]
 
     outs4 = jnp.concatenate([mixed4, input4], axis=2)
     slot_out = ring_reduce_scatter(outs4, "etp", shares).astype(jnp.bfloat16)

time: 262 us -> 281 us (1.073)
  waiting for transfers between devices: 108 us -> 72.4 us
  starting transfers between devices: 76.8 us -> 106 us
  local copies, waits for them, and re-layouts: 34.3 us -> 54.2 us
  other arithmetic: 10.5 us -> 26.3 us
  between operations: 14.8 us -> 1.47 us
    all_to_all x1, waiting for transfers between devices: 28 us -> 0.01 us  [on_device(): lax.all_to_all(slot_out.reshape(experts, capacity, 2 * part), 'expert', s...]
    ppermute x2 -> x6, starting transfers between devices: 9.09 us -> 24.8 us  [ring_reduce_scatter(): lax.ppermute(to_left.astype(chunks.dtype), axis, bwd).astype(jnp.float32)]
    ppermute x2 -> x6, starting transfers between devices: 4.06 us -> 13.1 us  [ring_reduce_scatter(): lax.ppermute(to_right.astype(chunks.dtype), axis, fwd).astype(jnp.float32)]
    ppermute x2 -> x6, waiting for transfers between devices: 5.27 us -> 11.9 us  [ring_reduce_scatter(): lax.ppermute(to_right.astype(chunks.dtype), axis, fwd).astype(jnp.float32)]
    scatter-add x0 -> x2, local copies, waits for them, and re-layouts: none -> 6.43 us  [the longest x1 3.31 us: ring_reduce_scatter(): to_right = own_r.at[:m].add(got_left)]
    ppermute x2, waiting for transfers between devices: 8.12 us -> 2.29 us  [step(): self.left = lax.ppermute(self.left[:m], self.axis, fwd)]
    ppermute x2 -> x6, waiting for transfers between devices: 22.2 us -> 16.6 us  [ring_reduce_scatter(): lax.ppermute(to_left.astype(chunks.dtype), axis, bwd).astype(jnp.float32)]
    dynamic_update_slice x9, local copies, waits for them, and re-layouts: 10.9 us -> 16.5 us  [result(): lax.dynamic_update_index_in_dim(out, val, (idx + offset) % self.n, self.a...]
  transfers between devices with their start and end apart: 20 -> 26, of which waited for: 11 -> 13; matrix products, arithmetic and copies ran while one was open for 14% -> 24% of each run, Pallas kernels for 0% -> 0%
where the time goes in v8:
time: 281 us; the launch traced here: 277 us
  starting transfers between devices  106 us (38%)
  waiting for transfers between devices  72.4 us (26%)
  local copies, waits for them, and re-layouts  54.2 us (19%)
  other arithmetic  26.3 us (9%)
  matrix products  17.1 us (6%)
    ppermute x4, waiting for transfers between devices, step(): self.left = lax.ppermute(self.left, self.axis, fwd)  35.4 us
    ppermute x6, starting transfers between devices, ring_reduce_scatter(): lax.ppermute(to_left.astype(chunks.dtype), axis, bwd).astype(jnp.float32)  24.8 us
    ppermute x4, starting transfers between devices, step(): self.right = lax.ppermute(self.right, self.axis, bwd)  22 us
    ppermute x6, waiting for transfers between devices, ring_reduce_scatter(): lax.ppermute(to_left.astype(chunks.dtype), axis, bwd).astype(jnp.float32)  16.6 us
    dynamic_update_slice x9, local copies, waits for them, and re-layouts, result(): lax.dynamic_update_index_in_dim(out, val, (idx + offset) % self.n, self.a...  16.5 us
    ppermute x6, starting transfers between devices, ring_reduce_scatter(): lax.ppermute(to_right.astype(chunks.dtype), axis, fwd).astype(jnp.float32)  13.1 us
    all_to_all x1, starting transfers between devices, on_device(): lax.all_to_all(slot_out.reshape(experts, capacity, 2 * part), 'expert', s...  12.3 us
    ppermute x6, waiting for transfers between devices, ring_reduce_scatter(): lax.ppermute(to_right.astype(chunks.dtype), axis, fwd).astype(jnp.float32)  11.9 us
  transfers between devices with their start and end apart: 26, of which 13 were waited for; matrix products, arithmetic and copies ran while one was open for 24% of the time, Pallas kernels for 0%

profile of v8, /device:TPU:1, one launch (start us, length us, event | category | flops | bytes accessed | tf_op | source)
XLA Modules:
  0.0 277.0 jit_solution(5204251217237337660)
XLA Ops:
  8.2 10.3 %all-to-all-start = ((bf16[16,16,2048]{2,1,0:T(8,128)(2,1)}), bf16[16,16,2048]{2,1,0:T(8,128)(2,1)S(1)}, u32[]{:S(2)}, u32[]{:S(2)}) async-start(bf16[16,16,2048]{2,1,0:T(8,128)(2,1)} %bitcast.13), calls=%async_computation | async-start | bytes 2097152 | tf_op jit(solution)/shard_map/all_to_all | solution.py:104
  21.7 8.6 %collective-permute-start.1 = (bf16[384,3,512]{0,2,1:T(8,128)(2,1)S(1)}, bf16[384,3,512]{0,2,1:T(8,128)(2,1)}, u32[]{:S(2)}, u32[]{:S(2)}) collective-permute-start(bf16[384,3,512]{0,2,1:T(8,128)(2,1)S(1)} %pad_maximum_fusion), channel_id=1, source_target_pairs={{0,448},{64,0},{128,64},{192,128},{256,192},{320,256},{384,320},{4... | collective-permute-start | bytes 3538952 | tf_op jit(solution)/shard_map/ppermute | solution.py:49
  30.3 24.4 %collective-permute-done = bf16[384,3,512]{0,2,1:T(8,128)(2,1)} collective-permute-done((bf16[384,3,512]{0,2,1:T(8,128)(2,1)S(1)}, bf16[384,3,512]{0,2,1:T(8,128)(2,1)}, u32[]{:S(2)}, u32[]{:S(2)}) %collective-permute-start) | collective-permute-done | bytes 1179680 | tf_op jit(solution)/shard_map/ppermute | solution.py:48
  57.5 5.4 %collective-permute-start.3 = (bf16[384,3,512]{0,2,1:T(8,128)(2,1)}, bf16[384,3,512]{0,2,1:T(8,128)(2,1)}, u32[]{:S(2)}, u32[]{:S(2)}) collective-permute-start(bf16[384,3,512]{0,2,1:T(8,128)(2,1)} %collective-permute-done.1), channel_id=1, source_target_pairs={{0,448},{64,0},{128,64},{192,128},{256,192},{320,256},{384,320},{4... | collective-permute-start | bytes 3538952 | tf_op jit(solution)/shard_map/ppermute | solution.py:49
  62.9 3.1 %collective-permute-start.4 = (bf16[256,2048]{1,0:T(8,128)(2,1)S(1)}, bf16[256,2048]{1,0:T(8,128)(2,1)}, u32[]{:S(2)}, u32[]{:S(2)}) collective-permute-start(bf16[256,2048]{1,0:T(8,128)(2,1)S(1)} %bitcast.163), channel_id=1, source_target_pairs={{0,1},{1,2},{2,3},{3,0},{4,5},{5,6},{6,7},{7,4},{8,9},{9,10},{10,1... | collective-permute-start | bytes 3145736 | tf_op jit(solution)/shard_map/ppermute | solution.py:48
  66.1 3.4 %collective-permute-start.5 = (bf16[256,2048]{1,0:T(8,128)(2,1)S(1)}, bf16[256,2048]{1,0:T(8,128)(2,1)S(1)}, u32[]{:S(2)}, u32[]{:S(2)}) collective-permute-start(bf16[256,2048]{1,0:T(8,128)(2,1)S(1)} %bitcast.164), channel_id=1, source_target_pairs={{0,3},{1,0},{2,1},{3,2},{4,7},{5,4},{6,5},{7,6},{8,11},{9,8},{10,9... | collective-permute-start | bytes 3145736 | tf_op jit(solution)/shard_map/ppermute | solution.py:49
  69.7 5.0 %broadcast_in_dim.67 = bf16[384,3,8,512]{0,3,2,1:T(8,128)(2,1)} broadcast(bf16[]{:T(256)} %constant.331.clone.1), dimensions={} | broadcast | bytes 9437186 | tf_op jit(solution)/shard_map/broadcast_in_dim | solution.py:65
  84.4 5.3 %collective-permute-done.4 = bf16[256,2048]{1,0:T(8,128)(2,1)} collective-permute-done((bf16[256,2048]{1,0:T(8,128)(2,1)S(1)}, bf16[256,2048]{1,0:T(8,128)(2,1)}, u32[]{:S(2)}, u32[]{:S(2)}) %collective-permute-start.4) | collective-permute-done | bytes 1048608 | tf_op jit(solution)/shard_map/ppermute | solution.py:48
  93.2 4.6 %collective-permute-start.7 = (bf16[384,3,512]{0,2,1:T(8,128)(2,1)}, bf16[384,3,512]{0,2,1:T(8,128)(2,1)S(1)}, u32[]{:S(2)}, u32[]{:S(2)}) collective-permute-start(bf16[384,3,512]{0,2,1:T(8,128)(2,1)} %collective-permute-done.3), channel_id=1, source_target_pairs={{0,448},{64,0},{128,64},{192,128},{256,192},{320,256},{384,320},{4... | collective-permute-start | bytes 3538952 | tf_op jit(solution)/shard_map/ppermute | solution.py:49
  98.9 3.0 %collective-permute-start.8 = (bf16[128,2048]{1,0:T(8,128)(2,1)S(1)}, bf16[128,2048]{1,0:T(8,128)(2,1)S(1)}, u32[]{:S(2)}, u32[]{:S(2)}) collective-permute-start(bf16[128,2048]{1,0:T(8,128)(2,1)S(1)} %slice.133), channel_id=1, source_target_pairs={{0,1},{1,2},{2,3},{3,0},{4,5},{5,6},{6,7},{7,4},{8,9},{9,10},{10,1... | collective-permute-start | bytes 1572872 | tf_op jit(solution)/shard_map/ppermute | solution.py:52
  101.9 3.5 %collective-permute-start.9 = (bf16[128,2048]{1,0:T(8,128)(2,1)S(1)}, bf16[128,2048]{1,0:T(8,128)(2,1)S(1)}, u32[]{:S(2)}, u32[]{:S(2)}) collective-permute-start(bf16[128,2048]{1,0:T(8,128)(2,1)S(1)} %slice.134), channel_id=1, source_target_pairs={{0,3},{1,0},{2,1},{3,2},{4,7},{5,4},{6,5},{7,6},{8,11},{9,8},{10,9... | collective-permute-start | bytes 1572872 | tf_op jit(solution)/shard_map/ppermute | solution.py:53
  114.1 5.7 %collective-permute-done.6 = bf16[384,3,512]{0,2,1:T(8,128)(2,1)S(1)} collective-permute-done((bf16[384,3,512]{0,2,1:T(8,128)(2,1)}, bf16[384,3,512]{0,2,1:T(8,128)(2,1)S(1)}, u32[]{:S(2)}, u32[]{:S(2)}) %collective-permute-start.6) | collective-permute-done | bytes 1179680 | tf_op jit(solution)/shard_map/ppermute | solution.py:48
  125.3 5.4 %collective-permute-start.11 = (bf16[192,3,512]{2,0,1:T(8,128)(2,1)}, bf16[192,3,512]{2,0,1:T(8,128)(2,1)S(1)}, u32[]{:S(2)}, u32[]{:S(2)}) collective-permute-start(bf16[192,3,512]{2,0,1:T(8,128)(2,1)} %copy.94), channel_id=1, source_target_pairs={{0,448},{64,0},{128,64},{192,128},{256,192},{320,256},{384,320},{4... | collective-permute-start | bytes 1769480 | tf_op jit(solution)/shard_map/ppermute | solution.py:53
  143.1 4.3 %fusion.64 = (bf16[384,1,8,512]{0,3,2,1:T(8,128)(2,1)S(1)}, bf16[384,1,8,512]{0,3,2,1:T(8,128)(2,1)S(1)}, bf16[384,1,8,512]{0,3,2,1:T(8,128)(2,1)S(1)}) fusion(bf16[384,3,8,512]{0,3,2,1:T(8,128)(2,1)} %fusion.19), kind=kLoop, calls=%fused_computation.115 | loop fusion | bytes 18874368 | tf_op jit(solution)/shard_map/slice | solution.py:113
  147.4 2.9 %fusion.13 = f32[256,384]{1,0:T(8,128)S(1)} fusion(bf16[384,4,1024]{0,2,1:T(8,128)(2,1)S(1)} %bitcast.161, bf16[4,256,2048]{2,1,0:T(8,128)(2,1)} %fusion.30), kind=kOutput, calls=%fused_computation.28 | convolution fusion | flops 805306368 | bytes 5636096 | tf_op jit(solution)/shard_map/jsc,fjc->sf/dot_general | solution.py:124
  150.3 2.9 %fusion.16 = f32[256,384]{1,0:T(8,128)S(1)} fusion(bf16[384,4,1024]{0,2,1:T(8,128)(2,1)S(1)} %bitcast.172, bf16[4,256,2048]{2,1,0:T(8,128)(2,1)} %fusion.30), kind=kOutput, calls=%fused_computation.29 | convolution fusion | flops 805306368 | bytes 5636096 | tf_op jit(solution)/shard_map/jsc,fjc->sf/dot_general | solution.py:131
  153.2 3.0 %multiply_convert_fusion.1 = (bf16[256,384]{1,0:T(8,128)(2,1)S(1)}, f32[256,384]{1,0:T(8,128)S(1)}) fusion(f32[256,384]{1,0:T(8,128)S(1)} %fusion.16, f32[256,384]{1,0:T(8,128)S(1)} %fusion.13, bf16[384,4,1024]{0,2,1:T(8,128)(2,1)S(1)} %bitcast.151, bf16[4,256,2048]{2,1,0:T(8,128)(2,1)} %fusion.30), kind=kOutput, calls=%fused_computation.90 | convolution fusion | flops 806289408 | bytes 6619136 | tf_op jit(solution)/shard_map/jsc,fjc->sf/dot_general | solution.py:123
  160.4 4.3 %collective-permute-start.14 = (bf16[128,2048]{0,1:T(8,128)(2,1)S(1)}, bf16[128,2048]{0,1:T(8,128)(2,1)}, u32[]{:S(2)}, u32[]{:S(2)}) collective-permute-start(bf16[128,2048]{0,1:T(8,128)(2,1)S(1)} %get-tuple-element.96), channel_id=1, source_target_pairs={{0,3},{1,0},{2,1},{3,2},{4,7},{5,4},{6,5},{7,6},{8,11},{9,8},{10,9... | collective-permute-start | bytes 1572872 | tf_op jit(solution)/shard_map/ppermute | solution.py:18
  168.4 3.0 %collective-permute-done.14 = bf16[128,2048]{0,1:T(8,128)(2,1)} collective-permute-done((bf16[128,2048]{0,1:T(8,128)(2,1)S(1)}, bf16[128,2048]{0,1:T(8,128)(2,1)}, u32[]{:S(2)}, u32[]{:S(2)}) %collective-permute-start.14) | collective-permute-done | bytes 524320 | tf_op jit(solution)/shard_map/ppermute | solution.py:18
  173.7 5.4 %collective-permute-start.15 = (bf16[256,2048]{0,1:T(8,128)(2,1)}, bf16[256,2048]{0,1:T(8,128)(2,1)}, u32[]{:S(2)}, u32[]{:S(2)}) collective-permute-start(bf16[256,2048]{0,1:T(8,128)(2,1)} %convert_element_type.216), channel_id=1, source_target_pairs={{0,3},{1,0},{2,1},{3,2},{4,7},{5,4},{6,5},{7,6},{8,11},{9,8},{10,9... | collective-permute-start | bytes 3145736 | tf_op jit(solution)/shard_map/ppermute | solution.py:28
  182.4 4.3 %convolution_convert_fusion = bf16[384,4,1024]{2,0,1:T(8,128)(2,1)} fusion(bf16[4,256,2048]{2,1,0:T(8,128)(2,1)} %fusion.30, bf16[256,384]{1,0:T(8,128)(2,1)S(1)} %get-tuple-element.107), kind=kOutput, calls=%fused_computation.14 | convolution fusion | flops 806879232 | bytes 5439488 | tf_op jit(solution)/shard_map/sf,jsc->fjc/dot_general | solution.py:140
  186.7 4.7 %copy.102 = bf16[384,4,1024]{0,2,1:T(8,128)(2,1)} copy(bf16[384,4,1024]{2,0,1:T(8,128)(2,1)} %convolution_convert_fusion) | data formatting | bytes 6291456 | tf_op jit(solution)/shard_map/convert_element_type | solution.py:142
  195.2 5.2 %collective-permute-start.20 = (bf16[192,512]{0,1:T(8,128)(2,1)}, bf16[192,512]{0,1:T(8,128)(2,1)}, u32[]{:S(2)}, u32[]{:S(2)}) collective-permute-start(bf16[192,512]{0,1:T(8,128)(2,1)} %get-tuple-element.102), channel_id=1, source_target_pairs={{0,448},{64,0},{128,64},{192,128},{256,192},{320,256},{384,320},{4... | collective-permute-start | bytes 589832 | tf_op jit(solution)/shard_map/ppermute | solution.py:18
  202.6 3.3 %scatter-add.16 = bf16[384,512]{0,1:T(8,128)(2,1)} dynamic-update-slice(bf16[384,512]{0,1:T(8,128)(2,1)} %get-tuple-element.105, bf16[192,512]{0,1:T(8,128)(2,1)S(1)} %fusion.46, s32[]{:T(128)} %constant.332.clone.1, s32[]{:T(128)} %constant.332.clone.1) | dynamic-update-slice | bytes 393220 | tf_op jit(solution)/shard_map/scatter-add | solution.py:22
  209.0 3.1 %scatter-add.19 = bf16[384,512]{0,1:T(8,128)(2,1)} dynamic-update-slice(bf16[384,512]{0,1:T(8,128)(2,1)} %get-tuple-element.104, bf16[192,512]{0,1:T(8,128)(2,1)S(1)} %fusion.45, s32[]{:T(128)} %constant.355.clone.1, s32[]{:T(128)} %constant.332.clone.1) | dynamic-update-slice | bytes 393220 | tf_op jit(solution)/shard_map/scatter-add | solution.py:23
  212.2 4.6 %collective-permute-start.21 = (bf16[384,512]{0,1:T(8,128)(2,1)}, bf16[384,512]{0,1:T(8,128)(2,1)}, u32[]{:S(2)}, u32[]{:S(2)}) collective-permute-start(bf16[384,512]{0,1:T(8,128)(2,1)} %scatter-add.19), channel_id=1, source_target_pairs={{0,448},{64,0},{128,64},{192,128},{256,192},{320,256},{384,320},{4... | collective-permute-start | bytes 1179656 | tf_op jit(solution)/shard_map/ppermute | solution.py:18
  220.2 12.3 %all-to-all-start.1 = ((bf16[16,16,2048]{2,1,0:T(8,128)(2,1)}), bf16[16,16,2048]{2,1,0:T(8,128)(2,1)S(1)}, u32[]{:S(2)}, u32[]{:S(2)}) async-start(bf16[16,16,2048]{2,1,0:T(8,128)(2,1)} %bitcast.45), calls=%async_computation.1 | async-start | bytes 2097152 | tf_op jit(solution)/shard_map/all_to_all | solution.py:149
  235.6 11.8 %collective-permute-done.18 = bf16[384,512]{0,1:T(8,128)(2,1)S(1)} collective-permute-done((bf16[384,512]{0,1:T(8,128)(2,1)S(1)}, bf16[384,512]{0,1:T(8,128)(2,1)S(1)}, u32[]{:S(2)}, u32[]{:S(2)}) %collective-permute-start.18) | collective-permute-done | bytes 393248 | tf_op jit(solution)/shard_map/ppermute | solution.py:17
  250.8 3.4 %collective-permute-start.19 = (bf16[384,512]{0,1:T(8,128)(2,1)S(1)}, bf16[384,512]{0,1:T(8,128)(2,1)S(1)}, u32[]{:S(2)}, u32[]{:S(2)}) collective-permute-start(bf16[384,512]{0,1:T(8,128)(2,1)S(1)} %get-tuple-element.99), channel_id=1, source_target_pairs={{0,64},{64,128},{128,192},{192,256},{256,320},{320,384},{384,448},... | collective-permute-start | bytes 1179656 | tf_op jit(solution)/shard_map/ppermute | solution.py:27
  254.2 6.4 %collective-permute-done.22 = bf16[384,512]{0,1:T(8,128)(2,1)S(1)} collective-permute-done((bf16[384,512]{0,1:T(8,128)(2,1)S(1)}, bf16[384,512]{0,1:T(8,128)(2,1)S(1)}, u32[]{:S(2)}, u32[]{:S(2)}) %collective-permute-start.22) | collective-permute-done | bytes 393248 | tf_op jit(solution)/shard_map/ppermute | solution.py:18
  261.6 3.4 %collective-permute-start.23 = (bf16[384,512]{0,1:T(8,128)(2,1)S(1)}, bf16[384,512]{0,1:T(8,128)(2,1)S(1)}, u32[]{:S(2)}, u32[]{:S(2)}) collective-permute-start(bf16[384,512]{0,1:T(8,128)(2,1)S(1)} %fusion.37), channel_id=1, source_target_pairs={{0,448},{64,0},{128,64},{192,128},{256,192},{320,256},{384,320},{4... | collective-permute-start | bytes 1179656 | tf_op jit(solution)/shard_map/ppermute | solution.py:28
  265.1 7.2 %collective-permute-done.23 = bf16[384,512]{0,1:T(8,128)(2,1)S(1)} collective-permute-done((bf16[384,512]{0,1:T(8,128)(2,1)S(1)}, bf16[384,512]{0,1:T(8,128)(2,1)S(1)}, u32[]{:S(2)}, u32[]{:S(2)}) %collective-permute-start.23) | collective-permute-done | bytes 393248 | tf_op jit(solution)/shard_map/ppermute | solution.py:28
  (112 shorter events, 92.5 us)
Async XLA Ops:
  4.0 14.6 %copy-start.3 = (bf16[1,384,512]{2,1,0:T(8,128)(2,1)S(1)}, bf16[1,384,512]{2,1,0:T(8,128)(2,1)}, u32[]{:S(2)}) copy-start(bf16[1,384,512]{2,1,0:T(8,128)(2,1)} %param.21) | copy-start | bytes 1179652
  4.0 14.8 %copy-start.4 = (bf16[1,384,512]{2,1,0:T(8,128)(2,1)S(1)}, bf16[1,384,512]{2,1,0:T(8,128)(2,1)}, u32[]{:S(2)}) copy-start(bf16[1,384,512]{2,1,0:T(8,128)(2,1)} %param.20) | copy-start | bytes 1179652
  5.2 13.8 %copy-start.5 = (bf16[1,384,512]{2,1,0:T(8,128)(2,1)S(1)}, bf16[1,384,512]{2,1,0:T(8,128)(2,1)}, u32[]{:S(2)}) copy-start(bf16[1,384,512]{2,1,0:T(8,128)(2,1)} %param.19) | copy-start | bytes 1179652
  8.2 47.4 %all-to-all-start = ((bf16[16,16,2048]{2,1,0:T(8,128)(2,1)}), bf16[16,16,2048]{2,1,0:T(8,128)(2,1)S(1)}, u32[]{:S(2)}, u32[]{:S(2)}) async-start(bf16[16,16,2048]{2,1,0:T(8,128)(2,1)} %bitcast.13), calls=%async_computation | async-start | bytes 2097152 | tf_op jit(solution)/shard_map/all_to_all | solution.py:104
  19.4 35.3 %collective-permute-start = (bf16[384,3,512]{0,2,1:T(8,128)(2,1)S(1)}, bf16[384,3,512]{0,2,1:T(8,128)(2,1)}, u32[]{:S(2)}, u32[]{:S(2)}) collective-permute-start(bf16[384,3,512]{0,2,1:T(8,128)(2,1)S(1)} %pad_maximum_fusion), channel_id=1, source_target_pairs={{0,64},{64,128},{128,192},{192,256},{256,320},{320,384},{384,448},... | collective-permute-start | bytes 3538952 | tf_op jit(solution)/shard_map/ppermute | solution.py:48
  21.7 33.9 %collective-permute-start.1 = (bf16[384,3,512]{0,2,1:T(8,128)(2,1)S(1)}, bf16[384,3,512]{0,2,1:T(8,128)(2,1)}, u32[]{:S(2)}, u32[]{:S(2)}) collective-permute-start(bf16[384,3,512]{0,2,1:T(8,128)(2,1)S(1)} %pad_maximum_fusion), channel_id=1, source_target_pairs={{0,448},{64,0},{128,64},{192,128},{256,192},{320,256},{384,320},{4... | collective-permute-start | bytes 3538952 | tf_op jit(solution)/shard_map/ppermute | solution.py:49
  55.6 35.7 %collective-permute-start.2 = (bf16[384,3,512]{0,2,1:T(8,128)(2,1)}, bf16[384,3,512]{0,2,1:T(8,128)(2,1)}, u32[]{:S(2)}, u32[]{:S(2)}) collective-permute-start(bf16[384,3,512]{0,2,1:T(8,128)(2,1)} %collective-permute-done), channel_id=1, source_target_pairs={{0,64},{64,128},{128,192},{192,256},{256,320},{320,384},{384,448},... | collective-permute-start | bytes 3538952 | tf_op jit(solution)/shard_map/ppermute | solution.py:48
  57.5 33.8 %collective-permute-start.3 = (bf16[384,3,512]{0,2,1:T(8,128)(2,1)}, bf16[384,3,512]{0,2,1:T(8,128)(2,1)}, u32[]{:S(2)}, u32[]{:S(2)}) collective-permute-start(bf16[384,3,512]{0,2,1:T(8,128)(2,1)} %collective-permute-done.1), channel_id=1, source_target_pairs={{0,448},{64,0},{128,64},{192,128},{256,192},{320,256},{384,320},{4... | collective-permute-start | bytes 3538952 | tf_op jit(solution)/shard_map/ppermute | solution.py:49
  62.9 26.7 %collective-permute-start.4 = (bf16[256,2048]{1,0:T(8,128)(2,1)S(1)}, bf16[256,2048]{1,0:T(8,128)(2,1)}, u32[]{:S(2)}, u32[]{:S(2)}) collective-permute-start(bf16[256,2048]{1,0:T(8,128)(2,1)S(1)} %bitcast.163), channel_id=1, source_target_pairs={{0,1},{1,2},{2,3},{3,0},{4,5},{5,6},{6,7},{7,4},{8,9},{9,10},{10,1... | collective-permute-start | bytes 3145736 | tf_op jit(solution)/shard_map/ppermute | solution.py:48
  66.1 25.2 %collective-permute-start.5 = (bf16[256,2048]{1,0:T(8,128)(2,1)S(1)}, bf16[256,2048]{1,0:T(8,128)(2,1)S(1)}, u32[]{:S(2)}, u32[]{:S(2)}) collective-permute-start(bf16[256,2048]{1,0:T(8,128)(2,1)S(1)} %bitcast.164), channel_id=1, source_target_pairs={{0,3},{1,0},{2,1},{3,2},{4,7},{5,4},{6,5},{7,6},{8,11},{9,8},{10,9... | collective-permute-start | bytes 3145736 | tf_op jit(solution)/shard_map/ppermute | solution.py:49
  91.3 28.5 %collective-permute-start.6 = (bf16[384,3,512]{0,2,1:T(8,128)(2,1)}, bf16[384,3,512]{0,2,1:T(8,128)(2,1)S(1)}, u32[]{:S(2)}, u32[]{:S(2)}) collective-permute-start(bf16[384,3,512]{0,2,1:T(8,128)(2,1)} %collective-permute-done.2), channel_id=1, source_target_pairs={{0,64},{64,128},{128,192},{192,256},{256,320},{320,384},{384,448},... | collective-permute-start | bytes 3538952 | tf_op jit(solution)/shard_map/ppermute | solution.py:48
  93.2 27.6 %collective-permute-start.7 = (bf16[384,3,512]{0,2,1:T(8,128)(2,1)}, bf16[384,3,512]{0,2,1:T(8,128)(2,1)S(1)}, u32[]{:S(2)}, u32[]{:S(2)}) collective-permute-start(bf16[384,3,512]{0,2,1:T(8,128)(2,1)} %collective-permute-done.3), channel_id=1, source_target_pairs={{0,448},{64,0},{128,64},{192,128},{256,192},{320,256},{384,320},{4... | collective-permute-start | bytes 3538952 | tf_op jit(solution)/shard_map/ppermute | solution.py:49
  98.9 14.8 %collective-permute-start.8 = (bf16[128,2048]{1,0:T(8,128)(2,1)S(1)}, bf16[128,2048]{1,0:T(8,128)(2,1)S(1)}, u32[]{:S(2)}, u32[]{:S(2)}) collective-permute-start(bf16[128,2048]{1,0:T(8,128)(2,1)S(1)} %slice.133), channel_id=1, source_target_pairs={{0,1},{1,2},{2,3},{3,0},{4,5},{5,6},{6,7},{7,4},{8,9},{9,10},{10,1... | collective-permute-start | bytes 1572872 | tf_op jit(solution)/shard_map/ppermute | solution.py:52
  101.9 12.1 %collective-permute-start.9 = (bf16[128,2048]{1,0:T(8,128)(2,1)S(1)}, bf16[128,2048]{1,0:T(8,128)(2,1)S(1)}, u32[]{:S(2)}, u32[]{:S(2)}) collective-permute-start(bf16[128,2048]{1,0:T(8,128)(2,1)S(1)} %slice.134), channel_id=1, source_target_pairs={{0,3},{1,0},{2,1},{3,2},{4,7},{5,4},{6,5},{7,6},{8,11},{9,8},{10,9... | collective-permute-start | bytes 1572872 | tf_op jit(solution)/shard_map/ppermute | solution.py:53
  113.7 7.1 %copy-start.1 = (bf16[128,2048]{1,0:T(8,128)(2,1)}, bf16[128,2048]{1,0:T(8,128)(2,1)S(1)}, u32[]{:S(2)}) copy-start(bf16[128,2048]{1,0:T(8,128)(2,1)S(1)} %collective-permute-done.8) | copy-start | bytes 1572868
  114.1 6.8 %copy-start.2 = (bf16[128,2048]{1,0:T(8,128)(2,1)}, bf16[128,2048]{1,0:T(8,128)(2,1)S(1)}, u32[]{:S(2)}) copy-start(bf16[128,2048]{1,0:T(8,128)(2,1)S(1)} %collective-permute-done.9) | copy-start | bytes 1572868
  122.0 15.7 %collective-permute-start.10 = (bf16[192,3,512]{2,0,1:T(8,128)(2,1)}, bf16[192,3,512]{2,0,1:T(8,128)(2,1)}, u32[]{:S(2)}, u32[]{:S(2)}) collective-permute-start(bf16[192,3,512]{2,0,1:T(8,128)(2,1)} %copy.93), channel_id=1, source_target_pairs={{0,64},{64,128},{128,192},{192,256},{256,320},{320,384},{384,448},... | collective-permute-start | bytes 1769480 | tf_op jit(solution)/shard_map/ppermute | solution.py:52
  125.3 14.7 %collective-permute-start.11 = (bf16[192,3,512]{2,0,1:T(8,128)(2,1)}, bf16[192,3,512]{2,0,1:T(8,128)(2,1)S(1)}, u32[]{:S(2)}, u32[]{:S(2)}) collective-permute-start(bf16[192,3,512]{2,0,1:T(8,128)(2,1)} %copy.94), channel_id=1, source_target_pairs={{0,448},{64,0},{128,64},{192,128},{256,192},{320,256},{384,320},{4... | collective-permute-start | bytes 1769480 | tf_op jit(solution)/shard_map/ppermute | solution.py:53
  157.5 2.7 copy-start
  160.4 11.0 %collective-permute-start.14 = (bf16[128,2048]{0,1:T(8,128)(2,1)S(1)}, bf16[128,2048]{0,1:T(8,128)(2,1)}, u32[]{:S(2)}, u32[]{:S(2)}) collective-permute-start(bf16[128,2048]{0,1:T(8,128)(2,1)S(1)} %get-tuple-element.96), channel_id=1, source_target_pairs={{0,3},{1,0},{2,1},{3,2},{4,7},{5,4},{6,5},{7,6},{8,11},{9,8},{10,9... | collective-permute-start | bytes 1572872 | tf_op jit(solution)/shard_map/ppermute | solution.py:18
  164.7 14.4 %collective-permute-start.12 = (bf16[128,2048]{0,1:T(8,128)(2,1)S(1)}, bf16[128,2048]{0,1:T(8,128)(2,1)S(1)}, u32[]{:S(2)}, u32[]{:S(2)}) collective-permute-start(bf16[128,2048]{0,1:T(8,128)(2,1)S(1)} %get-tuple-element.95), channel_id=1, source_target_pairs={{0,1},{1,2},{2,3},{3,0},{4,5},{5,6},{6,7},{7,4},{8,9},{9,10},{10,1... | collective-permute-start | bytes 1572872 | tf_op jit(solution)/shard_map/ppermute | solution.py:17
  173.7 43.1 %collective-permute-start.15 = (bf16[256,2048]{0,1:T(8,128)(2,1)}, bf16[256,2048]{0,1:T(8,128)(2,1)}, u32[]{:S(2)}, u32[]{:S(2)}) collective-permute-start(bf16[256,2048]{0,1:T(8,128)(2,1)} %convert_element_type.216), channel_id=1, source_target_pairs={{0,3},{1,0},{2,1},{3,2},{4,7},{5,4},{6,5},{7,6},{8,11},{9,8},{10,9... | collective-permute-start | bytes 3145736 | tf_op jit(solution)/shard_map/ppermute | solution.py:28
  180.3 36.4 %collective-permute-start.13 = (bf16[256,2048]{0,1:T(8,128)(2,1)}, bf16[256,2048]{0,1:T(8,128)(2,1)}, u32[]{:S(2)}, u32[]{:S(2)}) collective-permute-start(bf16[256,2048]{0,1:T(8,128)(2,1)} %convert_element_type.210), channel_id=1, source_target_pairs={{0,1},{1,2},{2,3},{3,0},{4,5},{5,6},{6,7},{7,4},{8,9},{9,10},{10,1... | collective-permute-start | bytes 3145736 | tf_op jit(solution)/shard_map/ppermute | solution.py:27
  193.3 9.3 %collective-permute-start.16 = (bf16[192,512]{0,1:T(8,128)(2,1)S(1)}, bf16[192,512]{0,1:T(8,128)(2,1)S(1)}, u32[]{:S(2)}, u32[]{:S(2)}) collective-permute-start(bf16[192,512]{0,1:T(8,128)(2,1)S(1)} %get-tuple-element.101), channel_id=1, source_target_pairs={{0,64},{64,128},{128,192},{192,256},{256,320},{320,384},{384,448},... | collective-permute-start | bytes 589832 | tf_op jit(solution)/shard_map/ppermute | solution.py:17
  195.2 12.7 %collective-permute-start.20 = (bf16[192,512]{0,1:T(8,128)(2,1)}, bf16[192,512]{0,1:T(8,128)(2,1)}, u32[]{:S(2)}, u32[]{:S(2)}) collective-permute-start(bf16[192,512]{0,1:T(8,128)(2,1)} %get-tuple-element.102), channel_id=1, source_target_pairs={{0,448},{64,0},{128,64},{192,128},{256,192},{320,256},{384,320},{4... | collective-permute-start | bytes 589832 | tf_op jit(solution)/shard_map/ppermute | solution.py:18
  205.9 26.6 %collective-permute-start.17 = (bf16[384,512]{0,1:T(8,128)(2,1)}, bf16[384,512]{0,1:T(8,128)(2,1)S(1)}, u32[]{:S(2)}, u32[]{:S(2)}) collective-permute-start(bf16[384,512]{0,1:T(8,128)(2,1)} %scatter-add.16), channel_id=1, source_target_pairs={{0,64},{64,128},{128,192},{192,256},{256,320},{320,384},{384,448},... | collective-permute-start | bytes 1179656 | tf_op jit(solution)/shard_map/ppermute | solution.py:17
  212.2 23.4 %collective-permute-start.21 = (bf16[384,512]{0,1:T(8,128)(2,1)}, bf16[384,512]{0,1:T(8,128)(2,1)}, u32[]{:S(2)}, u32[]{:S(2)}) collective-permute-start(bf16[384,512]{0,1:T(8,128)(2,1)} %scatter-add.19), channel_id=1, source_target_pairs={{0,448},{64,0},{128,64},{192,128},{256,192},{320,256},{384,320},{4... | collective-permute-start | bytes 1179656 | tf_op jit(solution)/shard_map/ppermute | solution.py:18
  220.2 54.4 %all-to-all-start.1 = ((bf16[16,16,2048]{2,1,0:T(8,128)(2,1)}), bf16[16,16,2048]{2,1,0:T(8,128)(2,1)S(1)}, u32[]{:S(2)}, u32[]{:S(2)}) async-start(bf16[16,16,2048]{2,1,0:T(8,128)(2,1)} %bitcast.45), calls=%async_computation.1 | async-start | bytes 2097152 | tf_op jit(solution)/shard_map/all_to_all | solution.py:149
  233.6 13.8 %collective-permute-start.18 = (bf16[384,512]{0,1:T(8,128)(2,1)S(1)}, bf16[384,512]{0,1:T(8,128)(2,1)S(1)}, u32[]{:S(2)}, u32[]{:S(2)}) collective-permute-start(bf16[384,512]{0,1:T(8,128)(2,1)S(1)} %fusion.38), channel_id=1, source_target_pairs={{0,64},{64,128},{128,192},{192,256},{256,320},{320,384},{384,448},... | collective-permute-start | bytes 1179656 | tf_op jit(solution)/shard_map/ppermute | solution.py:17
  248.9 11.7 %collective-permute-start.22 = (bf16[384,512]{0,1:T(8,128)(2,1)S(1)}, bf16[384,512]{0,1:T(8,128)(2,1)S(1)}, u32[]{:S(2)}, u32[]{:S(2)}) collective-permute-start(bf16[384,512]{0,1:T(8,128)(2,1)S(1)} %get-tuple-element.100), channel_id=1, source_target_pairs={{0,448},{64,0},{128,64},{192,128},{256,192},{320,256},{384,320},{4... | collective-permute-start | bytes 1179656 | tf_op jit(solution)/shard_map/ppermute | solution.py:18
  250.8 14.3 %collective-permute-start.19 = (bf16[384,512]{0,1:T(8,128)(2,1)S(1)}, bf16[384,512]{0,1:T(8,128)(2,1)S(1)}, u32[]{:S(2)}, u32[]{:S(2)}) collective-permute-start(bf16[384,512]{0,1:T(8,128)(2,1)S(1)} %get-tuple-element.99), channel_id=1, source_target_pairs={{0,64},{64,128},{128,192},{192,256},{256,320},{320,384},{384,448},... | collective-permute-start | bytes 1179656 | tf_op jit(solution)/shard_map/ppermute | solution.py:27
  261.6 10.7 %collective-permute-start.23 = (bf16[384,512]{0,1:T(8,128)(2,1)S(1)}, bf16[384,512]{0,1:T(8,128)(2,1)S(1)}, u32[]{:S(2)}, u32[]{:S(2)}) collective-permute-start(bf16[384,512]{0,1:T(8,128)(2,1)S(1)} %fusion.37), channel_id=1, source_target_pairs={{0,448},{64,0},{128,64},{192,128},{256,192},{320,256},{384,320},{4... | collective-permute-start | bytes 1179656 | tf_op jit(solution)/shard_map/ppermute | solution.py:28
  (1 other events, 1.9 us)

commit v9 on v7

--- a/solution.py
+++ b/solution.py
@@ -2,31 +2,6 @@
 import jax.numpy as jnp
 from jax import lax
 from jax.sharding import PartitionSpec as P
-
-
-def ring_reduce_scatter(chunks, axis, n):
-    idx = lax.axis_index(axis)
-    fwd = [(i, (i + 1) % n) for i in range(n)]
-    bwd = [(i, (i - 1) % n) for i in range(n)]
-    pick = lambda at: lax.dynamic_index_in_dim(chunks, at % n, 0, keepdims=False).astype(jnp.float32)
-    half = n // 2
-    m = chunks.shape[1] // 2
-    to_right = pick(idx + half)[:m]
-    to_left = pick(idx - half)[m:]
-    for k in range(2, half + 1):
-        got_left = lax.ppermute(to_right.astype(chunks.dtype), axis, fwd).astype(jnp.float32)
-        got_right = lax.ppermute(to_left.astype(chunks.dtype), axis, bwd).astype(jnp.float32)
-        own_r = pick(idx + half - k + 1)
-        own_l = pick(idx - half + k - 1)
-        if k == 2:
-            to_right = own_r.at[:m].add(got_left)
-            to_left = own_l.at[m:].add(got_right)
-        else:
-            to_right = own_r + got_left
-            to_left = own_l + got_right
-    got_left = lax.ppermute(to_right.astype(chunks.dtype), axis, fwd).astype(jnp.float32)
-    got_right = lax.ppermute(to_left.astype(chunks.dtype), axis, bwd).astype(jnp.float32)
-    return pick(idx) + got_left + got_right
 
 
 class Ring:
@@ -59,13 +34,10 @@
             self.got.append((self.hop, jnp.concatenate([self.left, self.right], axis=0)))
 
     def result(self):
+        by_offset = dict([(0, self.piece)] + [(off % self.n, val) for off, val in self.got])
+        ordered = jnp.stack([by_offset[k] for k in range(self.n)], axis=self.along)
         idx = lax.axis_index(self.axis)
-        shape = list(self.piece.shape)
-        shape.insert(self.along, self.n)
-        out = jnp.zeros(shape, self.piece.dtype)
-        for offset, val in [(0, self.piece)] + self.got:
-            out = lax.dynamic_update_index_in_dim(out, val, (idx + offset) % self.n, self.along)
-        return out
+        return jnp.take(ordered, (jnp.arange(self.n) - idx) % self.n, axis=self.along)
 
 
 def lockstep(rings):
@@ -76,6 +48,31 @@
     for r, (left, right) in zip(live, held):
         r.left, r.right = left, right
         r.record()
+
+
+def ring_reduce_scatter(chunks, axis, n):
+    idx = lax.axis_index(axis)
+    fwd = [(i, (i + 1) % n) for i in range(n)]
+    bwd = [(i, (i - 1) % n) for i in range(n)]
+    pick = lambda at: lax.dynamic_index_in_dim(chunks, at % n, 0, keepdims=False).astype(jnp.float32)
+    half = n // 2
+    m = chunks.shape[1] // 2
+    to_right = pick(idx + half)[:m]
+    to_left = pick(idx - half)[m:]
+    for k in range(2, half + 1):
+        got_left = lax.ppermute(to_right.astype(chunks.dtype), axis, fwd).astype(jnp.float32)
+        got_right = lax.ppermute(to_left.astype(chunks.dtype), axis, bwd).astype(jnp.float32)
+        own_r = pick(idx + half - k + 1)
+        own_l = pick(idx - half + k - 1)
+        if k == 2:
+            to_right = own_r.at[:m].add(got_left)
+            to_left = own_l.at[m:].add(got_right)
+        else:
+            to_right = own_r + got_left
+            to_left = own_l + got_right
+    got_left = lax.ppermute(to_right.astype(chunks.dtype), axis, fwd).astype(jnp.float32)
+    got_right = lax.ppermute(to_left.astype(chunks.dtype), axis, bwd).astype(jnp.float32)
+    return pick(idx) + got_left + got_right
 
 
 def on_device(tokens, cotangent, route_weights, expert_ids, w_gate, w_up, w_down):
@@ -104,14 +101,14 @@
     recv = lax.all_to_all(send, "expert", split_axis=0, concat_axis=0, tiled=True)
 
     gate_full = lax.all_gather(w_gate[0], "dp", axis=1, tiled=True)
-    weights = Ring(jnp.stack([w_up[0], w_down[0]], axis=1), "dp", lax.axis_size("dp"), along=2)
-    lockstep([weights])
-    weights.left, weights.right, recv = lax.optimization_barrier((weights.left, weights.right, recv))
+    up_full = lax.all_gather(w_up[0], "dp", axis=1, tiled=True)
+    downs = Ring(w_down[0], "dp", lax.axis_size("dp"), along=1)
+    lockstep([downs])
+    downs.left, downs.right, recv = lax.optimization_barrier((downs.left, downs.right, recv))
     rows = Ring(recv.reshape(slot_rows, 2 * part), "etp", shares)
-    while weights.active() or rows.active():
-        lockstep([weights, rows])
-    pair = weights.result()
-    up_full, down_full = (pair[:, i].reshape(w_up.shape[1], model_width) for i in range(2))
+    while downs.active() or rows.active():
+        lockstep([downs, rows])
+    down_full = downs.result().reshape(w_down.shape[1], model_width)
     gathered = rows.result()
     rows4 = gathered[:, :, :part]
     grads4 = gathered[:, :, part:]

time: 262 us -> 280 us (1.069)
  other arithmetic: 10.5 us -> 27.1 us
  waiting for transfers between devices: 108 us -> 95.8 us
  starting transfers between devices: 76.8 us -> 82.8 us
  local copies, waits for them, and re-layouts: 34.3 us -> 38.4 us
  matrix products: 16.6 us -> 20 us
    dynamic_update_slice x9 -> x0, local copies, waits for them, and re-layouts: 10.9 us -> none  [result(): lax.dynamic_update_index_in_dim(out, val, (idx + offset) % self.n, self.a...]
    gather x0 -> x3, local copies, waits for them, and re-layouts: none -> 10.6 us  [result(): jnp.take(ordered, (jnp.arange(self.n) - idx) % self.n, axis=self.along)]
    unnamed x36 -> x61, local copies, waits for them, and re-layouts: 7.01 us -> 16.3 us
    ppermute x2, waiting for transfers between devices: 8.12 us -> 0.01 us  [step(): self.left = lax.ppermute(self.left[:m], self.axis, fwd)]
    select_n x0 -> x4, other arithmetic: none -> 7.19 us  [result(): jnp.take(ordered, (jnp.arange(self.n) - idx) % self.n, axis=self.along)]
    ppermute x4, starting transfers between devices: 22 us -> 28.6 us  [step(): self.right = lax.ppermute(self.right, self.axis, bwd)]
    ppermute x2, waiting for transfers between devices: 4.84 us -> 0.01 us  [step(): self.right = lax.ppermute(self.right[m:], self.axis, bwd)]
    broadcast_in_dim x2 -> x1, local copies, waits for them, and re-layouts: 3.97 us -> 0.07 us  [result(): jnp.take(ordered, (jnp.arange(self.n) - idx) % self.n, axis=self.along)]
  transfers between devices with their start and end apart: 20 -> 21, of which waited for: 11 -> 13; matrix products, arithmetic and copies ran while one was open for 14% -> 23% of each run, Pallas kernels for 0% -> 0%
where the time goes in v9:
time: 280 us; the launch traced here: 278 us
  waiting for transfers between devices  95.8 us (34%)
  starting transfers between devices  82.8 us (30%)
  local copies, waits for them, and re-layouts  38.4 us (14%)
  other arithmetic  27.1 us (10%)
  matrix products  20 us (7%)
  between operations  14.3 us (5%)
    ppermute x4, waiting for transfers between devices, step(): self.left = lax.ppermute(self.left, self.axis, fwd)  33.6 us
    ppermute x4, starting transfers between devices, step(): self.right = lax.ppermute(self.right, self.axis, bwd)  28.6 us
    all_to_all x1, waiting for transfers between devices, on_device(): lax.all_to_all(slot_out.reshape(experts, capacity, 2 * part), 'expert', s...  28 us
    ppermute x2, waiting for transfers between devices, ring_reduce_scatter(): lax.ppermute(to_left.astype(chunks.dtype), axis, bwd).astype(jnp.float32)  22.4 us
    unnamed x61, local copies, waits for them, and re-layouts  16.3 us
    gather x3, local copies, waits for them, and re-layouts, result(): jnp.take(ordered, (jnp.arange(self.n) - idx) % self.n, axis=self.along)  10.6 us
    ppermute x4, starting transfers between devices, step(): self.left = lax.ppermute(self.left, self.axis, fwd)  10.5 us
    all_to_all x1, starting transfers between devices, on_device(): lax.all_to_all(send, 'expert', split_axis=0, concat_axis=0, tiled=True)  10.3 us
  transfers between devices with their start and end apart: 21, of which 13 were waited for; matrix products, arithmetic and copies ran while one was open for 23% of the time, Pallas kernels for 0%

profile of v9, /device:TPU:1, one launch (start us, length us, event | category | flops | bytes accessed | tf_op | source)
XLA Modules:
  0.0 278.3 jit_solution(7598670439843237072)
XLA Ops:
  13.9 2.8 %scatter_custom_fusion = bf16[256,2048]{1,0:T(8,128)(2,1)} fusion(s32[192]{0:T(256)S(1)} %bitcast.126, bf16[192,1024]{1,0:T(8,128)(2,1)S(1)} %fusion.34, bf16[]{:T(256)} %constant.222, bf16[192,1024]{1,0:T(8,128)(2,1)S(1)} %broadcast_bitcast_fusion, bf16[]{:T(256)} %constant.185.clone.1), kind=kCustom, calls=%fused_computation.51 | custom fusion | flops 1572864 | bytes 1835012 | tf_op jit(solution)/shard_map/scatter | solution.py:100
  16.7 10.3 %all-to-all-start = ((bf16[16,16,2048]{2,1,0:T(8,128)(2,1)}), bf16[16,16,2048]{2,1,0:T(8,128)(2,1)S(1)}, u32[]{:S(2)}, u32[]{:S(2)}) async-start(bf16[16,16,2048]{2,1,0:T(8,128)(2,1)} %bitcast.8), calls=%async_computation | async-start | bytes 2097152 | tf_op jit(solution)/shard_map/all_to_all | solution.py:101
  27.1 2.3 collective-permute-start
  29.4 8.6 %collective-permute-start.1 = (bf16[384,512]{1,0:T(8,128)(2,1)S(1)}, bf16[384,512]{1,0:T(8,128)(2,1)S(1)}, u32[]{:S(2)}, u32[]{:S(2)}) collective-permute-start(bf16[384,512]{1,0:T(8,128)(2,1)S(1)} %bitcast.124), channel_id=1, source_target_pairs={{0,448},{64,0},{128,64},{192,128},{256,192},{320,256},{384,320},{4... | collective-permute-start | bytes 1179656 | tf_op jit(solution)/shard_map/ppermute | solution.py:24
  39.0 15.1 %collective-permute-done = bf16[384,512]{1,0:T(8,128)(2,1)S(1)} collective-permute-done((bf16[384,512]{1,0:T(8,128)(2,1)S(1)}, bf16[384,512]{1,0:T(8,128)(2,1)S(1)}, u32[]{:S(2)}, u32[]{:S(2)}) %collective-permute-start) | collective-permute-done | bytes 393248 | tf_op jit(solution)/shard_map/ppermute | solution.py:23
  55.5 3.1 %collective-permute-start.4 = (bf16[256,2048]{1,0:T(8,128)(2,1)S(1)}, bf16[256,2048]{1,0:T(8,128)(2,1)S(1)}, u32[]{:S(2)}, u32[]{:S(2)}) collective-permute-start(bf16[256,2048]{1,0:T(8,128)(2,1)S(1)} %bitcast.114), channel_id=1, source_target_pairs={{0,1},{1,2},{2,3},{3,0},{4,5},{5,6},{6,7},{7,4},{8,9},{9,10},{10,1... | collective-permute-start | bytes 3145736 | tf_op jit(solution)/shard_map/ppermute | solution.py:23
  58.6 3.4 %collective-permute-start.5 = (bf16[256,2048]{1,0:T(8,128)(2,1)S(1)}, bf16[256,2048]{1,0:T(8,128)(2,1)S(1)}, u32[]{:S(2)}, u32[]{:S(2)}) collective-permute-start(bf16[256,2048]{1,0:T(8,128)(2,1)S(1)} %bitcast.115), channel_id=1, source_target_pairs={{0,3},{1,0},{2,1},{3,2},{4,7},{5,4},{6,5},{7,6},{8,11},{9,8},{10,9... | collective-permute-start | bytes 3145736 | tf_op jit(solution)/shard_map/ppermute | solution.py:24
  64.5 8.4 %collective-permute-start.3 = (bf16[384,512]{1,0:T(8,128)(2,1)}, bf16[384,512]{1,0:T(8,128)(2,1)S(1)}, u32[]{:S(2)}, u32[]{:S(2)}) collective-permute-start(bf16[384,512]{1,0:T(8,128)(2,1)} %copy-done.15), channel_id=1, source_target_pairs={{0,448},{64,0},{128,64},{192,128},{256,192},{320,256},{384,320},{4... | collective-permute-start | bytes 1179656 | tf_op jit(solution)/shard_map/ppermute | solution.py:24
  74.4 6.2 %collective-permute-done.2 = bf16[384,512]{1,0:T(8,128)(2,1)S(1)} collective-permute-done((bf16[384,512]{1,0:T(8,128)(2,1)}, bf16[384,512]{1,0:T(8,128)(2,1)S(1)}, u32[]{:S(2)}, u32[]{:S(2)}) %collective-permute-start.2) | collective-permute-done | bytes 393248 | tf_op jit(solution)/shard_map/ppermute | solution.py:23
  84.7 3.1 %collective-permute-start.8 = (bf16[128,2048]{1,0:T(8,128)(2,1)}, bf16[128,2048]{1,0:T(8,128)(2,1)}, u32[]{:S(2)}, u32[]{:S(2)}) collective-permute-start(bf16[128,2048]{1,0:T(8,128)(2,1)} %slice.74), channel_id=1, source_target_pairs={{0,1},{1,2},{2,3},{3,0},{4,5},{5,6},{6,7},{7,4},{8,9},{9,10},{10,1... | collective-permute-start | bytes 1572872 | tf_op jit(solution)/shard_map/ppermute | solution.py:27
  88.7 3.4 %collective-permute-start.9 = (bf16[128,2048]{1,0:T(8,128)(2,1)}, bf16[128,2048]{1,0:T(8,128)(2,1)}, u32[]{:S(2)}, u32[]{:S(2)}) collective-permute-start(bf16[128,2048]{1,0:T(8,128)(2,1)} %slice.75), channel_id=1, source_target_pairs={{0,3},{1,0},{2,1},{3,2},{4,7},{5,4},{6,5},{7,6},{8,11},{9,8},{10,9... | collective-permute-start | bytes 1572872 | tf_op jit(solution)/shard_map/ppermute | solution.py:28
  92.6 3.2 %collective-permute-start.6 = (bf16[384,512]{1,0:T(8,128)(2,1)}, bf16[384,512]{1,0:T(8,128)(2,1)S(1)}, u32[]{:S(2)}, u32[]{:S(2)}) collective-permute-start(bf16[384,512]{1,0:T(8,128)(2,1)} %copy-done.13), channel_id=1, source_target_pairs={{0,64},{64,128},{128,192},{192,256},{256,320},{320,384},{384,448},... | collective-permute-start | bytes 1179656 | tf_op jit(solution)/shard_map/ppermute | solution.py:23
  95.8 8.2 %collective-permute-start.7 = (bf16[384,512]{1,0:T(8,128)(2,1)}, bf16[384,512]{1,0:T(8,128)(2,1)S(1)}, u32[]{:S(2)}, u32[]{:S(2)}) collective-permute-start(bf16[384,512]{1,0:T(8,128)(2,1)} %copy-done.16), channel_id=1, source_target_pairs={{0,448},{64,0},{128,64},{192,128},{256,192},{320,256},{384,320},{4... | collective-permute-start | bytes 1179656 | tf_op jit(solution)/shard_map/ppermute | solution.py:24
  107.6 12.1 %collective-permute-done.6 = bf16[384,512]{1,0:T(8,128)(2,1)S(1)} collective-permute-done((bf16[384,512]{1,0:T(8,128)(2,1)}, bf16[384,512]{1,0:T(8,128)(2,1)S(1)}, u32[]{:S(2)}, u32[]{:S(2)}) %collective-permute-start.6) | collective-permute-done | bytes 393248 | tf_op jit(solution)/shard_map/ppermute | solution.py:23
  124.5 5.5 %collective-permute-start.11 = (bf16[192,512]{1,0:T(8,128)(2,1)}, bf16[192,512]{1,0:T(8,128)(2,1)}, u32[]{:S(2)}, u32[]{:S(2)}) collective-permute-start(bf16[192,512]{1,0:T(8,128)(2,1)} %slice.77), channel_id=1, source_target_pairs={{0,448},{64,0},{128,64},{192,128},{256,192},{320,256},{384,320},{4... | collective-permute-start | bytes 589832 | tf_op jit(solution)/shard_map/ppermute | solution.py:28
  133.6 5.2 %gather_fusion.1 = bf16[4,256,2048]{2,1,0:T(8,128)(2,1)} fusion(bf16[4,256,2048]{2,1,0:T(8,128)(2,1)} %pad_maximum_fusion, s32[1024]{0:T(1024)} %get-tuple-element.76), kind=kCustom, calls=%fused_computation.1 | custom fusion | bytes 8388624 | tf_op jit(solution)/shard_map/jit(_take)/gather | solution.py:40
  138.7 4.8 %broadcast_select_fusion = bf16[4,256,2048]{2,1,0:T(8,128)(2,1)} fusion(bf16[4,256,2048]{2,1,0:T(8,128)(2,1)} %gather_fusion.1, pred[4]{0:T(512)(128)(4,1)S(1)} %copy-done.20), kind=kLoop, calls=%fused_computation.17 | loop fusion | flops 2097152 | bytes 8388612 | tf_op jit(solution)/shard_map/jit(_take)/select_n | solution.py:40
  148.5 2.6 gather_fusion
  151.1 2.8 %copy.66 = bf16[384,8,512]{0,2,1:T(8,128)(2,1)} copy(bf16[384,8,512]{2,0,1:T(8,128)(2,1)S(1)} %bitcast.112) | data formatting | bytes 6291456 | tf_op jit(solution)/shard_map/jit(_take)/gather | solution.py:40
  154.0 2.4 bitcast_select_fusion
  159.4 3.8 %fusion.13 = f32[256,384]{1,0:T(8,128)S(1)} fusion(bf16[384,4,1024]{0,2,1:T(8,128)(2,1)} %bitcast.119, bf16[4,256,2048]{2,1,0:T(8,128)(2,1)} %broadcast_select_fusion), kind=kOutput, calls=%fused_computation.33 | convolution fusion | flops 805306368 | bytes 5636096 | tf_op jit(solution)/shard_map/jsc,fjc->sf/dot_general | solution.py:122
  163.2 4.7 %multiply_convert_fusion.1 = (bf16[256,384]{1,0:T(8,128)(2,1)S(1)}, f32[256,384]{1,0:T(8,128)}) fusion(f32[256,384]{1,0:T(8,128)S(1)} %fusion.16, f32[256,384]{1,0:T(8,128)S(1)} %fusion.13, bf16[384,4,1024]{0,2,1:T(8,128)(2,1)} %bitcast.117, bf16[4,256,2048]{2,1,0:T(8,128)(2,1)} %broadcast_select_fusion), kind=kOutput, calls=%fused_computation.74 | convolution fusion | flops 806289408 | bytes 6619136 | tf_op jit(solution)/shard_map/jsc,fjc->sf/dot_general | solution.py:121
  167.9 3.3 %fusion.47 = f32[256,4,1024]{0,2,1:T(8,128)} fusion(bf16[384,4,1024]{0,2,1:T(8,128)(2,1)S(1)} %bitcast.118, bf16[256,384]{1,0:T(8,128)(2,1)S(1)} %get-tuple-element.72), kind=kOutput, calls=%fused_computation.81 | convolution fusion | flops 805306368 | bytes 7536640 | tf_op jit(solution)/shard_map/sf,fjc->jsc/dot_general | solution.py:135
  172.2 2.8 %copy.78 = bf16[384,4,1024]{0,2,1:T(8,128)(2,1)} copy(bf16[384,4,1024]{2,0,1:T(8,128)(2,1)S(1)} %convolution_convert_fusion) | data formatting | bytes 6291456 | tf_op jit(solution)/shard_map/convert_element_type | solution.py:140
  176.0 4.6 %fusion.4 = bf16[4,256,1024]{1,2,0:T(8,128)(2,1)S(1)} fusion(f32[256,4,1024]{0,2,1:T(8,128)} %fusion.47, bf16[384,4,1024]{0,2,1:T(8,128)(2,1)} %bitcast.120, f32[256,384]{1,0:T(8,128)S(1)} %fusion.16, f32[256,384]{1,0:T(8,128)S(1)} %copy-done.8), kind=kOutput, calls=%fused_computation.26 | convolution fusion | flops 807993344 | bytes 10223616 | tf_op jit(solution)/shard_map/sf,fjc->jsc/dot_general | solution.py:136
  184.3 3.2 %collective-permute-start.14 = (bf16[128,2048]{0,1:T(8,128)(2,1)S(1)}, bf16[128,2048]{0,1:T(8,128)(2,1)S(1)}, u32[]{:S(2)}, u32[]{:S(2)}) collective-permute-start(bf16[128,2048]{0,1:T(8,128)(2,1)S(1)} %get-tuple-element.69), channel_id=1, source_target_pairs={{0,3},{1,0},{2,1},{3,2},{4,7},{5,4},{6,5},{7,6},{8,11},{9,8},{10,9... | collective-permute-start | bytes 1572872 | tf_op jit(solution)/shard_map/ppermute | solution.py:64
  191.6 6.0 %collective-permute-done.14 = bf16[128,2048]{0,1:T(8,128)(2,1)S(1)} collective-permute-done((bf16[128,2048]{0,1:T(8,128)(2,1)S(1)}, bf16[128,2048]{0,1:T(8,128)(2,1)S(1)}, u32[]{:S(2)}, u32[]{:S(2)}) %collective-permute-start.14) | collective-permute-done | bytes 524320 | tf_op jit(solution)/shard_map/ppermute | solution.py:64
  197.9 4.1 %collective-permute-start.15 = (bf16[256,2048]{0,1:T(8,128)(2,1)S(1)}, bf16[256,2048]{0,1:T(8,128)(2,1)}, u32[]{:S(2)}, u32[]{:S(2)}) collective-permute-start(bf16[256,2048]{0,1:T(8,128)(2,1)S(1)} %convert_element_type.121), channel_id=1, source_target_pairs={{0,3},{1,0},{2,1},{3,2},{4,7},{5,4},{6,5},{7,6},{8,11},{9,8},{10,9... | collective-permute-start | bytes 3145736 | tf_op jit(solution)/shard_map/ppermute | solution.py:74
  205.2 16.4 %collective-permute-done.15 = bf16[256,2048]{0,1:T(8,128)(2,1)} collective-permute-done((bf16[256,2048]{0,1:T(8,128)(2,1)S(1)}, bf16[256,2048]{0,1:T(8,128)(2,1)}, u32[]{:S(2)}, u32[]{:S(2)}) %collective-permute-start.15) | collective-permute-done | bytes 1048608 | tf_op jit(solution)/shard_map/ppermute | solution.py:74
  221.6 6.2 %collective-permute-done.13 = bf16[256,2048]{0,1:T(8,128)(2,1)} collective-permute-done((bf16[256,2048]{0,1:T(8,128)(2,1)}, bf16[256,2048]{0,1:T(8,128)(2,1)}, u32[]{:S(2)}, u32[]{:S(2)}) %collective-permute-start.13) | collective-permute-done | bytes 1048608 | tf_op jit(solution)/shard_map/ppermute | solution.py:73
  231.4 7.8 %all-to-all-start.1 = ((bf16[16,16,2048]{2,1,0:T(8,128)(2,1)}), bf16[16,16,2048]{2,1,0:T(8,128)(2,1)S(1)}, u32[]{:S(2)}, u32[]{:S(2)}) async-start(bf16[16,16,2048]{2,1,0:T(8,128)(2,1)} %bitcast.41), calls=%async_computation.1 | async-start | bytes 2097152 | tf_op jit(solution)/shard_map/all_to_all | solution.py:146
  239.2 28.0 %all-to-all-done.1 = bf16[16,16,2048]{2,1,0:T(8,128)(2,1)S(1)} async-done(((bf16[16,16,2048]{2,1,0:T(8,128)(2,1)}), bf16[16,16,2048]{2,1,0:T(8,128)(2,1)S(1)}, u32[]{:S(2)}, u32[]{:S(2)}) %all-to-all-start.1) | async-done | bytes 1048608 | tf_op jit(solution)/shard_map/all_to_all | solution.py:146
  (130 shorter events, 59.6 us)
Async XLA Ops:
  7.2 152.2 %all-gather.7.cloned.1.call-start = ((), (), s32[]{:S(2)}) async-start(), calls=%async_computation.5 | async-start | bytes 3538944 | tf_op jit(solution)/shard_map/all_gather | solution.py:104
  12.5 14.6 %copy-start.10 = (bf16[1,384,512]{2,1,0:T(8,128)(2,1)S(1)}, bf16[1,384,512]{2,1,0:T(8,128)(2,1)}, u32[]{:S(2)}) copy-start(bf16[1,384,512]{2,1,0:T(8,128)(2,1)} %param.17) | copy-start | bytes 1179652
  12.5 25.5 %copy-start.9 = (bf16[1,384,512]{2,1,0:T(8,128)(2,1)S(1)}, bf16[1,384,512]{2,1,0:T(8,128)(2,1)}, u32[]{:S(2)}) copy-start(bf16[1,384,512]{2,1,0:T(8,128)(2,1)} %param.15) | copy-start | bytes 1179652
  16.7 38.3 %all-to-all-start = ((bf16[16,16,2048]{2,1,0:T(8,128)(2,1)}), bf16[16,16,2048]{2,1,0:T(8,128)(2,1)S(1)}, u32[]{:S(2)}, u32[]{:S(2)}) async-start(bf16[16,16,2048]{2,1,0:T(8,128)(2,1)} %bitcast.8), calls=%async_computation | async-start | bytes 2097152 | tf_op jit(solution)/shard_map/all_to_all | solution.py:101
  27.0 136.1 %all-gather.5.cloned.1.call-start = ((), (), s32[]{:S(2)}) async-start(), calls=%async_computation.4 | async-start | bytes 3538944 | tf_op jit(solution)/shard_map/all_gather | solution.py:103
  27.1 27.0 %collective-permute-start = (bf16[384,512]{1,0:T(8,128)(2,1)S(1)}, bf16[384,512]{1,0:T(8,128)(2,1)S(1)}, u32[]{:S(2)}, u32[]{:S(2)}) collective-permute-start(bf16[384,512]{1,0:T(8,128)(2,1)S(1)} %bitcast.123), channel_id=1, source_target_pairs={{0,64},{64,128},{128,192},{192,256},{256,320},{320,384},{384,448},... | collective-permute-start | bytes 1179656 | tf_op jit(solution)/shard_map/ppermute | solution.py:23
  29.4 25.3 %collective-permute-start.1 = (bf16[384,512]{1,0:T(8,128)(2,1)S(1)}, bf16[384,512]{1,0:T(8,128)(2,1)S(1)}, u32[]{:S(2)}, u32[]{:S(2)}) collective-permute-start(bf16[384,512]{1,0:T(8,128)(2,1)S(1)} %bitcast.124), channel_id=1, source_target_pairs={{0,448},{64,0},{128,64},{192,128},{256,192},{320,256},{384,320},{4... | collective-permute-start | bytes 1179656 | tf_op jit(solution)/shard_map/ppermute | solution.py:24
  39.0 230.6 %reduce-scatter.2.cloned.1.call-start = ((), (), s32[]{:S(2)}) async-start(), calls=%async_computation.3 | async-start | bytes 3538944 | tf_op jit(solution)/shard_map/reduce_scatter | solution.py:141
  55.5 26.8 %collective-permute-start.4 = (bf16[256,2048]{1,0:T(8,128)(2,1)S(1)}, bf16[256,2048]{1,0:T(8,128)(2,1)S(1)}, u32[]{:S(2)}, u32[]{:S(2)}) collective-permute-start(bf16[256,2048]{1,0:T(8,128)(2,1)S(1)} %bitcast.114), channel_id=1, source_target_pairs={{0,1},{1,2},{2,3},{3,0},{4,5},{5,6},{6,7},{7,4},{8,9},{9,10},{10,1... | collective-permute-start | bytes 3145736 | tf_op jit(solution)/shard_map/ppermute | solution.py:23
  58.6 25.3 %collective-permute-start.5 = (bf16[256,2048]{1,0:T(8,128)(2,1)S(1)}, bf16[256,2048]{1,0:T(8,128)(2,1)S(1)}, u32[]{:S(2)}, u32[]{:S(2)}) collective-permute-start(bf16[256,2048]{1,0:T(8,128)(2,1)S(1)} %bitcast.115), channel_id=1, source_target_pairs={{0,3},{1,0},{2,1},{3,2},{4,7},{5,4},{6,5},{7,6},{8,11},{9,8},{10,9... | collective-permute-start | bytes 3145736 | tf_op jit(solution)/shard_map/ppermute | solution.py:24
  62.6 18.0 %collective-permute-start.2 = (bf16[384,512]{1,0:T(8,128)(2,1)}, bf16[384,512]{1,0:T(8,128)(2,1)S(1)}, u32[]{:S(2)}, u32[]{:S(2)}) collective-permute-start(bf16[384,512]{1,0:T(8,128)(2,1)} %copy-done.11), channel_id=1, source_target_pairs={{0,64},{64,128},{128,192},{192,256},{256,320},{320,384},{384,448},... | collective-permute-start | bytes 1179656 | tf_op jit(solution)/shard_map/ppermute | solution.py:23
  64.5 17.5 %collective-permute-start.3 = (bf16[384,512]{1,0:T(8,128)(2,1)}, bf16[384,512]{1,0:T(8,128)(2,1)S(1)}, u32[]{:S(2)}, u32[]{:S(2)}) collective-permute-start(bf16[384,512]{1,0:T(8,128)(2,1)} %copy-done.15), channel_id=1, source_target_pairs={{0,448},{64,0},{128,64},{192,128},{256,192},{320,256},{384,320},{4... | collective-permute-start | bytes 1179656 | tf_op jit(solution)/shard_map/ppermute | solution.py:24
  84.7 36.4 %collective-permute-start.8 = (bf16[128,2048]{1,0:T(8,128)(2,1)}, bf16[128,2048]{1,0:T(8,128)(2,1)}, u32[]{:S(2)}, u32[]{:S(2)}) collective-permute-start(bf16[128,2048]{1,0:T(8,128)(2,1)} %slice.74), channel_id=1, source_target_pairs={{0,1},{1,2},{2,3},{3,0},{4,5},{5,6},{6,7},{7,4},{8,9},{9,10},{10,1... | collective-permute-start | bytes 1572872 | tf_op jit(solution)/shard_map/ppermute | solution.py:27
  88.7 32.4 %collective-permute-start.9 = (bf16[128,2048]{1,0:T(8,128)(2,1)}, bf16[128,2048]{1,0:T(8,128)(2,1)}, u32[]{:S(2)}, u32[]{:S(2)}) collective-permute-start(bf16[128,2048]{1,0:T(8,128)(2,1)} %slice.75), channel_id=1, source_target_pairs={{0,3},{1,0},{2,1},{3,2},{4,7},{5,4},{6,5},{7,6},{8,11},{9,8},{10,9... | collective-permute-start | bytes 1572872 | tf_op jit(solution)/shard_map/ppermute | solution.py:28
  92.6 27.1 %collective-permute-start.6 = (bf16[384,512]{1,0:T(8,128)(2,1)}, bf16[384,512]{1,0:T(8,128)(2,1)S(1)}, u32[]{:S(2)}, u32[]{:S(2)}) collective-permute-start(bf16[384,512]{1,0:T(8,128)(2,1)} %copy-done.13), channel_id=1, source_target_pairs={{0,64},{64,128},{128,192},{192,256},{256,320},{320,384},{384,448},... | collective-permute-start | bytes 1179656 | tf_op jit(solution)/shard_map/ppermute | solution.py:23
  95.8 25.3 %collective-permute-start.7 = (bf16[384,512]{1,0:T(8,128)(2,1)}, bf16[384,512]{1,0:T(8,128)(2,1)S(1)}, u32[]{:S(2)}, u32[]{:S(2)}) collective-permute-start(bf16[384,512]{1,0:T(8,128)(2,1)} %copy-done.16), channel_id=1, source_target_pairs={{0,448},{64,0},{128,64},{192,128},{256,192},{320,256},{384,320},{4... | collective-permute-start | bytes 1179656 | tf_op jit(solution)/shard_map/ppermute | solution.py:24
  121.9 22.4 %collective-permute-start.10 = (bf16[192,512]{1,0:T(8,128)(2,1)}, bf16[192,512]{1,0:T(8,128)(2,1)}, u32[]{:S(2)}, u32[]{:S(2)}) collective-permute-start(bf16[192,512]{1,0:T(8,128)(2,1)} %slice.76), channel_id=1, source_target_pairs={{0,64},{64,128},{128,192},{192,256},{256,320},{320,384},{384,448},... | collective-permute-start | bytes 589832 | tf_op jit(solution)/shard_map/ppermute | solution.py:27
  124.5 19.8 %collective-permute-start.11 = (bf16[192,512]{1,0:T(8,128)(2,1)}, bf16[192,512]{1,0:T(8,128)(2,1)}, u32[]{:S(2)}, u32[]{:S(2)}) collective-permute-start(bf16[192,512]{1,0:T(8,128)(2,1)} %slice.77), channel_id=1, source_target_pairs={{0,448},{64,0},{128,64},{192,128},{256,192},{320,256},{384,320},{4... | collective-permute-start | bytes 589832 | tf_op jit(solution)/shard_map/ppermute | solution.py:28
  133.6 5.2 %copy-start.20 = (pred[4]{0:T(512)(128)(4,1)S(1)}, pred[4]{0:T(512)(128)(4,1)}, u32[]{:S(2)}) copy-start(pred[4]{0:T(512)(128)(4,1)} %compare_and_fusion) | copy-start | bytes 16
  138.7 4.8 %copy-start.7 = (bf16[384,512]{1,0:T(8,128)(2,1)S(1)}, bf16[384,512]{1,0:T(8,128)(2,1)}, u32[]{:S(2)}) copy-start(bf16[384,512]{1,0:T(8,128)(2,1)} %copy-done.6) | copy-start | bytes 1179652
  138.7 8.1 %copy-start.14 = (bf16[384,512]{1,0:T(8,128)(2,1)S(1)}, bf16[384,512]{1,0:T(8,128)(2,1)}, u32[]{:S(2)}) copy-start(bf16[384,512]{1,0:T(8,128)(2,1)} %copy-done.13) | copy-start | bytes 1179652
  143.5 4.2 %copy-start.12 = (bf16[384,512]{1,0:T(8,128)(2,1)S(1)}, bf16[384,512]{1,0:T(8,128)(2,1)}, u32[]{:S(2)}) copy-start(bf16[384,512]{1,0:T(8,128)(2,1)} %copy-done.11) | copy-start | bytes 1179652
  163.2 4.7 %copy-start.22 = (f32[256,384]{1,0:T(8,128)}, f32[256,384]{1,0:T(8,128)S(1)}, u32[]{:S(2)}) copy-start(f32[256,384]{1,0:T(8,128)S(1)} %fusion.13) | copy-start | bytes 1179652
  163.2 4.7 %copy-start.3 = (bf16[1,384,4096]{1,2,0:T(8,128)(2,1)S(1)}, bf16[1,384,4096]{1,2,0:T(8,128)(2,1)}, u32[]{:S(2)}) copy-start(bf16[1,384,4096]{1,2,0:T(8,128)(2,1)} %all-gather.5.cloned.1.call-done) | copy-start | bytes 9437188
  176.0 4.6 %copy-start.5 = (bf16[384,4,1024]{0,2,1:T(8,128)(2,1)S(1)}, bf16[384,4,1024]{0,2,1:T(8,128)(2,1)}, u32[]{:S(2)}) copy-start(bf16[384,4,1024]{0,2,1:T(8,128)(2,1)} %copy-done.4) | copy-start | bytes 9437188
  176.0 4.6 %copy-start.23 = (f32[256,384]{1,0:T(8,128)S(1)}, f32[256,384]{1,0:T(8,128)}, u32[]{:S(2)}) copy-start(f32[256,384]{1,0:T(8,128)} %copy-done.22) | copy-start | bytes 1179652
  184.3 13.4 %collective-permute-start.14 = (bf16[128,2048]{0,1:T(8,128)(2,1)S(1)}, bf16[128,2048]{0,1:T(8,128)(2,1)S(1)}, u32[]{:S(2)}, u32[]{:S(2)}) collective-permute-start(bf16[128,2048]{0,1:T(8,128)(2,1)S(1)} %get-tuple-element.69), channel_id=1, source_target_pairs={{0,3},{1,0},{2,1},{3,2},{4,7},{5,4},{6,5},{7,6},{8,11},{9,8},{10,9... | collective-permute-start | bytes 1572872 | tf_op jit(solution)/shard_map/ppermute | solution.py:64
  187.5 14.5 %collective-permute-start.12 = (bf16[128,2048]{0,1:T(8,128)(2,1)}, bf16[128,2048]{0,1:T(8,128)(2,1)S(1)}, u32[]{:S(2)}, u32[]{:S(2)}) collective-permute-start(bf16[128,2048]{0,1:T(8,128)(2,1)} %get-tuple-element.68), channel_id=1, source_target_pairs={{0,1},{1,2},{2,3},{3,0},{4,5},{5,6},{6,7},{7,4},{8,9},{9,10},{10,1... | collective-permute-start | bytes 1572872 | tf_op jit(solution)/shard_map/ppermute | solution.py:63
  197.9 23.8 %collective-permute-start.15 = (bf16[256,2048]{0,1:T(8,128)(2,1)S(1)}, bf16[256,2048]{0,1:T(8,128)(2,1)}, u32[]{:S(2)}, u32[]{:S(2)}) collective-permute-start(bf16[256,2048]{0,1:T(8,128)(2,1)S(1)} %convert_element_type.121), channel_id=1, source_target_pairs={{0,3},{1,0},{2,1},{3,2},{4,7},{5,4},{6,5},{7,6},{8,11},{9,8},{10,9... | collective-permute-start | bytes 3145736 | tf_op jit(solution)/shard_map/ppermute | solution.py:74
  203.3 24.6 %collective-permute-start.13 = (bf16[256,2048]{0,1:T(8,128)(2,1)}, bf16[256,2048]{0,1:T(8,128)(2,1)}, u32[]{:S(2)}, u32[]{:S(2)}) collective-permute-start(bf16[256,2048]{0,1:T(8,128)(2,1)} %convert_element_type.115), channel_id=1, source_target_pairs={{0,1},{1,2},{2,3},{3,0},{4,5},{5,6},{6,7},{7,4},{8,9},{9,10},{10,1... | collective-permute-start | bytes 3145736 | tf_op jit(solution)/shard_map/ppermute | solution.py:73
  229.9 9.3 %copy-start.18 = (s32[192,1]{0,1:T(1,128)S(1)}, s32[192,1]{0,1:T(1,128)}, u32[]{:S(2)}) copy-start(s32[192,1]{0,1:T(1,128)} %copy-done.17) | copy-start | bytes 2308
  231.4 35.8 %all-to-all-start.1 = ((bf16[16,16,2048]{2,1,0:T(8,128)(2,1)}), bf16[16,16,2048]{2,1,0:T(8,128)(2,1)S(1)}, u32[]{:S(2)}, u32[]{:S(2)}) async-start(bf16[16,16,2048]{2,1,0:T(8,128)(2,1)} %bitcast.41), calls=%async_computation.1 | async-start | bytes 2097152 | tf_op jit(solution)/shard_map/all_to_all | solution.py:146
  (13 other events, 30.1 us)
Sparse Core Ops, SparseCore 0:
  10.1 63.5 all-gather.6
  75.7 61.7 all-gather.4
  175.2 43.2 reduce-scatter.1

commit v10 on v4

--- a/solution.py
+++ b/solution.py
@@ -77,17 +77,15 @@
     both = jnp.concatenate([copies, scaled], axis=2).reshape(-1, 2 * part)
     empty_slots = jnp.zeros((slot_rows, 2 * part), jnp.bfloat16)
     send = empty_slots.at[slot_index].set(both).reshape(experts, capacity, 2 * part)
-    stacked = jnp.stack([w_gate[0], w_up[0], w_down[0]], axis=1)
-    full, send = ring_gather(stacked, "dp", lax.axis_size("dp"), along=2, tie=send)
-    gate_full, up_full, down_full = (
-        full[:, i].reshape(w_gate.shape[1], model_width) for i in range(3)
-    )
     recv = lax.all_to_all(send, "expert", split_axis=0, concat_axis=0, tiled=True)
-    recv = recv.reshape(1, slot_rows, 2 * part)
-    gathered = lax.all_gather(recv[0], "etp", axis=0, tiled=False)
+    down_ring, recv = ring_gather(w_down[0], "dp", lax.axis_size("dp"), along=1, tie=recv)
+    down_full = down_ring.reshape(w_down.shape[1], -1)
+    gathered = ring_gather(recv.reshape(slot_rows, 2 * part), "etp", shares)
     rows4 = gathered[:, :, :part]
     grads4 = gathered[:, :, part:]
 
+    gate_full = lax.all_gather(w_gate[0], "dp", axis=1, tiled=True)
+    up_full = lax.all_gather(w_up[0], "dp", axis=1, tiled=True)
     hidden_units = gate_full.shape[0]
     gate4 = gate_full.reshape(hidden_units, shares, part)
     up4 = up_full.reshape(hidden_units, shares, part)

time: 300 us -> 255 us (0.85)
  blocking collectives: 37.1 us -> 0 us
  starting transfers between devices: 54.4 us -> 79.6 us
  local copies, waits for them, and re-layouts: 42.9 us -> 25.3 us
  waiting for transfers between devices: 115 us -> 103 us
  other arithmetic: 15.4 us -> 9.24 us
  matrix products: 19.3 us -> 22.9 us
    all_to_all x1 -> x0, blocking collectives: 37.1 us -> none  [on_device(): lax.all_to_all(send, 'expert', split_axis=0, concat_axis=0, tiled=True)]
    ppermute x3 -> x4, waiting for transfers between devices: 53.1 us -> 19.5 us  [ring_gather(): left = lax.ppermute(left, axis, fwd)]
    ppermute x2, waiting for transfers between devices: 24.5 us -> 3.26 us  [ring_reduce_scatter(): lax.ppermute(to_right.astype(chunks.dtype), axis, fwd).astype(jnp.float32)]
    ppermute x2, waiting for transfers between devices: 2.35 us -> 20.4 us  [ring_reduce_scatter(): lax.ppermute(to_left.astype(chunks.dtype), axis, bwd).astype(jnp.float32)]
    all_to_all x0 -> x1, starting transfers between devices: none -> 10.3 us  [on_device(): lax.all_to_all(send, 'expert', split_axis=0, concat_axis=0, tiled=True)]
    ppermute x3 -> x4, waiting for transfers between devices: 0.87 us -> 10.2 us  [ring_gather(): right = lax.ppermute(right, axis, bwd)]
    ppermute x1 -> x2, waiting for transfers between devices: 2.08 us -> 9.94 us  [ring_gather(): first = lax.ppermute(left[:m], axis, fwd)]
    ppermute x1 -> x2, waiting for transfers between devices: 3.81 us -> 11.3 us  [ring_gather(): second = lax.ppermute(right[m:], axis, bwd)]
  transfers between devices with their start and end apart: 15 -> 21, of which waited for: 10 -> 12; matrix products, arithmetic and copies ran while one was open for 18% -> 15% of each run, Pallas kernels for 0% -> 0%
where the time goes in v10:
time: 255 us; the launch traced here: 254 us
  waiting for transfers between devices  103 us (40%)
  starting transfers between devices  79.6 us (31%)
  local copies, waits for them, and re-layouts  25.3 us (10%)
  matrix products  22.9 us (9%)
  between operations  14.5 us (6%)
  other arithmetic  9.24 us (4%)
    all_to_all x1, waiting for transfers between devices, on_device(): lax.all_to_all(slot_out.reshape(experts, capacity, 2 * part), 'expert', s...  27.9 us
    ppermute x4, starting transfers between devices, ring_gather(): right = lax.ppermute(right, axis, bwd)  24.4 us
    ppermute x2, waiting for transfers between devices, ring_reduce_scatter(): lax.ppermute(to_left.astype(chunks.dtype), axis, bwd).astype(jnp.float32)  20.4 us
    ppermute x4, waiting for transfers between devices, ring_gather(): left = lax.ppermute(left, axis, fwd)  19.5 us
    ppermute x2, waiting for transfers between devices, ring_gather(): second = lax.ppermute(right[m:], axis, bwd)  11.3 us
    all_to_all x1, starting transfers between devices, on_device(): lax.all_to_all(slot_out.reshape(experts, capacity, 2 * part), 'expert', s...  11 us
    all_to_all x1, starting transfers between devices, on_device(): lax.all_to_all(send, 'expert', split_axis=0, concat_axis=0, tiled=True)  10.3 us
    ppermute x4, waiting for transfers between devices, ring_gather(): right = lax.ppermute(right, axis, bwd)  10.2 us
  transfers between devices with their start and end apart: 21, of which 12 were waited for; matrix products, arithmetic and copies ran while one was open for 15% of the time, Pallas kernels for 0%

profile of v10, /device:TPU:1, one launch (start us, length us, event | category | flops | bytes accessed | tf_op | source)
XLA Modules:
  0.0 254.2 jit_solution(15537724863267939635)
XLA Ops:
  13.9 2.9 %scatter_custom_fusion = bf16[256,2048]{1,0:T(8,128)(2,1)} fusion(s32[192]{0:T(256)S(1)} %bitcast.119, bf16[192,1024]{1,0:T(8,128)(2,1)S(1)} %fusion.35, bf16[]{:T(256)} %constant.256, bf16[192,1024]{1,0:T(8,128)(2,1)S(1)} %broadcast_bitcast_fusion, bf16[]{:T(256)} %constant.213.clone.1), kind=kCustom, calls=%fused_computation.50 | custom fusion | flops 1572864 | bytes 1835012 | tf_op jit(solution)/shard_map/scatter | solution.py:79
  16.8 10.3 %all-to-all-start = ((bf16[16,16,2048]{2,1,0:T(8,128)(2,1)}), bf16[16,16,2048]{2,1,0:T(8,128)(2,1)S(1)}, u32[]{:S(2)}, u32[]{:S(2)}) async-start(bf16[16,16,2048]{2,1,0:T(8,128)(2,1)} %bitcast.6), calls=%async_computation | async-start | bytes 2097152 | tf_op jit(solution)/shard_map/all_to_all | solution.py:80
  28.4 2.3 collective-permute-start
  30.8 8.6 %collective-permute-start.1 = (bf16[384,512]{0,1:T(8,128)(2,1)S(1)}, bf16[384,512]{0,1:T(8,128)(2,1)S(1)}, u32[]{:S(2)}, u32[]{:S(2)}) collective-permute-start(bf16[384,512]{0,1:T(8,128)(2,1)S(1)} %bitcast.118), channel_id=1, source_target_pairs={{0,448},{64,0},{128,64},{192,128},{256,192},{320,256},{384,320},{4... | collective-permute-start | bytes 1179656 | tf_op jit(solution)/shard_map/ppermute | solution.py:20
  42.4 13.1 %collective-permute-done = bf16[384,512]{0,1:T(8,128)(2,1)S(1)} collective-permute-done((bf16[384,512]{0,1:T(8,128)(2,1)S(1)}, bf16[384,512]{0,1:T(8,128)(2,1)S(1)}, u32[]{:S(2)}, u32[]{:S(2)}) %collective-permute-start) | collective-permute-done | bytes 393248 | tf_op jit(solution)/shard_map/ppermute | solution.py:19
  56.3 3.1 %collective-permute-start.8 = (bf16[256,2048]{1,0:T(8,128)(2,1)S(1)}, bf16[256,2048]{1,0:T(8,128)(2,1)S(1)}, u32[]{:S(2)}, u32[]{:S(2)}) collective-permute-start(bf16[256,2048]{1,0:T(8,128)(2,1)S(1)} %bitcast.110), channel_id=1, source_target_pairs={{0,1},{1,2},{2,3},{3,0},{4,5},{5,6},{6,7},{7,4},{8,9},{9,10},{10,1... | collective-permute-start | bytes 3145736 | tf_op jit(solution)/shard_map/ppermute | solution.py:19
  59.4 3.4 %collective-permute-start.9 = (bf16[256,2048]{1,0:T(8,128)(2,1)S(1)}, bf16[256,2048]{1,0:T(8,128)(2,1)S(1)}, u32[]{:S(2)}, u32[]{:S(2)}) collective-permute-start(bf16[256,2048]{1,0:T(8,128)(2,1)S(1)} %bitcast.111), channel_id=1, source_target_pairs={{0,3},{1,0},{2,1},{3,2},{4,7},{5,4},{6,5},{7,6},{8,11},{9,8},{10,9... | collective-permute-start | bytes 3145736 | tf_op jit(solution)/shard_map/ppermute | solution.py:20
  64.7 7.8 %collective-permute-start.3 = (bf16[384,512]{0,1:T(8,128)(2,1)S(1)}, bf16[384,512]{0,1:T(8,128)(2,1)S(1)}, u32[]{:S(2)}, u32[]{:S(2)}) collective-permute-start(bf16[384,512]{0,1:T(8,128)(2,1)S(1)} %collective-permute-done.1), channel_id=1, source_target_pairs={{0,448},{64,0},{128,64},{192,128},{256,192},{320,256},{384,320},{4... | collective-permute-start | bytes 1179656 | tf_op jit(solution)/shard_map/ppermute | solution.py:20
  74.7 6.4 %collective-permute-done.2 = bf16[384,512]{0,1:T(8,128)(2,1)S(1)} collective-permute-done((bf16[384,512]{0,1:T(8,128)(2,1)S(1)}, bf16[384,512]{0,1:T(8,128)(2,1)S(1)}, u32[]{:S(2)}, u32[]{:S(2)}) %collective-permute-start.2) | collective-permute-done | bytes 393248 | tf_op jit(solution)/shard_map/ppermute | solution.py:19
  83.0 4.6 %collective-permute-start.5 = (bf16[384,512]{0,1:T(8,128)(2,1)S(1)}, bf16[384,512]{0,1:T(8,128)(2,1)S(1)}, u32[]{:S(2)}, u32[]{:S(2)}) collective-permute-start(bf16[384,512]{0,1:T(8,128)(2,1)S(1)} %collective-permute-done.3), channel_id=1, source_target_pairs={{0,448},{64,0},{128,64},{192,128},{256,192},{320,256},{384,320},{4... | collective-permute-start | bytes 1179656 | tf_op jit(solution)/shard_map/ppermute | solution.py:20
  89.2 9.4 %collective-permute-done.5 = bf16[384,512]{0,1:T(8,128)(2,1)S(1)} collective-permute-done((bf16[384,512]{0,1:T(8,128)(2,1)S(1)}, bf16[384,512]{0,1:T(8,128)(2,1)S(1)}, u32[]{:S(2)}, u32[]{:S(2)}) %collective-permute-start.5) | collective-permute-done | bytes 393248 | tf_op jit(solution)/shard_map/ppermute | solution.py:20
  98.8 5.4 %collective-permute-start.7 = (bf16[192,512]{0,1:T(8,128)(2,1)S(1)}, bf16[192,512]{0,1:T(8,128)(2,1)S(1)}, u32[]{:S(2)}, u32[]{:S(2)}) collective-permute-start(bf16[192,512]{0,1:T(8,128)(2,1)S(1)} %slice.91), channel_id=1, source_target_pairs={{0,448},{64,0},{128,64},{192,128},{256,192},{320,256},{384,320},{4... | collective-permute-start | bytes 589832 | tf_op jit(solution)/shard_map/ppermute | solution.py:27
  107.8 6.9 %collective-permute-done.7 = bf16[192,512]{0,1:T(8,128)(2,1)S(1)} collective-permute-done((bf16[192,512]{0,1:T(8,128)(2,1)S(1)}, bf16[192,512]{0,1:T(8,128)(2,1)S(1)}, u32[]{:S(2)}, u32[]{:S(2)}) %collective-permute-start.7) | collective-permute-done | bytes 196640 | tf_op jit(solution)/shard_map/ppermute | solution.py:27
  114.7 4.8 %collective-permute-done.6 = bf16[192,512]{0,1:T(8,128)(2,1)S(1)} collective-permute-done((bf16[192,512]{0,1:T(8,128)(2,1)S(1)}, bf16[192,512]{0,1:T(8,128)(2,1)S(1)}, u32[]{:S(2)}, u32[]{:S(2)}) %collective-permute-start.6) | collective-permute-done | bytes 196640 | tf_op jit(solution)/shard_map/ppermute | solution.py:26
  120.4 4.6 %collective-permute-start.11 = (bf16[128,2048]{1,0:T(8,128)(2,1)S(1)}, bf16[128,2048]{1,0:T(8,128)(2,1)S(1)}, u32[]{:S(2)}, u32[]{:S(2)}) collective-permute-start(bf16[128,2048]{1,0:T(8,128)(2,1)S(1)} %slice.93), channel_id=1, source_target_pairs={{0,3},{1,0},{2,1},{3,2},{4,7},{5,4},{6,5},{7,6},{8,11},{9,8},{10,9... | collective-permute-start | bytes 1572872 | tf_op jit(solution)/shard_map/ppermute | solution.py:27
  127.5 4.5 %collective-permute-done.11 = bf16[128,2048]{1,0:T(8,128)(2,1)S(1)} collective-permute-done((bf16[128,2048]{1,0:T(8,128)(2,1)S(1)}, bf16[128,2048]{1,0:T(8,128)(2,1)S(1)}, u32[]{:S(2)}, u32[]{:S(2)}) %collective-permute-start.11) | collective-permute-done | bytes 524320 | tf_op jit(solution)/shard_map/ppermute | solution.py:27
  131.9 5.1 %collective-permute-done.10 = bf16[128,2048]{1,0:T(8,128)(2,1)S(1)} collective-permute-done((bf16[128,2048]{1,0:T(8,128)(2,1)S(1)}, bf16[128,2048]{1,0:T(8,128)(2,1)S(1)}, u32[]{:S(2)}, u32[]{:S(2)}) %collective-permute-start.10) | collective-permute-done | bytes 524320 | tf_op jit(solution)/shard_map/ppermute | solution.py:26
  139.1 3.1 %fusion.16 = f32[256,384]{1,0:T(8,128)S(1)} fusion(bf16[384,4,1024]{0,2,1:T(8,128)(2,1)} %bitcast.14, bf16[4,256,2048]{2,1,0:T(8,128)(2,1)S(1)} %fusion.29), kind=kOutput, calls=%fused_computation.29 | convolution fusion | flops 805306368 | bytes 5636096 | tf_op jit(solution)/shard_map/jsc,fjc->sf/dot_general | solution.py:102
  142.2 3.8 %fusion.13 = f32[256,384]{1,0:T(8,128)S(1)} fusion(bf16[384,4,1024]{0,2,1:T(8,128)(2,1)} %bitcast.115, bf16[4,256,2048]{2,1,0:T(8,128)(2,1)} %copy-done), kind=kOutput, calls=%fused_computation.28 | convolution fusion | flops 805306368 | bytes 5636096 | tf_op jit(solution)/shard_map/jsc,fjc->sf/dot_general | solution.py:95
  146.1 4.7 %multiply_convert_fusion.1 = (bf16[256,384]{1,0:T(8,128)(2,1)S(1)}, f32[256,384]{1,0:T(8,128)}) fusion(f32[256,384]{1,0:T(8,128)S(1)} %fusion.16, f32[256,384]{1,0:T(8,128)S(1)} %fusion.13, bf16[384,4,1024]{0,2,1:T(8,128)(2,1)} %bitcast.113, bf16[4,256,2048]{2,1,0:T(8,128)(2,1)} %copy-done), kind=kOutput, calls=%fused_computation.73 | convolution fusion | flops 806289408 | bytes 6619136 | tf_op jit(solution)/shard_map/jsc,fjc->sf/dot_general | solution.py:94
  150.8 3.3 %fusion.48 = f32[256,4,1024]{0,2,1:T(8,128)} fusion(bf16[384,4,1024]{0,2,1:T(8,128)(2,1)S(1)} %bitcast.114, bf16[256,384]{1,0:T(8,128)(2,1)S(1)} %get-tuple-element.45), kind=kOutput, calls=%fused_computation.80 | convolution fusion | flops 805306368 | bytes 7536640 | tf_op jit(solution)/shard_map/sf,fjc->jsc/dot_general | solution.py:108
  155.1 2.8 %copy.60 = bf16[384,4,1024]{0,2,1:T(8,128)(2,1)} copy(bf16[384,4,1024]{2,0,1:T(8,128)(2,1)S(1)} %convolution_convert_fusion) | data formatting | bytes 6291456 | tf_op jit(solution)/shard_map/convert_element_type | solution.py:113
  159.9 3.7 %fusion.4 = bf16[4,256,1024]{1,2,0:T(8,128)(2,1)S(1)} fusion(f32[256,4,1024]{0,2,1:T(8,128)} %fusion.48, bf16[384,4,1024]{0,2,1:T(8,128)(2,1)S(1)} %bitcast.116, f32[256,384]{1,0:T(8,128)S(1)} %fusion.16, f32[256,384]{1,0:T(8,128)} %get-tuple-element.46), kind=kOutput, calls=%fused_computation.21 | convolution fusion | flops 807993344 | bytes 10223616 | tf_op jit(solution)/shard_map/sf,fjc->jsc/dot_general | solution.py:109
  163.6 3.2 %convert_bitcast_fusion = bf16[4,256,1024]{1,2,0:T(8,128)(2,1)S(1)} fusion(bf16[384,4,1024]{0,2,1:T(8,128)(2,1)} %bitcast.14, f32[256,384]{1,0:T(8,128)S(1)} %copy-done.9, f32[256,384]{1,0:T(8,128)S(1)} %copy-done.4), kind=kOutput, calls=%fused_computation.20 | convolution fusion | flops 806944768 | bytes 6029312 | tf_op jit(solution)/shard_map/sf,fjc->jsc/dot_general | solution.py:99
  168.9 3.4 %collective-permute-start.12 = (bf16[128,2048]{0,1:T(8,128)(2,1)S(1)}, bf16[128,2048]{0,1:T(8,128)(2,1)S(1)}, u32[]{:S(2)}, u32[]{:S(2)}) collective-permute-start(bf16[128,2048]{0,1:T(8,128)(2,1)S(1)} %get-tuple-element.41), channel_id=1, source_target_pairs={{0,1},{1,2},{2,3},{3,0},{4,5},{5,6},{6,7},{7,4},{8,9},{9,10},{10,1... | collective-permute-start | bytes 1572872 | tf_op jit(solution)/shard_map/ppermute | solution.py:42
  172.9 4.4 %collective-permute-done.14 = bf16[128,2048]{0,1:T(8,128)(2,1)S(1)} collective-permute-done((bf16[128,2048]{0,1:T(8,128)(2,1)S(1)}, bf16[128,2048]{0,1:T(8,128)(2,1)S(1)}, u32[]{:S(2)}, u32[]{:S(2)}) %collective-permute-start.14) | collective-permute-done | bytes 524320 | tf_op jit(solution)/shard_map/ppermute | solution.py:43
  177.5 3.1 %collective-permute-start.15 = (bf16[256,2048]{0,1:T(8,128)(2,1)S(1)}, bf16[256,2048]{0,1:T(8,128)(2,1)S(1)}, u32[]{:S(2)}, u32[]{:S(2)}) collective-permute-start(bf16[256,2048]{0,1:T(8,128)(2,1)S(1)} %convert_element_type.121), channel_id=1, source_target_pairs={{0,3},{1,0},{2,1},{3,2},{4,7},{5,4},{6,5},{7,6},{8,11},{9,8},{10,9... | collective-permute-start | bytes 3145736 | tf_op jit(solution)/shard_map/ppermute | solution.py:53
  180.8 2.2 collective-permute-start.13
  183.0 16.0 %collective-permute-done.15 = bf16[256,2048]{0,1:T(8,128)(2,1)S(1)} collective-permute-done((bf16[256,2048]{0,1:T(8,128)(2,1)S(1)}, bf16[256,2048]{0,1:T(8,128)(2,1)S(1)}, u32[]{:S(2)}, u32[]{:S(2)}) %collective-permute-start.15) | collective-permute-done | bytes 1048608 | tf_op jit(solution)/shard_map/ppermute | solution.py:53
  199.0 3.3 %collective-permute-done.13 = bf16[256,2048]{0,1:T(8,128)(2,1)S(1)} collective-permute-done((bf16[256,2048]{0,1:T(8,128)(2,1)S(1)}, bf16[256,2048]{0,1:T(8,128)(2,1)S(1)}, u32[]{:S(2)}, u32[]{:S(2)}) %collective-permute-start.13) | collective-permute-done | bytes 1048608 | tf_op jit(solution)/shard_map/ppermute | solution.py:52
  204.1 11.0 %all-to-all-start.1 = ((bf16[16,16,2048]{2,1,0:T(8,128)(2,1)}), bf16[16,16,2048]{2,1,0:T(8,128)(2,1)S(1)}, u32[]{:S(2)}, u32[]{:S(2)}) async-start(bf16[16,16,2048]{2,1,0:T(8,128)(2,1)} %bitcast.37), calls=%async_computation.1 | async-start | bytes 2097152 | tf_op jit(solution)/shard_map/all_to_all | solution.py:119
  215.1 27.9 %all-to-all-done.1 = bf16[16,16,2048]{2,1,0:T(8,128)(2,1)S(1)} async-done(((bf16[16,16,2048]{2,1,0:T(8,128)(2,1)}), bf16[16,16,2048]{2,1,0:T(8,128)(2,1)S(1)}, u32[]{:S(2)}, u32[]{:S(2)}) %all-to-all-start.1) | async-done | bytes 1048608 | tf_op jit(solution)/shard_map/all_to_all | solution.py:119
  (96 shorter events, 40.6 us)
Async XLA Ops:
  7.2 135.1 %all-gather.7.cloned.1.call-start = ((), (), s32[]{:S(2)}) async-start(), calls=%async_computation.5 | async-start | bytes 3538944 | tf_op jit(solution)/shard_map/all_gather | solution.py:88
  10.9 1.8 copy-start.7
  12.5 14.7 %copy-start.5 = (bf16[1,384,512]{2,1,0:T(8,128)(2,1)S(1)}, bf16[1,384,512]{2,1,0:T(8,128)(2,1)}, u32[]{:S(2)}) copy-start(bf16[1,384,512]{2,1,0:T(8,128)(2,1)} %param.15) | copy-start | bytes 1179652
  12.9 15.4 %copy-start.6 = (bf16[1,384,512]{2,1,0:T(8,128)(2,1)S(1)}, bf16[1,384,512]{2,1,0:T(8,128)(2,1)}, u32[]{:S(2)}) copy-start(bf16[1,384,512]{2,1,0:T(8,128)(2,1)} %param.17) | copy-start | bytes 1179652
  16.8 39.4 %all-to-all-start = ((bf16[16,16,2048]{2,1,0:T(8,128)(2,1)}), bf16[16,16,2048]{2,1,0:T(8,128)(2,1)S(1)}, u32[]{:S(2)}, u32[]{:S(2)}) async-start(bf16[16,16,2048]{2,1,0:T(8,128)(2,1)} %bitcast.6), calls=%async_computation | async-start | bytes 2097152 | tf_op jit(solution)/shard_map/all_to_all | solution.py:80
  27.2 118.9 %all-gather.5.cloned.1.call-start = ((), (), s32[]{:S(2)}) async-start(), calls=%async_computation.4 | async-start | bytes 3538944 | tf_op jit(solution)/shard_map/all_gather | solution.py:87
  28.2 217.3 %reduce-scatter.2.cloned.1.call-start = ((), (), s32[]{:S(2)}) async-start(), calls=%async_computation.3 | async-start | bytes 3538944 | tf_op jit(solution)/shard_map/reduce_scatter | solution.py:114
  28.4 27.0 %collective-permute-start = (bf16[384,512]{0,1:T(8,128)(2,1)S(1)}, bf16[384,512]{0,1:T(8,128)(2,1)S(1)}, u32[]{:S(2)}, u32[]{:S(2)}) collective-permute-start(bf16[384,512]{0,1:T(8,128)(2,1)S(1)} %bitcast.117), channel_id=1, source_target_pairs={{0,64},{64,128},{128,192},{192,256},{256,320},{320,384},{384,448},... | collective-permute-start | bytes 1179656 | tf_op jit(solution)/shard_map/ppermute | solution.py:19
  30.8 25.5 %collective-permute-start.1 = (bf16[384,512]{0,1:T(8,128)(2,1)S(1)}, bf16[384,512]{0,1:T(8,128)(2,1)S(1)}, u32[]{:S(2)}, u32[]{:S(2)}) collective-permute-start(bf16[384,512]{0,1:T(8,128)(2,1)S(1)} %bitcast.118), channel_id=1, source_target_pairs={{0,448},{64,0},{128,64},{192,128},{256,192},{320,256},{384,320},{4... | collective-permute-start | bytes 1179656 | tf_op jit(solution)/shard_map/ppermute | solution.py:20
  56.3 68.8 %collective-permute-start.8 = (bf16[256,2048]{1,0:T(8,128)(2,1)S(1)}, bf16[256,2048]{1,0:T(8,128)(2,1)S(1)}, u32[]{:S(2)}, u32[]{:S(2)}) collective-permute-start(bf16[256,2048]{1,0:T(8,128)(2,1)S(1)} %bitcast.110), channel_id=1, source_target_pairs={{0,1},{1,2},{2,3},{3,0},{4,5},{5,6},{6,7},{7,4},{8,9},{9,10},{10,1... | collective-permute-start | bytes 3145736 | tf_op jit(solution)/shard_map/ppermute | solution.py:19
  59.4 61.0 %collective-permute-start.9 = (bf16[256,2048]{1,0:T(8,128)(2,1)S(1)}, bf16[256,2048]{1,0:T(8,128)(2,1)S(1)}, u32[]{:S(2)}, u32[]{:S(2)}) collective-permute-start(bf16[256,2048]{1,0:T(8,128)(2,1)S(1)} %bitcast.111), channel_id=1, source_target_pairs={{0,3},{1,0},{2,1},{3,2},{4,7},{5,4},{6,5},{7,6},{8,11},{9,8},{10,9... | collective-permute-start | bytes 3145736 | tf_op jit(solution)/shard_map/ppermute | solution.py:20
  62.8 18.3 %collective-permute-start.2 = (bf16[384,512]{0,1:T(8,128)(2,1)S(1)}, bf16[384,512]{0,1:T(8,128)(2,1)S(1)}, u32[]{:S(2)}, u32[]{:S(2)}) collective-permute-start(bf16[384,512]{0,1:T(8,128)(2,1)S(1)} %collective-permute-done), channel_id=1, source_target_pairs={{0,64},{64,128},{128,192},{192,256},{256,320},{320,384},{384,448},... | collective-permute-start | bytes 1179656 | tf_op jit(solution)/shard_map/ppermute | solution.py:19
  64.7 18.3 %collective-permute-start.3 = (bf16[384,512]{0,1:T(8,128)(2,1)S(1)}, bf16[384,512]{0,1:T(8,128)(2,1)S(1)}, u32[]{:S(2)}, u32[]{:S(2)}) collective-permute-start(bf16[384,512]{0,1:T(8,128)(2,1)S(1)} %collective-permute-done.1), channel_id=1, source_target_pairs={{0,448},{64,0},{128,64},{192,128},{256,192},{320,256},{384,320},{4... | collective-permute-start | bytes 1179656 | tf_op jit(solution)/shard_map/ppermute | solution.py:20
  81.1 23.1 %collective-permute-start.4 = (bf16[384,512]{0,1:T(8,128)(2,1)S(1)}, bf16[384,512]{0,1:T(8,128)(2,1)S(1)}, u32[]{:S(2)}, u32[]{:S(2)}) collective-permute-start(bf16[384,512]{0,1:T(8,128)(2,1)S(1)} %collective-permute-done.2), channel_id=1, source_target_pairs={{0,64},{64,128},{128,192},{192,256},{256,320},{320,384},{384,448},... | collective-permute-start | bytes 1179656 | tf_op jit(solution)/shard_map/ppermute | solution.py:19
  83.0 15.6 %collective-permute-start.5 = (bf16[384,512]{0,1:T(8,128)(2,1)S(1)}, bf16[384,512]{0,1:T(8,128)(2,1)S(1)}, u32[]{:S(2)}, u32[]{:S(2)}) collective-permute-start(bf16[384,512]{0,1:T(8,128)(2,1)S(1)} %collective-permute-done.3), channel_id=1, source_target_pairs={{0,448},{64,0},{128,64},{192,128},{256,192},{320,256},{384,320},{4... | collective-permute-start | bytes 1179656 | tf_op jit(solution)/shard_map/ppermute | solution.py:20
  98.8 15.9 %collective-permute-start.7 = (bf16[192,512]{0,1:T(8,128)(2,1)S(1)}, bf16[192,512]{0,1:T(8,128)(2,1)S(1)}, u32[]{:S(2)}, u32[]{:S(2)}) collective-permute-start(bf16[192,512]{0,1:T(8,128)(2,1)S(1)} %slice.91), channel_id=1, source_target_pairs={{0,448},{64,0},{128,64},{192,128},{256,192},{320,256},{384,320},{4... | collective-permute-start | bytes 589832 | tf_op jit(solution)/shard_map/ppermute | solution.py:27
  104.2 15.3 %collective-permute-start.6 = (bf16[192,512]{0,1:T(8,128)(2,1)S(1)}, bf16[192,512]{0,1:T(8,128)(2,1)S(1)}, u32[]{:S(2)}, u32[]{:S(2)}) collective-permute-start(bf16[192,512]{0,1:T(8,128)(2,1)S(1)} %slice.90), channel_id=1, source_target_pairs={{0,64},{64,128},{128,192},{192,256},{256,320},{320,384},{384,448},... | collective-permute-start | bytes 589832 | tf_op jit(solution)/shard_map/ppermute | solution.py:26
  120.4 11.5 %collective-permute-start.11 = (bf16[128,2048]{1,0:T(8,128)(2,1)S(1)}, bf16[128,2048]{1,0:T(8,128)(2,1)S(1)}, u32[]{:S(2)}, u32[]{:S(2)}) collective-permute-start(bf16[128,2048]{1,0:T(8,128)(2,1)S(1)} %slice.93), channel_id=1, source_target_pairs={{0,3},{1,0},{2,1},{3,2},{4,7},{5,4},{6,5},{7,6},{8,11},{9,8},{10,9... | collective-permute-start | bytes 1572872 | tf_op jit(solution)/shard_map/ppermute | solution.py:27
  125.1 11.9 %collective-permute-start.10 = (bf16[128,2048]{1,0:T(8,128)(2,1)S(1)}, bf16[128,2048]{1,0:T(8,128)(2,1)S(1)}, u32[]{:S(2)}, u32[]{:S(2)}) collective-permute-start(bf16[128,2048]{1,0:T(8,128)(2,1)S(1)} %slice.92), channel_id=1, source_target_pairs={{0,1},{1,2},{2,3},{3,0},{4,5},{5,6},{6,7},{7,4},{8,9},{9,10},{10,1... | collective-permute-start | bytes 1572872 | tf_op jit(solution)/shard_map/ppermute | solution.py:26
  137.1 2.0 copy-start
  146.0 4.8 %copy-start.8 = (f32[256,384]{1,0:T(8,128)}, f32[256,384]{1,0:T(8,128)S(1)}, u32[]{:S(2)}) copy-start(f32[256,384]{1,0:T(8,128)S(1)} %fusion.13) | copy-start | bytes 1179652
  146.1 4.7 %copy-start.2 = (bf16[1,384,4096]{1,2,0:T(8,128)(2,1)S(1)}, bf16[1,384,4096]{1,2,0:T(8,128)(2,1)}, u32[]{:S(2)}) copy-start(bf16[1,384,4096]{1,2,0:T(8,128)(2,1)} %all-gather.5.cloned.1.call-done) | copy-start | bytes 9437188
  150.8 3.3 %copy-start.1 = (bf16[4,256,2048]{2,1,0:T(8,128)(2,1)S(1)}, bf16[4,256,2048]{2,1,0:T(8,128)(2,1)}, u32[]{:S(2)}) copy-start(bf16[4,256,2048]{2,1,0:T(8,128)(2,1)} %copy-done) | copy-start | bytes 12582916
  158.0 1.9 copy-start.3
  159.9 3.7 %copy-start.4 = (f32[256,384]{1,0:T(8,128)S(1)}, f32[256,384]{1,0:T(8,128)}, u32[]{:S(2)}) copy-start(f32[256,384]{1,0:T(8,128)} %get-tuple-element.46) | copy-start | bytes 1179652
  159.9 3.7 %copy-start.9 = (f32[256,384]{1,0:T(8,128)S(1)}, f32[256,384]{1,0:T(8,128)}, u32[]{:S(2)}) copy-start(f32[256,384]{1,0:T(8,128)} %copy-done.8) | copy-start | bytes 1179652
  166.9 10.3 %collective-permute-start.14 = (bf16[128,2048]{0,1:T(8,128)(2,1)S(1)}, bf16[128,2048]{0,1:T(8,128)(2,1)S(1)}, u32[]{:S(2)}, u32[]{:S(2)}) collective-permute-start(bf16[128,2048]{0,1:T(8,128)(2,1)S(1)} %get-tuple-element.42), channel_id=1, source_target_pairs={{0,3},{1,0},{2,1},{3,2},{4,7},{5,4},{6,5},{7,6},{8,11},{9,8},{10,9... | collective-permute-start | bytes 1572872 | tf_op jit(solution)/shard_map/ppermute | solution.py:43
  168.9 11.7 %collective-permute-start.12 = (bf16[128,2048]{0,1:T(8,128)(2,1)S(1)}, bf16[128,2048]{0,1:T(8,128)(2,1)S(1)}, u32[]{:S(2)}, u32[]{:S(2)}) collective-permute-start(bf16[128,2048]{0,1:T(8,128)(2,1)S(1)} %get-tuple-element.41), channel_id=1, source_target_pairs={{0,1},{1,2},{2,3},{3,0},{4,5},{5,6},{6,7},{7,4},{8,9},{9,10},{10,1... | collective-permute-start | bytes 1572872 | tf_op jit(solution)/shard_map/ppermute | solution.py:42
  177.5 21.5 %collective-permute-start.15 = (bf16[256,2048]{0,1:T(8,128)(2,1)S(1)}, bf16[256,2048]{0,1:T(8,128)(2,1)S(1)}, u32[]{:S(2)}, u32[]{:S(2)}) collective-permute-start(bf16[256,2048]{0,1:T(8,128)(2,1)S(1)} %convert_element_type.121), channel_id=1, source_target_pairs={{0,3},{1,0},{2,1},{3,2},{4,7},{5,4},{6,5},{7,6},{8,11},{9,8},{10,9... | collective-permute-start | bytes 3145736 | tf_op jit(solution)/shard_map/ppermute | solution.py:53
  180.8 21.4 %collective-permute-start.13 = (bf16[256,2048]{0,1:T(8,128)(2,1)S(1)}, bf16[256,2048]{0,1:T(8,128)(2,1)S(1)}, u32[]{:S(2)}, u32[]{:S(2)}) collective-permute-start(bf16[256,2048]{0,1:T(8,128)(2,1)S(1)} %convert_element_type.115), channel_id=1, source_target_pairs={{0,1},{1,2},{2,3},{3,0},{4,5},{5,6},{6,7},{7,4},{8,9},{9,10},{10,1... | collective-permute-start | bytes 3145736 | tf_op jit(solution)/shard_map/ppermute | solution.py:52
  204.1 38.9 %all-to-all-start.1 = ((bf16[16,16,2048]{2,1,0:T(8,128)(2,1)}), bf16[16,16,2048]{2,1,0:T(8,128)(2,1)S(1)}, u32[]{:S(2)}, u32[]{:S(2)}) async-start(bf16[16,16,2048]{2,1,0:T(8,128)(2,1)} %bitcast.37), calls=%async_computation.1 | async-start | bytes 2097152 | tf_op jit(solution)/shard_map/all_to_all | solution.py:119
Sparse Core Ops, SparseCore 0:
  10.7 64.4 all-gather.6
  77.2 55.0 all-gather.4
  158.1 43.1 reduce-scatter.1

commit v11 on v9

--- a/solution.py
+++ b/solution.py
@@ -34,10 +34,13 @@
             self.got.append((self.hop, jnp.concatenate([self.left, self.right], axis=0)))
 
     def result(self):
-        by_offset = dict([(0, self.piece)] + [(off % self.n, val) for off, val in self.got])
-        ordered = jnp.stack([by_offset[k] for k in range(self.n)], axis=self.along)
         idx = lax.axis_index(self.axis)
-        return jnp.take(ordered, (jnp.arange(self.n) - idx) % self.n, axis=self.along)
+        shape = list(self.piece.shape)
+        shape.insert(self.along, self.n)
+        out = jnp.zeros(shape, self.piece.dtype)
+        for offset, val in [(0, self.piece)] + self.got:
+            out = lax.dynamic_update_index_in_dim(out, val, (idx + offset) % self.n, self.along)
+        return out
 
 
 def lockstep(rings):
@@ -100,19 +103,21 @@
     send = empty_slots.at[slot_index].set(both).reshape(experts, capacity, 2 * part)
     recv = lax.all_to_all(send, "expert", split_axis=0, concat_axis=0, tiled=True)
 
-    gate_full = lax.all_gather(w_gate[0], "dp", axis=1, tiled=True)
-    up_full = lax.all_gather(w_up[0], "dp", axis=1, tiled=True)
     downs = Ring(w_down[0], "dp", lax.axis_size("dp"), along=1)
     lockstep([downs])
     downs.left, downs.right, recv = lax.optimization_barrier((downs.left, downs.right, recv))
     rows = Ring(recv.reshape(slot_rows, 2 * part), "etp", shares)
-    while downs.active() or rows.active():
-        lockstep([downs, rows])
+    lockstep([downs, rows])
+    for ring in (downs, rows, downs):
+        ring.step()
+        ring.record()
     down_full = downs.result().reshape(w_down.shape[1], model_width)
     gathered = rows.result()
     rows4 = gathered[:, :, :part]
     grads4 = gathered[:, :, part:]
 
+    gate_full = lax.all_gather(w_gate[0], "dp", axis=1, tiled=True)
+    up_full = lax.all_gather(w_up[0], "dp", axis=1, tiled=True)
     hidden_units = gate_full.shape[0]
     gate4 = gate_full.reshape(hidden_units, shares, part)
     up4 = up_full.reshape(hidden_units, shares, part)

time: 280 us -> 254 us (0.907)
  local copies, waits for them, and re-layouts: 38.4 us -> 19.6 us
  other arithmetic: 27.1 us -> 8.53 us
  waiting for transfers between devices: 95.8 us -> 107 us
    gather x3 -> x0, local copies, waits for them, and re-layouts: 10.6 us -> none  [result(): jnp.take(ordered, (jnp.arange(self.n) - idx) % self.n, axis=self.along)]
    ppermute x4, waiting for transfers between devices: 33.6 us -> 24.1 us  [step(): self.left = lax.ppermute(self.left, self.axis, fwd)]
    ppermute x2, waiting for transfers between devices: 0.01 us -> 8.28 us  [step(): self.right = lax.ppermute(self.right[m:], self.axis, bwd)]
    ppermute x4, waiting for transfers between devices: 5.11 us -> 12.8 us  [step(): self.right = lax.ppermute(self.right, self.axis, bwd)]
    select_n x4 -> x0, other arithmetic: 7.19 us -> none  [result(): jnp.take(ordered, (jnp.arange(self.n) - idx) % self.n, axis=self.along)]
    unnamed x61 -> x40, local copies, waits for them, and re-layouts: 16.3 us -> 10.3 us
    ppermute x2, waiting for transfers between devices: 0.01 us -> 5.52 us  [step(): self.left = lax.ppermute(self.left[:m], self.axis, fwd)]
    another operation x2 -> x0, other arithmetic: 3.59 us -> none  [result(): ordered = jnp.stack([by_offset[k] for k in range(self.n)], axis=self.along)]
  transfers between devices with their start and end apart: 21 -> 21, of which waited for: 13 -> 13; matrix products, arithmetic and copies ran while one was open for 23% -> 10% of each run, Pallas kernels for 0% -> 0%
where the time goes in v11:
time: 254 us; the launch traced here: 253 us
  waiting for transfers between devices  107 us (42%)
  starting transfers between devices  83.8 us (33%)
  local copies, waits for them, and re-layouts  19.6 us (8%)
  matrix products  19.2 us (8%)
  between operations  14.6 us (6%)
  other arithmetic  8.53 us (3%)
    ppermute x4, starting transfers between devices, step(): self.right = lax.ppermute(self.right, self.axis, bwd)  28.2 us
    all_to_all x1, waiting for transfers between devices, on_device(): lax.all_to_all(slot_out.reshape(experts, capacity, 2 * part), 'expert', s...  28 us
    ppermute x4, waiting for transfers between devices, step(): self.left = lax.ppermute(self.left, self.axis, fwd)  24.1 us
    ppermute x2, waiting for transfers between devices, ring_reduce_scatter(): lax.ppermute(to_left.astype(chunks.dtype), axis, bwd).astype(jnp.float32)  23.2 us
    ppermute x4, waiting for transfers between devices, step(): self.right = lax.ppermute(self.right, self.axis, bwd)  12.8 us
    all_to_all x1, starting transfers between devices, on_device(): lax.all_to_all(send, 'expert', split_axis=0, concat_axis=0, tiled=True)  10.3 us
    unnamed x40, local copies, waits for them, and re-layouts  10.3 us
    ppermute x2, starting transfers between devices, ring_reduce_scatter(): lax.ppermute(to_left.astype(chunks.dtype), axis, bwd).astype(jnp.float32)  10.1 us
  transfers between devices with their start and end apart: 21, of which 13 were waited for; matrix products, arithmetic and copies ran while one was open for 10% of the time, Pallas kernels for 0%

profile of v11, /device:TPU:1, one launch (start us, length us, event | category | flops | bytes accessed | tf_op | source)
XLA Modules:
  0.0 252.9 jit_solution(5139256598222399801)
XLA Ops:
  13.9 2.9 %scatter_custom_fusion = bf16[256,2048]{1,0:T(8,128)(2,1)} fusion(s32[192]{0:T(256)S(1)} %bitcast.121, bf16[192,1024]{1,0:T(8,128)(2,1)S(1)} %fusion.35, bf16[]{:T(256)} %constant.255, bf16[192,1024]{1,0:T(8,128)(2,1)S(1)} %broadcast_bitcast_fusion, bf16[]{:T(256)} %constant.212.clone.1), kind=kCustom, calls=%fused_computation.50 | custom fusion | flops 1572864 | bytes 1835012 | tf_op jit(solution)/shard_map/scatter | solution.py:103
  16.9 10.3 %all-to-all-start = ((bf16[16,16,2048]{2,1,0:T(8,128)(2,1)}), bf16[16,16,2048]{2,1,0:T(8,128)(2,1)S(1)}, u32[]{:S(2)}, u32[]{:S(2)}) async-start(bf16[16,16,2048]{2,1,0:T(8,128)(2,1)} %bitcast.8), calls=%async_computation | async-start | bytes 2097152 | tf_op jit(solution)/shard_map/all_to_all | solution.py:104
  28.5 2.3 collective-permute-start
  30.8 8.6 %collective-permute-start.1 = (bf16[384,512]{0,1:T(8,128)(2,1)S(1)}, bf16[384,512]{0,1:T(8,128)(2,1)S(1)}, u32[]{:S(2)}, u32[]{:S(2)}) collective-permute-start(bf16[384,512]{0,1:T(8,128)(2,1)S(1)} %bitcast.120), channel_id=1, source_target_pairs={{0,448},{64,0},{128,64},{192,128},{256,192},{320,256},{384,320},{4... | collective-permute-start | bytes 1179656 | tf_op jit(solution)/shard_map/ppermute | solution.py:24
  39.4 16.1 %collective-permute-done = bf16[384,512]{0,1:T(8,128)(2,1)S(1)} collective-permute-done((bf16[384,512]{0,1:T(8,128)(2,1)S(1)}, bf16[384,512]{0,1:T(8,128)(2,1)S(1)}, u32[]{:S(2)}, u32[]{:S(2)}) %collective-permute-start) | collective-permute-done | bytes 393248 | tf_op jit(solution)/shard_map/ppermute | solution.py:23
  56.9 3.1 %collective-permute-start.4 = (bf16[256,2048]{1,0:T(8,128)(2,1)S(1)}, bf16[256,2048]{1,0:T(8,128)(2,1)S(1)}, u32[]{:S(2)}, u32[]{:S(2)}) collective-permute-start(bf16[256,2048]{1,0:T(8,128)(2,1)S(1)} %bitcast.110), channel_id=1, source_target_pairs={{0,1},{1,2},{2,3},{3,0},{4,5},{5,6},{6,7},{7,4},{8,9},{9,10},{10,1... | collective-permute-start | bytes 3145736 | tf_op jit(solution)/shard_map/ppermute | solution.py:23
  60.0 3.4 %collective-permute-start.5 = (bf16[256,2048]{1,0:T(8,128)(2,1)S(1)}, bf16[256,2048]{1,0:T(8,128)(2,1)S(1)}, u32[]{:S(2)}, u32[]{:S(2)}) collective-permute-start(bf16[256,2048]{1,0:T(8,128)(2,1)S(1)} %bitcast.111), channel_id=1, source_target_pairs={{0,3},{1,0},{2,1},{3,2},{4,7},{5,4},{6,5},{7,6},{8,11},{9,8},{10,9... | collective-permute-start | bytes 3145736 | tf_op jit(solution)/shard_map/ppermute | solution.py:24
  64.6 1.9 collective-permute-start.2
  66.6 7.2 %collective-permute-start.3 = (bf16[384,512]{0,1:T(8,128)(2,1)S(1)}, bf16[384,512]{0,1:T(8,128)(2,1)S(1)}, u32[]{:S(2)}, u32[]{:S(2)}) collective-permute-start(bf16[384,512]{0,1:T(8,128)(2,1)S(1)} %copy-done.12), channel_id=1, source_target_pairs={{0,448},{64,0},{128,64},{192,128},{256,192},{320,256},{384,320},{4... | collective-permute-start | bytes 1179656 | tf_op jit(solution)/shard_map/ppermute | solution.py:24
  74.5 7.0 %collective-permute-done.2 = bf16[384,512]{0,1:T(8,128)(2,1)S(1)} collective-permute-done((bf16[384,512]{0,1:T(8,128)(2,1)S(1)}, bf16[384,512]{0,1:T(8,128)(2,1)S(1)}, u32[]{:S(2)}, u32[]{:S(2)}) %collective-permute-start.2) | collective-permute-done | bytes 393248 | tf_op jit(solution)/shard_map/ppermute | solution.py:23
  87.1 9.1 %collective-permute-start.7 = (bf16[384,512]{0,1:T(8,128)(2,1)S(1)}, bf16[384,512]{0,1:T(8,128)(2,1)S(1)}, u32[]{:S(2)}, u32[]{:S(2)}) collective-permute-start(bf16[384,512]{0,1:T(8,128)(2,1)S(1)} %collective-permute-done.3), channel_id=1, source_target_pairs={{0,448},{64,0},{128,64},{192,128},{256,192},{320,256},{384,320},{4... | collective-permute-start | bytes 1179656 | tf_op jit(solution)/shard_map/ppermute | solution.py:24
  96.2 4.6 %collective-permute-start.11 = (bf16[128,2048]{1,0:T(8,128)(2,1)S(1)}, bf16[128,2048]{1,0:T(8,128)(2,1)S(1)}, u32[]{:S(2)}, u32[]{:S(2)}) collective-permute-start(bf16[128,2048]{1,0:T(8,128)(2,1)S(1)} %slice.77), channel_id=1, source_target_pairs={{0,3},{1,0},{2,1},{3,2},{4,7},{5,4},{6,5},{7,6},{8,11},{9,8},{10,9... | collective-permute-start | bytes 1572872 | tf_op jit(solution)/shard_map/ppermute | solution.py:28
  100.8 1.9 collective-permute-start.10
  103.1 9.5 %collective-permute-done.7 = bf16[384,512]{0,1:T(8,128)(2,1)S(1)} collective-permute-done((bf16[384,512]{0,1:T(8,128)(2,1)S(1)}, bf16[384,512]{0,1:T(8,128)(2,1)S(1)}, u32[]{:S(2)}, u32[]{:S(2)}) %collective-permute-start.7) | collective-permute-done | bytes 393248 | tf_op jit(solution)/shard_map/ppermute | solution.py:24
  112.8 5.4 %collective-permute-start.9 = (bf16[192,512]{0,1:T(8,128)(2,1)S(1)}, bf16[192,512]{0,1:T(8,128)(2,1)S(1)}, u32[]{:S(2)}, u32[]{:S(2)}) collective-permute-start(bf16[192,512]{0,1:T(8,128)(2,1)S(1)} %slice.91), channel_id=1, source_target_pairs={{0,448},{64,0},{128,64},{192,128},{256,192},{320,256},{384,320},{4... | collective-permute-start | bytes 589832 | tf_op jit(solution)/shard_map/ppermute | solution.py:28
  118.3 2.1 collective-permute-start.8
  120.7 8.3 %collective-permute-done.9 = bf16[192,512]{0,1:T(8,128)(2,1)S(1)} collective-permute-done((bf16[192,512]{0,1:T(8,128)(2,1)S(1)}, bf16[192,512]{0,1:T(8,128)(2,1)S(1)}, u32[]{:S(2)}, u32[]{:S(2)}) %collective-permute-start.9) | collective-permute-done | bytes 196640 | tf_op jit(solution)/shard_map/ppermute | solution.py:28
  128.9 5.5 %collective-permute-done.8 = bf16[192,512]{0,1:T(8,128)(2,1)S(1)} collective-permute-done((bf16[192,512]{0,1:T(8,128)(2,1)S(1)}, bf16[192,512]{0,1:T(8,128)(2,1)S(1)}, u32[]{:S(2)}, u32[]{:S(2)}) %collective-permute-start.8) | collective-permute-done | bytes 196640 | tf_op jit(solution)/shard_map/ppermute | solution.py:27
  137.6 3.8 %fusion.13 = f32[256,384]{1,0:T(8,128)S(1)} fusion(bf16[384,4,1024]{0,2,1:T(8,128)(2,1)} %bitcast.117, bf16[4,256,2048]{2,1,0:T(8,128)(2,1)} %copy-done), kind=kOutput, calls=%fused_computation.28 | convolution fusion | flops 805306368 | bytes 5636096 | tf_op jit(solution)/shard_map/jsc,fjc->sf/dot_general | solution.py:127
  141.4 4.7 %multiply_convert_fusion.1 = (bf16[256,384]{1,0:T(8,128)(2,1)S(1)}, f32[256,384]{1,0:T(8,128)}) fusion(f32[256,384]{1,0:T(8,128)S(1)} %fusion.16, f32[256,384]{1,0:T(8,128)S(1)} %fusion.13, bf16[384,4,1024]{0,2,1:T(8,128)(2,1)} %bitcast.113, bf16[4,256,2048]{2,1,0:T(8,128)(2,1)} %copy-done), kind=kOutput, calls=%fused_computation.73 | convolution fusion | flops 806289408 | bytes 6619136 | tf_op jit(solution)/shard_map/jsc,fjc->sf/dot_general | solution.py:126
  146.1 3.3 %fusion.48 = f32[256,4,1024]{0,2,1:T(8,128)} fusion(bf16[384,4,1024]{0,2,1:T(8,128)(2,1)S(1)} %bitcast.114, bf16[256,384]{1,0:T(8,128)(2,1)S(1)} %get-tuple-element.57), kind=kOutput, calls=%fused_computation.80 | convolution fusion | flops 805306368 | bytes 7536640 | tf_op jit(solution)/shard_map/sf,fjc->jsc/dot_general | solution.py:140
  150.5 2.8 %copy.60 = bf16[384,4,1024]{0,2,1:T(8,128)(2,1)} copy(bf16[384,4,1024]{2,0,1:T(8,128)(2,1)S(1)} %convolution_convert_fusion) | data formatting | bytes 6291456 | tf_op jit(solution)/shard_map/convert_element_type | solution.py:145
  155.2 3.8 %fusion.4 = bf16[4,256,1024]{1,2,0:T(8,128)(2,1)S(1)} fusion(f32[256,4,1024]{0,2,1:T(8,128)} %fusion.48, bf16[384,4,1024]{0,2,1:T(8,128)(2,1)S(1)} %bitcast.118, f32[256,384]{1,0:T(8,128)S(1)} %fusion.16, f32[256,384]{1,0:T(8,128)} %get-tuple-element.58), kind=kOutput, calls=%fused_computation.21 | convolution fusion | flops 807993344 | bytes 10223616 | tf_op jit(solution)/shard_map/sf,fjc->jsc/dot_general | solution.py:141
  160.4 4.7 %collective-permute-start.14 = (bf16[128,2048]{0,1:T(8,128)(2,1)S(1)}, bf16[128,2048]{0,1:T(8,128)(2,1)S(1)}, u32[]{:S(2)}, u32[]{:S(2)}) collective-permute-start(bf16[128,2048]{0,1:T(8,128)(2,1)S(1)} %get-tuple-element.54), channel_id=1, source_target_pairs={{0,3},{1,0},{2,1},{3,2},{4,7},{5,4},{6,5},{7,6},{8,11},{9,8},{10,9... | collective-permute-start | bytes 1572872 | tf_op jit(solution)/shard_map/ppermute | solution.py:67
  165.2 1.9 collective-permute-start.12
  167.7 6.2 %collective-permute-done.14 = bf16[128,2048]{0,1:T(8,128)(2,1)S(1)} collective-permute-done((bf16[128,2048]{0,1:T(8,128)(2,1)S(1)}, bf16[128,2048]{0,1:T(8,128)(2,1)S(1)}, u32[]{:S(2)}, u32[]{:S(2)}) %collective-permute-start.14) | collective-permute-done | bytes 524320 | tf_op jit(solution)/shard_map/ppermute | solution.py:67
  174.2 5.4 %collective-permute-start.15 = (bf16[256,2048]{0,1:T(8,128)(2,1)S(1)}, bf16[256,2048]{0,1:T(8,128)(2,1)S(1)}, u32[]{:S(2)}, u32[]{:S(2)}) collective-permute-start(bf16[256,2048]{0,1:T(8,128)(2,1)S(1)} %convert_element_type.121), channel_id=1, source_target_pairs={{0,3},{1,0},{2,1},{3,2},{4,7},{5,4},{6,5},{7,6},{8,11},{9,8},{10,9... | collective-permute-start | bytes 3145736 | tf_op jit(solution)/shard_map/ppermute | solution.py:77
  179.8 1.9 collective-permute-start.13
  181.8 17.0 %collective-permute-done.15 = bf16[256,2048]{0,1:T(8,128)(2,1)S(1)} collective-permute-done((bf16[256,2048]{0,1:T(8,128)(2,1)S(1)}, bf16[256,2048]{0,1:T(8,128)(2,1)S(1)}, u32[]{:S(2)}, u32[]{:S(2)}) %collective-permute-start.15) | collective-permute-done | bytes 1048608 | tf_op jit(solution)/shard_map/ppermute | solution.py:77
  198.8 5.3 %collective-permute-done.13 = bf16[256,2048]{0,1:T(8,128)(2,1)S(1)} collective-permute-done((bf16[256,2048]{0,1:T(8,128)(2,1)S(1)}, bf16[256,2048]{0,1:T(8,128)(2,1)S(1)}, u32[]{:S(2)}, u32[]{:S(2)}) %collective-permute-start.13) | collective-permute-done | bytes 1048608 | tf_op jit(solution)/shard_map/ppermute | solution.py:76
  205.9 7.9 %all-to-all-start.1 = ((bf16[16,16,2048]{2,1,0:T(8,128)(2,1)}), bf16[16,16,2048]{2,1,0:T(8,128)(2,1)S(1)}, u32[]{:S(2)}, u32[]{:S(2)}) async-start(bf16[16,16,2048]{2,1,0:T(8,128)(2,1)} %bitcast.37), calls=%async_computation.1 | async-start | bytes 2097152 | tf_op jit(solution)/shard_map/all_to_all | solution.py:151
  213.8 28.0 %all-to-all-done.1 = bf16[16,16,2048]{2,1,0:T(8,128)(2,1)S(1)} async-done(((bf16[16,16,2048]{2,1,0:T(8,128)(2,1)}), bf16[16,16,2048]{2,1,0:T(8,128)(2,1)S(1)}, u32[]{:S(2)}, u32[]{:S(2)}) %all-to-all-start.1) | async-done | bytes 1048608 | tf_op jit(solution)/shard_map/all_to_all | solution.py:151
  (108 shorter events, 32.4 us)
Async XLA Ops:
  7.2 130.4 %all-gather.7.cloned.1.call-start = ((), (), s32[]{:S(2)}) async-start(), calls=%async_computation.5 | async-start | bytes 3538944 | tf_op jit(solution)/shard_map/all_gather | solution.py:120
  12.5 14.7 %copy-start.7 = (bf16[1,384,512]{2,1,0:T(8,128)(2,1)S(1)}, bf16[1,384,512]{2,1,0:T(8,128)(2,1)}, u32[]{:S(2)}) copy-start(bf16[1,384,512]{2,1,0:T(8,128)(2,1)} %param.15) | copy-start | bytes 1179652
  12.9 15.4 %copy-start.8 = (bf16[1,384,512]{2,1,0:T(8,128)(2,1)S(1)}, bf16[1,384,512]{2,1,0:T(8,128)(2,1)}, u32[]{:S(2)}) copy-start(bf16[1,384,512]{2,1,0:T(8,128)(2,1)} %param.17) | copy-start | bytes 1179652
  16.9 39.3 %all-to-all-start = ((bf16[16,16,2048]{2,1,0:T(8,128)(2,1)}), bf16[16,16,2048]{2,1,0:T(8,128)(2,1)S(1)}, u32[]{:S(2)}, u32[]{:S(2)}) async-start(bf16[16,16,2048]{2,1,0:T(8,128)(2,1)} %bitcast.8), calls=%async_computation | async-start | bytes 2097152 | tf_op jit(solution)/shard_map/all_to_all | solution.py:104
  27.2 114.2 %all-gather.5.cloned.1.call-start = ((), (), s32[]{:S(2)}) async-start(), calls=%async_computation.4 | async-start | bytes 3538944 | tf_op jit(solution)/shard_map/all_gather | solution.py:119
  28.2 216.0 %reduce-scatter.2.cloned.1.call-start = ((), (), s32[]{:S(2)}) async-start(), calls=%async_computation.3 | async-start | bytes 3538944 | tf_op jit(solution)/shard_map/reduce_scatter | solution.py:146
  28.5 27.0 %collective-permute-start = (bf16[384,512]{0,1:T(8,128)(2,1)S(1)}, bf16[384,512]{0,1:T(8,128)(2,1)S(1)}, u32[]{:S(2)}, u32[]{:S(2)}) collective-permute-start(bf16[384,512]{0,1:T(8,128)(2,1)S(1)} %bitcast.119), channel_id=1, source_target_pairs={{0,64},{64,128},{128,192},{192,256},{256,320},{320,384},{384,448},... | collective-permute-start | bytes 1179656 | tf_op jit(solution)/shard_map/ppermute | solution.py:23
  30.8 25.3 %collective-permute-start.1 = (bf16[384,512]{0,1:T(8,128)(2,1)S(1)}, bf16[384,512]{0,1:T(8,128)(2,1)S(1)}, u32[]{:S(2)}, u32[]{:S(2)}) collective-permute-start(bf16[384,512]{0,1:T(8,128)(2,1)S(1)} %bitcast.120), channel_id=1, source_target_pairs={{0,448},{64,0},{128,64},{192,128},{256,192},{320,256},{384,320},{4... | collective-permute-start | bytes 1179656 | tf_op jit(solution)/shard_map/ppermute | solution.py:24
  56.9 26.6 %collective-permute-start.4 = (bf16[256,2048]{1,0:T(8,128)(2,1)S(1)}, bf16[256,2048]{1,0:T(8,128)(2,1)S(1)}, u32[]{:S(2)}, u32[]{:S(2)}) collective-permute-start(bf16[256,2048]{1,0:T(8,128)(2,1)S(1)} %bitcast.110), channel_id=1, source_target_pairs={{0,1},{1,2},{2,3},{3,0},{4,5},{5,6},{6,7},{7,4},{8,9},{9,10},{10,1... | collective-permute-start | bytes 3145736 | tf_op jit(solution)/shard_map/ppermute | solution.py:23
  60.0 25.2 %collective-permute-start.5 = (bf16[256,2048]{1,0:T(8,128)(2,1)S(1)}, bf16[256,2048]{1,0:T(8,128)(2,1)S(1)}, u32[]{:S(2)}, u32[]{:S(2)}) collective-permute-start(bf16[256,2048]{1,0:T(8,128)(2,1)S(1)} %bitcast.111), channel_id=1, source_target_pairs={{0,3},{1,0},{2,1},{3,2},{4,7},{5,4},{6,5},{7,6},{8,11},{9,8},{10,9... | collective-permute-start | bytes 3145736 | tf_op jit(solution)/shard_map/ppermute | solution.py:24
  63.6 3.0 %copy-start.12 = (bf16[384,512]{0,1:T(8,128)(2,1)S(1)}, bf16[384,512]{0,1:T(8,128)(2,1)}, u32[]{:S(2)}) copy-start(bf16[384,512]{0,1:T(8,128)(2,1)} %copy-done.11) | copy-start | bytes 1179652
  64.6 16.8 %collective-permute-start.2 = (bf16[384,512]{0,1:T(8,128)(2,1)S(1)}, bf16[384,512]{0,1:T(8,128)(2,1)S(1)}, u32[]{:S(2)}, u32[]{:S(2)}) collective-permute-start(bf16[384,512]{0,1:T(8,128)(2,1)S(1)} %copy-done.10), channel_id=1, source_target_pairs={{0,64},{64,128},{128,192},{192,256},{256,320},{320,384},{384,448},... | collective-permute-start | bytes 1179656 | tf_op jit(solution)/shard_map/ppermute | solution.py:23
  66.6 15.9 %collective-permute-start.3 = (bf16[384,512]{0,1:T(8,128)(2,1)S(1)}, bf16[384,512]{0,1:T(8,128)(2,1)S(1)}, u32[]{:S(2)}, u32[]{:S(2)}) collective-permute-start(bf16[384,512]{0,1:T(8,128)(2,1)S(1)} %copy-done.12), channel_id=1, source_target_pairs={{0,448},{64,0},{128,64},{192,128},{256,192},{320,256},{384,320},{4... | collective-permute-start | bytes 1179656 | tf_op jit(solution)/shard_map/ppermute | solution.py:24
  85.1 33.1 %collective-permute-start.6 = (bf16[384,512]{0,1:T(8,128)(2,1)S(1)}, bf16[384,512]{0,1:T(8,128)(2,1)S(1)}, u32[]{:S(2)}, u32[]{:S(2)}) collective-permute-start(bf16[384,512]{0,1:T(8,128)(2,1)S(1)} %collective-permute-done.2), channel_id=1, source_target_pairs={{0,64},{64,128},{128,192},{192,256},{256,320},{320,384},{384,448},... | collective-permute-start | bytes 1179656 | tf_op jit(solution)/shard_map/ppermute | solution.py:23
  87.1 25.6 %collective-permute-start.7 = (bf16[384,512]{0,1:T(8,128)(2,1)S(1)}, bf16[384,512]{0,1:T(8,128)(2,1)S(1)}, u32[]{:S(2)}, u32[]{:S(2)}) collective-permute-start(bf16[384,512]{0,1:T(8,128)(2,1)S(1)} %collective-permute-done.3), channel_id=1, source_target_pairs={{0,448},{64,0},{128,64},{192,128},{256,192},{320,256},{384,320},{4... | collective-permute-start | bytes 1179656 | tf_op jit(solution)/shard_map/ppermute | solution.py:24
  96.2 24.4 %collective-permute-start.11 = (bf16[128,2048]{1,0:T(8,128)(2,1)S(1)}, bf16[128,2048]{1,0:T(8,128)(2,1)S(1)}, u32[]{:S(2)}, u32[]{:S(2)}) collective-permute-start(bf16[128,2048]{1,0:T(8,128)(2,1)S(1)} %slice.77), channel_id=1, source_target_pairs={{0,3},{1,0},{2,1},{3,2},{4,7},{5,4},{6,5},{7,6},{8,11},{9,8},{10,9... | collective-permute-start | bytes 1572872 | tf_op jit(solution)/shard_map/ppermute | solution.py:28
  100.8 19.8 %collective-permute-start.10 = (bf16[128,2048]{1,0:T(8,128)(2,1)S(1)}, bf16[128,2048]{1,0:T(8,128)(2,1)S(1)}, u32[]{:S(2)}, u32[]{:S(2)}) collective-permute-start(bf16[128,2048]{1,0:T(8,128)(2,1)S(1)} %slice.76), channel_id=1, source_target_pairs={{0,1},{1,2},{2,3},{3,0},{4,5},{5,6},{6,7},{7,4},{8,9},{9,10},{10,1... | collective-permute-start | bytes 1572872 | tf_op jit(solution)/shard_map/ppermute | solution.py:27
  112.8 16.1 %collective-permute-start.9 = (bf16[192,512]{0,1:T(8,128)(2,1)S(1)}, bf16[192,512]{0,1:T(8,128)(2,1)S(1)}, u32[]{:S(2)}, u32[]{:S(2)}) collective-permute-start(bf16[192,512]{0,1:T(8,128)(2,1)S(1)} %slice.91), channel_id=1, source_target_pairs={{0,448},{64,0},{128,64},{192,128},{256,192},{320,256},{384,320},{4... | collective-permute-start | bytes 589832 | tf_op jit(solution)/shard_map/ppermute | solution.py:28
  118.3 16.2 %collective-permute-start.8 = (bf16[192,512]{0,1:T(8,128)(2,1)S(1)}, bf16[192,512]{0,1:T(8,128)(2,1)S(1)}, u32[]{:S(2)}, u32[]{:S(2)}) collective-permute-start(bf16[192,512]{0,1:T(8,128)(2,1)S(1)} %slice.90), channel_id=1, source_target_pairs={{0,64},{64,128},{128,192},{192,256},{256,320},{320,384},{384,448},... | collective-permute-start | bytes 589832 | tf_op jit(solution)/shard_map/ppermute | solution.py:27
  120.7 14.0 %copy-start = (bf16[4,256,2048]{2,1,0:T(8,128)(2,1)}, bf16[4,256,2048]{2,1,0:T(8,128)(2,1)S(1)}, u32[]{:S(2)}) copy-start(bf16[4,256,2048]{2,1,0:T(8,128)(2,1)S(1)} %fusion.29) | copy-start | bytes 12582916
  141.4 4.8 %copy-start.14 = (f32[256,384]{1,0:T(8,128)}, f32[256,384]{1,0:T(8,128)S(1)}, u32[]{:S(2)}) copy-start(f32[256,384]{1,0:T(8,128)S(1)} %fusion.13) | copy-start | bytes 1179652
  141.4 4.7 %copy-start.2 = (bf16[1,384,4096]{1,2,0:T(8,128)(2,1)S(1)}, bf16[1,384,4096]{1,2,0:T(8,128)(2,1)}, u32[]{:S(2)}) copy-start(bf16[1,384,4096]{1,2,0:T(8,128)(2,1)} %all-gather.5.cloned.1.call-done) | copy-start | bytes 9437188
  146.1 3.3 %copy-start.1 = (bf16[4,256,2048]{2,1,0:T(8,128)(2,1)S(1)}, bf16[4,256,2048]{2,1,0:T(8,128)(2,1)}, u32[]{:S(2)}) copy-start(bf16[4,256,2048]{2,1,0:T(8,128)(2,1)} %copy-done) | copy-start | bytes 12582916
  153.3 1.9 copy-start.5
  155.2 3.8 %copy-start.4 = (bf16[384,8,512]{0,2,1:T(8,128)(2,1)S(1)}, bf16[384,8,512]{0,2,1:T(8,128)(2,1)}, u32[]{:S(2)}) copy-start(bf16[384,8,512]{0,2,1:T(8,128)(2,1)} %copy-done.3) | copy-start | bytes 9437188
  155.2 3.8 %copy-start.6 = (f32[256,384]{1,0:T(8,128)S(1)}, f32[256,384]{1,0:T(8,128)}, u32[]{:S(2)}) copy-start(f32[256,384]{1,0:T(8,128)} %get-tuple-element.58) | copy-start | bytes 1179652
  155.2 3.8 %copy-start.15 = (f32[256,384]{1,0:T(8,128)S(1)}, f32[256,384]{1,0:T(8,128)}, u32[]{:S(2)}) copy-start(f32[256,384]{1,0:T(8,128)} %copy-done.14) | copy-start | bytes 1179652
  160.4 13.5 %collective-permute-start.14 = (bf16[128,2048]{0,1:T(8,128)(2,1)S(1)}, bf16[128,2048]{0,1:T(8,128)(2,1)S(1)}, u32[]{:S(2)}, u32[]{:S(2)}) collective-permute-start(bf16[128,2048]{0,1:T(8,128)(2,1)S(1)} %get-tuple-element.54), channel_id=1, source_target_pairs={{0,3},{1,0},{2,1},{3,2},{4,7},{5,4},{6,5},{7,6},{8,11},{9,8},{10,9... | collective-permute-start | bytes 1572872 | tf_op jit(solution)/shard_map/ppermute | solution.py:67
  165.2 14.4 %collective-permute-start.12 = (bf16[128,2048]{0,1:T(8,128)(2,1)S(1)}, bf16[128,2048]{0,1:T(8,128)(2,1)S(1)}, u32[]{:S(2)}, u32[]{:S(2)}) collective-permute-start(bf16[128,2048]{0,1:T(8,128)(2,1)S(1)} %get-tuple-element.53), channel_id=1, source_target_pairs={{0,1},{1,2},{2,3},{3,0},{4,5},{5,6},{6,7},{7,4},{8,9},{9,10},{10,1... | collective-permute-start | bytes 1572872 | tf_op jit(solution)/shard_map/ppermute | solution.py:66
  174.2 24.6 %collective-permute-start.15 = (bf16[256,2048]{0,1:T(8,128)(2,1)S(1)}, bf16[256,2048]{0,1:T(8,128)(2,1)S(1)}, u32[]{:S(2)}, u32[]{:S(2)}) collective-permute-start(bf16[256,2048]{0,1:T(8,128)(2,1)S(1)} %convert_element_type.121), channel_id=1, source_target_pairs={{0,3},{1,0},{2,1},{3,2},{4,7},{5,4},{6,5},{7,6},{8,11},{9,8},{10,9... | collective-permute-start | bytes 3145736 | tf_op jit(solution)/shard_map/ppermute | solution.py:77
  179.8 24.2 %collective-permute-start.13 = (bf16[256,2048]{0,1:T(8,128)(2,1)S(1)}, bf16[256,2048]{0,1:T(8,128)(2,1)S(1)}, u32[]{:S(2)}, u32[]{:S(2)}) collective-permute-start(bf16[256,2048]{0,1:T(8,128)(2,1)S(1)} %convert_element_type.115), channel_id=1, source_target_pairs={{0,1},{1,2},{2,3},{3,0},{4,5},{5,6},{6,7},{7,4},{8,9},{9,10},{10,1... | collective-permute-start | bytes 3145736 | tf_op jit(solution)/shard_map/ppermute | solution.py:76
  205.9 35.9 %all-to-all-start.1 = ((bf16[16,16,2048]{2,1,0:T(8,128)(2,1)}), bf16[16,16,2048]{2,1,0:T(8,128)(2,1)S(1)}, u32[]{:S(2)}, u32[]{:S(2)}) async-start(bf16[16,16,2048]{2,1,0:T(8,128)(2,1)} %bitcast.37), calls=%async_computation.1 | async-start | bytes 2097152 | tf_op jit(solution)/shard_map/all_to_all | solution.py:151
  (5 other events, 6.0 us)
Sparse Core Ops, SparseCore 0:
  10.1 62.3 all-gather.6
  74.6 62.7 all-gather.4
  153.4 44.6 reduce-scatter.1

commit v12 on v11

--- a/solution.py
+++ b/solution.py
@@ -116,8 +116,7 @@
     rows4 = gathered[:, :, :part]
     grads4 = gathered[:, :, part:]
 
-    gate_full = lax.all_gather(w_gate[0], "dp", axis=1, tiled=True)
-    up_full = lax.all_gather(w_up[0], "dp", axis=1, tiled=True)
+    gate_full, up_full = lax.all_gather(jnp.stack([w_gate[0], w_up[0]]), "dp", axis=2, tiled=True)
     hidden_units = gate_full.shape[0]
     gate4 = gate_full.reshape(hidden_units, shares, part)
     up4 = up_full.reshape(hidden_units, shares, part)

time: 254 us -> 246 us (0.969)
  matrix products: 19.2 us -> 14 us
  starting transfers between devices: 83.8 us -> 78.9 us
  local copies, waits for them, and re-layouts: 19.6 us -> 22.5 us
    ppermute x2, waiting for transfers between devices: 23.2 us -> 1.02 us  [ring_reduce_scatter(): lax.ppermute(to_left.astype(chunks.dtype), axis, bwd).astype(jnp.float32)]
    ppermute x4, waiting for transfers between devices: 24.1 us -> 45 us  [step(): self.left = lax.ppermute(self.left, self.axis, fwd)]
    ppermute x2, waiting for transfers between devices: 5.3 us -> 25.8 us  [ring_reduce_scatter(): lax.ppermute(to_right.astype(chunks.dtype), axis, fwd).astype(jnp.float32)]
    ppermute x4, waiting for transfers between devices: 12.8 us -> 1.87 us  [step(): self.right = lax.ppermute(self.right, self.axis, bwd)]
    ppermute x2, waiting for transfers between devices: 8.28 us -> 1.02 us  [step(): self.right = lax.ppermute(self.right[m:], self.axis, bwd)]
    another operation x0 -> x1, local copies, waits for them, and re-layouts: none -> 3.62 us  [on_device(): gate_full, up_full = lax.all_gather(jnp.stack([w_gate[0], w_up[0]]), 'dp'...]
    ppermute x4, starting transfers between devices: 28.2 us -> 25.1 us  [step(): self.right = lax.ppermute(self.right, self.axis, bwd)]
    dot_general x1, matrix products: 4.7 us -> 2.02 us  [on_device(): jnp.einsum('jsc,fjc->sf', rows4, gate4, preferred_element_type=jnp.float32)]
  transfers between devices with their start and end apart: 21 -> 20, of which waited for: 13 -> 11; matrix products, arithmetic and copies ran while one was open for 10% -> 8% of each run, Pallas kernels for 0% -> 0%
where the time goes in v12:
time: 246 us; the launch traced here: 245 us
  waiting for transfers between devices  106 us (43%)
  starting transfers between devices  78.9 us (32%)
  local copies, waits for them, and re-layouts  22.5 us (9%)
  between operations  14.9 us (6%)
  matrix products  14 us (6%)
  other arithmetic  8.63 us (4%)
    ppermute x4, waiting for transfers between devices, step(): self.left = lax.ppermute(self.left, self.axis, fwd)  45 us
    all_to_all x1, waiting for transfers between devices, on_device(): lax.all_to_all(slot_out.reshape(experts, capacity, 2 * part), 'expert', s...  27.9 us
    ppermute x2, waiting for transfers between devices, ring_reduce_scatter(): lax.ppermute(to_right.astype(chunks.dtype), axis, fwd).astype(jnp.float32)  25.8 us
    ppermute x4, starting transfers between devices, step(): self.right = lax.ppermute(self.right, self.axis, bwd)  25.1 us
    all_to_all x1, starting transfers between devices, on_device(): lax.all_to_all(send, 'expert', split_axis=0, concat_axis=0, tiled=True)  10.3 us
    unnamed x40, local copies, waits for them, and re-layouts  9.58 us
    ppermute x4, starting transfers between devices, step(): self.left = lax.ppermute(self.left, self.axis, fwd)  9.54 us
    ppermute x2, starting transfers between devices, step(): self.right = lax.ppermute(self.right[m:], self.axis, bwd)  9.22 us
  transfers between devices with their start and end apart: 20, of which 11 were waited for; matrix products, arithmetic and copies ran while one was open for 8% of the time, Pallas kernels for 0%

profile of v12, /device:TPU:1, one launch (start us, length us, event | category | flops | bytes accessed | tf_op | source)
XLA Modules:
  0.0 244.8 jit_solution(3377083699699430769)
XLA Ops:
  14.0 2.8 %scatter_custom_fusion = bf16[256,2048]{1,0:T(8,128)(2,1)} fusion(s32[192]{0:T(256)S(1)} %bitcast.121, bf16[192,1024]{1,0:T(8,128)(2,1)S(1)} %fusion.35, bf16[]{:T(256)} %constant.255, bf16[192,1024]{1,0:T(8,128)(2,1)S(1)} %broadcast_bitcast_fusion, bf16[]{:T(256)} %constant.212.clone.1), kind=kCustom, calls=%fused_computation.50 | custom fusion | flops 1572864 | bytes 1835012 | tf_op jit(solution)/shard_map/scatter | solution.py:103
  16.8 10.3 %all-to-all-start = ((bf16[16,16,2048]{2,1,0:T(8,128)(2,1)}), bf16[16,16,2048]{2,1,0:T(8,128)(2,1)S(1)}, u32[]{:S(2)}, u32[]{:S(2)}) async-start(bf16[16,16,2048]{2,1,0:T(8,128)(2,1)} %bitcast.8), calls=%async_computation | async-start | bytes 2097152 | tf_op jit(solution)/shard_map/all_to_all | solution.py:104
  27.4 2.3 collective-permute-start
  29.7 8.6 %collective-permute-start.1 = (bf16[384,512]{0,1:T(8,128)(2,1)S(1)}, bf16[384,512]{0,1:T(8,128)(2,1)S(1)}, u32[]{:S(2)}, u32[]{:S(2)}) collective-permute-start(bf16[384,512]{0,1:T(8,128)(2,1)S(1)} %bitcast.120), channel_id=1, source_target_pairs={{0,448},{64,0},{128,64},{192,128},{256,192},{320,256},{384,320},{4... | collective-permute-start | bytes 1179656 | tf_op jit(solution)/shard_map/ppermute | solution.py:24
  38.3 16.1 %collective-permute-done = bf16[384,512]{0,1:T(8,128)(2,1)S(1)} collective-permute-done((bf16[384,512]{0,1:T(8,128)(2,1)S(1)}, bf16[384,512]{0,1:T(8,128)(2,1)S(1)}, u32[]{:S(2)}, u32[]{:S(2)}) %collective-permute-start) | collective-permute-done | bytes 393248 | tf_op jit(solution)/shard_map/ppermute | solution.py:23
  56.0 3.4 %collective-permute-start.4 = (bf16[256,2048]{1,0:T(8,128)(2,1)S(1)}, bf16[256,2048]{1,0:T(8,128)(2,1)S(1)}, u32[]{:S(2)}, u32[]{:S(2)}) collective-permute-start(bf16[256,2048]{1,0:T(8,128)(2,1)S(1)} %bitcast.114), channel_id=1, source_target_pairs={{0,1},{1,2},{2,3},{3,0},{4,5},{5,6},{6,7},{7,4},{8,9},{9,10},{10,1... | collective-permute-start | bytes 3145736 | tf_op jit(solution)/shard_map/ppermute | solution.py:23
  59.4 3.2 %collective-permute-start.5 = (bf16[256,2048]{1,0:T(8,128)(2,1)S(1)}, bf16[256,2048]{1,0:T(8,128)(2,1)S(1)}, u32[]{:S(2)}, u32[]{:S(2)}) collective-permute-start(bf16[256,2048]{1,0:T(8,128)(2,1)S(1)} %bitcast.115), channel_id=1, source_target_pairs={{0,3},{1,0},{2,1},{3,2},{4,7},{5,4},{6,5},{7,6},{8,11},{9,8},{10,9... | collective-permute-start | bytes 3145736 | tf_op jit(solution)/shard_map/ppermute | solution.py:24
  63.8 1.9 collective-permute-start.2
  65.8 8.0 %collective-permute-start.3 = (bf16[384,512]{0,1:T(8,128)(2,1)S(1)}, bf16[384,512]{0,1:T(8,128)(2,1)S(1)}, u32[]{:S(2)}, u32[]{:S(2)}) collective-permute-start(bf16[384,512]{0,1:T(8,128)(2,1)S(1)} %copy-done.11), channel_id=1, source_target_pairs={{0,448},{64,0},{128,64},{192,128},{256,192},{320,256},{384,320},{4... | collective-permute-start | bytes 1179656 | tf_op jit(solution)/shard_map/ppermute | solution.py:24
  74.5 15.3 %collective-permute-done.2 = bf16[384,512]{0,1:T(8,128)(2,1)S(1)} collective-permute-done((bf16[384,512]{0,1:T(8,128)(2,1)S(1)}, bf16[384,512]{0,1:T(8,128)(2,1)S(1)}, u32[]{:S(2)}, u32[]{:S(2)}) %collective-permute-start.2) | collective-permute-done | bytes 393248 | tf_op jit(solution)/shard_map/ppermute | solution.py:23
  91.0 2.0 collective-permute-start.10
  93.1 4.5 %collective-permute-start.11 = (bf16[128,2048]{1,0:T(8,128)(2,1)S(1)}, bf16[128,2048]{1,0:T(8,128)(2,1)S(1)}, u32[]{:S(2)}, u32[]{:S(2)}) collective-permute-start(bf16[128,2048]{1,0:T(8,128)(2,1)S(1)} %slice.77), channel_id=1, source_target_pairs={{0,3},{1,0},{2,1},{3,2},{4,7},{5,4},{6,5},{7,6},{8,11},{9,8},{10,9... | collective-permute-start | bytes 1572872 | tf_op jit(solution)/shard_map/ppermute | solution.py:28
  97.6 1.9 collective-permute-start.6
  99.5 5.4 %collective-permute-start.7 = (bf16[384,512]{0,1:T(8,128)(2,1)S(1)}, bf16[384,512]{0,1:T(8,128)(2,1)S(1)}, u32[]{:S(2)}, u32[]{:S(2)}) collective-permute-start(bf16[384,512]{0,1:T(8,128)(2,1)S(1)} %collective-permute-done.3), channel_id=1, source_target_pairs={{0,448},{64,0},{128,64},{192,128},{256,192},{320,256},{384,320},{4... | collective-permute-start | bytes 1179656 | tf_op jit(solution)/shard_map/ppermute | solution.py:24
  105.3 13.5 %collective-permute-done.6 = bf16[384,512]{0,1:T(8,128)(2,1)S(1)} collective-permute-done((bf16[384,512]{0,1:T(8,128)(2,1)S(1)}, bf16[384,512]{0,1:T(8,128)(2,1)S(1)}, u32[]{:S(2)}, u32[]{:S(2)}) %collective-permute-start.6) | collective-permute-done | bytes 393248 | tf_op jit(solution)/shard_map/ppermute | solution.py:23
  118.9 1.9 collective-permute-start.8
  120.9 4.8 %collective-permute-start.9 = (bf16[192,512]{0,1:T(8,128)(2,1)S(1)}, bf16[192,512]{0,1:T(8,128)(2,1)S(1)}, u32[]{:S(2)}, u32[]{:S(2)}) collective-permute-start(bf16[192,512]{0,1:T(8,128)(2,1)S(1)} %slice.91), channel_id=1, source_target_pairs={{0,448},{64,0},{128,64},{192,128},{256,192},{320,256},{384,320},{4... | collective-permute-start | bytes 589832 | tf_op jit(solution)/shard_map/ppermute | solution.py:28
  126.0 3.1 %collective-permute-done.8 = bf16[192,512]{0,1:T(8,128)(2,1)S(1)} collective-permute-done((bf16[192,512]{0,1:T(8,128)(2,1)S(1)}, bf16[192,512]{0,1:T(8,128)(2,1)S(1)}, u32[]{:S(2)}, u32[]{:S(2)}) %collective-permute-start.8) | collective-permute-done | bytes 196640 | tf_op jit(solution)/shard_map/ppermute | solution.py:27
  133.2 3.6 %fusion.54 = (bf16[1,384,4096]{1,2,0:T(8,128)(2,1)S(1)}, bf16[1,384,4096]{1,2,0:T(8,128)(2,1)S(1)}) fusion(bf16[2,384,4096]{1,2,0:T(8,128)(2,1)} %all-gather.2.cloned.1.call-done), kind=kLoop, calls=%fused_computation.95 | loop fusion | bytes 12582912 | tf_op jit(solution)/shard_map/unstack | solution.py:119
  138.6 2.0 multiply_convert_fusion.1
  141.6 3.3 %fusion.48 = f32[4,1024,256]{2,1,0:T(8,128)} fusion(bf16[384,4,1024]{0,2,1:T(8,128)(2,1)S(1)} %bitcast.108, bf16[256,384]{1,0:T(8,128)(2,1)S(1)} %get-tuple-element.59), kind=kOutput, calls=%fused_computation.81 | convolution fusion | flops 805306368 | bytes 7536640 | tf_op jit(solution)/shard_map/sf,fjc->jsc/dot_general | solution.py:139
  145.0 2.8 %copy.52 = bf16[384,4,1024]{0,2,1:T(8,128)(2,1)} copy(bf16[384,4,1024]{2,0,1:T(8,128)(2,1)S(1)} %convolution_convert_fusion) | data formatting | bytes 6291456 | tf_op jit(solution)/shard_map/convert_element_type | solution.py:144
  147.8 1.9 copy-done.1
  149.7 3.8 %fusion.4 = bf16[4,256,1024]{1,2,0:T(8,128)(2,1)S(1)} fusion(f32[4,1024,256]{2,1,0:T(8,128)} %fusion.48, bf16[384,4,1024]{0,2,1:T(8,128)(2,1)S(1)} %bitcast.113, f32[256,384]{1,0:T(8,128)S(1)} %fusion.16, f32[256,384]{1,0:T(8,128)} %get-tuple-element.60), kind=kOutput, calls=%fused_computation.21 | convolution fusion | flops 807993344 | bytes 10223616 | tf_op jit(solution)/shard_map/sf,fjc->jsc/dot_general | solution.py:140
  154.9 2.5 %collective-permute-start.12 = (bf16[128,2048]{0,1:T(8,128)(2,1)S(1)}, bf16[128,2048]{0,1:T(8,128)(2,1)S(1)}, u32[]{:S(2)}, u32[]{:S(2)}) collective-permute-start(bf16[128,2048]{0,1:T(8,128)(2,1)S(1)} %get-tuple-element.55), channel_id=1, source_target_pairs={{0,1},{1,2},{2,3},{3,0},{4,5},{5,6},{6,7},{7,4},{8,9},{9,10},{10,1... | collective-permute-start | bytes 1572872 | tf_op jit(solution)/shard_map/ppermute | solution.py:66
  157.4 4.0 %collective-permute-start.14 = (bf16[128,2048]{0,1:T(8,128)(2,1)S(1)}, bf16[128,2048]{0,1:T(8,128)(2,1)S(1)}, u32[]{:S(2)}, u32[]{:S(2)}) collective-permute-start(bf16[128,2048]{0,1:T(8,128)(2,1)S(1)} %get-tuple-element.56), channel_id=1, source_target_pairs={{0,3},{1,0},{2,1},{3,2},{4,7},{5,4},{6,5},{7,6},{8,11},{9,8},{10,9... | collective-permute-start | bytes 1572872 | tf_op jit(solution)/shard_map/ppermute | solution.py:67
  162.1 7.6 %collective-permute-done.12 = bf16[128,2048]{0,1:T(8,128)(2,1)S(1)} collective-permute-done((bf16[128,2048]{0,1:T(8,128)(2,1)S(1)}, bf16[128,2048]{0,1:T(8,128)(2,1)S(1)}, u32[]{:S(2)}, u32[]{:S(2)}) %collective-permute-start.12) | collective-permute-done | bytes 524320 | tf_op jit(solution)/shard_map/ppermute | solution.py:66
  169.9 1.9 collective-permute-start.13
  172.0 4.8 %collective-permute-start.15 = (bf16[256,2048]{0,1:T(8,128)(2,1)S(1)}, bf16[256,2048]{0,1:T(8,128)(2,1)S(1)}, u32[]{:S(2)}, u32[]{:S(2)}) collective-permute-start(bf16[256,2048]{0,1:T(8,128)(2,1)S(1)} %convert_element_type.121), channel_id=1, source_target_pairs={{0,3},{1,0},{2,1},{3,2},{4,7},{5,4},{6,5},{7,6},{8,11},{9,8},{10,9... | collective-permute-start | bytes 3145736 | tf_op jit(solution)/shard_map/ppermute | solution.py:77
  176.8 18.2 %collective-permute-done.13 = bf16[256,2048]{0,1:T(8,128)(2,1)S(1)} collective-permute-done((bf16[256,2048]{0,1:T(8,128)(2,1)S(1)}, bf16[256,2048]{0,1:T(8,128)(2,1)S(1)}, u32[]{:S(2)}, u32[]{:S(2)}) %collective-permute-start.13) | collective-permute-done | bytes 1048608 | tf_op jit(solution)/shard_map/ppermute | solution.py:76
  197.9 7.5 %all-to-all-start.1 = ((bf16[16,16,2048]{2,1,0:T(8,128)(2,1)}), bf16[16,16,2048]{2,1,0:T(8,128)(2,1)S(1)}, u32[]{:S(2)}, u32[]{:S(2)}) async-start(bf16[16,16,2048]{2,1,0:T(8,128)(2,1)} %bitcast.37), calls=%async_computation.1 | async-start | bytes 2097152 | tf_op jit(solution)/shard_map/all_to_all | solution.py:150
  205.4 27.9 %all-to-all-done.1 = bf16[16,16,2048]{2,1,0:T(8,128)(2,1)S(1)} async-done(((bf16[16,16,2048]{2,1,0:T(8,128)(2,1)}), bf16[16,16,2048]{2,1,0:T(8,128)(2,1)S(1)}, u32[]{:S(2)}, u32[]{:S(2)}) %all-to-all-start.1) | async-done | bytes 1048608 | tf_op jit(solution)/shard_map/all_to_all | solution.py:150
  (107 shorter events, 29.0 us)
Async XLA Ops:
  7.2 3.5 %copy-start.13 = (f32[24,8]{0,1:T(8,128)S(1)}, f32[24,8]{0,1:T(8,128)}, u32[]{:S(2)}) copy-start(f32[24,8]{0,1:T(8,128)} %param.13) | copy-start | bytes 2308
  7.2 3.7 %copy-start.12 = (s32[24,8]{0,1:T(8,128)S(1)}, s32[24,8]{0,1:T(8,128)}, u32[]{:S(2)}) copy-start(s32[24,8]{0,1:T(8,128)} %param.14) | copy-start | bytes 2308
  7.2 126.0 %all-gather.2.cloned.1.call-start = ((), (), s32[]{:S(2)}) async-start(), calls=%async_computation.3 | async-start | bytes 7077888 | tf_op jit(solution)/shard_map/all_gather | solution.py:119
  12.8 14.4 %copy-start.7 = (bf16[1,384,512]{2,1,0:T(8,128)(2,1)S(1)}, bf16[1,384,512]{2,1,0:T(8,128)(2,1)}, u32[]{:S(2)}) copy-start(bf16[1,384,512]{2,1,0:T(8,128)(2,1)} %param.17) | copy-start | bytes 1179652
  16.8 38.4 %all-to-all-start = ((bf16[16,16,2048]{2,1,0:T(8,128)(2,1)}), bf16[16,16,2048]{2,1,0:T(8,128)(2,1)S(1)}, u32[]{:S(2)}, u32[]{:S(2)}) async-start(bf16[16,16,2048]{2,1,0:T(8,128)(2,1)} %bitcast.8), calls=%async_computation | async-start | bytes 2097152 | tf_op jit(solution)/shard_map/all_to_all | solution.py:104
  27.1 208.7 %reduce-scatter.2.cloned.1.call-start = ((), (), s32[]{:S(2)}) async-start(), calls=%async_computation.4 | async-start | bytes 3538944 | tf_op jit(solution)/shard_map/reduce_scatter | solution.py:145
  27.4 27.0 %collective-permute-start = (bf16[384,512]{0,1:T(8,128)(2,1)S(1)}, bf16[384,512]{0,1:T(8,128)(2,1)S(1)}, u32[]{:S(2)}, u32[]{:S(2)}) collective-permute-start(bf16[384,512]{0,1:T(8,128)(2,1)S(1)} %bitcast.119), channel_id=1, source_target_pairs={{0,64},{64,128},{128,192},{192,256},{256,320},{320,384},{384,448},... | collective-permute-start | bytes 1179656 | tf_op jit(solution)/shard_map/ppermute | solution.py:23
  29.7 25.5 %collective-permute-start.1 = (bf16[384,512]{0,1:T(8,128)(2,1)S(1)}, bf16[384,512]{0,1:T(8,128)(2,1)S(1)}, u32[]{:S(2)}, u32[]{:S(2)}) collective-permute-start(bf16[384,512]{0,1:T(8,128)(2,1)S(1)} %bitcast.120), channel_id=1, source_target_pairs={{0,448},{64,0},{128,64},{192,128},{256,192},{320,256},{384,320},{4... | collective-permute-start | bytes 1179656 | tf_op jit(solution)/shard_map/ppermute | solution.py:24
  56.0 35.0 %collective-permute-start.4 = (bf16[256,2048]{1,0:T(8,128)(2,1)S(1)}, bf16[256,2048]{1,0:T(8,128)(2,1)S(1)}, u32[]{:S(2)}, u32[]{:S(2)}) collective-permute-start(bf16[256,2048]{1,0:T(8,128)(2,1)S(1)} %bitcast.114), channel_id=1, source_target_pairs={{0,1},{1,2},{2,3},{3,0},{4,5},{5,6},{6,7},{7,4},{8,9},{9,10},{10,1... | collective-permute-start | bytes 3145736 | tf_op jit(solution)/shard_map/ppermute | solution.py:23
  59.4 31.6 %collective-permute-start.5 = (bf16[256,2048]{1,0:T(8,128)(2,1)S(1)}, bf16[256,2048]{1,0:T(8,128)(2,1)S(1)}, u32[]{:S(2)}, u32[]{:S(2)}) collective-permute-start(bf16[256,2048]{1,0:T(8,128)(2,1)S(1)} %bitcast.115), channel_id=1, source_target_pairs={{0,3},{1,0},{2,1},{3,2},{4,7},{5,4},{6,5},{7,6},{8,11},{9,8},{10,9... | collective-permute-start | bytes 3145736 | tf_op jit(solution)/shard_map/ppermute | solution.py:24
  62.8 3.0 %copy-start.11 = (bf16[384,512]{0,1:T(8,128)(2,1)S(1)}, bf16[384,512]{0,1:T(8,128)(2,1)}, u32[]{:S(2)}) copy-start(bf16[384,512]{0,1:T(8,128)(2,1)} %copy-done.10) | copy-start | bytes 1179652
  63.8 26.0 %collective-permute-start.2 = (bf16[384,512]{0,1:T(8,128)(2,1)S(1)}, bf16[384,512]{0,1:T(8,128)(2,1)S(1)}, u32[]{:S(2)}, u32[]{:S(2)}) collective-permute-start(bf16[384,512]{0,1:T(8,128)(2,1)S(1)} %copy-done.9), channel_id=1, source_target_pairs={{0,64},{64,128},{128,192},{192,256},{256,320},{320,384},{384,448},... | collective-permute-start | bytes 1179656 | tf_op jit(solution)/shard_map/ppermute | solution.py:23
  65.8 25.2 %collective-permute-start.3 = (bf16[384,512]{0,1:T(8,128)(2,1)S(1)}, bf16[384,512]{0,1:T(8,128)(2,1)S(1)}, u32[]{:S(2)}, u32[]{:S(2)}) collective-permute-start(bf16[384,512]{0,1:T(8,128)(2,1)S(1)} %copy-done.11), channel_id=1, source_target_pairs={{0,448},{64,0},{128,64},{192,128},{256,192},{320,256},{384,320},{4... | collective-permute-start | bytes 1179656 | tf_op jit(solution)/shard_map/ppermute | solution.py:24
  91.0 34.9 %collective-permute-start.10 = (bf16[128,2048]{1,0:T(8,128)(2,1)S(1)}, bf16[128,2048]{1,0:T(8,128)(2,1)S(1)}, u32[]{:S(2)}, u32[]{:S(2)}) collective-permute-start(bf16[128,2048]{1,0:T(8,128)(2,1)S(1)} %slice.76), channel_id=1, source_target_pairs={{0,1},{1,2},{2,3},{3,0},{4,5},{5,6},{6,7},{7,4},{8,9},{9,10},{10,1... | collective-permute-start | bytes 1572872 | tf_op jit(solution)/shard_map/ppermute | solution.py:27
  93.1 32.8 %collective-permute-start.11 = (bf16[128,2048]{1,0:T(8,128)(2,1)S(1)}, bf16[128,2048]{1,0:T(8,128)(2,1)S(1)}, u32[]{:S(2)}, u32[]{:S(2)}) collective-permute-start(bf16[128,2048]{1,0:T(8,128)(2,1)S(1)} %slice.77), channel_id=1, source_target_pairs={{0,3},{1,0},{2,1},{3,2},{4,7},{5,4},{6,5},{7,6},{8,11},{9,8},{10,9... | collective-permute-start | bytes 1572872 | tf_op jit(solution)/shard_map/ppermute | solution.py:28
  97.6 21.3 %collective-permute-start.6 = (bf16[384,512]{0,1:T(8,128)(2,1)S(1)}, bf16[384,512]{0,1:T(8,128)(2,1)S(1)}, u32[]{:S(2)}, u32[]{:S(2)}) collective-permute-start(bf16[384,512]{0,1:T(8,128)(2,1)S(1)} %collective-permute-done.2), channel_id=1, source_target_pairs={{0,64},{64,128},{128,192},{192,256},{256,320},{320,384},{384,448},... | collective-permute-start | bytes 1179656 | tf_op jit(solution)/shard_map/ppermute | solution.py:23
  99.5 21.3 %collective-permute-start.7 = (bf16[384,512]{0,1:T(8,128)(2,1)S(1)}, bf16[384,512]{0,1:T(8,128)(2,1)S(1)}, u32[]{:S(2)}, u32[]{:S(2)}) collective-permute-start(bf16[384,512]{0,1:T(8,128)(2,1)S(1)} %collective-permute-done.3), channel_id=1, source_target_pairs={{0,448},{64,0},{128,64},{192,128},{256,192},{320,256},{384,320},{4... | collective-permute-start | bytes 1179656 | tf_op jit(solution)/shard_map/ppermute | solution.py:24
  118.9 10.3 %collective-permute-start.8 = (bf16[192,512]{0,1:T(8,128)(2,1)S(1)}, bf16[192,512]{0,1:T(8,128)(2,1)S(1)}, u32[]{:S(2)}, u32[]{:S(2)}) collective-permute-start(bf16[192,512]{0,1:T(8,128)(2,1)S(1)} %slice.90), channel_id=1, source_target_pairs={{0,64},{64,128},{128,192},{192,256},{256,320},{320,384},{384,448},... | collective-permute-start | bytes 589832 | tf_op jit(solution)/shard_map/ppermute | solution.py:27
  120.9 9.2 %collective-permute-start.9 = (bf16[192,512]{0,1:T(8,128)(2,1)S(1)}, bf16[192,512]{0,1:T(8,128)(2,1)S(1)}, u32[]{:S(2)}, u32[]{:S(2)}) collective-permute-start(bf16[192,512]{0,1:T(8,128)(2,1)S(1)} %slice.91), channel_id=1, source_target_pairs={{0,448},{64,0},{128,64},{192,128},{256,192},{320,256},{384,320},{4... | collective-permute-start | bytes 589832 | tf_op jit(solution)/shard_map/ppermute | solution.py:28
  126.0 4.3 %copy-start.2 = (bf16[4,256,2048]{2,1,0:T(8,128)(2,1)}, bf16[4,256,2048]{2,1,0:T(8,128)(2,1)S(1)}, u32[]{:S(2)}) copy-start(bf16[4,256,2048]{2,1,0:T(8,128)(2,1)S(1)} %fusion.29) | copy-start | bytes 12582916
  133.2 4.0 %copy-start.3 = (bf16[4,256,2048]{2,1,0:T(8,128)(2,1)S(1)}, bf16[4,256,2048]{2,1,0:T(8,128)(2,1)}, u32[]{:S(2)}) copy-start(bf16[4,256,2048]{2,1,0:T(8,128)(2,1)} %copy-done.2) | copy-start | bytes 12582916
  136.9 1.7 copy-start
  138.6 2.0 copy-start.14
  147.8 1.9 copy-start.1
  149.7 3.8 %copy-start.5 = (bf16[384,8,512]{0,2,1:T(8,128)(2,1)S(1)}, bf16[384,8,512]{0,2,1:T(8,128)(2,1)}, u32[]{:S(2)}) copy-start(bf16[384,8,512]{0,2,1:T(8,128)(2,1)} %copy-done.4) | copy-start | bytes 9437188
  149.7 3.8 %copy-start.6 = (f32[256,384]{1,0:T(8,128)S(1)}, f32[256,384]{1,0:T(8,128)}, u32[]{:S(2)}) copy-start(f32[256,384]{1,0:T(8,128)} %get-tuple-element.60) | copy-start | bytes 1179652
  149.7 3.8 %copy-start.15 = (f32[256,384]{1,0:T(8,128)S(1)}, f32[256,384]{1,0:T(8,128)}, u32[]{:S(2)}) copy-start(f32[256,384]{1,0:T(8,128)} %copy-done.14) | copy-start | bytes 1179652
  154.9 14.7 %collective-permute-start.12 = (bf16[128,2048]{0,1:T(8,128)(2,1)S(1)}, bf16[128,2048]{0,1:T(8,128)(2,1)S(1)}, u32[]{:S(2)}, u32[]{:S(2)}) collective-permute-start(bf16[128,2048]{0,1:T(8,128)(2,1)S(1)} %get-tuple-element.55), channel_id=1, source_target_pairs={{0,1},{1,2},{2,3},{3,0},{4,5},{5,6},{6,7},{7,4},{8,9},{9,10},{10,1... | collective-permute-start | bytes 1572872 | tf_op jit(solution)/shard_map/ppermute | solution.py:66
  157.4 14.4 %collective-permute-start.14 = (bf16[128,2048]{0,1:T(8,128)(2,1)S(1)}, bf16[128,2048]{0,1:T(8,128)(2,1)S(1)}, u32[]{:S(2)}, u32[]{:S(2)}) collective-permute-start(bf16[128,2048]{0,1:T(8,128)(2,1)S(1)} %get-tuple-element.56), channel_id=1, source_target_pairs={{0,3},{1,0},{2,1},{3,2},{4,7},{5,4},{6,5},{7,6},{8,11},{9,8},{10,9... | collective-permute-start | bytes 1572872 | tf_op jit(solution)/shard_map/ppermute | solution.py:67
  169.9 25.2 %collective-permute-start.13 = (bf16[256,2048]{0,1:T(8,128)(2,1)S(1)}, bf16[256,2048]{0,1:T(8,128)(2,1)S(1)}, u32[]{:S(2)}, u32[]{:S(2)}) collective-permute-start(bf16[256,2048]{0,1:T(8,128)(2,1)S(1)} %convert_element_type.115), channel_id=1, source_target_pairs={{0,1},{1,2},{2,3},{3,0},{4,5},{5,6},{6,7},{7,4},{8,9},{9,10},{10,1... | collective-permute-start | bytes 3145736 | tf_op jit(solution)/shard_map/ppermute | solution.py:76
  172.0 24.0 %collective-permute-start.15 = (bf16[256,2048]{0,1:T(8,128)(2,1)S(1)}, bf16[256,2048]{0,1:T(8,128)(2,1)S(1)}, u32[]{:S(2)}, u32[]{:S(2)}) collective-permute-start(bf16[256,2048]{0,1:T(8,128)(2,1)S(1)} %convert_element_type.121), channel_id=1, source_target_pairs={{0,3},{1,0},{2,1},{3,2},{4,7},{5,4},{6,5},{7,6},{8,11},{9,8},{10,9... | collective-permute-start | bytes 3145736 | tf_op jit(solution)/shard_map/ppermute | solution.py:77
  197.9 35.4 %all-to-all-start.1 = ((bf16[16,16,2048]{2,1,0:T(8,128)(2,1)}), bf16[16,16,2048]{2,1,0:T(8,128)(2,1)S(1)}, u32[]{:S(2)}, u32[]{:S(2)}) async-start(bf16[16,16,2048]{2,1,0:T(8,128)(2,1)} %bitcast.37), calls=%async_computation.1 | async-start | bytes 2097152 | tf_op jit(solution)/shard_map/all_to_all | solution.py:150
  (4 other events, 4.2 us)
Sparse Core Ops, SparseCore 0:
  10.8 106.2 all-gather.1
  147.9 45.5 reduce-scatter.1

commit v13 on v12

--- a/solution.py
+++ b/solution.py
@@ -96,11 +96,15 @@
 
     tok_part = lax.dynamic_slice_in_dim(tokens, share_idx * part, part, axis=1)
     cot_part = lax.dynamic_slice_in_dim(cotangent, share_idx * part, part, axis=1)
-    copies = jnp.broadcast_to(tok_part[:, None, :], (tok_count, top_count, part))
-    scaled = (route_weights[:, :, None] * cot_part[:, None, :].astype(jnp.float32)).astype(jnp.bfloat16)
-    both = jnp.concatenate([copies, scaled], axis=2).reshape(-1, 2 * part)
-    empty_slots = jnp.zeros((slot_rows, 2 * part), jnp.bfloat16)
-    send = empty_slots.at[slot_index].set(both).reshape(experts, capacity, 2 * part)
+    routes = tok_count * top_count
+    owner = jnp.full((slot_rows,), routes, jnp.int32).at[slot_index].set(jnp.arange(routes, dtype=jnp.int32))
+    owner_tok = owner // top_count
+    zero_row = jnp.zeros((1, part), tokens.dtype)
+    tok_pad = jnp.concatenate([tok_part, zero_row], axis=0)
+    cot_pad = jnp.concatenate([cot_part, zero_row], axis=0)
+    weight_pad = jnp.concatenate([route_weights.reshape(-1), jnp.zeros((1,), route_weights.dtype)])
+    scaled = (weight_pad[owner][:, None] * cot_pad[owner_tok].astype(jnp.float32)).astype(jnp.bfloat16)
+    send = jnp.concatenate([tok_pad[owner_tok], scaled], axis=1).reshape(experts, capacity, 2 * part)
     recv = lax.all_to_all(send, "expert", split_axis=0, concat_axis=0, tiled=True)
 
     downs = Ring(w_down[0], "dp", lax.axis_size("dp"), along=1)

time: 246 us -> 247 us (level)
  local copies, waits for them, and re-layouts: 22.5 us -> 28.9 us
  waiting for transfers between devices: 106 us -> 102 us
    gather x0 -> x3, local copies, waits for them, and re-layouts: none -> 4.28 us  [the longest x1 1.94 us: on_device(): weight_pad[owner][:, None] * cot_pad[owner_tok].astype(jnp.float32)]
    ppermute x4, waiting for transfers between devices: 45 us -> 41.2 us  [step(): self.left = lax.ppermute(self.left, self.axis, fwd)]
    scatter x1 -> x0, other arithmetic: 2.8 us -> none  [on_device(): empty_slots.at[slot_index].set(both).reshape(experts, capacity, 2 * part)]
  transfers between devices with their start and end apart: 20 -> 20, of which waited for: 11 -> 11; matrix products, arithmetic and copies ran while one was open for 8% -> 10% of each run, Pallas kernels for 0% -> 0%
where the time goes in v13:
time: 247 us; the launch traced here: 246 us
  waiting for transfers between devices  102 us (41%)
  starting transfers between devices  80.1 us (32%)
  local copies, waits for them, and re-layouts  28.9 us (12%)
  between operations  14.9 us (6%)
  matrix products  14 us (6%)
  other arithmetic  6.19 us (3%)
    ppermute x4, waiting for transfers between devices, step(): self.left = lax.ppermute(self.left, self.axis, fwd)  41.2 us
    all_to_all x1, waiting for transfers between devices, on_device(): lax.all_to_all(slot_out.reshape(experts, capacity, 2 * part), 'expert', s...  27.9 us
    ppermute x2, waiting for transfers between devices, ring_reduce_scatter(): lax.ppermute(to_right.astype(chunks.dtype), axis, fwd).astype(jnp.float32)  25.6 us
    ppermute x4, starting transfers between devices, step(): self.right = lax.ppermute(self.right, self.axis, bwd)  25.2 us
    all_to_all x1, starting transfers between devices, on_device(): lax.all_to_all(send, 'expert', split_axis=0, concat_axis=0, tiled=True)  10.3 us
    unnamed x40, local copies, waits for them, and re-layouts  9.59 us
    ppermute x4, starting transfers between devices, step(): self.left = lax.ppermute(self.left, self.axis, fwd)  9.56 us
    ppermute x2, starting transfers between devices, step(): self.right = lax.ppermute(self.right[m:], self.axis, bwd)  8.98 us
  transfers between devices with their start and end apart: 20, of which 11 were waited for; matrix products, arithmetic and copies ran while one was open for 10% of the time, Pallas kernels for 0%

profile of v13, /device:TPU:1, one launch (start us, length us, event | category | flops | bytes accessed | tf_op | source)
XLA Modules:
  0.0 245.7 jit_solution(7405616833074203001)
XLA Ops:
  14.3 1.9 gather_fusion.1
  20.8 10.3 %all-to-all-start = ((bf16[16,16,2048]{2,1,0:T(8,128)(2,1)}), bf16[16,16,2048]{2,1,0:T(8,128)(2,1)S(1)}, u32[]{:S(2)}, u32[]{:S(2)}) async-start(bf16[16,16,2048]{2,1,0:T(8,128)(2,1)} %pad_maximum_fusion), calls=%async_computation | async-start | bytes 2097152 | tf_op jit(solution)/shard_map/all_to_all | solution.py:108
  31.4 2.3 collective-permute-start
  33.7 8.6 %collective-permute-start.1 = (bf16[384,512]{0,1:T(8,128)(2,1)S(1)}, bf16[384,512]{0,1:T(8,128)(2,1)S(1)}, u32[]{:S(2)}, u32[]{:S(2)}) collective-permute-start(bf16[384,512]{0,1:T(8,128)(2,1)S(1)} %bitcast.118), channel_id=1, source_target_pairs={{0,448},{64,0},{128,64},{192,128},{256,192},{320,256},{384,320},{4... | collective-permute-start | bytes 1179656 | tf_op jit(solution)/shard_map/ppermute | solution.py:24
  42.3 16.1 %collective-permute-done = bf16[384,512]{0,1:T(8,128)(2,1)S(1)} collective-permute-done((bf16[384,512]{0,1:T(8,128)(2,1)S(1)}, bf16[384,512]{0,1:T(8,128)(2,1)S(1)}, u32[]{:S(2)}, u32[]{:S(2)}) %collective-permute-start) | collective-permute-done | bytes 393248 | tf_op jit(solution)/shard_map/ppermute | solution.py:23
  59.9 3.4 %collective-permute-start.4 = (bf16[256,2048]{1,0:T(8,128)(2,1)S(1)}, bf16[256,2048]{1,0:T(8,128)(2,1)S(1)}, u32[]{:S(2)}, u32[]{:S(2)}) collective-permute-start(bf16[256,2048]{1,0:T(8,128)(2,1)S(1)} %bitcast.110), channel_id=1, source_target_pairs={{0,1},{1,2},{2,3},{3,0},{4,5},{5,6},{6,7},{7,4},{8,9},{9,10},{10,1... | collective-permute-start | bytes 3145736 | tf_op jit(solution)/shard_map/ppermute | solution.py:23
  63.3 3.2 %collective-permute-start.5 = (bf16[256,2048]{1,0:T(8,128)(2,1)S(1)}, bf16[256,2048]{1,0:T(8,128)(2,1)S(1)}, u32[]{:S(2)}, u32[]{:S(2)}) collective-permute-start(bf16[256,2048]{1,0:T(8,128)(2,1)S(1)} %bitcast.111), channel_id=1, source_target_pairs={{0,3},{1,0},{2,1},{3,2},{4,7},{5,4},{6,5},{7,6},{8,11},{9,8},{10,9... | collective-permute-start | bytes 3145736 | tf_op jit(solution)/shard_map/ppermute | solution.py:24
  67.8 1.9 collective-permute-start.2
  69.7 8.0 %collective-permute-start.3 = (bf16[384,512]{0,1:T(8,128)(2,1)S(1)}, bf16[384,512]{0,1:T(8,128)(2,1)S(1)}, u32[]{:S(2)}, u32[]{:S(2)}) collective-permute-start(bf16[384,512]{0,1:T(8,128)(2,1)S(1)} %copy-done.11), channel_id=1, source_target_pairs={{0,448},{64,0},{128,64},{192,128},{256,192},{320,256},{384,320},{4... | collective-permute-start | bytes 1179656 | tf_op jit(solution)/shard_map/ppermute | solution.py:24
  78.4 15.3 %collective-permute-done.2 = bf16[384,512]{0,1:T(8,128)(2,1)S(1)} collective-permute-done((bf16[384,512]{0,1:T(8,128)(2,1)S(1)}, bf16[384,512]{0,1:T(8,128)(2,1)S(1)}, u32[]{:S(2)}, u32[]{:S(2)}) %collective-permute-start.2) | collective-permute-done | bytes 393248 | tf_op jit(solution)/shard_map/ppermute | solution.py:23
  94.7 2.3 collective-permute-start.10
  97.0 4.2 %collective-permute-start.11 = (bf16[128,2048]{1,0:T(8,128)(2,1)S(1)}, bf16[128,2048]{1,0:T(8,128)(2,1)S(1)}, u32[]{:S(2)}, u32[]{:S(2)}) collective-permute-start(bf16[128,2048]{1,0:T(8,128)(2,1)S(1)} %slice.77), channel_id=1, source_target_pairs={{0,3},{1,0},{2,1},{3,2},{4,7},{5,4},{6,5},{7,6},{8,11},{9,8},{10,9... | collective-permute-start | bytes 1572872 | tf_op jit(solution)/shard_map/ppermute | solution.py:28
  101.3 1.9 collective-permute-start.6
  103.2 5.4 %collective-permute-start.7 = (bf16[384,512]{0,1:T(8,128)(2,1)S(1)}, bf16[384,512]{0,1:T(8,128)(2,1)S(1)}, u32[]{:S(2)}, u32[]{:S(2)}) collective-permute-start(bf16[384,512]{0,1:T(8,128)(2,1)S(1)} %collective-permute-done.3), channel_id=1, source_target_pairs={{0,448},{64,0},{128,64},{192,128},{256,192},{320,256},{384,320},{4... | collective-permute-start | bytes 1179656 | tf_op jit(solution)/shard_map/ppermute | solution.py:24
  109.0 9.8 %collective-permute-done.6 = bf16[384,512]{0,1:T(8,128)(2,1)S(1)} collective-permute-done((bf16[384,512]{0,1:T(8,128)(2,1)S(1)}, bf16[384,512]{0,1:T(8,128)(2,1)S(1)}, u32[]{:S(2)}, u32[]{:S(2)}) %collective-permute-start.6) | collective-permute-done | bytes 393248 | tf_op jit(solution)/shard_map/ppermute | solution.py:23
  118.8 1.9 collective-permute-start.8
  120.9 4.8 %collective-permute-start.9 = (bf16[192,512]{0,1:T(8,128)(2,1)S(1)}, bf16[192,512]{0,1:T(8,128)(2,1)S(1)}, u32[]{:S(2)}, u32[]{:S(2)}) collective-permute-start(bf16[192,512]{0,1:T(8,128)(2,1)S(1)} %slice.97), channel_id=1, source_target_pairs={{0,448},{64,0},{128,64},{192,128},{256,192},{320,256},{384,320},{4... | collective-permute-start | bytes 589832 | tf_op jit(solution)/shard_map/ppermute | solution.py:28
  125.9 3.1 %collective-permute-done.8 = bf16[192,512]{0,1:T(8,128)(2,1)S(1)} collective-permute-done((bf16[192,512]{0,1:T(8,128)(2,1)S(1)}, bf16[192,512]{0,1:T(8,128)(2,1)S(1)}, u32[]{:S(2)}, u32[]{:S(2)}) %collective-permute-start.8) | collective-permute-done | bytes 196640 | tf_op jit(solution)/shard_map/ppermute | solution.py:27
  133.1 3.6 %fusion.51 = (bf16[1,384,4096]{1,2,0:T(8,128)(2,1)S(1)}, bf16[1,384,4096]{1,2,0:T(8,128)(2,1)S(1)}) fusion(bf16[2,384,4096]{1,2,0:T(8,128)(2,1)} %all-gather.2.cloned.1.call-done), kind=kLoop, calls=%fused_computation.104 | loop fusion | bytes 12582912 | tf_op jit(solution)/shard_map/unstack | solution.py:123
  138.5 2.0 multiply_convert_fusion.1
  141.5 3.3 %fusion.43 = f32[4,1024,256]{2,1,0:T(8,128)} fusion(bf16[384,4,1024]{0,2,1:T(8,128)(2,1)S(1)} %bitcast.104, bf16[256,384]{1,0:T(8,128)(2,1)S(1)} %get-tuple-element.61), kind=kOutput, calls=%fused_computation.80 | convolution fusion | flops 805306368 | bytes 7536640 | tf_op jit(solution)/shard_map/sf,fjc->jsc/dot_general | solution.py:143
  144.9 2.8 %copy.52 = bf16[384,4,1024]{0,2,1:T(8,128)(2,1)} copy(bf16[384,4,1024]{2,0,1:T(8,128)(2,1)S(1)} %convolution_convert_fusion) | data formatting | bytes 6291456 | tf_op jit(solution)/shard_map/convert_element_type | solution.py:148
  147.7 1.9 copy-done.1
  149.6 3.8 %fusion.4 = bf16[4,256,1024]{1,2,0:T(8,128)(2,1)S(1)} fusion(f32[4,1024,256]{2,1,0:T(8,128)} %fusion.43, bf16[384,4,1024]{0,2,1:T(8,128)(2,1)S(1)} %bitcast.109, f32[256,384]{1,0:T(8,128)S(1)} %fusion.16, f32[256,384]{1,0:T(8,128)} %get-tuple-element.62), kind=kOutput, calls=%fused_computation.24 | convolution fusion | flops 807993344 | bytes 10223616 | tf_op jit(solution)/shard_map/sf,fjc->jsc/dot_general | solution.py:144
  154.8 3.2 %collective-permute-start.12 = (bf16[128,2048]{0,1:T(8,128)(2,1)S(1)}, bf16[128,2048]{0,1:T(8,128)(2,1)S(1)}, u32[]{:S(2)}, u32[]{:S(2)}) collective-permute-start(bf16[128,2048]{0,1:T(8,128)(2,1)S(1)} %get-tuple-element.55), channel_id=1, source_target_pairs={{0,1},{1,2},{2,3},{3,0},{4,5},{5,6},{6,7},{7,4},{8,9},{9,10},{10,1... | collective-permute-start | bytes 1572872 | tf_op jit(solution)/shard_map/ppermute | solution.py:66
  158.0 3.3 %collective-permute-start.14 = (bf16[128,2048]{0,1:T(8,128)(2,1)S(1)}, bf16[128,2048]{0,1:T(8,128)(2,1)S(1)}, u32[]{:S(2)}, u32[]{:S(2)}) collective-permute-start(bf16[128,2048]{0,1:T(8,128)(2,1)S(1)} %get-tuple-element.56), channel_id=1, source_target_pairs={{0,3},{1,0},{2,1},{3,2},{4,7},{5,4},{6,5},{7,6},{8,11},{9,8},{10,9... | collective-permute-start | bytes 1572872 | tf_op jit(solution)/shard_map/ppermute | solution.py:67
  162.0 7.5 %collective-permute-done.12 = bf16[128,2048]{0,1:T(8,128)(2,1)S(1)} collective-permute-done((bf16[128,2048]{0,1:T(8,128)(2,1)S(1)}, bf16[128,2048]{0,1:T(8,128)(2,1)S(1)}, u32[]{:S(2)}, u32[]{:S(2)}) %collective-permute-start.12) | collective-permute-done | bytes 524320 | tf_op jit(solution)/shard_map/ppermute | solution.py:66
  169.7 2.0 collective-permute-start.13
  172.0 4.7 %collective-permute-start.15 = (bf16[256,2048]{0,1:T(8,128)(2,1)S(1)}, bf16[256,2048]{0,1:T(8,128)(2,1)S(1)}, u32[]{:S(2)}, u32[]{:S(2)}) collective-permute-start(bf16[256,2048]{0,1:T(8,128)(2,1)S(1)} %convert_element_type.125), channel_id=1, source_target_pairs={{0,3},{1,0},{2,1},{3,2},{4,7},{5,4},{6,5},{7,6},{8,11},{9,8},{10,9... | collective-permute-start | bytes 3145736 | tf_op jit(solution)/shard_map/ppermute | solution.py:77
  176.7 18.1 %collective-permute-done.13 = bf16[256,2048]{0,1:T(8,128)(2,1)S(1)} collective-permute-done((bf16[256,2048]{0,1:T(8,128)(2,1)S(1)}, bf16[256,2048]{0,1:T(8,128)(2,1)S(1)}, u32[]{:S(2)}, u32[]{:S(2)}) %collective-permute-start.13) | collective-permute-done | bytes 1048608 | tf_op jit(solution)/shard_map/ppermute | solution.py:76
  197.7 8.6 %all-to-all-start.1 = ((bf16[16,16,2048]{2,1,0:T(8,128)(2,1)}), bf16[16,16,2048]{2,1,0:T(8,128)(2,1)S(1)}, u32[]{:S(2)}, u32[]{:S(2)}) async-start(bf16[16,16,2048]{2,1,0:T(8,128)(2,1)} %bitcast.36), calls=%async_computation.1 | async-start | bytes 2097152 | tf_op jit(solution)/shard_map/all_to_all | solution.py:154
  206.3 27.9 %all-to-all-done.1 = bf16[16,16,2048]{2,1,0:T(8,128)(2,1)S(1)} async-done(((bf16[16,16,2048]{2,1,0:T(8,128)(2,1)}), bf16[16,16,2048]{2,1,0:T(8,128)(2,1)S(1)}, u32[]{:S(2)}, u32[]{:S(2)}) %all-to-all-start.1) | async-done | bytes 1048608 | tf_op jit(solution)/shard_map/all_to_all | solution.py:154
  (117 shorter events, 33.6 us)
Async XLA Ops:
  7.2 3.5 %copy-start.12 = (s32[24,8]{0,1:T(8,128)S(1)}, s32[24,8]{0,1:T(8,128)}, u32[]{:S(2)}) copy-start(s32[24,8]{0,1:T(8,128)} %param.14) | copy-start | bytes 2308
  7.2 125.9 %all-gather.2.cloned.1.call-start = ((), (), s32[]{:S(2)}) async-start(), calls=%async_computation.3 | async-start | bytes 7077888 | tf_op jit(solution)/shard_map/all_gather | solution.py:123
  11.0 1.8 copy-start.13
  19.5 11.6 %copy-start.7 = (bf16[1,384,512]{2,1,0:T(8,128)(2,1)S(1)}, bf16[1,384,512]{2,1,0:T(8,128)(2,1)}, u32[]{:S(2)}) copy-start(bf16[1,384,512]{2,1,0:T(8,128)(2,1)} %param.17) | copy-start | bytes 1179652
  20.8 38.4 %all-to-all-start = ((bf16[16,16,2048]{2,1,0:T(8,128)(2,1)}), bf16[16,16,2048]{2,1,0:T(8,128)(2,1)S(1)}, u32[]{:S(2)}, u32[]{:S(2)}) async-start(bf16[16,16,2048]{2,1,0:T(8,128)(2,1)} %pad_maximum_fusion), calls=%async_computation | async-start | bytes 2097152 | tf_op jit(solution)/shard_map/all_to_all | solution.py:108
  31.1 205.6 %reduce-scatter.2.cloned.1.call-start = ((), (), s32[]{:S(2)}) async-start(), calls=%async_computation.4 | async-start | bytes 3538944 | tf_op jit(solution)/shard_map/reduce_scatter | solution.py:149
  31.4 27.0 %collective-permute-start = (bf16[384,512]{0,1:T(8,128)(2,1)S(1)}, bf16[384,512]{0,1:T(8,128)(2,1)S(1)}, u32[]{:S(2)}, u32[]{:S(2)}) collective-permute-start(bf16[384,512]{0,1:T(8,128)(2,1)S(1)} %bitcast.117), channel_id=1, source_target_pairs={{0,64},{64,128},{128,192},{192,256},{256,320},{320,384},{384,448},... | collective-permute-start | bytes 1179656 | tf_op jit(solution)/shard_map/ppermute | solution.py:23
  33.7 25.4 %collective-permute-start.1 = (bf16[384,512]{0,1:T(8,128)(2,1)S(1)}, bf16[384,512]{0,1:T(8,128)(2,1)S(1)}, u32[]{:S(2)}, u32[]{:S(2)}) collective-permute-start(bf16[384,512]{0,1:T(8,128)(2,1)S(1)} %bitcast.118), channel_id=1, source_target_pairs={{0,448},{64,0},{128,64},{192,128},{256,192},{320,256},{384,320},{4... | collective-permute-start | bytes 1179656 | tf_op jit(solution)/shard_map/ppermute | solution.py:24
  59.9 34.8 %collective-permute-start.4 = (bf16[256,2048]{1,0:T(8,128)(2,1)S(1)}, bf16[256,2048]{1,0:T(8,128)(2,1)S(1)}, u32[]{:S(2)}, u32[]{:S(2)}) collective-permute-start(bf16[256,2048]{1,0:T(8,128)(2,1)S(1)} %bitcast.110), channel_id=1, source_target_pairs={{0,1},{1,2},{2,3},{3,0},{4,5},{5,6},{6,7},{7,4},{8,9},{9,10},{10,1... | collective-permute-start | bytes 3145736 | tf_op jit(solution)/shard_map/ppermute | solution.py:23
  63.3 31.4 %collective-permute-start.5 = (bf16[256,2048]{1,0:T(8,128)(2,1)S(1)}, bf16[256,2048]{1,0:T(8,128)(2,1)S(1)}, u32[]{:S(2)}, u32[]{:S(2)}) collective-permute-start(bf16[256,2048]{1,0:T(8,128)(2,1)S(1)} %bitcast.111), channel_id=1, source_target_pairs={{0,3},{1,0},{2,1},{3,2},{4,7},{5,4},{6,5},{7,6},{8,11},{9,8},{10,9... | collective-permute-start | bytes 3145736 | tf_op jit(solution)/shard_map/ppermute | solution.py:24
  66.7 3.0 %copy-start.11 = (bf16[384,512]{0,1:T(8,128)(2,1)S(1)}, bf16[384,512]{0,1:T(8,128)(2,1)}, u32[]{:S(2)}) copy-start(bf16[384,512]{0,1:T(8,128)(2,1)} %copy-done.10) | copy-start | bytes 1179652
  67.8 26.0 %collective-permute-start.2 = (bf16[384,512]{0,1:T(8,128)(2,1)S(1)}, bf16[384,512]{0,1:T(8,128)(2,1)S(1)}, u32[]{:S(2)}, u32[]{:S(2)}) collective-permute-start(bf16[384,512]{0,1:T(8,128)(2,1)S(1)} %copy-done.9), channel_id=1, source_target_pairs={{0,64},{64,128},{128,192},{192,256},{256,320},{320,384},{384,448},... | collective-permute-start | bytes 1179656 | tf_op jit(solution)/shard_map/ppermute | solution.py:23
  69.7 24.9 %collective-permute-start.3 = (bf16[384,512]{0,1:T(8,128)(2,1)S(1)}, bf16[384,512]{0,1:T(8,128)(2,1)S(1)}, u32[]{:S(2)}, u32[]{:S(2)}) collective-permute-start(bf16[384,512]{0,1:T(8,128)(2,1)S(1)} %copy-done.11), channel_id=1, source_target_pairs={{0,448},{64,0},{128,64},{192,128},{256,192},{320,256},{384,320},{4... | collective-permute-start | bytes 1179656 | tf_op jit(solution)/shard_map/ppermute | solution.py:24
  94.7 31.1 %collective-permute-start.10 = (bf16[128,2048]{1,0:T(8,128)(2,1)S(1)}, bf16[128,2048]{1,0:T(8,128)(2,1)S(1)}, u32[]{:S(2)}, u32[]{:S(2)}) collective-permute-start(bf16[128,2048]{1,0:T(8,128)(2,1)S(1)} %slice.76), channel_id=1, source_target_pairs={{0,1},{1,2},{2,3},{3,0},{4,5},{5,6},{6,7},{7,4},{8,9},{9,10},{10,1... | collective-permute-start | bytes 1572872 | tf_op jit(solution)/shard_map/ppermute | solution.py:27
  97.0 28.8 %collective-permute-start.11 = (bf16[128,2048]{1,0:T(8,128)(2,1)S(1)}, bf16[128,2048]{1,0:T(8,128)(2,1)S(1)}, u32[]{:S(2)}, u32[]{:S(2)}) collective-permute-start(bf16[128,2048]{1,0:T(8,128)(2,1)S(1)} %slice.77), channel_id=1, source_target_pairs={{0,3},{1,0},{2,1},{3,2},{4,7},{5,4},{6,5},{7,6},{8,11},{9,8},{10,9... | collective-permute-start | bytes 1572872 | tf_op jit(solution)/shard_map/ppermute | solution.py:28
  101.3 17.5 %collective-permute-start.6 = (bf16[384,512]{0,1:T(8,128)(2,1)S(1)}, bf16[384,512]{0,1:T(8,128)(2,1)S(1)}, u32[]{:S(2)}, u32[]{:S(2)}) collective-permute-start(bf16[384,512]{0,1:T(8,128)(2,1)S(1)} %collective-permute-done.2), channel_id=1, source_target_pairs={{0,64},{64,128},{128,192},{192,256},{256,320},{320,384},{384,448},... | collective-permute-start | bytes 1179656 | tf_op jit(solution)/shard_map/ppermute | solution.py:23
  103.2 17.6 %collective-permute-start.7 = (bf16[384,512]{0,1:T(8,128)(2,1)S(1)}, bf16[384,512]{0,1:T(8,128)(2,1)S(1)}, u32[]{:S(2)}, u32[]{:S(2)}) collective-permute-start(bf16[384,512]{0,1:T(8,128)(2,1)S(1)} %collective-permute-done.3), channel_id=1, source_target_pairs={{0,448},{64,0},{128,64},{192,128},{256,192},{320,256},{384,320},{4... | collective-permute-start | bytes 1179656 | tf_op jit(solution)/shard_map/ppermute | solution.py:24
  118.8 10.2 %collective-permute-start.8 = (bf16[192,512]{0,1:T(8,128)(2,1)S(1)}, bf16[192,512]{0,1:T(8,128)(2,1)S(1)}, u32[]{:S(2)}, u32[]{:S(2)}) collective-permute-start(bf16[192,512]{0,1:T(8,128)(2,1)S(1)} %slice.96), channel_id=1, source_target_pairs={{0,64},{64,128},{128,192},{192,256},{256,320},{320,384},{384,448},... | collective-permute-start | bytes 589832 | tf_op jit(solution)/shard_map/ppermute | solution.py:27
  120.9 9.1 %collective-permute-start.9 = (bf16[192,512]{0,1:T(8,128)(2,1)S(1)}, bf16[192,512]{0,1:T(8,128)(2,1)S(1)}, u32[]{:S(2)}, u32[]{:S(2)}) collective-permute-start(bf16[192,512]{0,1:T(8,128)(2,1)S(1)} %slice.97), channel_id=1, source_target_pairs={{0,448},{64,0},{128,64},{192,128},{256,192},{320,256},{384,320},{4... | collective-permute-start | bytes 589832 | tf_op jit(solution)/shard_map/ppermute | solution.py:28
  125.9 4.3 %copy-start.2 = (bf16[4,256,2048]{2,1,0:T(8,128)(2,1)}, bf16[4,256,2048]{2,1,0:T(8,128)(2,1)S(1)}, u32[]{:S(2)}) copy-start(bf16[4,256,2048]{2,1,0:T(8,128)(2,1)S(1)} %fusion.29) | copy-start | bytes 12582916
  133.1 4.0 %copy-start.3 = (bf16[4,256,2048]{2,1,0:T(8,128)(2,1)S(1)}, bf16[4,256,2048]{2,1,0:T(8,128)(2,1)}, u32[]{:S(2)}) copy-start(bf16[4,256,2048]{2,1,0:T(8,128)(2,1)} %copy-done.2) | copy-start | bytes 12582916
  136.8 1.7 copy-start
  138.5 2.0 copy-start.14
  147.7 1.9 copy-start.1
  149.6 3.8 %copy-start.5 = (bf16[384,8,512]{0,2,1:T(8,128)(2,1)S(1)}, bf16[384,8,512]{0,2,1:T(8,128)(2,1)}, u32[]{:S(2)}) copy-start(bf16[384,8,512]{0,2,1:T(8,128)(2,1)} %copy-done.4) | copy-start | bytes 9437188
  149.6 3.8 %copy-start.6 = (f32[256,384]{1,0:T(8,128)S(1)}, f32[256,384]{1,0:T(8,128)}, u32[]{:S(2)}) copy-start(f32[256,384]{1,0:T(8,128)} %get-tuple-element.62) | copy-start | bytes 1179652
  149.6 3.8 %copy-start.15 = (f32[256,384]{1,0:T(8,128)S(1)}, f32[256,384]{1,0:T(8,128)}, u32[]{:S(2)}) copy-start(f32[256,384]{1,0:T(8,128)} %copy-done.14) | copy-start | bytes 1179652
  154.8 14.7 %collective-permute-start.12 = (bf16[128,2048]{0,1:T(8,128)(2,1)S(1)}, bf16[128,2048]{0,1:T(8,128)(2,1)S(1)}, u32[]{:S(2)}, u32[]{:S(2)}) collective-permute-start(bf16[128,2048]{0,1:T(8,128)(2,1)S(1)} %get-tuple-element.55), channel_id=1, source_target_pairs={{0,1},{1,2},{2,3},{3,0},{4,5},{5,6},{6,7},{7,4},{8,9},{9,10},{10,1... | collective-permute-start | bytes 1572872 | tf_op jit(solution)/shard_map/ppermute | solution.py:66
  158.0 13.7 %collective-permute-start.14 = (bf16[128,2048]{0,1:T(8,128)(2,1)S(1)}, bf16[128,2048]{0,1:T(8,128)(2,1)S(1)}, u32[]{:S(2)}, u32[]{:S(2)}) collective-permute-start(bf16[128,2048]{0,1:T(8,128)(2,1)S(1)} %get-tuple-element.56), channel_id=1, source_target_pairs={{0,3},{1,0},{2,1},{3,2},{4,7},{5,4},{6,5},{7,6},{8,11},{9,8},{10,9... | collective-permute-start | bytes 1572872 | tf_op jit(solution)/shard_map/ppermute | solution.py:67
  169.7 25.0 %collective-permute-start.13 = (bf16[256,2048]{0,1:T(8,128)(2,1)S(1)}, bf16[256,2048]{0,1:T(8,128)(2,1)S(1)}, u32[]{:S(2)}, u32[]{:S(2)}) collective-permute-start(bf16[256,2048]{0,1:T(8,128)(2,1)S(1)} %convert_element_type.119), channel_id=1, source_target_pairs={{0,1},{1,2},{2,3},{3,0},{4,5},{5,6},{6,7},{7,4},{8,9},{9,10},{10,1... | collective-permute-start | bytes 3145736 | tf_op jit(solution)/shard_map/ppermute | solution.py:76
  172.0 23.9 %collective-permute-start.15 = (bf16[256,2048]{0,1:T(8,128)(2,1)S(1)}, bf16[256,2048]{0,1:T(8,128)(2,1)S(1)}, u32[]{:S(2)}, u32[]{:S(2)}) collective-permute-start(bf16[256,2048]{0,1:T(8,128)(2,1)S(1)} %convert_element_type.125), channel_id=1, source_target_pairs={{0,3},{1,0},{2,1},{3,2},{4,7},{5,4},{6,5},{7,6},{8,11},{9,8},{10,9... | collective-permute-start | bytes 3145736 | tf_op jit(solution)/shard_map/ppermute | solution.py:77
  197.7 36.5 %all-to-all-start.1 = ((bf16[16,16,2048]{2,1,0:T(8,128)(2,1)}), bf16[16,16,2048]{2,1,0:T(8,128)(2,1)S(1)}, u32[]{:S(2)}, u32[]{:S(2)}) async-start(bf16[16,16,2048]{2,1,0:T(8,128)(2,1)} %bitcast.36), calls=%async_computation.1 | async-start | bytes 2097152 | tf_op jit(solution)/shard_map/all_to_all | solution.py:154
  (4 other events, 4.2 us)
Sparse Core Ops, SparseCore 0:
  10.8 102.4 all-gather.1
  147.8 47.0 reduce-scatter.1
